TPU v7x, 256 devices: a whole 4x4x8 slice. The times are simulated.
256 devices in a mesh: probe: 16 (over z, x_lo), slab: 16 (over x_hi, y, core).
Axes of the slice: x: 4 (x_hi: 2, x_lo: 2; x = x_hi * 2 + x_lo), y: 4, z: 8, core: 2. Of those that a mesh axis runs over, the one named last changes fastest.
Arguments:
- u_prev: float32 [512, 128, 128], P('slab', 'probe'), may hold values from -6 to 6
- u_cur: float32 [512, 128, 128], P('slab', 'probe'), may hold values from -6 to 6
- buoyancy: float32 [512, 128, 128], P('slab'), may hold values from 0.6 to 1.4
- kappa: float32 [512, 128, 128], P('slab'), may hold values from 0.06 to 0.14
- dkappa: float32 [16, 512, 128, 128], P('probe', 'slab'), may hold values from -0.3 to 0.3
- du_prev: float32 [16, 512, 128, 128], P('probe', 'slab'), may hold values from -6 to 6
- du_cur: float32 [16, 512, 128, 128], P('probe', 'slab'), may hold values from -6 to 6
Outputs:
- background_first: float32 [512, 128, 128], P('slab', 'probe')
- background_second: float32 [512, 128, 128], P('slab', 'probe')
- born_first: float32 [16, 512, 128, 128], P('probe', 'slab')
- born_second: float32 [16, 512, 128, 128], P('probe', 'slab')
All inputs are finite; a program needn't handle non-finite values.
Results may differ from a plain program's by a relative error of at most 0.00002.
Values sent between devices are 32-bit elements; how exact they have to be, the bound alone decides.
No kernel may reach another device: no remote copies, remote signals or barrier semaphores. Data moves between devices by JAX's collectives and lax.ppermute only.
A program may use at most 128 MiB of HBM per device.

v0:
```python
import jax
import jax.numpy as jnp
from jax import lax
from jax.sharding import PartitionSpec as P

SECOND = (-205.0 / 72.0, 8.0 / 5.0, -1.0 / 5.0, 8.0 / 315.0, -1.0 / 560.0)
FIRST = (0.0, 4.0 / 5.0, -1.0 / 5.0, 4.0 / 105.0, -1.0 / 280.0)


def extended_2(cells, sides, width):
    for axis, dim in sides:
        count = lax.axis_size(axis)
        ends = count - 1
        head = lax.slice_in_dim(cells, 0, width, axis=dim)
        tail = lax.slice_in_dim(cells, cells.shape[dim] - width, cells.shape[dim], axis=dim)
        cells = jnp.concatenate(
            [
                lax.ppermute(tail, axis, [(i, (i + 1) % count) for i in range(ends)]),
                cells,
                lax.ppermute(head, axis, [((i + 1) % count, i) for i in range(ends)]),
            ],
            axis=dim,
        )
    return cells


def derivatives(extended):
    array_rank = extended.ndim
    center = extended[..., 4:-4, 4:-4, 4:-4]
    cores = (
        extended[..., :, 4:-4, 4:-4],
        extended[..., 4:-4, :, 4:-4],
        extended[..., 4:-4, 4:-4, :],
    )
    second = 3.0 * SECOND[0] * center
    gradients = []
    for dimension in range(3):
        source = cores[dimension]
        axis_place = array_rank - 3 + dimension
        extent = center.shape[axis_place]
        gradient = jnp.zeros_like(center)
        for distance in range(1, 5):
            higher = lax.slice_in_dim(source, 4 + distance, 4 + distance + extent, axis=axis_place)
            deeper = lax.slice_in_dim(source, 4 - distance, 4 - distance + extent, axis=axis_place)
            second = second + SECOND[distance] * (higher + deeper)
            gradient = gradient + FIRST[distance] * (higher - deeper)
        gradients.append(gradient)
    return (second, gradients[0], gradients[1], gradients[2])


def operate(extended, buoyancy, slopes):
    second, depth_slope, cross_slope, lateral_slope = derivatives(extended)
    return (
        buoyancy * second
        + slopes[0] * depth_slope
        + slopes[1] * cross_slope
        + slopes[2] * lateral_slope
    )


def local(u_prev, u_cur, buoyancy, kappa, dkappa, du_prev, du_cur):
    strip = u_cur.shape[1]
    offset = lax.axis_index("probe") * strip
    rimmed = extended_2(buoyancy, (("slab", 0),), 4)
    buoyancy_widths = [(0, 0), (4, 4), (4, 4)]
    unused, slope_one, slope_two, slope_three = derivatives(jnp.pad(rimmed, buoyancy_widths))
    slopes = (slope_one, slope_two, slope_three)
    probe_kappa = dkappa[0]
    older = du_prev[0]
    newer = du_cur[0]
    born_states = []
    background_states = []

    def cut_strip(field):
        return lax.dynamic_slice_in_dim(field, offset, strip, 1)

    strip_buoyancy = cut_strip(buoyancy)
    strip_kappa = cut_strip(kappa)
    strip_slopes = (cut_strip(slope_one), cut_strip(slope_two), cut_strip(slope_three))
    background_old = u_prev
    background_new = u_cur
    for repeat in range(2):
        extended = extended_2(background_new, (("probe", 1), ("slab", 0)), 4)
        extended = jnp.pad(extended, [(0, 0), (0, 0), (4, 4)])
        image_strip = operate(extended, strip_buoyancy, strip_slopes)
        background_next = 2.0 * background_new - background_old + strip_kappa * image_strip
        image_whole = lax.all_gather(image_strip, "probe", axis=1, tiled=True)
        born_rimmed = extended_2(newer, (("slab", 0),), 4)
        born_image = operate(jnp.pad(born_rimmed, [(0, 0), (4, 4), (4, 4)]), buoyancy, slopes)
        born_next = 2.0 * newer - older + kappa * born_image + probe_kappa * image_whole
        background_states.append(background_next)
        born_states.append(born_next)
        background_old, background_new = (background_new, background_next)
        older, newer = (newer, born_next)
    return (background_states[0], background_states[1], born_states[0][None], born_states[1][None])


def solution(mesh):
    return jax.shard_map(
        local,
        mesh=mesh,
        in_specs=(
            P("slab", "probe", None),
            P("slab", "probe", None),
            P("slab", None, None),
            P("slab", None, None),
            P("probe", "slab", None, None),
            P("probe", "slab", None, None),
            P("probe", "slab", None, None),
        ),
        out_specs=(
            P("slab", "probe", None),
            P("slab", "probe", None),
            P("probe", "slab", None, None),
            P("probe", "slab", None, None),
        ),
        check_vma=False,
    )
```

profile of v0, /device:TPU:6, one launch (start us, length us, event | category | flops | bytes accessed | tf_op | source)
XLA Modules:
  0.0 289.8 jit_solution(7251088802055237671)
XLA Ops:
  8.3 5.2 %collective-permute-start.4 = (f32[4,128,128]{2,1,0:T(8,128)S(1)}, f32[4,128,128]{2,1,0:T(8,128)S(1)}, u32[]{:S(2)}, u32[]{:S(2)}) collective-permute-start(f32[4,128,128]{2,1,0:T(8,128)S(1)} %get-tuple-element.17), channel_id=1, source_target_pairs={{1,0},{2,1},{3,2},{4,3},{5,4},{6,5},{7,6},{8,7},{9,8},{10,9},{11,1... | collective-permute-start | bytes 786440 | tf_op jit(solution)/shard_map/ppermute | solution.py:20
  13.5 1.9 collective-permute-start.5
  16.5 1.9 collective-permute-start.1
  18.4 4.8 %collective-permute-start = (f32[32,4,128]{2,1,0:T(4,128)S(1)}, f32[32,4,128]{2,1,0:T(4,128)S(1)}, u32[]{:S(2)}, u32[]{:S(2)}) collective-permute-start(f32[32,4,128]{2,1,0:T(4,128)S(1)} %get-tuple-element.28), channel_id=1, source_target_pairs={{0,16},{16,32},{32,48},{48,64},{64,80},{80,96},{96,112},{112,128},... | collective-permute-start | bytes 196616 | tf_op jit(solution)/shard_map/ppermute | solution.py:18
  25.9 6.1 %collective-permute-start.2 = (f32[4,16,128]{2,1,0:T(8,128)S(1)}, f32[4,16,128]{2,1,0:T(8,128)S(1)}, u32[]{:S(2)}, u32[]{:S(2)}) collective-permute-start(f32[4,16,128]{2,1,0:T(8,128)S(1)} %get-tuple-element.25), channel_id=1, source_target_pairs={{1,0},{2,1},{3,2},{4,3},{5,4},{6,5},{7,6},{8,7},{9,8},{10,9},{11,1... | collective-permute-start | bytes 98312 | tf_op jit(solution)/shard_map/ppermute | solution.py:20
  32.0 1.9 collective-permute-start.3
  34.7 6.2 %collective-permute-done.3 = f32[4,16,128]{2,1,0:T(8,128)S(1)} collective-permute-done((f32[4,16,128]{2,1,0:T(8,128)S(1)}, f32[4,16,128]{2,1,0:T(8,128)S(1)}, u32[]{:S(2)}, u32[]{:S(2)}) %collective-permute-start.3) | collective-permute-done | bytes 32800 | tf_op jit(solution)/shard_map/ppermute | solution.py:18
  42.7 4.6 %select_maximum_fusion.4 = f32[40,136,136]{2,1,0:T(8,128)S(1)} fusion(f32[4,128,128]{2,1,0:T(8,128)} %copy-done.8, f32[32,128,128]{2,1,0:T(8,128)S(1)} %copy-done, f32[4,128,128]{2,1,0:T(8,128)} %collective-permute-done.5), kind=kLoop, calls=%fused_computation.8 | loop fusion | flops 11097600 | bytes 5580800 | tf_op jit(solution)/shard_map/concatenate | solution.py:16
  47.3 9.8 %fusion.23 = (f32[32,128,128]{2,1,0:T(8,128)}, f32[32,128,128]{2,1,0:T(8,128)}) fusion(f32[40,136,136]{2,1,0:T(8,128)S(1)} %select_maximum_fusion.4), kind=kLoop, calls=%fused_computation.66 | loop fusion | flops 11534336 | bytes 37748736 | tf_op jit(solution)/shard_map/add | solution.py:46
  58.1 2.1 constant_dynamic-update-slice_fusion.3
  60.3 2.0 fusion.30
  62.3 1.4 copy-done.2
  63.7 2.3 multiply_add_fusion.2
  67.1 1.9 collective-permute-start.10
  69.0 2.4 collective-permute-start.11
  71.5 1.9 collective-permute-start.7
  73.4 4.8 %collective-permute-start.6 = (f32[32,4,128]{2,1,0:T(4,128)S(1)}, f32[32,4,128]{2,1,0:T(4,128)S(1)}, u32[]{:S(2)}, u32[]{:S(2)}) collective-permute-start(f32[32,4,128]{2,1,0:T(4,128)S(1)} %get-tuple-element.26), channel_id=1, source_target_pairs={{0,16},{16,32},{32,48},{48,64},{64,80},{80,96},{96,112},{112,128},... | collective-permute-start | bytes 196616 | tf_op jit(solution)/shard_map/ppermute | solution.py:18
  78.6 2.4 collective-permute-done.6
  81.0 5.2 %collective-permute-start.8 = (f32[4,16,128]{2,1,0:T(8,128)S(1)}, f32[4,16,128]{2,1,0:T(8,128)S(1)}, u32[]{:S(2)}, u32[]{:S(2)}) collective-permute-start(f32[4,16,128]{2,1,0:T(8,128)S(1)} %get-tuple-element.21), channel_id=1, source_target_pairs={{1,0},{2,1},{3,2},{4,3},{5,4},{6,5},{7,6},{8,7},{9,8},{10,9},{11,1... | collective-permute-start | bytes 98312 | tf_op jit(solution)/shard_map/ppermute | solution.py:20
  86.3 2.1 collective-permute-start.9
  88.4 6.5 %select_maximum_fusion.2 = f32[40,136,136]{2,1,0:T(8,128)} fusion(f32[4,128,128]{2,1,0:T(8,128)S(1)} %collective-permute-done.10, f32[32,128,128]{2,1,0:T(8,128)} %bitcast.24, f32[4,128,128]{2,1,0:T(8,128)S(1)} %collective-permute-done.11), kind=kLoop, calls=%fused_computation.6 | loop fusion | flops 11097600 | bytes 5580800 | tf_op jit(solution)/shard_map/concatenate | solution.py:16
  94.9 1.2 collective-permute-done.9
  96.6 2.4 multiply_add_fusion
  99.0 53.2 %all-gather.3.cloned.1.call-done = f32[32,128,128]{2,1,0:T(8,128)} async-done(((f32[32,8,128]{2,1,0:T(8,128)}), f32[32,128,128]{2,1,0:T(8,128)}) %all-gather.3.cloned.1.call-update) | async-done | bytes 2097168 | tf_op jit(solution)/shard_map/all_gather | solution.py:87
  152.3 48.3 %fusion.36 = f32[32,128,128]{2,1,0:T(8,128)} fusion(f32[32,128,128]{2,1,0:T(8,128)} %all-gather.3.cloned.1.call-done, f32[1,32,128,128]{3,2,1,0:T(8,128)} %param.11, f32[1,32,128,128]{3,2,1,0:T(8,128)} %param.12, f32[32,128,128]{2,1,0:T(8,128)} %param.10, f32[32,128,128]{2,1,0:T(8,128)} %get-tuple-element.9, f32[32,128,128]{2,1,0:T(8,128)} %get-tuple-element.8, ...), kind=kLoop, calls=%fused_computation.88 | loop fusion | flops 47710208 | bytes 55050240 | tf_op jit(solution)/shard_map/add | solution.py:90
  201.6 1.9 collective-permute-start.12
  203.6 2.6 collective-permute-start.13
  206.2 6.6 %collective-permute-done.12 = f32[4,128,128]{2,1,0:T(8,128)S(1)} collective-permute-done((f32[4,128,128]{2,1,0:T(8,128)S(1)}, f32[4,128,128]{2,1,0:T(8,128)S(1)}, u32[]{:S(2)}, u32[]{:S(2)}) %collective-permute-start.12) | collective-permute-done | bytes 262176 | tf_op jit(solution)/shard_map/ppermute | solution.py:20
  212.8 5.7 %collective-permute-done.13 = f32[4,128,128]{2,1,0:T(8,128)S(1)} collective-permute-done((f32[4,128,128]{2,1,0:T(8,128)S(1)}, f32[4,128,128]{2,1,0:T(8,128)S(1)}, u32[]{:S(2)}, u32[]{:S(2)}) %collective-permute-start.13) | collective-permute-done | bytes 262176 | tf_op jit(solution)/shard_map/ppermute | solution.py:18
  218.5 6.5 %select_maximum_fusion = f32[40,136,136]{2,1,0:T(8,128)} fusion(f32[4,128,128]{2,1,0:T(8,128)S(1)} %collective-permute-done.12, f32[32,128,128]{2,1,0:T(8,128)} %fusion.36, f32[4,128,128]{2,1,0:T(8,128)S(1)} %collective-permute-done.13), kind=kLoop, calls=%fused_computation.4 | loop fusion | flops 11097600 | bytes 5580800 | tf_op jit(solution)/shard_map/concatenate | solution.py:16
  225.0 8.6 %all-gather.5.cloned.1.call-done = f32[32,128,128]{2,1,0:T(8,128)} async-done(((f32[32,8,128]{2,1,0:T(8,128)}), f32[32,128,128]{2,1,0:T(8,128)}) %all-gather.5.cloned.1.call-update) | async-done | bytes 2097168 | tf_op jit(solution)/shard_map/all_gather | solution.py:87
  233.6 49.3 %fusion.38 = f32[1,32,128,128]{3,2,1,0:T(8,128)} fusion(f32[32,128,128]{2,1,0:T(8,128)} %all-gather.5.cloned.1.call-done, f32[1,32,128,128]{3,2,1,0:T(8,128)} %param.11, f32[32,128,128]{2,1,0:T(8,128)} %param.10, f32[32,128,128]{2,1,0:T(8,128)} %get-tuple-element.9, f32[32,128,128]{2,1,0:T(8,128)} %get-tuple-element.8, f32[32,128,128]{2,1,0:T(8,128)} %copy-done.2, ...), kind=kLoop, calls=%fused_computation.90 | loop fusion | flops 47710208 | bytes 55050240 | tf_op jit(solution)/shard_map/broadcast_in_dim | solution.py:95
  (49 shorter events, 11.4 us)
Async XLA Ops:
  7.2 33.7 %copy-start.3 = (f32[32,8,128]{2,1,0:T(8,128)S(1)}, f32[32,8,128]{2,1,0:T(8,128)}, u32[]{:S(2)}) copy-start(f32[32,8,128]{2,1,0:T(8,128)} %param.8) | copy-start | bytes 393220
  7.2 145.1 %all-gather.3.cloned.1.call-start = ((), (), s32[]{:S(2)}) async-start(), calls=%async_computation | async-start | bytes 2228224 | tf_op jit(solution)/shard_map/all_gather | solution.py:87
  8.3 33.7 %collective-permute-start.4 = (f32[4,128,128]{2,1,0:T(8,128)S(1)}, f32[4,128,128]{2,1,0:T(8,128)S(1)}, u32[]{:S(2)}, u32[]{:S(2)}) collective-permute-start(f32[4,128,128]{2,1,0:T(8,128)S(1)} %get-tuple-element.17), channel_id=1, source_target_pairs={{1,0},{2,1},{3,2},{4,3},{5,4},{6,5},{7,6},{8,7},{9,8},{10,9},{11,1... | collective-permute-start | bytes 786440 | tf_op jit(solution)/shard_map/ppermute | solution.py:20
  13.5 29.2 %collective-permute-start.5 = (f32[4,128,128]{2,1,0:T(8,128)S(1)}, f32[4,128,128]{2,1,0:T(8,128)}, u32[]{:S(2)}, u32[]{:S(2)}) collective-permute-start(f32[4,128,128]{2,1,0:T(8,128)S(1)} %get-tuple-element.16), channel_id=1, source_target_pairs={{0,1},{1,2},{2,3},{3,4},{4,5},{5,6},{6,7},{7,8},{8,9},{9,10},{10,1... | collective-permute-start | bytes 786440 | tf_op jit(solution)/shard_map/ppermute | solution.py:18
  16.5 7.8 %collective-permute-start.1 = (f32[32,4,128]{2,1,0:T(4,128)S(1)}, f32[32,4,128]{2,1,0:T(4,128)S(1)}, u32[]{:S(2)}, u32[]{:S(2)}) collective-permute-start(f32[32,4,128]{2,1,0:T(4,128)S(1)} %get-tuple-element.29), channel_id=1, source_target_pairs={{16,0},{32,16},{48,32},{64,48},{80,64},{96,80},{112,96},{128,112},... | collective-permute-start | bytes 196616 | tf_op jit(solution)/shard_map/ppermute | solution.py:20
  18.4 6.7 %collective-permute-start = (f32[32,4,128]{2,1,0:T(4,128)S(1)}, f32[32,4,128]{2,1,0:T(4,128)S(1)}, u32[]{:S(2)}, u32[]{:S(2)}) collective-permute-start(f32[32,4,128]{2,1,0:T(4,128)S(1)} %get-tuple-element.28), channel_id=1, source_target_pairs={{0,16},{16,32},{32,48},{48,64},{64,80},{80,96},{96,112},{112,128},... | collective-permute-start | bytes 196616 | tf_op jit(solution)/shard_map/ppermute | solution.py:18
  23.2 19.5 %copy-start = (f32[32,128,128]{2,1,0:T(8,128)S(1)}, f32[32,128,128]{2,1,0:T(8,128)}, u32[]{:S(2)}) copy-start(f32[32,128,128]{2,1,0:T(8,128)} %param.9) | copy-start | bytes 6291460
  25.9 8.1 %collective-permute-start.2 = (f32[4,16,128]{2,1,0:T(8,128)S(1)}, f32[4,16,128]{2,1,0:T(8,128)S(1)}, u32[]{:S(2)}, u32[]{:S(2)}) collective-permute-start(f32[4,16,128]{2,1,0:T(8,128)S(1)} %get-tuple-element.25), channel_id=1, source_target_pairs={{1,0},{2,1},{3,2},{4,3},{5,4},{6,5},{7,6},{8,7},{9,8},{10,9},{11,1... | collective-permute-start | bytes 98312 | tf_op jit(solution)/shard_map/ppermute | solution.py:20
  32.0 8.8 %collective-permute-start.3 = (f32[4,16,128]{2,1,0:T(8,128)S(1)}, f32[4,16,128]{2,1,0:T(8,128)S(1)}, u32[]{:S(2)}, u32[]{:S(2)}) collective-permute-start(f32[4,16,128]{2,1,0:T(8,128)S(1)} %get-tuple-element.24), channel_id=1, source_target_pairs={{0,1},{1,2},{2,3},{3,4},{4,5},{5,6},{6,7},{7,8},{8,9},{9,10},{10,1... | collective-permute-start | bytes 98312 | tf_op jit(solution)/shard_map/ppermute | solution.py:18
  34.0 0.7 copy-start.6
  42.0 0.7 copy-start.8
  58.1 2.2 copy-start.9
  60.3 3.4 %copy-start.1 = (f32[32,128,128]{2,1,0:T(8,128)S(1)}, f32[32,128,128]{2,1,0:T(8,128)}, u32[]{:S(2)}) copy-start(f32[32,128,128]{2,1,0:T(8,128)} %param.9) | copy-start | bytes 6291460
  60.3 3.4 %copy-start.5 = (f32[36,16,128]{2,1,0:T(8,128)S(1)}, f32[36,16,128]{2,1,0:T(8,128)}, u32[]{:S(2)}) copy-start(f32[36,16,128]{2,1,0:T(8,128)} %get-tuple-element.23) | copy-start | bytes 884740
  60.3 3.4 %copy-start.7 = (f32[32,12,128]{2,1,0:T(8,128)S(1)}, f32[32,12,128]{2,1,0:T(8,128)}, u32[]{:S(2)}) copy-start(f32[32,12,128]{2,1,0:T(8,128)} %copy-done.6) | copy-start | bytes 589828
  60.3 3.4 %copy-start.10 = (f32[32,8,128]{2,1,0:T(8,128)S(1)}, f32[32,8,128]{2,1,0:T(8,128)}, u32[]{:S(2)}) copy-start(f32[32,8,128]{2,1,0:T(8,128)} %param.7) | copy-start | bytes 393220
  62.3 1.4 copy-start.2
  66.0 30.6 %copy-start.4 = (f32[32,8,128]{2,1,0:T(8,128)}, f32[32,8,128]{2,1,0:T(8,128)S(1)}, u32[]{:S(2)}) copy-start(f32[32,8,128]{2,1,0:T(8,128)S(1)} %get-tuple-element.6) | copy-start | bytes 393220
  66.0 167.6 %all-gather.5.cloned.1.call-start = ((), (), s32[]{:S(2)}) async-start(), calls=%async_computation.1 | async-start | bytes 2228224 | tf_op jit(solution)/shard_map/all_gather | solution.py:87
  67.1 21.3 %collective-permute-start.10 = (f32[4,128,128]{2,1,0:T(8,128)S(1)}, f32[4,128,128]{2,1,0:T(8,128)S(1)}, u32[]{:S(2)}, u32[]{:S(2)}) collective-permute-start(f32[4,128,128]{2,1,0:T(8,128)S(1)} %get-tuple-element.13), channel_id=1, source_target_pairs={{1,0},{2,1},{3,2},{4,3},{5,4},{6,5},{7,6},{8,7},{9,8},{10,9},{11,1... | collective-permute-start | bytes 786440 | tf_op jit(solution)/shard_map/ppermute | solution.py:20
  69.0 19.4 %collective-permute-start.11 = (f32[4,128,128]{2,1,0:T(8,128)S(1)}, f32[4,128,128]{2,1,0:T(8,128)S(1)}, u32[]{:S(2)}, u32[]{:S(2)}) collective-permute-start(f32[4,128,128]{2,1,0:T(8,128)S(1)} %get-tuple-element.12), channel_id=1, source_target_pairs={{0,1},{1,2},{2,3},{3,4},{4,5},{5,6},{6,7},{7,8},{8,9},{9,10},{10,1... | collective-permute-start | bytes 786440 | tf_op jit(solution)/shard_map/ppermute | solution.py:18
  71.5 7.1 %collective-permute-start.7 = (f32[32,4,128]{2,1,0:T(4,128)S(1)}, f32[32,4,128]{2,1,0:T(4,128)S(1)}, u32[]{:S(2)}, u32[]{:S(2)}) collective-permute-start(f32[32,4,128]{2,1,0:T(4,128)S(1)} %get-tuple-element.27), channel_id=1, source_target_pairs={{16,0},{32,16},{48,32},{64,48},{80,64},{96,80},{112,96},{128,112},... | collective-permute-start | bytes 196616 | tf_op jit(solution)/shard_map/ppermute | solution.py:20
  73.4 7.6 %collective-permute-start.6 = (f32[32,4,128]{2,1,0:T(4,128)S(1)}, f32[32,4,128]{2,1,0:T(4,128)S(1)}, u32[]{:S(2)}, u32[]{:S(2)}) collective-permute-start(f32[32,4,128]{2,1,0:T(4,128)S(1)} %get-tuple-element.26), channel_id=1, source_target_pairs={{0,16},{16,32},{32,48},{48,64},{64,80},{80,96},{96,112},{112,128},... | collective-permute-start | bytes 196616 | tf_op jit(solution)/shard_map/ppermute | solution.py:18
  81.0 13.9 %collective-permute-start.8 = (f32[4,16,128]{2,1,0:T(8,128)S(1)}, f32[4,16,128]{2,1,0:T(8,128)S(1)}, u32[]{:S(2)}, u32[]{:S(2)}) collective-permute-start(f32[4,16,128]{2,1,0:T(8,128)S(1)} %get-tuple-element.21), channel_id=1, source_target_pairs={{1,0},{2,1},{3,2},{4,3},{5,4},{6,5},{7,6},{8,7},{9,8},{10,9},{11,1... | collective-permute-start | bytes 98312 | tf_op jit(solution)/shard_map/ppermute | solution.py:20
  86.3 9.8 %collective-permute-start.9 = (f32[4,16,128]{2,1,0:T(8,128)S(1)}, f32[4,16,128]{2,1,0:T(8,128)S(1)}, u32[]{:S(2)}, u32[]{:S(2)}) collective-permute-start(f32[4,16,128]{2,1,0:T(8,128)S(1)} %get-tuple-element.20), channel_id=1, source_target_pairs={{0,1},{1,2},{2,3},{3,4},{4,5},{5,6},{6,7},{7,8},{8,9},{9,10},{10,1... | collective-permute-start | bytes 98312 | tf_op jit(solution)/shard_map/ppermute | solution.py:18
  201.6 11.1 %collective-permute-start.12 = (f32[4,128,128]{2,1,0:T(8,128)S(1)}, f32[4,128,128]{2,1,0:T(8,128)S(1)}, u32[]{:S(2)}, u32[]{:S(2)}) collective-permute-start(f32[4,128,128]{2,1,0:T(8,128)S(1)} %get-tuple-element.11), channel_id=1, source_target_pairs={{1,0},{2,1},{3,2},{4,3},{5,4},{6,5},{7,6},{8,7},{9,8},{10,9},{11,1... | collective-permute-start | bytes 786440 | tf_op jit(solution)/shard_map/ppermute | solution.py:20
  203.6 14.9 %collective-permute-start.13 = (f32[4,128,128]{2,1,0:T(8,128)S(1)}, f32[4,128,128]{2,1,0:T(8,128)S(1)}, u32[]{:S(2)}, u32[]{:S(2)}) collective-permute-start(f32[4,128,128]{2,1,0:T(8,128)S(1)} %get-tuple-element.10), channel_id=1, source_target_pairs={{0,1},{1,2},{2,3},{3,4},{4,5},{5,6},{6,7},{7,8},{8,9},{9,10},{10,1... | collective-permute-start | bytes 786440 | tf_op jit(solution)/shard_map/ppermute | solution.py:18
Sparse Core Ops, SparseCore 0:
  66.1 86.1 all-gather.2
  154.0 79.5 all-gather.4
where the time goes:
time: 291 us; the launch traced here: 290 us
  other arithmetic  134 us (46%)
  waiting for transfers between devices  85.2 us (29%)
  starting transfers between devices  45 us (15%)
  between operations  14.4 us (5%)
  local copies, waits for them, and re-layouts  11.3 us (4%)
    all_gather x2, waiting for transfers between devices, local(): image_whole = lax.all_gather(image_strip, 'probe', axis=1, tiled=True)  61.9 us
    broadcast_in_dim x1, other arithmetic, local(): born_states[1][None]  49.3 us
    add x1, other arithmetic, local(): 2.0 * newer - older + kappa * born_image + probe_kappa * image_whole  48.3 us
    ppermute x7, starting transfers between devices, extended_2(): lax.ppermute(head, axis, [((i + 1) % count, i) for i in range(ends)])  24.3 us
    ppermute x7, starting transfers between devices, extended_2(): lax.ppermute(tail, axis, [(i, (i + 1) % count) for i in range(ends)])  20.6 us
    concatenate x9, other arithmetic, extended_2(): jnp.concatenate([lax.ppermute(tail, axis, [(i, (i + 1) % count) for i in...  19.9 us
    ppermute x7, waiting for transfers between devices, extended_2(): lax.ppermute(tail, axis, [(i, (i + 1) % count) for i in range(ends)])  16.3 us
    add x2, other arithmetic, derivatives(): gradient = gradient + FIRST[distance] * (higher - deeper)  11.8 us
  transfers between devices with their start and end apart: 16, of which 9 were waited for; matrix products, arithmetic and copies ran while one was open for 24% of the time, Pallas kernels for 0%

commit v1 on v0

v1 whole, which is shorter than its diff:
```python
import functools

import numpy as np
import jax
import jax.numpy as jnp
from jax import lax
from jax.experimental import pallas as pl
from jax.experimental.pallas import tpu as pltpu
from jax.sharding import PartitionSpec as P

SECOND = (-205.0 / 72.0, 8.0 / 5.0, -1.0 / 5.0, 8.0 / 315.0, -1.0 / 560.0)
FIRST = (0.0, 4.0 / 5.0, -1.0 / 5.0, 4.0 / 105.0, -1.0 / 280.0)

BZ = 8
HALO = 4
INTERPRET = False
HI = lax.Precision.HIGHEST


def band_matrices(n):
    ms = np.zeros((n, n), np.float32)
    mg = np.zeros((n, n), np.float32)
    for i in range(n):
        for k in range(1, 5):
            for j, sign in ((i + k, 1.0), (i - k, -1.0)):
                if 0 <= j < n:
                    ms[i, j] = SECOND[k]
                    mg[i, j] = sign * FIRST[k]
    return ms, mg


def halo_depth(cells):
    count = lax.axis_size("slab")
    ends = count - 1
    head = cells[:HALO]
    tail = cells[cells.shape[0] - HALO:]
    return jnp.concatenate(
        [
            lax.ppermute(tail, "slab", [(i, i + 1) for i in range(ends)]),
            cells,
            lax.ppermute(head, "slab", [(i + 1, i) for i in range(ends)]),
        ],
        axis=0,
    )


def _ext(lo_ref, hi_ref, idx):
    if idx < BZ:
        return lo_ref[idx]
    return hi_ref[idx - BZ]


def _depth_terms(lo_ref, hi_ref, j):
    c = j + HALO
    centre = _ext(lo_ref, hi_ref, c)
    second = (3.0 * SECOND[0]) * centre
    grad = None
    for k in range(1, 5):
        up = _ext(lo_ref, hi_ref, c + k)
        down = _ext(lo_ref, hi_ref, c - k)
        second = second + SECOND[k] * (up + down)
        term = FIRST[k] * (up - down)
        grad = term if grad is None else grad + term
    return centre, second, grad


def _slope_kernel(lo_ref, hi_ref, mlane_ref, msub_ref, g0_ref, g1_ref, g2_ref):
    n = mlane_ref.shape[0]
    for j in range(BZ):
        centre, _, grad = _depth_terms(lo_ref, hi_ref, j)
        lane = jnp.dot(centre, mlane_ref[...], precision=HI, preferred_element_type=jnp.float32)
        sub = jnp.dot(msub_ref[...], centre, precision=HI, preferred_element_type=jnp.float32)
        g0_ref[j] = grad
        g1_ref[j] = sub[n:]
        g2_ref[j] = lane[:, n:]


def _op_kernel(flags, *refs):
    with_prev, with_img, want_image, want_step = flags
    refs = list(refs)
    lo_ref, hi_ref, b_ref, g0_ref, g1_ref, g2_ref, mlane_ref, msub_ref = refs[:8]
    rest = refs[8:]
    kappa_ref = prev_ref = dk_ref = img_ref = None
    if want_step:
        kappa_ref = rest.pop(0)
        if with_prev:
            prev_ref = rest.pop(0)
        if with_img:
            dk_ref = rest.pop(0)
            img_ref = rest.pop(0)
    outs = rest
    n = mlane_ref.shape[0]
    for j in range(BZ):
        centre, second, grad = _depth_terms(lo_ref, hi_ref, j)
        lane = jnp.dot(centre, mlane_ref[...], precision=HI, preferred_element_type=jnp.float32)
        sub = jnp.dot(msub_ref[...], centre, precision=HI, preferred_element_type=jnp.float32)
        second = second + sub[:n] + lane[:, :n]
        image = (
            b_ref[j] * second
            + g0_ref[j] * grad
            + g1_ref[j] * sub[n:]
            + g2_ref[j] * lane[:, n:]
        )
        at = 0
        if want_image:
            outs[at][j] = image
            at += 1
        if want_step:
            step = 2.0 * centre + kappa_ref[j] * image
            if with_prev:
                step = step - prev_ref[j]
            if with_img:
                step = step + dk_ref[j] * img_ref[j]
            outs[at][j] = step


def _specs(n, count):
    blk = pl.BlockSpec((BZ, n, n), lambda i: (i, 0, 0))
    return [blk] * count


def _ext_specs(n):
    return [
        pl.BlockSpec((BZ, n, n), lambda i: (i, 0, 0)),
        pl.BlockSpec((BZ, n, n), lambda i: (i + 1, 0, 0)),
    ]


def _mat_specs(n):
    return [
        pl.BlockSpec((n, 2 * n), lambda i: (0, 0)),
        pl.BlockSpec((2 * n, n), lambda i: (0, 0)),
    ]


def slopes_of(b_ext, mlane, msub):
    depth = b_ext.shape[0] - 2 * HALO
    n = b_ext.shape[1]
    shape = jax.ShapeDtypeStruct((depth, n, n), jnp.float32)
    return pl.pallas_call(
        _slope_kernel,
        grid=(depth // BZ,),
        in_specs=_ext_specs(n) + _mat_specs(n),
        out_specs=_specs(n, 3),
        out_shape=[shape] * 3,
        compiler_params=pltpu.CompilerParams(vmem_limit_bytes=48 * 1024 * 1024),
        interpret=INTERPRET,
    )(b_ext, b_ext, mlane, msub)


def apply_op(f_ext, b, slopes, mlane, msub, kappa=None, prev=None, dk=None, img=None, want_image=False):
    depth = f_ext.shape[0] - 2 * HALO
    n = f_ext.shape[1]
    want_step = kappa is not None
    with_prev = prev is not None
    with_img = img is not None
    args = [f_ext, f_ext, b, *slopes, mlane, msub]
    in_specs = _ext_specs(n) + _specs(n, 4) + _mat_specs(n)
    if want_step:
        extra = [kappa] + ([prev] if with_prev else []) + ([dk, img] if with_img else [])
        args += extra
        in_specs += _specs(n, len(extra))
    n_out = int(want_image) + int(want_step)
    shape = jax.ShapeDtypeStruct((depth, n, n), jnp.float32)
    outs = pl.pallas_call(
        functools.partial(_op_kernel, (with_prev, with_img, want_image, want_step)),
        grid=(depth // BZ,),
        in_specs=in_specs,
        out_specs=_specs(n, n_out),
        out_shape=[shape] * n_out,
        compiler_params=pltpu.CompilerParams(vmem_limit_bytes=48 * 1024 * 1024),
        interpret=INTERPRET,
    )(*args)
    return outs


def local(u_prev, u_cur, buoyancy, kappa, dkappa, du_prev, du_cur):
    n = buoyancy.shape[1]
    strip = u_cur.shape[1]
    offset = lax.axis_index("probe") * strip
    ms, mg = band_matrices(n)
    mlane = jnp.asarray(np.concatenate([ms, mg.T], axis=1))
    msub = jnp.asarray(np.concatenate([ms, mg], axis=0))

    u_cur_ext = lax.all_gather(halo_depth(u_cur), "probe", axis=1, tiled=True)
    u_prev_all = lax.all_gather(u_prev, "probe", axis=1, tiled=True)

    slopes = slopes_of(halo_depth(buoyancy), mlane, msub)

    probe_kappa = dkappa[0]
    older = du_prev[0]
    newer = du_cur[0]

    (partial_first,) = apply_op(halo_depth(newer), buoyancy, slopes, mlane, msub, kappa=kappa, prev=older)

    image_first, background_first = apply_op(
        u_cur_ext, buoyancy, slopes, mlane, msub, kappa=kappa, prev=u_prev_all, want_image=True
    )
    born_first = partial_first + probe_kappa * image_first

    (image_second,) = apply_op(halo_depth(background_first), buoyancy, slopes, mlane, msub, want_image=True)

    def cut_strip(field):
        return lax.dynamic_slice_in_dim(field, offset, strip, 1)

    background_first_strip = cut_strip(background_first)
    background_second = (
        2.0 * background_first_strip - u_cur + cut_strip(kappa) * cut_strip(image_second)
    )

    (born_second,) = apply_op(
        halo_depth(born_first), buoyancy, slopes, mlane, msub,
        kappa=kappa, prev=newer, dk=probe_kappa, img=image_second,
    )
    return background_first_strip, background_second, born_first[None], born_second[None]


def solution(mesh):
    return jax.shard_map(
        local,
        mesh=mesh,
        in_specs=(
            P("slab", "probe", None),
            P("slab", "probe", None),
            P("slab", None, None),
            P("slab", None, None),
            P("probe", "slab", None, None),
            P("probe", "slab", None, None),
            P("probe", "slab", None, None),
        ),
        out_specs=(
            P("slab", "probe", None),
            P("slab", "probe", None),
            P("probe", "slab", None, None),
            P("probe", "slab", None, None),
        ),
        check_vma=False,
    )
```

time: 291 us -> 253 us (0.87)
  the two profiles are of different devices: /device:TPU:6 before, /device:TPU:25 now
where the time goes in v1:
time: 253 us
  waiting for transfers between devices  110 us (43%)
  starting transfers between devices  58 us (23%)
  Pallas kernels  51.6 us (20%)
  between operations  14.3 us (6%)
  other arithmetic  11.5 us (5%)
  local copies, waits for them, and re-layouts  7.06 us (3%)
    all_gather x1, waiting for transfers between devices, local(): u_cur_ext = lax.all_gather(halo_depth(u_cur), 'probe', axis=1, tiled=True)  94.2 us
    pallas_call x4, Pallas kernels, apply_op(): pl.pallas_call(functools.partial(_op_kernel, (with_prev, with_img, want_i...  41.3 us
    ppermute x5, starting transfers between devices, halo_depth(): lax.ppermute(tail, 'slab', [(i, i + 1) for i in range(ends)])  38.5 us
    ppermute x5, starting transfers between devices, halo_depth(): lax.ppermute(head, 'slab', [(i + 1, i) for i in range(ends)])  19.5 us
    all_gather x1, waiting for transfers between devices, local(): u_prev_all = lax.all_gather(u_prev, 'probe', axis=1, tiled=True)  14.5 us
    pallas_call x1, Pallas kernels, slopes_of(): pl.pallas_call(_slope_kernel, grid=(depth // BZ,), in_specs=_ext_specs(n)...  10.3 us
    concatenate x5, other arithmetic, halo_depth(): jnp.concatenate([lax.ppermute(tail, 'slab', [(i, i + 1) for i in range(en...  9.08 us
  transfers between devices with their start and end apart: 12, of which 3 were waited for; matrix products, arithmetic and copies ran while one was open for 6% of the time, Pallas kernels for 12%

profile of v1, /device:TPU:25, one launch (start us, length us, event | category | flops | bytes accessed | tf_op | source)
XLA Modules:
  0.0 252.9 jit_solution(15562597011902521108)
XLA Ops:
  7.2 0.7 all-gather.5.cloned.1.call-update
  8.0 0.7 fusion.3
  8.7 2.6 %collective-permute-start.1 = (f32[4,8,128]{2,1,0:T(8,128)S(1)}, f32[4,8,128]{2,1,0:T(8,128)S(1)}, u32[]{:S(2)}, u32[]{:S(2)}) collective-permute-start(f32[4,8,128]{2,1,0:T(8,128)S(1)} %get-tuple-element.25), channel_id=1, source_target_pairs={{1,0},{2,1},{3,2},{4,3},{5,4},{6,5},{7,6},{8,7},{9,8},{10,9},{11,1... | collective-permute-start | bytes 49160 | tf_op jit(solution)/shard_map/ppermute | solution.py:41
  11.3 6.6 %collective-permute-start = (f32[4,8,128]{2,1,0:T(8,128)S(1)}, f32[4,8,128]{2,1,0:T(8,128)S(1)}, u32[]{:S(2)}, u32[]{:S(2)}) collective-permute-start(f32[4,8,128]{2,1,0:T(8,128)S(1)} %get-tuple-element.24), channel_id=1, source_target_pairs={{0,1},{1,2},{2,3},{3,4},{4,5},{5,6},{6,7},{7,8},{8,9},{9,10},{10,1... | collective-permute-start | bytes 49160 | tf_op jit(solution)/shard_map/ppermute | solution.py:39
  17.9 0.8 collective-permute-done
  18.7 1.6 pad_maximum_fusion.4
  20.3 1.9 fusion.2
  22.2 1.9 collective-permute-start.3
  24.1 7.8 %collective-permute-start.2 = (f32[4,128,128]{2,1,0:T(8,128)}, f32[4,128,128]{2,1,0:T(8,128)S(1)}, u32[]{:S(2)}, u32[]{:S(2)}) collective-permute-start(f32[4,128,128]{2,1,0:T(8,128)} %get-tuple-element.22), channel_id=1, source_target_pairs={{0,1},{1,2},{2,3},{3,4},{4,5},{5,6},{6,7},{7,8},{8,9},{9,10},{10,1... | collective-permute-start | bytes 786440 | tf_op jit(solution)/shard_map/ppermute | solution.py:39
  31.9 1.9 slice_bitcast_fusion.1
  33.8 1.9 collective-permute-start.7
  35.7 7.3 %collective-permute-start.6 = (f32[4,128,128]{2,1,0:T(8,128)}, f32[4,128,128]{2,1,0:T(8,128)S(1)}, u32[]{:S(2)}, u32[]{:S(2)}) collective-permute-start(f32[4,128,128]{2,1,0:T(8,128)} %get-tuple-element.18), channel_id=1, source_target_pairs={{0,1},{1,2},{2,3},{3,4},{4,5},{5,6},{6,7},{7,8},{8,9},{9,10},{10,1... | collective-permute-start | bytes 786440 | tf_op jit(solution)/shard_map/ppermute | solution.py:39
  43.0 1.8 pad_maximum_fusion.lo_ref.hi_ref
  44.9 10.3 %shard_map.120 = (f32[32,128,128]{2,1,0:T(8,128)S(1)}, f32[32,128,128]{2,1,0:T(8,128)S(1)}, f32[32,128,128]{2,1,0:T(8,128)}) custom-call(f32[40,128,128]{2,1,0:T(8,128)} %pad_maximum_fusion.lo_ref.hi_ref, f32[40,128,128]{2,1,0:T(8,128)} %pad_maximum_fusion.lo_ref.hi_ref, f32[128,256]{1,0:T(8,128)S(1)} %copy-done.8, f32[256,128]{1,0:T(8,128)S(1)} %copy-done.9), custom_call_target="tpu_custom_call" | custom-call | tf_op jit(solution)/shard_map/pallas_call | solution.py:140
  55.2 2.1 pad_maximum_fusion.2.refs_0_.refs_1_
  57.3 0.7 copy-done.4
  58.0 9.9 %shard_map.123 = f32[32,128,128]{2,1,0:T(8,128)S(1)} custom-call(f32[40,128,128]{2,1,0:T(8,128)} %pad_maximum_fusion.2.refs_0_.refs_1_, f32[40,128,128]{2,1,0:T(8,128)} %pad_maximum_fusion.2.refs_0_.refs_1_, f32[32,128,128]{2,1,0:T(8,128)S(1)} %copy-done, f32[32,128,128]{2,1,0:T(8,128)} %copy-done.2, f32[32,128,128]{2,1,0:T(8,128)} %copy-done.4, ...), custom_call_target="tpu_custom_call" | custom-call | tf_op jit(solution)/shard_map/pallas_call | solution.py:165
  67.9 1.3 copy-done.6
  69.2 14.5 %all-gather.5.cloned.1.call-done.refs_9_ = f32[32,128,128]{2,1,0:T(8,128)} async-done(((f32[32,8,128]{2,1,0:T(8,128)}), f32[32,128,128]{2,1,0:T(8,128)}) %all-gather.5.cloned.1.call-update) | async-done | bytes 2097168 | tf_op jit(solution)/shard_map/all_gather | solution.py:186
  83.7 94.2 %all-gather.3.cloned.1.call-done.refs_0_.refs_1_ = f32[40,128,128]{2,1,0:T(8,128)} async-done(((f32[40,8,128]{2,1,0:T(8,128)}), f32[40,128,128]{2,1,0:T(8,128)}) %all-gather.3.cloned.1.call-update) | async-done | bytes 2621456 | tf_op jit(solution)/shard_map/all_gather | solution.py:185
  177.9 10.4 %shard_map.121 = (f32[32,128,128]{2,1,0:T(8,128)S(1)}, f32[32,128,128]{2,1,0:T(8,128)S(1)}) custom-call(f32[40,128,128]{2,1,0:T(8,128)} %all-gather.3.cloned.1.call-done.refs_0_.refs_1_, f32[40,128,128]{2,1,0:T(8,128)} %all-gather.3.cloned.1.call-done.refs_0_.refs_1_, f32[32,128,128]{2,1,0:T(8,128)} %refs_2_.7, f32[32,128,128]{2,1,0:T(8,128)} %copy-done.2, ...), custom_call_target="tpu_custom_call" | custom-call | tf_op jit(solution)/shard_map/pallas_call | solution.py:165
  188.4 11.1 %collective-permute-start.5 = (f32[4,128,128]{2,1,0:T(8,128)S(1)}, f32[4,128,128]{2,1,0:T(8,128)S(1)}, u32[]{:S(2)}, u32[]{:S(2)}) collective-permute-start(f32[4,128,128]{2,1,0:T(8,128)S(1)} %get-tuple-element.21), channel_id=1, source_target_pairs={{1,0},{2,1},{3,2},{4,3},{5,4},{6,5},{7,6},{8,7},{9,8},{10,9},{11,1... | collective-permute-start | bytes 786440 | tf_op jit(solution)/shard_map/ppermute | solution.py:41
  199.6 9.3 %collective-permute-start.4 = (f32[4,128,128]{2,1,0:T(8,128)S(1)}, f32[4,128,128]{2,1,0:T(8,128)S(1)}, u32[]{:S(2)}, u32[]{:S(2)}) collective-permute-start(f32[4,128,128]{2,1,0:T(8,128)S(1)} %get-tuple-element.20), channel_id=1, source_target_pairs={{0,1},{1,2},{2,3},{3,4},{4,5},{5,6},{6,7},{7,8},{8,9},{9,10},{10,1... | collective-permute-start | bytes 786440 | tf_op jit(solution)/shard_map/ppermute | solution.py:39
  208.8 0.6 multiply_add_fusion
  209.5 1.9 collective-permute-start.9
  211.5 7.6 %collective-permute-start.8 = (f32[4,128,128]{2,1,0:T(8,128)S(1)}, f32[4,128,128]{2,1,0:T(8,128)S(1)}, u32[]{:S(2)}, u32[]{:S(2)}) collective-permute-start(f32[4,128,128]{2,1,0:T(8,128)S(1)} %get-tuple-element.16), channel_id=1, source_target_pairs={{0,1},{1,2},{2,3},{3,4},{4,5},{5,6},{6,7},{7,8},{8,9},{9,10},{10,1... | collective-permute-start | bytes 786440 | tf_op jit(solution)/shard_map/ppermute | solution.py:39
  219.1 1.8 pad_maximum_fusion.1.refs_0_.refs_1_
  220.9 9.6 %shard_map.122.refs_11_ = f32[32,128,128]{2,1,0:T(8,128)S(1)} custom-call(f32[40,128,128]{2,1,0:T(8,128)} %pad_maximum_fusion.1.refs_0_.refs_1_, f32[40,128,128]{2,1,0:T(8,128)} %pad_maximum_fusion.1.refs_0_.refs_1_, f32[32,128,128]{2,1,0:T(8,128)S(1)} %copy-done.1, f32[32,128,128]{2,1,0:T(8,128)} %copy-done.2, f32[32,128,128]{2,1,0:T(8,128)} %copy-done.4, ...), custom_call_target="tpu_custom_call" | custom-call | tf_op jit(solution)/shard_map/pallas_call | solution.py:165
  230.5 1.8 multiply_add_fusion.1
  232.3 1.8 pad_maximum_fusion.3.refs_0_.refs_1_
  234.2 0.5 copy-done.3
  234.6 11.4 %shard_map.124 = f32[32,128,128]{2,1,0:T(8,128)} custom-call(f32[40,128,128]{2,1,0:T(8,128)} %pad_maximum_fusion.3.refs_0_.refs_1_, f32[40,128,128]{2,1,0:T(8,128)} %pad_maximum_fusion.3.refs_0_.refs_1_, f32[32,128,128]{2,1,0:T(8,128)S(1)} %copy-done.1, f32[32,128,128]{2,1,0:T(8,128)S(1)} %copy-done.3, f32[32,128,128]{2,1,0:T(8,128)} %copy-done.4, ...), custom_call_target="tpu_custom_call" | custom-call | tf_op jit(solution)/shard_map/pallas_call | solution.py:165
  (39 shorter events, 0.3 us)
Async XLA Ops:
  7.2 35.9 %copy-start = (f32[32,128,128]{2,1,0:T(8,128)S(1)}, f32[32,128,128]{2,1,0:T(8,128)}, u32[]{:S(2)}) copy-start(f32[32,128,128]{2,1,0:T(8,128)} %refs_2_.7) | copy-start | bytes 6291460
  7.2 76.5 %all-gather.5.cloned.1.call-start = ((), (), s32[]{:S(2)}) async-start(), calls=%async_computation.1 | async-start | bytes 2228224 | tf_op jit(solution)/shard_map/all_gather | solution.py:186
  7.9 170.0 %all-gather.3.cloned.1.call-start = ((), (), s32[]{:S(2)}) async-start(), calls=%async_computation | async-start | bytes 2785280 | tf_op jit(solution)/shard_map/all_gather | solution.py:185
  8.7 9.2 %collective-permute-start.1 = (f32[4,8,128]{2,1,0:T(8,128)S(1)}, f32[4,8,128]{2,1,0:T(8,128)S(1)}, u32[]{:S(2)}, u32[]{:S(2)}) collective-permute-start(f32[4,8,128]{2,1,0:T(8,128)S(1)} %get-tuple-element.25), channel_id=1, source_target_pairs={{1,0},{2,1},{3,2},{4,3},{5,4},{6,5},{7,6},{8,7},{9,8},{10,9},{11,1... | collective-permute-start | bytes 49160 | tf_op jit(solution)/shard_map/ppermute | solution.py:41
  11.3 7.4 %collective-permute-start = (f32[4,8,128]{2,1,0:T(8,128)S(1)}, f32[4,8,128]{2,1,0:T(8,128)S(1)}, u32[]{:S(2)}, u32[]{:S(2)}) collective-permute-start(f32[4,8,128]{2,1,0:T(8,128)S(1)} %get-tuple-element.24), channel_id=1, source_target_pairs={{0,1},{1,2},{2,3},{3,4},{4,5},{5,6},{6,7},{7,8},{8,9},{9,10},{10,1... | collective-permute-start | bytes 49160 | tf_op jit(solution)/shard_map/ppermute | solution.py:39
  22.2 20.8 %collective-permute-start.3 = (f32[4,128,128]{2,1,0:T(8,128)}, f32[4,128,128]{2,1,0:T(8,128)S(1)}, u32[]{:S(2)}, u32[]{:S(2)}) collective-permute-start(f32[4,128,128]{2,1,0:T(8,128)} %get-tuple-element.23), channel_id=1, source_target_pairs={{1,0},{2,1},{3,2},{4,3},{5,4},{6,5},{7,6},{8,7},{9,8},{10,9},{11,1... | collective-permute-start | bytes 786440 | tf_op jit(solution)/shard_map/ppermute | solution.py:41
  24.1 18.9 %collective-permute-start.2 = (f32[4,128,128]{2,1,0:T(8,128)}, f32[4,128,128]{2,1,0:T(8,128)S(1)}, u32[]{:S(2)}, u32[]{:S(2)}) collective-permute-start(f32[4,128,128]{2,1,0:T(8,128)} %get-tuple-element.22), channel_id=1, source_target_pairs={{0,1},{1,2},{2,3},{3,4},{4,5},{5,6},{6,7},{7,8},{8,9},{9,10},{10,1... | collective-permute-start | bytes 786440 | tf_op jit(solution)/shard_map/ppermute | solution.py:39
  33.8 21.4 %collective-permute-start.7 = (f32[4,128,128]{2,1,0:T(8,128)}, f32[4,128,128]{2,1,0:T(8,128)S(1)}, u32[]{:S(2)}, u32[]{:S(2)}) collective-permute-start(f32[4,128,128]{2,1,0:T(8,128)} %get-tuple-element.19), channel_id=1, source_target_pairs={{1,0},{2,1},{3,2},{4,3},{5,4},{6,5},{7,6},{8,7},{9,8},{10,9},{11,1... | collective-permute-start | bytes 786440 | tf_op jit(solution)/shard_map/ppermute | solution.py:41
  35.7 19.5 %collective-permute-start.6 = (f32[4,128,128]{2,1,0:T(8,128)}, f32[4,128,128]{2,1,0:T(8,128)S(1)}, u32[]{:S(2)}, u32[]{:S(2)}) collective-permute-start(f32[4,128,128]{2,1,0:T(8,128)} %get-tuple-element.18), channel_id=1, source_target_pairs={{0,1},{1,2},{2,3},{3,4},{4,5},{5,6},{6,7},{7,8},{8,9},{9,10},{10,1... | collective-permute-start | bytes 786440 | tf_op jit(solution)/shard_map/ppermute | solution.py:39
  43.0 1.9 copy-start.8
  43.0 1.9 copy-start.9
  44.9 10.3 %copy-start.10 = (f32[1,32,128,128]{3,2,1,0:T(8,128)S(1)}, f32[1,32,128,128]{3,2,1,0:T(8,128)}, u32[]{:S(2)}) copy-start(f32[1,32,128,128]{3,2,1,0:T(8,128)} %param.15) | copy-start | bytes 6291460
  55.2 2.1 copy-start.2
  55.2 2.8 %copy-start.4 = (f32[32,128,128]{2,1,0:T(8,128)}, f32[32,128,128]{2,1,0:T(8,128)S(1)}, u32[]{:S(2)}) copy-start(f32[32,128,128]{2,1,0:T(8,128)S(1)} %get-tuple-element.10.refs_4_) | copy-start | bytes 6291460
  67.9 1.3 copy-start.6
  177.9 30.9 %copy-start.7 = (f32[32,128,128]{2,1,0:T(8,128)S(1)}, f32[32,128,128]{2,1,0:T(8,128)}, u32[]{:S(2)}) copy-start(f32[32,128,128]{2,1,0:T(8,128)} %copy-done.6) | copy-start | bytes 6291460
  177.9 30.9 %copy-start.12 = (f32[1,32,128,128]{3,2,1,0:T(8,128)S(1)}, f32[1,32,128,128]{3,2,1,0:T(8,128)}, u32[]{:S(2)}) copy-start(f32[1,32,128,128]{3,2,1,0:T(8,128)} %param.13) | copy-start | bytes 6291460
  188.4 30.7 %collective-permute-start.5 = (f32[4,128,128]{2,1,0:T(8,128)S(1)}, f32[4,128,128]{2,1,0:T(8,128)S(1)}, u32[]{:S(2)}, u32[]{:S(2)}) collective-permute-start(f32[4,128,128]{2,1,0:T(8,128)S(1)} %get-tuple-element.21), channel_id=1, source_target_pairs={{1,0},{2,1},{3,2},{4,3},{5,4},{6,5},{7,6},{8,7},{9,8},{10,9},{11,1... | collective-permute-start | bytes 786440 | tf_op jit(solution)/shard_map/ppermute | solution.py:41
  199.6 19.5 %collective-permute-start.4 = (f32[4,128,128]{2,1,0:T(8,128)S(1)}, f32[4,128,128]{2,1,0:T(8,128)S(1)}, u32[]{:S(2)}, u32[]{:S(2)}) collective-permute-start(f32[4,128,128]{2,1,0:T(8,128)S(1)} %get-tuple-element.20), channel_id=1, source_target_pairs={{0,1},{1,2},{2,3},{3,4},{4,5},{5,6},{6,7},{7,8},{8,9},{9,10},{10,1... | collective-permute-start | bytes 786440 | tf_op jit(solution)/shard_map/ppermute | solution.py:39
  209.5 22.9 %copy-start.11 = (f32[32,128,128]{2,1,0:T(8,128)}, f32[32,128,128]{2,1,0:T(8,128)S(1)}, u32[]{:S(2)}) copy-start(f32[32,128,128]{2,1,0:T(8,128)S(1)} %multiply_add_fusion) | copy-start | bytes 6291460
  209.5 22.8 %collective-permute-start.9 = (f32[4,128,128]{2,1,0:T(8,128)S(1)}, f32[4,128,128]{2,1,0:T(8,128)S(1)}, u32[]{:S(2)}, u32[]{:S(2)}) collective-permute-start(f32[4,128,128]{2,1,0:T(8,128)S(1)} %get-tuple-element.17), channel_id=1, source_target_pairs={{1,0},{2,1},{3,2},{4,3},{5,4},{6,5},{7,6},{8,7},{9,8},{10,9},{11,1... | collective-permute-start | bytes 786440 | tf_op jit(solution)/shard_map/ppermute | solution.py:41
  211.5 9.4 %copy-start.1 = (f32[32,128,128]{2,1,0:T(8,128)S(1)}, f32[32,128,128]{2,1,0:T(8,128)}, u32[]{:S(2)}) copy-start(f32[32,128,128]{2,1,0:T(8,128)} %refs_2_.7) | copy-start | bytes 6291460
  211.5 20.9 %collective-permute-start.8 = (f32[4,128,128]{2,1,0:T(8,128)S(1)}, f32[4,128,128]{2,1,0:T(8,128)S(1)}, u32[]{:S(2)}, u32[]{:S(2)}) collective-permute-start(f32[4,128,128]{2,1,0:T(8,128)S(1)} %get-tuple-element.16), channel_id=1, source_target_pairs={{0,1},{1,2},{2,3},{3,4},{4,5},{5,6},{6,7},{7,8},{8,9},{9,10},{10,1... | collective-permute-start | bytes 786440 | tf_op jit(solution)/shard_map/ppermute | solution.py:39
  220.9 9.6 %copy-start.13 = (f32[32,8,128]{2,1,0:T(8,128)S(1)}, f32[32,8,128]{2,1,0:T(8,128)}, u32[]{:S(2)}) copy-start(f32[32,8,128]{2,1,0:T(8,128)} %param.10) | copy-start | bytes 393220
  230.5 3.7 %copy-start.5 = (f32[32,128,128]{2,1,0:T(8,128)}, f32[32,128,128]{2,1,0:T(8,128)S(1)}, u32[]{:S(2)}) copy-start(f32[32,128,128]{2,1,0:T(8,128)S(1)} %shard_map.122.refs_11_) | copy-start | bytes 6291460
  232.3 2.3 copy-start.3
Sparse Core Ops, SparseCore 0:
  9.7 73.9 all-gather.4
  85.4 92.4 all-gather.2

commit v2 on v1

--- a/solution.py
+++ b/solution.py
@@ -42,6 +42,34 @@
         ],
         axis=0,
     )
+
+
+def ring_gather(x):
+    n = lax.axis_size("probe")
+    rings = n // 2
+    p = lax.axis_index("probe")
+    partner = lax.ppermute(x, "probe", [(i, i ^ 1) for i in range(n)])
+    pair = jnp.where(p % 2 == 0, jnp.concatenate([x, partner], 1), jnp.concatenate([partner, x], 1))
+    ahead = [(i, (i + 2) % n) for i in range(n)]
+    behind = [(i, (i - 2) % n) for i in range(n)]
+    by_offset = {0: pair}
+    fwd = pair
+    bwd = pair
+    half = rings // 2
+    for k in range(1, half):
+        fwd = lax.ppermute(fwd, "probe", ahead)
+        bwd = lax.ppermute(bwd, "probe", behind)
+        by_offset[-k % rings] = fwd
+        by_offset[k] = bwd
+    cut = x.shape[0] // 2
+    far = jnp.concatenate(
+        [lax.ppermute(fwd[:cut], "probe", ahead), lax.ppermute(bwd[cut:], "probe", behind)], axis=0
+    )
+    by_offset[half] = far
+    ordered = jnp.concatenate([by_offset[d] for d in range(rings)] * 2, axis=1)
+    width = pair.shape[1]
+    start = ((rings - p // 2) % rings) * width
+    return lax.dynamic_slice_in_dim(ordered, start, rings * width, 1)
 
 
 def _ext(lo_ref, hi_ref, idx):
@@ -182,8 +210,10 @@
     mlane = jnp.asarray(np.concatenate([ms, mg.T], axis=1))
     msub = jnp.asarray(np.concatenate([ms, mg], axis=0))
 
-    u_cur_ext = lax.all_gather(halo_depth(u_cur), "probe", axis=1, tiled=True)
-    u_prev_all = lax.all_gather(u_prev, "probe", axis=1, tiled=True)
+    depth = u_cur.shape[0]
+    both = ring_gather(jnp.concatenate([halo_depth(u_cur), u_prev], axis=0))
+    u_cur_ext = both[: depth + 2 * HALO]
+    u_prev_all = both[depth + 2 * HALO:]
 
     slopes = slopes_of(halo_depth(buoyancy), mlane, msub)
 

time: 253 us -> 172 us (0.68)
  the two profiles are of different devices: /device:TPU:25 before, /device:TPU:6 now
where the time goes in v2:
time: 172 us; the launch traced here: 171 us
  starting transfers between devices  63.3 us (37%)
  Pallas kernels  52.4 us (30%)
  waiting for transfers between devices  26.3 us (15%)
  local copies, waits for them, and re-layouts  14.7 us (9%)
  other arithmetic  13.2 us (8%)
    pallas_call x4, Pallas kernels, apply_op(): pl.pallas_call(functools.partial(_op_kernel, (with_prev, with_img, want_i...  42.1 us
    ppermute x5, starting transfers between devices, halo_depth(): lax.ppermute(head, 'slab', [(i + 1, i) for i in range(ends)])  36.4 us
    ppermute x3, starting transfers between devices, ring_gather(): bwd = lax.ppermute(bwd, 'probe', behind)  12.8 us
    pallas_call x1, Pallas kernels, slopes_of(): pl.pallas_call(_slope_kernel, grid=(depth // BZ,), in_specs=_ext_specs(n)...  10.3 us
    ppermute x3, waiting for transfers between devices, ring_gather(): bwd = lax.ppermute(bwd, 'probe', behind)  10.1 us
    concatenate x4, other arithmetic, halo_depth(): jnp.concatenate([lax.ppermute(tail, 'slab', [(i, i + 1) for i in range(en...  9.67 us
    ppermute x5, starting transfers between devices, halo_depth(): lax.ppermute(tail, 'slab', [(i, i + 1) for i in range(ends)])  9.57 us
    unnamed x57, local copies, waits for them, and re-layouts  6.71 us
  transfers between devices with their start and end apart: 19, of which 5 were waited for; matrix products, arithmetic and copies ran while one was open for 9% of the time, Pallas kernels for 18%

profile of v2, /device:TPU:6, one launch (start us, length us, event | category | flops | bytes accessed | tf_op | source)
XLA Modules:
  0.0 171.2 jit_solution(2333721458170054500)
XLA Ops:
  1.5 1.9 %collective-permute-start = (f32[4,8,128]{2,1,0:T(8,128)S(1)}, f32[4,8,128]{2,1,0:T(8,128)S(1)}, u32[]{:S(2)}, u32[]{:S(2)}) collective-permute-start(f32[4,8,128]{2,1,0:T(8,128)S(1)} %get-tuple-element.27), channel_id=1, source_target_pairs={{0,1},{1,2},{2,3},{3,4},{4,5},{5,6},{6,7},{7,8},{8,9},{9,10},{10,1... | collective-permute-start | bytes 49160 | tf_op jit(solution)/shard_map/ppermute | solution.py:39
  3.4 7.3 %collective-permute-start.1 = (f32[4,8,128]{2,1,0:T(8,128)S(1)}, f32[4,8,128]{2,1,0:T(8,128)S(1)}, u32[]{:S(2)}, u32[]{:S(2)}) collective-permute-start(f32[4,8,128]{2,1,0:T(8,128)S(1)} %get-tuple-element.26), channel_id=1, source_target_pairs={{1,0},{2,1},{3,2},{4,3},{5,4},{6,5},{7,6},{8,7},{9,8},{10,9},{11,1... | collective-permute-start | bytes 49160 | tf_op jit(solution)/shard_map/ppermute | solution.py:41
  14.0 6.3 %collective-permute-done.2 = f32[72,8,128]{2,1,0:T(8,128)S(1)} collective-permute-done((f32[72,8,128]{2,1,0:T(8,128)S(1)}, f32[72,8,128]{2,1,0:T(8,128)S(1)}, u32[]{:S(2)}, u32[]{:S(2)}) %collective-permute-start.2) | collective-permute-done | bytes 294944 | tf_op jit(solution)/shard_map/ppermute | solution.py:51
  21.2 5.9 %collective-permute-start.3 = (f32[72,16,128]{2,1,0:T(8,128)S(1)}, f32[72,16,128]{2,1,0:T(8,128)S(1)}, u32[]{:S(2)}, u32[]{:S(2)}) collective-permute-start(f32[72,16,128]{2,1,0:T(8,128)S(1)} %get-tuple-element.17), channel_id=1, source_target_pairs={{0,224},{16,240},{32,0},{48,16},{64,32},{80,48},{96,64},{112,80},{... | collective-permute-start | bytes 1769480 | tf_op jit(solution)/shard_map/ppermute | solution.py:61
  27.0 10.1 %collective-permute-done.3 = f32[72,16,128]{2,1,0:T(8,128)S(1)} collective-permute-done((f32[72,16,128]{2,1,0:T(8,128)S(1)}, f32[72,16,128]{2,1,0:T(8,128)S(1)}, u32[]{:S(2)}, u32[]{:S(2)}) %collective-permute-start.3) | collective-permute-done | bytes 589856 | tf_op jit(solution)/shard_map/ppermute | solution.py:61
  37.1 3.7 %collective-permute-start.4 = (f32[72,16,128]{2,1,0:T(8,128)S(1)}, f32[72,16,128]{2,1,0:T(8,128)}, u32[]{:S(2)}, u32[]{:S(2)}) collective-permute-start(f32[72,16,128]{2,1,0:T(8,128)S(1)} %collective-permute-done.3), channel_id=1, source_target_pairs={{0,224},{16,240},{32,0},{48,16},{64,32},{80,48},{96,64},{112,80},{... | collective-permute-start | bytes 1769480 | tf_op jit(solution)/shard_map/ppermute | solution.py:61
  41.6 1.9 %collective-permute-start.11 = (f32[4,128,128]{2,1,0:T(8,128)S(1)}, f32[4,128,128]{2,1,0:T(8,128)S(1)}, u32[]{:S(2)}, u32[]{:S(2)}) collective-permute-start(f32[4,128,128]{2,1,0:T(8,128)S(1)} %get-tuple-element.24), channel_id=1, source_target_pairs={{0,1},{1,2},{2,3},{3,4},{4,5},{5,6},{6,7},{7,8},{8,9},{9,10},{10,1... | collective-permute-start | bytes 786440 | tf_op jit(solution)/shard_map/ppermute | solution.py:39
  43.5 7.3 %collective-permute-start.12 = (f32[4,128,128]{2,1,0:T(8,128)}, f32[4,128,128]{2,1,0:T(8,128)}, u32[]{:S(2)}, u32[]{:S(2)}) collective-permute-start(f32[4,128,128]{2,1,0:T(8,128)} %get-tuple-element.25), channel_id=1, source_target_pairs={{1,0},{2,1},{3,2},{4,3},{5,4},{6,5},{7,6},{8,7},{9,8},{10,9},{11,1... | collective-permute-start | bytes 786440 | tf_op jit(solution)/shard_map/ppermute | solution.py:41
  50.8 3.2 %collective-permute-start.5 = (f32[72,16,128]{2,1,0:T(8,128)}, f32[72,16,128]{2,1,0:T(8,128)S(1)}, u32[]{:S(2)}, u32[]{:S(2)}) collective-permute-start(f32[72,16,128]{2,1,0:T(8,128)} %collective-permute-done.4), channel_id=1, source_target_pairs={{0,224},{16,240},{32,0},{48,16},{64,32},{80,48},{96,64},{112,80},{... | collective-permute-start | bytes 1769480 | tf_op jit(solution)/shard_map/ppermute | solution.py:61
  54.2 1.9 %slice_bitcast_fusion.1 = (f32[4,128,128]{2,1,0:T(8,128)}, f32[4,128,128]{2,1,0:T(8,128)}) fusion(f32[1,32,128,128]{3,2,1,0:T(8,128)} %param.15), kind=kLoop, calls=%fused_computation.10 | loop fusion | bytes 1048576 | tf_op jit(solution)/shard_map/slice | solution.py:36
  56.0 1.9 %collective-permute-start.15 = (f32[4,128,128]{2,1,0:T(8,128)}, f32[4,128,128]{2,1,0:T(8,128)}, u32[]{:S(2)}, u32[]{:S(2)}) collective-permute-start(f32[4,128,128]{2,1,0:T(8,128)} %get-tuple-element.20), channel_id=1, source_target_pairs={{0,1},{1,2},{2,3},{3,4},{4,5},{5,6},{6,7},{7,8},{8,9},{9,10},{10,1... | collective-permute-start | bytes 786440 | tf_op jit(solution)/shard_map/ppermute | solution.py:39
  57.9 7.3 %collective-permute-start.16 = (f32[4,128,128]{2,1,0:T(8,128)}, f32[4,128,128]{2,1,0:T(8,128)}, u32[]{:S(2)}, u32[]{:S(2)}) collective-permute-start(f32[4,128,128]{2,1,0:T(8,128)} %get-tuple-element.21), channel_id=1, source_target_pairs={{1,0},{2,1},{3,2},{4,3},{5,4},{6,5},{7,6},{8,7},{9,8},{10,9},{11,1... | collective-permute-start | bytes 786440 | tf_op jit(solution)/shard_map/ppermute | solution.py:41
  65.3 2.8 %pad_maximum_fusion.lo_ref.hi_ref = f32[40,128,128]{2,1,0:T(8,128)} fusion(f32[4,128,128]{2,1,0:T(8,128)} %collective-permute-done.12, f32[32,128,128]{2,1,0:T(8,128)S(1)} %copy-done, f32[4,128,128]{2,1,0:T(8,128)S(1)} %collective-permute-done.11), kind=kLoop, calls=%fused_computation | loop fusion | flops 1310720 | bytes 5242880 | tf_op jit(solution)/shard_map/concatenate | solution.py:37
  68.1 10.3 %shard_map.120 = (f32[32,128,128]{2,1,0:T(8,128)S(1)}, f32[32,128,128]{2,1,0:T(8,128)S(1)}, f32[32,128,128]{2,1,0:T(8,128)}) custom-call(f32[40,128,128]{2,1,0:T(8,128)} %pad_maximum_fusion.lo_ref.hi_ref, f32[40,128,128]{2,1,0:T(8,128)} %pad_maximum_fusion.lo_ref.hi_ref, f32[128,256]{1,0:T(8,128)S(1)} %copy-done.6, f32[256,128]{1,0:T(8,128)S(1)} %copy-done.7), custom_call_target="tpu_custom_call" | custom-call | tf_op jit(solution)/shard_map/pallas_call | solution.py:168
  78.5 3.3 %pad_maximum_fusion.2.refs_0_.refs_1_ = f32[40,128,128]{2,1,0:T(8,128)} fusion(f32[4,128,128]{2,1,0:T(8,128)} %collective-permute-done.16, f32[32,128,128]{2,1,0:T(8,128)S(1)} %bitcast.11, f32[4,128,128]{2,1,0:T(8,128)} %collective-permute-done.15), kind=kLoop, calls=%fused_computation.2 | loop fusion | flops 1310720 | bytes 5242880 | tf_op jit(solution)/shard_map/concatenate | solution.py:37
  81.8 10.7 %shard_map.123 = f32[32,128,128]{2,1,0:T(8,128)S(1)} custom-call(f32[40,128,128]{2,1,0:T(8,128)} %pad_maximum_fusion.2.refs_0_.refs_1_, f32[40,128,128]{2,1,0:T(8,128)} %pad_maximum_fusion.2.refs_0_.refs_1_, f32[32,128,128]{2,1,0:T(8,128)S(1)} %copy-done, f32[32,128,128]{2,1,0:T(8,128)} %copy-done.2, f32[32,128,128]{2,1,0:T(8,128)} %copy-done.4, ...), custom_call_target="tpu_custom_call" | custom-call | tf_op jit(solution)/shard_map/pallas_call | solution.py:193
  92.6 3.3 %collective-permute-start.10 = (f32[36,16,128]{2,1,0:T(8,128)S(1)}, f32[36,16,128]{2,1,0:T(8,128)S(1)}, u32[]{:S(2)}, u32[]{:S(2)}) collective-permute-start(f32[36,16,128]{2,1,0:T(8,128)S(1)} %slice.65), channel_id=1, source_target_pairs={{0,224},{16,240},{32,0},{48,16},{64,32},{80,48},{96,64},{112,80},{... | collective-permute-start | bytes 884744 | tf_op jit(solution)/shard_map/ppermute | solution.py:66
  96.3 1.1 constant_dynamic-update-slice_fusion.15
  97.5 5.7 %collective-permute-done.10 = f32[36,16,128]{2,1,0:T(8,128)S(1)} collective-permute-done((f32[36,16,128]{2,1,0:T(8,128)S(1)}, f32[36,16,128]{2,1,0:T(8,128)S(1)}, u32[]{:S(2)}, u32[]{:S(2)}) %collective-permute-start.10) | collective-permute-done | bytes 294944 | tf_op jit(solution)/shard_map/ppermute | solution.py:66
  103.2 3.7 %collective-permute-done.9 = f32[36,16,128]{2,1,0:T(8,128)S(1)} collective-permute-done((f32[36,16,128]{2,1,0:T(8,128)S(1)}, f32[36,16,128]{2,1,0:T(8,128)S(1)}, u32[]{:S(2)}, u32[]{:S(2)}) %collective-permute-start.9) | collective-permute-done | bytes 294944 | tf_op jit(solution)/shard_map/ppermute | solution.py:66
  111.2 1.8 %constant_dynamic-slice_fusion.refs_0_.refs_1_ = f32[40,128,128]{2,1,0:T(8,128)} fusion(f32[72,256,128]{2,1,0:T(8,128)S(1)} %constant_dynamic-update-slice_fusion.4, s32[]{:T(128)S(6)} %select_n.36), kind=kLoop, calls=%fused_computation.30 | loop fusion | bytes 5242884 | tf_op jit(solution)/shard_map/slice | solution.py:215
  113.0 1.5 constant_dynamic-slice_fusion.2.refs_9_
  114.6 10.4 %shard_map.121 = (f32[32,128,128]{2,1,0:T(8,128)S(1)}, f32[32,128,128]{2,1,0:T(8,128)S(1)}) custom-call(f32[40,128,128]{2,1,0:T(8,128)} %constant_dynamic-slice_fusion.refs_0_.refs_1_, f32[40,128,128]{2,1,0:T(8,128)} %constant_dynamic-slice_fusion.refs_0_.refs_1_, f32[32,128,128]{2,1,0:T(8,128)} %refs_2_.7, f32[32,128,128]{2,1,0:T(8,128)} %copy-done.2, ...), custom_call_target="tpu_custom_call" | custom-call | tf_op jit(solution)/shard_map/pallas_call | solution.py:193
  125.0 1.9 %collective-permute-start.13 = (f32[4,128,128]{2,1,0:T(8,128)S(1)}, f32[4,128,128]{2,1,0:T(8,128)S(1)}, u32[]{:S(2)}, u32[]{:S(2)}) collective-permute-start(f32[4,128,128]{2,1,0:T(8,128)S(1)} %get-tuple-element.22), channel_id=1, source_target_pairs={{0,1},{1,2},{2,3},{3,4},{4,5},{5,6},{6,7},{7,8},{8,9},{9,10},{10,1... | collective-permute-start | bytes 786440 | tf_op jit(solution)/shard_map/ppermute | solution.py:39
  126.9 7.3 %collective-permute-start.14 = (f32[4,128,128]{2,1,0:T(8,128)S(1)}, f32[4,128,128]{2,1,0:T(8,128)S(1)}, u32[]{:S(2)}, u32[]{:S(2)}) collective-permute-start(f32[4,128,128]{2,1,0:T(8,128)S(1)} %get-tuple-element.23), channel_id=1, source_target_pairs={{1,0},{2,1},{3,2},{4,3},{5,4},{6,5},{7,6},{8,7},{9,8},{10,9},{11,1... | collective-permute-start | bytes 786440 | tf_op jit(solution)/shard_map/ppermute | solution.py:41
  134.9 1.9 %collective-permute-start.17 = (f32[4,128,128]{2,1,0:T(8,128)S(1)}, f32[4,128,128]{2,1,0:T(8,128)S(1)}, u32[]{:S(2)}, u32[]{:S(2)}) collective-permute-start(f32[4,128,128]{2,1,0:T(8,128)S(1)} %get-tuple-element.18), channel_id=1, source_target_pairs={{0,1},{1,2},{2,3},{3,4},{4,5},{5,6},{6,7},{7,8},{8,9},{9,10},{10,1... | collective-permute-start | bytes 786440 | tf_op jit(solution)/shard_map/ppermute | solution.py:39
  136.9 7.4 %collective-permute-start.18 = (f32[4,128,128]{2,1,0:T(8,128)S(1)}, f32[4,128,128]{2,1,0:T(8,128)S(1)}, u32[]{:S(2)}, u32[]{:S(2)}) collective-permute-start(f32[4,128,128]{2,1,0:T(8,128)S(1)} %get-tuple-element.19), channel_id=1, source_target_pairs={{1,0},{2,1},{3,2},{4,3},{5,4},{6,5},{7,6},{8,7},{9,8},{10,9},{11,1... | collective-permute-start | bytes 786440 | tf_op jit(solution)/shard_map/ppermute | solution.py:41
  144.3 1.8 %pad_maximum_fusion.1.refs_0_.refs_1_ = f32[40,128,128]{2,1,0:T(8,128)} fusion(f32[4,128,128]{2,1,0:T(8,128)S(1)} %collective-permute-done.14, f32[32,128,128]{2,1,0:T(8,128)S(1)} %get-tuple-element.12, f32[4,128,128]{2,1,0:T(8,128)S(1)} %collective-permute-done.13), kind=kLoop, calls=%fused_computation.1 | loop fusion | flops 1310720 | bytes 5242880 | tf_op jit(solution)/shard_map/concatenate | solution.py:37
  146.0 9.6 %shard_map.122.refs_11_ = f32[32,128,128]{2,1,0:T(8,128)S(1)} custom-call(f32[40,128,128]{2,1,0:T(8,128)} %pad_maximum_fusion.1.refs_0_.refs_1_, f32[40,128,128]{2,1,0:T(8,128)} %pad_maximum_fusion.1.refs_0_.refs_1_, f32[32,128,128]{2,1,0:T(8,128)S(1)} %copy-done.1, f32[32,128,128]{2,1,0:T(8,128)} %copy-done.2, f32[32,128,128]{2,1,0:T(8,128)} %copy-done.4, ...), custom_call_target="tpu_custom_call" | custom-call | tf_op jit(solution)/shard_map/pallas_call | solution.py:193
  155.7 1.8 %multiply_add_fusion.1 = (f32[32,8,128]{2,1,0:T(8,128)}, f32[32,8,128]{2,1,0:T(8,128)}) fusion(f32[32,128,128]{2,1,0:T(8,128)S(1)} %shard_map.122.refs_11_, s32[]{:T(128)S(6)} %select_n.37, f32[32,128,128]{2,1,0:T(8,128)} %refs_8_.5, f32[32,8,128]{2,1,0:T(8,128)S(1)} %copy-done.17, f32[32,128,128]{2,1,0:T(8,128)S(1)} %get-tuple-element.12), kind=kLoop, calls=%fused_computation.11 | loop fusion | flops 131072 | bytes 786436 | tf_op jit(solution)/shard_map/add | solution.py:238
  157.5 1.8 %pad_maximum_fusion.3.refs_0_.refs_1_ = f32[40,128,128]{2,1,0:T(8,128)} fusion(f32[4,128,128]{2,1,0:T(8,128)S(1)} %collective-permute-done.18, f32[32,128,128]{2,1,0:T(8,128)S(1)} %multiply_add_fusion, f32[4,128,128]{2,1,0:T(8,128)S(1)} %collective-permute-done.17), kind=kLoop, calls=%fused_computation.3 | loop fusion | flops 1310720 | bytes 5242880 | tf_op jit(solution)/shard_map/concatenate | solution.py:37
  159.8 11.4 %shard_map.124 = f32[32,128,128]{2,1,0:T(8,128)} custom-call(f32[40,128,128]{2,1,0:T(8,128)} %pad_maximum_fusion.3.refs_0_.refs_1_, f32[40,128,128]{2,1,0:T(8,128)} %pad_maximum_fusion.3.refs_0_.refs_1_, f32[32,128,128]{2,1,0:T(8,128)S(1)} %copy-done.1, f32[32,128,128]{2,1,0:T(8,128)S(1)} %copy-done.3, f32[32,128,128]{2,1,0:T(8,128)} %copy-done.4, ...), custom_call_target="tpu_custom_call" | custom-call | tf_op jit(solution)/shard_map/pallas_call | solution.py:193
  (89 shorter events, 11.9 us)
Async XLA Ops:
  0.6 40.2 %copy-start = (f32[32,128,128]{2,1,0:T(8,128)S(1)}, f32[32,128,128]{2,1,0:T(8,128)}, u32[]{:S(2)}) copy-start(f32[32,128,128]{2,1,0:T(8,128)} %refs_2_.7) | copy-start | bytes 6291460
  1.5 9.2 %collective-permute-start = (f32[4,8,128]{2,1,0:T(8,128)S(1)}, f32[4,8,128]{2,1,0:T(8,128)S(1)}, u32[]{:S(2)}, u32[]{:S(2)}) collective-permute-start(f32[4,8,128]{2,1,0:T(8,128)S(1)} %get-tuple-element.27), channel_id=1, source_target_pairs={{0,1},{1,2},{2,3},{3,4},{4,5},{5,6},{6,7},{7,8},{8,9},{9,10},{10,1... | collective-permute-start | bytes 49160 | tf_op jit(solution)/shard_map/ppermute | solution.py:39
  3.4 8.7 %collective-permute-start.1 = (f32[4,8,128]{2,1,0:T(8,128)S(1)}, f32[4,8,128]{2,1,0:T(8,128)S(1)}, u32[]{:S(2)}, u32[]{:S(2)}) collective-permute-start(f32[4,8,128]{2,1,0:T(8,128)S(1)} %get-tuple-element.26), channel_id=1, source_target_pairs={{1,0},{2,1},{3,2},{4,3},{5,4},{6,5},{7,6},{8,7},{9,8},{10,9},{11,1... | collective-permute-start | bytes 49160 | tf_op jit(solution)/shard_map/ppermute | solution.py:41
  13.1 7.2 %collective-permute-start.2 = (f32[72,8,128]{2,1,0:T(8,128)S(1)}, f32[72,8,128]{2,1,0:T(8,128)S(1)}, u32[]{:S(2)}, u32[]{:S(2)}) collective-permute-start(f32[72,8,128]{2,1,0:T(8,128)S(1)} %constant_dynamic-update-slice_fusion), channel_id=1, source_target_pairs={{0,16},{16,0},{32,48},{48,32},{64,80},{80,64},{96,112},{112,96},{1... | collective-permute-start | bytes 884744 | tf_op jit(solution)/shard_map/ppermute | solution.py:51
  21.2 33.0 %copy-start.15 = (f32[72,16,128]{2,1,0:T(8,128)}, f32[72,16,128]{2,1,0:T(8,128)S(1)}, u32[]{:S(2)}) copy-start(f32[72,16,128]{2,1,0:T(8,128)S(1)} %get-tuple-element.17) | copy-start | bytes 1769476
  21.2 15.9 %collective-permute-start.3 = (f32[72,16,128]{2,1,0:T(8,128)S(1)}, f32[72,16,128]{2,1,0:T(8,128)S(1)}, u32[]{:S(2)}, u32[]{:S(2)}) collective-permute-start(f32[72,16,128]{2,1,0:T(8,128)S(1)} %get-tuple-element.17), channel_id=1, source_target_pairs={{0,224},{16,240},{32,0},{48,16},{64,32},{80,48},{96,64},{112,80},{... | collective-permute-start | bytes 1769480 | tf_op jit(solution)/shard_map/ppermute | solution.py:61
  27.0 13.8 %collective-permute-start.6 = (f32[72,16,128]{2,1,0:T(8,128)S(1)}, f32[72,16,128]{2,1,0:T(8,128)S(1)}, u32[]{:S(2)}, u32[]{:S(2)}) collective-permute-start(f32[72,16,128]{2,1,0:T(8,128)S(1)} %get-tuple-element.17), channel_id=1, source_target_pairs={{0,32},{16,48},{32,64},{48,80},{64,96},{80,112},{96,128},{112,144}... | collective-permute-start | bytes 1769480 | tf_op jit(solution)/shard_map/ppermute | solution.py:60
  37.1 17.0 %copy-start.13 = (f32[72,16,128]{2,1,0:T(8,128)}, f32[72,16,128]{2,1,0:T(8,128)S(1)}, u32[]{:S(2)}) copy-start(f32[72,16,128]{2,1,0:T(8,128)S(1)} %collective-permute-done.3) | copy-start | bytes 1769476
  37.1 13.7 %collective-permute-start.4 = (f32[72,16,128]{2,1,0:T(8,128)S(1)}, f32[72,16,128]{2,1,0:T(8,128)}, u32[]{:S(2)}, u32[]{:S(2)}) collective-permute-start(f32[72,16,128]{2,1,0:T(8,128)S(1)} %collective-permute-done.3), channel_id=1, source_target_pairs={{0,224},{16,240},{32,0},{48,16},{64,32},{80,48},{96,64},{112,80},{... | collective-permute-start | bytes 1769480 | tf_op jit(solution)/shard_map/ppermute | solution.py:61
  40.8 13.3 %copy-start.11 = (f32[72,16,128]{2,1,0:T(8,128)}, f32[72,16,128]{2,1,0:T(8,128)S(1)}, u32[]{:S(2)}) copy-start(f32[72,16,128]{2,1,0:T(8,128)S(1)} %collective-permute-done.6) | copy-start | bytes 1769476
  40.8 13.3 %collective-permute-start.7 = (f32[72,16,128]{2,1,0:T(8,128)S(1)}, f32[72,16,128]{2,1,0:T(8,128)}, u32[]{:S(2)}, u32[]{:S(2)}) collective-permute-start(f32[72,16,128]{2,1,0:T(8,128)S(1)} %collective-permute-done.6), channel_id=1, source_target_pairs={{0,32},{16,48},{32,64},{48,80},{64,96},{80,112},{96,128},{112,144}... | collective-permute-start | bytes 1769480 | tf_op jit(solution)/shard_map/ppermute | solution.py:60
  41.6 16.3 %collective-permute-start.11 = (f32[4,128,128]{2,1,0:T(8,128)S(1)}, f32[4,128,128]{2,1,0:T(8,128)S(1)}, u32[]{:S(2)}, u32[]{:S(2)}) collective-permute-start(f32[4,128,128]{2,1,0:T(8,128)S(1)} %get-tuple-element.24), channel_id=1, source_target_pairs={{0,1},{1,2},{2,3},{3,4},{4,5},{5,6},{6,7},{7,8},{8,9},{9,10},{10,1... | collective-permute-start | bytes 786440 | tf_op jit(solution)/shard_map/ppermute | solution.py:39
  43.5 21.7 %collective-permute-start.12 = (f32[4,128,128]{2,1,0:T(8,128)}, f32[4,128,128]{2,1,0:T(8,128)}, u32[]{:S(2)}, u32[]{:S(2)}) collective-permute-start(f32[4,128,128]{2,1,0:T(8,128)} %get-tuple-element.25), channel_id=1, source_target_pairs={{1,0},{2,1},{3,2},{4,3},{5,4},{6,5},{7,6},{8,7},{9,8},{10,9},{11,1... | collective-permute-start | bytes 786440 | tf_op jit(solution)/shard_map/ppermute | solution.py:41
  50.8 41.7 %collective-permute-start.5 = (f32[72,16,128]{2,1,0:T(8,128)}, f32[72,16,128]{2,1,0:T(8,128)S(1)}, u32[]{:S(2)}, u32[]{:S(2)}) collective-permute-start(f32[72,16,128]{2,1,0:T(8,128)} %collective-permute-done.4), channel_id=1, source_target_pairs={{0,224},{16,240},{32,0},{48,16},{64,32},{80,48},{96,64},{112,80},{... | collective-permute-start | bytes 1769480 | tf_op jit(solution)/shard_map/ppermute | solution.py:61
  54.0 41.8 %collective-permute-start.8 = (f32[72,16,128]{2,1,0:T(8,128)}, f32[72,16,128]{2,1,0:T(8,128)S(1)}, u32[]{:S(2)}, u32[]{:S(2)}) collective-permute-start(f32[72,16,128]{2,1,0:T(8,128)} %collective-permute-done.7), channel_id=1, source_target_pairs={{0,32},{16,48},{32,64},{48,80},{64,96},{80,112},{96,128},{112,144}... | collective-permute-start | bytes 1769480 | tf_op jit(solution)/shard_map/ppermute | solution.py:60
  56.0 22.4 %collective-permute-start.15 = (f32[4,128,128]{2,1,0:T(8,128)}, f32[4,128,128]{2,1,0:T(8,128)}, u32[]{:S(2)}, u32[]{:S(2)}) collective-permute-start(f32[4,128,128]{2,1,0:T(8,128)} %get-tuple-element.20), channel_id=1, source_target_pairs={{0,1},{1,2},{2,3},{3,4},{4,5},{5,6},{6,7},{7,8},{8,9},{9,10},{10,1... | collective-permute-start | bytes 786440 | tf_op jit(solution)/shard_map/ppermute | solution.py:39
  57.9 20.5 %collective-permute-start.16 = (f32[4,128,128]{2,1,0:T(8,128)}, f32[4,128,128]{2,1,0:T(8,128)}, u32[]{:S(2)}, u32[]{:S(2)}) collective-permute-start(f32[4,128,128]{2,1,0:T(8,128)} %get-tuple-element.21), channel_id=1, source_target_pairs={{1,0},{2,1},{3,2},{4,3},{5,4},{6,5},{7,6},{8,7},{9,8},{10,9},{11,1... | collective-permute-start | bytes 786440 | tf_op jit(solution)/shard_map/ppermute | solution.py:41
  68.1 10.4 %copy-start.8 = (f32[1,32,128,128]{3,2,1,0:T(8,128)S(1)}, f32[1,32,128,128]{3,2,1,0:T(8,128)}, u32[]{:S(2)}) copy-start(f32[1,32,128,128]{3,2,1,0:T(8,128)} %param.15) | copy-start | bytes 6291460
  78.5 17.7 %slice-start = ((s8[9437184]{0:T(1024)(128)(4,1)}), s8[1048576]{0:T(1024)(128)(4,1)S(1)}, s32[]{:S(2)}) async-start(s8[9437184]{0:T(1024)(128)(4,1)} %bitcast.14), calls=%async_computation | async-start | bytes 2097152
  81.8 14.4 %slice-start.1 = ((s8[9437184]{0:T(1024)(128)(4,1)}), s8[4194304]{0:T(1024)(128)(4,1)S(1)}, s32[]{:S(2)}) async-start(s8[9437184]{0:T(1024)(128)(4,1)} %bitcast.14), calls=%async_computation.1 | async-start | bytes 8388608
  81.8 14.4 %slice-start.2 = ((s8[9437184]{0:T(1024)(128)(4,1)}), s8[4194304]{0:T(1024)(128)(4,1)S(1)}, s32[]{:S(2)}) async-start(s8[9437184]{0:T(1024)(128)(4,1)} %bitcast.14), calls=%async_computation.2 | async-start | bytes 8388608
  81.8 14.4 %copy-start.14 = (f32[72,16,128]{2,1,0:T(8,128)S(1)}, f32[72,16,128]{2,1,0:T(8,128)}, u32[]{:S(2)}) copy-start(f32[72,16,128]{2,1,0:T(8,128)} %copy-done.13) | copy-start | bytes 1769476
  92.6 10.7 %collective-permute-start.10 = (f32[36,16,128]{2,1,0:T(8,128)S(1)}, f32[36,16,128]{2,1,0:T(8,128)S(1)}, u32[]{:S(2)}, u32[]{:S(2)}) collective-permute-start(f32[36,16,128]{2,1,0:T(8,128)S(1)} %slice.65), channel_id=1, source_target_pairs={{0,224},{16,240},{32,0},{48,16},{64,32},{80,48},{96,64},{112,80},{... | collective-permute-start | bytes 884744 | tf_op jit(solution)/shard_map/ppermute | solution.py:66
  95.9 11.1 %collective-permute-start.9 = (f32[36,16,128]{2,1,0:T(8,128)S(1)}, f32[36,16,128]{2,1,0:T(8,128)S(1)}, u32[]{:S(2)}, u32[]{:S(2)}) collective-permute-start(f32[36,16,128]{2,1,0:T(8,128)S(1)} %slice.64), channel_id=1, source_target_pairs={{0,32},{16,48},{32,64},{48,80},{64,96},{80,112},{96,128},{112,144}... | collective-permute-start | bytes 884744 | tf_op jit(solution)/shard_map/ppermute | solution.py:66
  97.4 10.9 %copy-start.12 = (f32[72,16,128]{2,1,0:T(8,128)S(1)}, f32[72,16,128]{2,1,0:T(8,128)}, u32[]{:S(2)}) copy-start(f32[72,16,128]{2,1,0:T(8,128)} %copy-done.11) | copy-start | bytes 1769476
  97.5 10.9 %copy-start.16 = (f32[72,16,128]{2,1,0:T(8,128)S(1)}, f32[72,16,128]{2,1,0:T(8,128)}, u32[]{:S(2)}) copy-start(f32[72,16,128]{2,1,0:T(8,128)} %copy-done.15) | copy-start | bytes 1769476
  114.6 19.6 %copy-start.10 = (f32[1,32,128,128]{3,2,1,0:T(8,128)S(1)}, f32[1,32,128,128]{3,2,1,0:T(8,128)}, u32[]{:S(2)}) copy-start(f32[1,32,128,128]{3,2,1,0:T(8,128)} %param.13) | copy-start | bytes 6291460
  125.0 19.2 %collective-permute-start.13 = (f32[4,128,128]{2,1,0:T(8,128)S(1)}, f32[4,128,128]{2,1,0:T(8,128)S(1)}, u32[]{:S(2)}, u32[]{:S(2)}) collective-permute-start(f32[4,128,128]{2,1,0:T(8,128)S(1)} %get-tuple-element.22), channel_id=1, source_target_pairs={{0,1},{1,2},{2,3},{3,4},{4,5},{5,6},{6,7},{7,8},{8,9},{9,10},{10,1... | collective-permute-start | bytes 786440 | tf_op jit(solution)/shard_map/ppermute | solution.py:39
  126.9 17.3 %collective-permute-start.14 = (f32[4,128,128]{2,1,0:T(8,128)S(1)}, f32[4,128,128]{2,1,0:T(8,128)S(1)}, u32[]{:S(2)}, u32[]{:S(2)}) collective-permute-start(f32[4,128,128]{2,1,0:T(8,128)S(1)} %get-tuple-element.23), channel_id=1, source_target_pairs={{1,0},{2,1},{3,2},{4,3},{5,4},{6,5},{7,6},{8,7},{9,8},{10,9},{11,1... | collective-permute-start | bytes 786440 | tf_op jit(solution)/shard_map/ppermute | solution.py:41
  134.9 22.6 %copy-start.9 = (f32[32,128,128]{2,1,0:T(8,128)}, f32[32,128,128]{2,1,0:T(8,128)S(1)}, u32[]{:S(2)}) copy-start(f32[32,128,128]{2,1,0:T(8,128)S(1)} %multiply_add_fusion) | copy-start | bytes 6291460
  134.9 22.6 %collective-permute-start.17 = (f32[4,128,128]{2,1,0:T(8,128)S(1)}, f32[4,128,128]{2,1,0:T(8,128)S(1)}, u32[]{:S(2)}, u32[]{:S(2)}) collective-permute-start(f32[4,128,128]{2,1,0:T(8,128)S(1)} %get-tuple-element.18), channel_id=1, source_target_pairs={{0,1},{1,2},{2,3},{3,4},{4,5},{5,6},{6,7},{7,8},{8,9},{9,10},{10,1... | collective-permute-start | bytes 786440 | tf_op jit(solution)/shard_map/ppermute | solution.py:39
  136.9 20.6 %collective-permute-start.18 = (f32[4,128,128]{2,1,0:T(8,128)S(1)}, f32[4,128,128]{2,1,0:T(8,128)S(1)}, u32[]{:S(2)}, u32[]{:S(2)}) collective-permute-start(f32[4,128,128]{2,1,0:T(8,128)S(1)} %get-tuple-element.19), channel_id=1, source_target_pairs={{1,0},{2,1},{3,2},{4,3},{5,4},{6,5},{7,6},{8,7},{9,8},{10,9},{11,1... | collective-permute-start | bytes 786440 | tf_op jit(solution)/shard_map/ppermute | solution.py:41
  (8 other events, 37.1 us)

commit v3 on v2

--- a/solution.py
+++ b/solution.py
@@ -7,6 +7,7 @@
 from jax.experimental import pallas as pl
 from jax.experimental.pallas import tpu as pltpu
 from jax.sharding import PartitionSpec as P
+
 
 SECOND = (-205.0 / 72.0, 8.0 / 5.0, -1.0 / 5.0, 8.0 / 315.0, -1.0 / 560.0)
 FIRST = (0.0, 4.0 / 5.0, -1.0 / 5.0, 4.0 / 105.0, -1.0 / 280.0)
@@ -202,7 +203,7 @@
     return outs
 
 
-def local(u_prev, u_cur, buoyancy, kappa, dkappa, du_prev, du_cur):
+def local_body(u_prev, u_cur, buoyancy, kappa, dkappa, du_prev, du_cur):
     n = buoyancy.shape[1]
     strip = u_cur.shape[1]
     offset = lax.axis_index("probe") * strip
@@ -215,13 +216,15 @@
     u_cur_ext = both[: depth + 2 * HALO]
     u_prev_all = both[depth + 2 * HALO:]
 
-    slopes = slopes_of(halo_depth(buoyancy), mlane, msub)
+    buoyancy_ext = halo_depth(buoyancy)
+    slopes = slopes_of(buoyancy_ext, mlane, msub)
 
     probe_kappa = dkappa[0]
     older = du_prev[0]
     newer = du_cur[0]
 
-    (partial_first,) = apply_op(halo_depth(newer), buoyancy, slopes, mlane, msub, kappa=kappa, prev=older)
+    newer_ext = halo_depth(newer)
+    (partial_first,) = apply_op(newer_ext, buoyancy, slopes, mlane, msub, kappa=kappa, prev=older)
 
     image_first, background_first = apply_op(
         u_cur_ext, buoyancy, slopes, mlane, msub, kappa=kappa, prev=u_prev_all, want_image=True
@@ -246,8 +249,12 @@
 
 
 def solution(mesh):
+    return shard_mapped(mesh)
+
+
+def shard_mapped(mesh):
     return jax.shard_map(
-        local,
+        local_body,
         mesh=mesh,
         in_specs=(
             P("slab", "probe", None),

time: 172 us -> 172 us (level)
  no operation moved by 1% of the time
where the time goes in v3:
time: 172 us; the launch traced here: 171 us
  starting transfers between devices  63.3 us (37%)
  Pallas kernels  52.4 us (30%)
  waiting for transfers between devices  26.3 us (15%)
  local copies, waits for them, and re-layouts  14.7 us (9%)
  other arithmetic  13.2 us (8%)
    pallas_call x4, Pallas kernels, apply_op(): pl.pallas_call(functools.partial(_op_kernel, (with_prev, with_img, want_i...  42.1 us
    ppermute x5, starting transfers between devices, halo_depth(): lax.ppermute(head, 'slab', [(i + 1, i) for i in range(ends)])  36.4 us
    ppermute x3, starting transfers between devices, ring_gather(): bwd = lax.ppermute(bwd, 'probe', behind)  12.8 us
    pallas_call x1, Pallas kernels, slopes_of(): pl.pallas_call(_slope_kernel, grid=(depth // BZ,), in_specs=_ext_specs(n)...  10.3 us
    ppermute x3, waiting for transfers between devices, ring_gather(): bwd = lax.ppermute(bwd, 'probe', behind)  10.1 us
    concatenate x4, other arithmetic, halo_depth(): jnp.concatenate([lax.ppermute(tail, 'slab', [(i, i + 1) for i in range(en...  9.67 us
    ppermute x5, starting transfers between devices, halo_depth(): lax.ppermute(tail, 'slab', [(i, i + 1) for i in range(ends)])  9.57 us
    unnamed x57, local copies, waits for them, and re-layouts  6.71 us
  transfers between devices with their start and end apart: 19, of which 5 were waited for; matrix products, arithmetic and copies ran while one was open for 9% of the time, Pallas kernels for 18%

profile of v3, /device:TPU:6, one launch (start us, length us, event | category | flops | bytes accessed | tf_op | source)
XLA Modules:
  0.0 171.2 jit_solution(2333721458170054500)
XLA Ops:
  1.5 1.9 %collective-permute-start = (f32[4,8,128]{2,1,0:T(8,128)S(1)}, f32[4,8,128]{2,1,0:T(8,128)S(1)}, u32[]{:S(2)}, u32[]{:S(2)}) collective-permute-start(f32[4,8,128]{2,1,0:T(8,128)S(1)} %get-tuple-element.27), channel_id=1, source_target_pairs={{0,1},{1,2},{2,3},{3,4},{4,5},{5,6},{6,7},{7,8},{8,9},{9,10},{10,1... | collective-permute-start | bytes 49160 | tf_op jit(solution)/shard_map/ppermute | solution.py:40
  3.4 7.3 %collective-permute-start.1 = (f32[4,8,128]{2,1,0:T(8,128)S(1)}, f32[4,8,128]{2,1,0:T(8,128)S(1)}, u32[]{:S(2)}, u32[]{:S(2)}) collective-permute-start(f32[4,8,128]{2,1,0:T(8,128)S(1)} %get-tuple-element.26), channel_id=1, source_target_pairs={{1,0},{2,1},{3,2},{4,3},{5,4},{6,5},{7,6},{8,7},{9,8},{10,9},{11,1... | collective-permute-start | bytes 49160 | tf_op jit(solution)/shard_map/ppermute | solution.py:42
  14.0 6.3 %collective-permute-done.2 = f32[72,8,128]{2,1,0:T(8,128)S(1)} collective-permute-done((f32[72,8,128]{2,1,0:T(8,128)S(1)}, f32[72,8,128]{2,1,0:T(8,128)S(1)}, u32[]{:S(2)}, u32[]{:S(2)}) %collective-permute-start.2) | collective-permute-done | bytes 294944 | tf_op jit(solution)/shard_map/ppermute | solution.py:52
  21.2 5.9 %collective-permute-start.3 = (f32[72,16,128]{2,1,0:T(8,128)S(1)}, f32[72,16,128]{2,1,0:T(8,128)S(1)}, u32[]{:S(2)}, u32[]{:S(2)}) collective-permute-start(f32[72,16,128]{2,1,0:T(8,128)S(1)} %get-tuple-element.17), channel_id=1, source_target_pairs={{0,224},{16,240},{32,0},{48,16},{64,32},{80,48},{96,64},{112,80},{... | collective-permute-start | bytes 1769480 | tf_op jit(solution)/shard_map/ppermute | solution.py:62
  27.0 10.1 %collective-permute-done.3 = f32[72,16,128]{2,1,0:T(8,128)S(1)} collective-permute-done((f32[72,16,128]{2,1,0:T(8,128)S(1)}, f32[72,16,128]{2,1,0:T(8,128)S(1)}, u32[]{:S(2)}, u32[]{:S(2)}) %collective-permute-start.3) | collective-permute-done | bytes 589856 | tf_op jit(solution)/shard_map/ppermute | solution.py:62
  37.1 3.7 %collective-permute-start.4 = (f32[72,16,128]{2,1,0:T(8,128)S(1)}, f32[72,16,128]{2,1,0:T(8,128)}, u32[]{:S(2)}, u32[]{:S(2)}) collective-permute-start(f32[72,16,128]{2,1,0:T(8,128)S(1)} %collective-permute-done.3), channel_id=1, source_target_pairs={{0,224},{16,240},{32,0},{48,16},{64,32},{80,48},{96,64},{112,80},{... | collective-permute-start | bytes 1769480 | tf_op jit(solution)/shard_map/ppermute | solution.py:62
  41.6 1.9 %collective-permute-start.11 = (f32[4,128,128]{2,1,0:T(8,128)S(1)}, f32[4,128,128]{2,1,0:T(8,128)S(1)}, u32[]{:S(2)}, u32[]{:S(2)}) collective-permute-start(f32[4,128,128]{2,1,0:T(8,128)S(1)} %get-tuple-element.24), channel_id=1, source_target_pairs={{0,1},{1,2},{2,3},{3,4},{4,5},{5,6},{6,7},{7,8},{8,9},{9,10},{10,1... | collective-permute-start | bytes 786440 | tf_op jit(solution)/shard_map/ppermute | solution.py:40
  43.5 7.3 %collective-permute-start.12 = (f32[4,128,128]{2,1,0:T(8,128)}, f32[4,128,128]{2,1,0:T(8,128)}, u32[]{:S(2)}, u32[]{:S(2)}) collective-permute-start(f32[4,128,128]{2,1,0:T(8,128)} %get-tuple-element.25), channel_id=1, source_target_pairs={{1,0},{2,1},{3,2},{4,3},{5,4},{6,5},{7,6},{8,7},{9,8},{10,9},{11,1... | collective-permute-start | bytes 786440 | tf_op jit(solution)/shard_map/ppermute | solution.py:42
  50.8 3.2 %collective-permute-start.5 = (f32[72,16,128]{2,1,0:T(8,128)}, f32[72,16,128]{2,1,0:T(8,128)S(1)}, u32[]{:S(2)}, u32[]{:S(2)}) collective-permute-start(f32[72,16,128]{2,1,0:T(8,128)} %collective-permute-done.4), channel_id=1, source_target_pairs={{0,224},{16,240},{32,0},{48,16},{64,32},{80,48},{96,64},{112,80},{... | collective-permute-start | bytes 1769480 | tf_op jit(solution)/shard_map/ppermute | solution.py:62
  54.2 1.9 %slice_bitcast_fusion.1 = (f32[4,128,128]{2,1,0:T(8,128)}, f32[4,128,128]{2,1,0:T(8,128)}) fusion(f32[1,32,128,128]{3,2,1,0:T(8,128)} %param.15), kind=kLoop, calls=%fused_computation.10 | loop fusion | bytes 1048576 | tf_op jit(solution)/shard_map/slice | solution.py:37
  56.0 1.9 %collective-permute-start.15 = (f32[4,128,128]{2,1,0:T(8,128)}, f32[4,128,128]{2,1,0:T(8,128)}, u32[]{:S(2)}, u32[]{:S(2)}) collective-permute-start(f32[4,128,128]{2,1,0:T(8,128)} %get-tuple-element.20), channel_id=1, source_target_pairs={{0,1},{1,2},{2,3},{3,4},{4,5},{5,6},{6,7},{7,8},{8,9},{9,10},{10,1... | collective-permute-start | bytes 786440 | tf_op jit(solution)/shard_map/ppermute | solution.py:40
  57.9 7.3 %collective-permute-start.16 = (f32[4,128,128]{2,1,0:T(8,128)}, f32[4,128,128]{2,1,0:T(8,128)}, u32[]{:S(2)}, u32[]{:S(2)}) collective-permute-start(f32[4,128,128]{2,1,0:T(8,128)} %get-tuple-element.21), channel_id=1, source_target_pairs={{1,0},{2,1},{3,2},{4,3},{5,4},{6,5},{7,6},{8,7},{9,8},{10,9},{11,1... | collective-permute-start | bytes 786440 | tf_op jit(solution)/shard_map/ppermute | solution.py:42
  65.3 2.8 %pad_maximum_fusion.lo_ref.hi_ref = f32[40,128,128]{2,1,0:T(8,128)} fusion(f32[4,128,128]{2,1,0:T(8,128)} %collective-permute-done.12, f32[32,128,128]{2,1,0:T(8,128)S(1)} %copy-done, f32[4,128,128]{2,1,0:T(8,128)S(1)} %collective-permute-done.11), kind=kLoop, calls=%fused_computation | loop fusion | flops 1310720 | bytes 5242880 | tf_op jit(solution)/shard_map/concatenate | solution.py:38
  68.1 10.3 %shard_map.120 = (f32[32,128,128]{2,1,0:T(8,128)S(1)}, f32[32,128,128]{2,1,0:T(8,128)S(1)}, f32[32,128,128]{2,1,0:T(8,128)}) custom-call(f32[40,128,128]{2,1,0:T(8,128)} %pad_maximum_fusion.lo_ref.hi_ref, f32[40,128,128]{2,1,0:T(8,128)} %pad_maximum_fusion.lo_ref.hi_ref, f32[128,256]{1,0:T(8,128)S(1)} %copy-done.6, f32[256,128]{1,0:T(8,128)S(1)} %copy-done.7), custom_call_target="tpu_custom_call" | custom-call | tf_op jit(solution)/shard_map/pallas_call | solution.py:169
  78.5 3.3 %pad_maximum_fusion.2.refs_0_.refs_1_ = f32[40,128,128]{2,1,0:T(8,128)} fusion(f32[4,128,128]{2,1,0:T(8,128)} %collective-permute-done.16, f32[32,128,128]{2,1,0:T(8,128)S(1)} %bitcast.11, f32[4,128,128]{2,1,0:T(8,128)} %collective-permute-done.15), kind=kLoop, calls=%fused_computation.2 | loop fusion | flops 1310720 | bytes 5242880 | tf_op jit(solution)/shard_map/concatenate | solution.py:38
  81.8 10.7 %shard_map.123 = f32[32,128,128]{2,1,0:T(8,128)S(1)} custom-call(f32[40,128,128]{2,1,0:T(8,128)} %pad_maximum_fusion.2.refs_0_.refs_1_, f32[40,128,128]{2,1,0:T(8,128)} %pad_maximum_fusion.2.refs_0_.refs_1_, f32[32,128,128]{2,1,0:T(8,128)S(1)} %copy-done, f32[32,128,128]{2,1,0:T(8,128)} %copy-done.2, f32[32,128,128]{2,1,0:T(8,128)} %copy-done.4, ...), custom_call_target="tpu_custom_call" | custom-call | tf_op jit(solution)/shard_map/pallas_call | solution.py:194
  92.6 3.3 %collective-permute-start.10 = (f32[36,16,128]{2,1,0:T(8,128)S(1)}, f32[36,16,128]{2,1,0:T(8,128)S(1)}, u32[]{:S(2)}, u32[]{:S(2)}) collective-permute-start(f32[36,16,128]{2,1,0:T(8,128)S(1)} %slice.65), channel_id=1, source_target_pairs={{0,224},{16,240},{32,0},{48,16},{64,32},{80,48},{96,64},{112,80},{... | collective-permute-start | bytes 884744 | tf_op jit(solution)/shard_map/ppermute | solution.py:67
  97.5 5.7 %collective-permute-done.10 = f32[36,16,128]{2,1,0:T(8,128)S(1)} collective-permute-done((f32[36,16,128]{2,1,0:T(8,128)S(1)}, f32[36,16,128]{2,1,0:T(8,128)S(1)}, u32[]{:S(2)}, u32[]{:S(2)}) %collective-permute-start.10) | collective-permute-done | bytes 294944 | tf_op jit(solution)/shard_map/ppermute | solution.py:67
  103.2 3.7 %collective-permute-done.9 = f32[36,16,128]{2,1,0:T(8,128)S(1)} collective-permute-done((f32[36,16,128]{2,1,0:T(8,128)S(1)}, f32[36,16,128]{2,1,0:T(8,128)S(1)}, u32[]{:S(2)}, u32[]{:S(2)}) %collective-permute-start.9) | collective-permute-done | bytes 294944 | tf_op jit(solution)/shard_map/ppermute | solution.py:67
  110.0 1.1 constant_dynamic-update-slice_fusion.5
  111.2 1.8 %constant_dynamic-slice_fusion.refs_0_.refs_1_ = f32[40,128,128]{2,1,0:T(8,128)} fusion(f32[72,256,128]{2,1,0:T(8,128)S(1)} %constant_dynamic-update-slice_fusion.4, s32[]{:T(128)S(6)} %select_n.36), kind=kLoop, calls=%fused_computation.30 | loop fusion | bytes 5242884 | tf_op jit(solution)/shard_map/slice | solution.py:216
  113.0 1.5 constant_dynamic-slice_fusion.2.refs_9_
  114.6 10.4 %shard_map.121 = (f32[32,128,128]{2,1,0:T(8,128)S(1)}, f32[32,128,128]{2,1,0:T(8,128)S(1)}) custom-call(f32[40,128,128]{2,1,0:T(8,128)} %constant_dynamic-slice_fusion.refs_0_.refs_1_, f32[40,128,128]{2,1,0:T(8,128)} %constant_dynamic-slice_fusion.refs_0_.refs_1_, f32[32,128,128]{2,1,0:T(8,128)} %refs_2_.7, f32[32,128,128]{2,1,0:T(8,128)} %copy-done.2, ...), custom_call_target="tpu_custom_call" | custom-call | tf_op jit(solution)/shard_map/pallas_call | solution.py:194
  125.0 1.9 %collective-permute-start.13 = (f32[4,128,128]{2,1,0:T(8,128)S(1)}, f32[4,128,128]{2,1,0:T(8,128)S(1)}, u32[]{:S(2)}, u32[]{:S(2)}) collective-permute-start(f32[4,128,128]{2,1,0:T(8,128)S(1)} %get-tuple-element.22), channel_id=1, source_target_pairs={{0,1},{1,2},{2,3},{3,4},{4,5},{5,6},{6,7},{7,8},{8,9},{9,10},{10,1... | collective-permute-start | bytes 786440 | tf_op jit(solution)/shard_map/ppermute | solution.py:40
  126.9 7.3 %collective-permute-start.14 = (f32[4,128,128]{2,1,0:T(8,128)S(1)}, f32[4,128,128]{2,1,0:T(8,128)S(1)}, u32[]{:S(2)}, u32[]{:S(2)}) collective-permute-start(f32[4,128,128]{2,1,0:T(8,128)S(1)} %get-tuple-element.23), channel_id=1, source_target_pairs={{1,0},{2,1},{3,2},{4,3},{5,4},{6,5},{7,6},{8,7},{9,8},{10,9},{11,1... | collective-permute-start | bytes 786440 | tf_op jit(solution)/shard_map/ppermute | solution.py:42
  134.9 1.9 %collective-permute-start.17 = (f32[4,128,128]{2,1,0:T(8,128)S(1)}, f32[4,128,128]{2,1,0:T(8,128)S(1)}, u32[]{:S(2)}, u32[]{:S(2)}) collective-permute-start(f32[4,128,128]{2,1,0:T(8,128)S(1)} %get-tuple-element.18), channel_id=1, source_target_pairs={{0,1},{1,2},{2,3},{3,4},{4,5},{5,6},{6,7},{7,8},{8,9},{9,10},{10,1... | collective-permute-start | bytes 786440 | tf_op jit(solution)/shard_map/ppermute | solution.py:40
  136.9 7.4 %collective-permute-start.18 = (f32[4,128,128]{2,1,0:T(8,128)S(1)}, f32[4,128,128]{2,1,0:T(8,128)S(1)}, u32[]{:S(2)}, u32[]{:S(2)}) collective-permute-start(f32[4,128,128]{2,1,0:T(8,128)S(1)} %get-tuple-element.19), channel_id=1, source_target_pairs={{1,0},{2,1},{3,2},{4,3},{5,4},{6,5},{7,6},{8,7},{9,8},{10,9},{11,1... | collective-permute-start | bytes 786440 | tf_op jit(solution)/shard_map/ppermute | solution.py:42
  144.3 1.8 %pad_maximum_fusion.1.refs_0_.refs_1_ = f32[40,128,128]{2,1,0:T(8,128)} fusion(f32[4,128,128]{2,1,0:T(8,128)S(1)} %collective-permute-done.14, f32[32,128,128]{2,1,0:T(8,128)S(1)} %get-tuple-element.12, f32[4,128,128]{2,1,0:T(8,128)S(1)} %collective-permute-done.13), kind=kLoop, calls=%fused_computation.1 | loop fusion | flops 1310720 | bytes 5242880 | tf_op jit(solution)/shard_map/concatenate | solution.py:38
  146.0 9.6 %shard_map.122.refs_11_ = f32[32,128,128]{2,1,0:T(8,128)S(1)} custom-call(f32[40,128,128]{2,1,0:T(8,128)} %pad_maximum_fusion.1.refs_0_.refs_1_, f32[40,128,128]{2,1,0:T(8,128)} %pad_maximum_fusion.1.refs_0_.refs_1_, f32[32,128,128]{2,1,0:T(8,128)S(1)} %copy-done.1, f32[32,128,128]{2,1,0:T(8,128)} %copy-done.2, f32[32,128,128]{2,1,0:T(8,128)} %copy-done.4, ...), custom_call_target="tpu_custom_call" | custom-call | tf_op jit(solution)/shard_map/pallas_call | solution.py:194
  155.7 1.8 %multiply_add_fusion.1 = (f32[32,8,128]{2,1,0:T(8,128)}, f32[32,8,128]{2,1,0:T(8,128)}) fusion(f32[32,128,128]{2,1,0:T(8,128)S(1)} %shard_map.122.refs_11_, s32[]{:T(128)S(6)} %select_n.37, f32[32,128,128]{2,1,0:T(8,128)} %refs_8_.5, f32[32,8,128]{2,1,0:T(8,128)S(1)} %copy-done.17, f32[32,128,128]{2,1,0:T(8,128)S(1)} %get-tuple-element.12), kind=kLoop, calls=%fused_computation.11 | loop fusion | flops 131072 | bytes 786436 | tf_op jit(solution)/shard_map/add | solution.py:241
  157.5 1.8 %pad_maximum_fusion.3.refs_0_.refs_1_ = f32[40,128,128]{2,1,0:T(8,128)} fusion(f32[4,128,128]{2,1,0:T(8,128)S(1)} %collective-permute-done.18, f32[32,128,128]{2,1,0:T(8,128)S(1)} %multiply_add_fusion, f32[4,128,128]{2,1,0:T(8,128)S(1)} %collective-permute-done.17), kind=kLoop, calls=%fused_computation.3 | loop fusion | flops 1310720 | bytes 5242880 | tf_op jit(solution)/shard_map/concatenate | solution.py:38
  159.8 11.4 %shard_map.124 = f32[32,128,128]{2,1,0:T(8,128)} custom-call(f32[40,128,128]{2,1,0:T(8,128)} %pad_maximum_fusion.3.refs_0_.refs_1_, f32[40,128,128]{2,1,0:T(8,128)} %pad_maximum_fusion.3.refs_0_.refs_1_, f32[32,128,128]{2,1,0:T(8,128)S(1)} %copy-done.1, f32[32,128,128]{2,1,0:T(8,128)S(1)} %copy-done.3, f32[32,128,128]{2,1,0:T(8,128)} %copy-done.4, ...), custom_call_target="tpu_custom_call" | custom-call | tf_op jit(solution)/shard_map/pallas_call | solution.py:194
  (89 shorter events, 11.9 us)
Async XLA Ops:
  0.6 40.2 %copy-start = (f32[32,128,128]{2,1,0:T(8,128)S(1)}, f32[32,128,128]{2,1,0:T(8,128)}, u32[]{:S(2)}) copy-start(f32[32,128,128]{2,1,0:T(8,128)} %refs_2_.7) | copy-start | bytes 6291460
  1.5 9.2 %collective-permute-start = (f32[4,8,128]{2,1,0:T(8,128)S(1)}, f32[4,8,128]{2,1,0:T(8,128)S(1)}, u32[]{:S(2)}, u32[]{:S(2)}) collective-permute-start(f32[4,8,128]{2,1,0:T(8,128)S(1)} %get-tuple-element.27), channel_id=1, source_target_pairs={{0,1},{1,2},{2,3},{3,4},{4,5},{5,6},{6,7},{7,8},{8,9},{9,10},{10,1... | collective-permute-start | bytes 49160 | tf_op jit(solution)/shard_map/ppermute | solution.py:40
  3.4 8.7 %collective-permute-start.1 = (f32[4,8,128]{2,1,0:T(8,128)S(1)}, f32[4,8,128]{2,1,0:T(8,128)S(1)}, u32[]{:S(2)}, u32[]{:S(2)}) collective-permute-start(f32[4,8,128]{2,1,0:T(8,128)S(1)} %get-tuple-element.26), channel_id=1, source_target_pairs={{1,0},{2,1},{3,2},{4,3},{5,4},{6,5},{7,6},{8,7},{9,8},{10,9},{11,1... | collective-permute-start | bytes 49160 | tf_op jit(solution)/shard_map/ppermute | solution.py:42
  13.1 7.2 %collective-permute-start.2 = (f32[72,8,128]{2,1,0:T(8,128)S(1)}, f32[72,8,128]{2,1,0:T(8,128)S(1)}, u32[]{:S(2)}, u32[]{:S(2)}) collective-permute-start(f32[72,8,128]{2,1,0:T(8,128)S(1)} %constant_dynamic-update-slice_fusion), channel_id=1, source_target_pairs={{0,16},{16,0},{32,48},{48,32},{64,80},{80,64},{96,112},{112,96},{1... | collective-permute-start | bytes 884744 | tf_op jit(solution)/shard_map/ppermute | solution.py:52
  21.2 33.0 %copy-start.15 = (f32[72,16,128]{2,1,0:T(8,128)}, f32[72,16,128]{2,1,0:T(8,128)S(1)}, u32[]{:S(2)}) copy-start(f32[72,16,128]{2,1,0:T(8,128)S(1)} %get-tuple-element.17) | copy-start | bytes 1769476
  21.2 15.9 %collective-permute-start.3 = (f32[72,16,128]{2,1,0:T(8,128)S(1)}, f32[72,16,128]{2,1,0:T(8,128)S(1)}, u32[]{:S(2)}, u32[]{:S(2)}) collective-permute-start(f32[72,16,128]{2,1,0:T(8,128)S(1)} %get-tuple-element.17), channel_id=1, source_target_pairs={{0,224},{16,240},{32,0},{48,16},{64,32},{80,48},{96,64},{112,80},{... | collective-permute-start | bytes 1769480 | tf_op jit(solution)/shard_map/ppermute | solution.py:62
  27.0 13.8 %collective-permute-start.6 = (f32[72,16,128]{2,1,0:T(8,128)S(1)}, f32[72,16,128]{2,1,0:T(8,128)S(1)}, u32[]{:S(2)}, u32[]{:S(2)}) collective-permute-start(f32[72,16,128]{2,1,0:T(8,128)S(1)} %get-tuple-element.17), channel_id=1, source_target_pairs={{0,32},{16,48},{32,64},{48,80},{64,96},{80,112},{96,128},{112,144}... | collective-permute-start | bytes 1769480 | tf_op jit(solution)/shard_map/ppermute | solution.py:61
  37.1 17.0 %copy-start.13 = (f32[72,16,128]{2,1,0:T(8,128)}, f32[72,16,128]{2,1,0:T(8,128)S(1)}, u32[]{:S(2)}) copy-start(f32[72,16,128]{2,1,0:T(8,128)S(1)} %collective-permute-done.3) | copy-start | bytes 1769476
  37.1 13.7 %collective-permute-start.4 = (f32[72,16,128]{2,1,0:T(8,128)S(1)}, f32[72,16,128]{2,1,0:T(8,128)}, u32[]{:S(2)}, u32[]{:S(2)}) collective-permute-start(f32[72,16,128]{2,1,0:T(8,128)S(1)} %collective-permute-done.3), channel_id=1, source_target_pairs={{0,224},{16,240},{32,0},{48,16},{64,32},{80,48},{96,64},{112,80},{... | collective-permute-start | bytes 1769480 | tf_op jit(solution)/shard_map/ppermute | solution.py:62
  40.8 13.3 %copy-start.11 = (f32[72,16,128]{2,1,0:T(8,128)}, f32[72,16,128]{2,1,0:T(8,128)S(1)}, u32[]{:S(2)}) copy-start(f32[72,16,128]{2,1,0:T(8,128)S(1)} %collective-permute-done.6) | copy-start | bytes 1769476
  40.8 13.3 %collective-permute-start.7 = (f32[72,16,128]{2,1,0:T(8,128)S(1)}, f32[72,16,128]{2,1,0:T(8,128)}, u32[]{:S(2)}, u32[]{:S(2)}) collective-permute-start(f32[72,16,128]{2,1,0:T(8,128)S(1)} %collective-permute-done.6), channel_id=1, source_target_pairs={{0,32},{16,48},{32,64},{48,80},{64,96},{80,112},{96,128},{112,144}... | collective-permute-start | bytes 1769480 | tf_op jit(solution)/shard_map/ppermute | solution.py:61
  41.6 16.3 %collective-permute-start.11 = (f32[4,128,128]{2,1,0:T(8,128)S(1)}, f32[4,128,128]{2,1,0:T(8,128)S(1)}, u32[]{:S(2)}, u32[]{:S(2)}) collective-permute-start(f32[4,128,128]{2,1,0:T(8,128)S(1)} %get-tuple-element.24), channel_id=1, source_target_pairs={{0,1},{1,2},{2,3},{3,4},{4,5},{5,6},{6,7},{7,8},{8,9},{9,10},{10,1... | collective-permute-start | bytes 786440 | tf_op jit(solution)/shard_map/ppermute | solution.py:40
  43.5 21.7 %collective-permute-start.12 = (f32[4,128,128]{2,1,0:T(8,128)}, f32[4,128,128]{2,1,0:T(8,128)}, u32[]{:S(2)}, u32[]{:S(2)}) collective-permute-start(f32[4,128,128]{2,1,0:T(8,128)} %get-tuple-element.25), channel_id=1, source_target_pairs={{1,0},{2,1},{3,2},{4,3},{5,4},{6,5},{7,6},{8,7},{9,8},{10,9},{11,1... | collective-permute-start | bytes 786440 | tf_op jit(solution)/shard_map/ppermute | solution.py:42
  50.8 41.7 %collective-permute-start.5 = (f32[72,16,128]{2,1,0:T(8,128)}, f32[72,16,128]{2,1,0:T(8,128)S(1)}, u32[]{:S(2)}, u32[]{:S(2)}) collective-permute-start(f32[72,16,128]{2,1,0:T(8,128)} %collective-permute-done.4), channel_id=1, source_target_pairs={{0,224},{16,240},{32,0},{48,16},{64,32},{80,48},{96,64},{112,80},{... | collective-permute-start | bytes 1769480 | tf_op jit(solution)/shard_map/ppermute | solution.py:62
  54.0 41.8 %collective-permute-start.8 = (f32[72,16,128]{2,1,0:T(8,128)}, f32[72,16,128]{2,1,0:T(8,128)S(1)}, u32[]{:S(2)}, u32[]{:S(2)}) collective-permute-start(f32[72,16,128]{2,1,0:T(8,128)} %collective-permute-done.7), channel_id=1, source_target_pairs={{0,32},{16,48},{32,64},{48,80},{64,96},{80,112},{96,128},{112,144}... | collective-permute-start | bytes 1769480 | tf_op jit(solution)/shard_map/ppermute | solution.py:61
  56.0 22.4 %collective-permute-start.15 = (f32[4,128,128]{2,1,0:T(8,128)}, f32[4,128,128]{2,1,0:T(8,128)}, u32[]{:S(2)}, u32[]{:S(2)}) collective-permute-start(f32[4,128,128]{2,1,0:T(8,128)} %get-tuple-element.20), channel_id=1, source_target_pairs={{0,1},{1,2},{2,3},{3,4},{4,5},{5,6},{6,7},{7,8},{8,9},{9,10},{10,1... | collective-permute-start | bytes 786440 | tf_op jit(solution)/shard_map/ppermute | solution.py:40
  57.9 20.5 %collective-permute-start.16 = (f32[4,128,128]{2,1,0:T(8,128)}, f32[4,128,128]{2,1,0:T(8,128)}, u32[]{:S(2)}, u32[]{:S(2)}) collective-permute-start(f32[4,128,128]{2,1,0:T(8,128)} %get-tuple-element.21), channel_id=1, source_target_pairs={{1,0},{2,1},{3,2},{4,3},{5,4},{6,5},{7,6},{8,7},{9,8},{10,9},{11,1... | collective-permute-start | bytes 786440 | tf_op jit(solution)/shard_map/ppermute | solution.py:42
  68.1 10.4 %copy-start.8 = (f32[1,32,128,128]{3,2,1,0:T(8,128)S(1)}, f32[1,32,128,128]{3,2,1,0:T(8,128)}, u32[]{:S(2)}) copy-start(f32[1,32,128,128]{3,2,1,0:T(8,128)} %param.15) | copy-start | bytes 6291460
  78.5 17.7 %slice-start = ((s8[9437184]{0:T(1024)(128)(4,1)}), s8[1048576]{0:T(1024)(128)(4,1)S(1)}, s32[]{:S(2)}) async-start(s8[9437184]{0:T(1024)(128)(4,1)} %bitcast.14), calls=%async_computation | async-start | bytes 2097152
  81.8 14.4 %slice-start.1 = ((s8[9437184]{0:T(1024)(128)(4,1)}), s8[4194304]{0:T(1024)(128)(4,1)S(1)}, s32[]{:S(2)}) async-start(s8[9437184]{0:T(1024)(128)(4,1)} %bitcast.14), calls=%async_computation.1 | async-start | bytes 8388608
  81.8 14.4 %slice-start.2 = ((s8[9437184]{0:T(1024)(128)(4,1)}), s8[4194304]{0:T(1024)(128)(4,1)S(1)}, s32[]{:S(2)}) async-start(s8[9437184]{0:T(1024)(128)(4,1)} %bitcast.14), calls=%async_computation.2 | async-start | bytes 8388608
  81.8 14.4 %copy-start.14 = (f32[72,16,128]{2,1,0:T(8,128)S(1)}, f32[72,16,128]{2,1,0:T(8,128)}, u32[]{:S(2)}) copy-start(f32[72,16,128]{2,1,0:T(8,128)} %copy-done.13) | copy-start | bytes 1769476
  92.6 10.7 %collective-permute-start.10 = (f32[36,16,128]{2,1,0:T(8,128)S(1)}, f32[36,16,128]{2,1,0:T(8,128)S(1)}, u32[]{:S(2)}, u32[]{:S(2)}) collective-permute-start(f32[36,16,128]{2,1,0:T(8,128)S(1)} %slice.65), channel_id=1, source_target_pairs={{0,224},{16,240},{32,0},{48,16},{64,32},{80,48},{96,64},{112,80},{... | collective-permute-start | bytes 884744 | tf_op jit(solution)/shard_map/ppermute | solution.py:67
  95.9 11.1 %collective-permute-start.9 = (f32[36,16,128]{2,1,0:T(8,128)S(1)}, f32[36,16,128]{2,1,0:T(8,128)S(1)}, u32[]{:S(2)}, u32[]{:S(2)}) collective-permute-start(f32[36,16,128]{2,1,0:T(8,128)S(1)} %slice.64), channel_id=1, source_target_pairs={{0,32},{16,48},{32,64},{48,80},{64,96},{80,112},{96,128},{112,144}... | collective-permute-start | bytes 884744 | tf_op jit(solution)/shard_map/ppermute | solution.py:67
  97.4 10.9 %copy-start.12 = (f32[72,16,128]{2,1,0:T(8,128)S(1)}, f32[72,16,128]{2,1,0:T(8,128)}, u32[]{:S(2)}) copy-start(f32[72,16,128]{2,1,0:T(8,128)} %copy-done.11) | copy-start | bytes 1769476
  97.5 10.9 %copy-start.16 = (f32[72,16,128]{2,1,0:T(8,128)S(1)}, f32[72,16,128]{2,1,0:T(8,128)}, u32[]{:S(2)}) copy-start(f32[72,16,128]{2,1,0:T(8,128)} %copy-done.15) | copy-start | bytes 1769476
  114.6 19.6 %copy-start.10 = (f32[1,32,128,128]{3,2,1,0:T(8,128)S(1)}, f32[1,32,128,128]{3,2,1,0:T(8,128)}, u32[]{:S(2)}) copy-start(f32[1,32,128,128]{3,2,1,0:T(8,128)} %param.13) | copy-start | bytes 6291460
  125.0 19.2 %collective-permute-start.13 = (f32[4,128,128]{2,1,0:T(8,128)S(1)}, f32[4,128,128]{2,1,0:T(8,128)S(1)}, u32[]{:S(2)}, u32[]{:S(2)}) collective-permute-start(f32[4,128,128]{2,1,0:T(8,128)S(1)} %get-tuple-element.22), channel_id=1, source_target_pairs={{0,1},{1,2},{2,3},{3,4},{4,5},{5,6},{6,7},{7,8},{8,9},{9,10},{10,1... | collective-permute-start | bytes 786440 | tf_op jit(solution)/shard_map/ppermute | solution.py:40
  126.9 17.3 %collective-permute-start.14 = (f32[4,128,128]{2,1,0:T(8,128)S(1)}, f32[4,128,128]{2,1,0:T(8,128)S(1)}, u32[]{:S(2)}, u32[]{:S(2)}) collective-permute-start(f32[4,128,128]{2,1,0:T(8,128)S(1)} %get-tuple-element.23), channel_id=1, source_target_pairs={{1,0},{2,1},{3,2},{4,3},{5,4},{6,5},{7,6},{8,7},{9,8},{10,9},{11,1... | collective-permute-start | bytes 786440 | tf_op jit(solution)/shard_map/ppermute | solution.py:42
  134.9 22.6 %copy-start.9 = (f32[32,128,128]{2,1,0:T(8,128)}, f32[32,128,128]{2,1,0:T(8,128)S(1)}, u32[]{:S(2)}) copy-start(f32[32,128,128]{2,1,0:T(8,128)S(1)} %multiply_add_fusion) | copy-start | bytes 6291460
  134.9 22.6 %collective-permute-start.17 = (f32[4,128,128]{2,1,0:T(8,128)S(1)}, f32[4,128,128]{2,1,0:T(8,128)S(1)}, u32[]{:S(2)}, u32[]{:S(2)}) collective-permute-start(f32[4,128,128]{2,1,0:T(8,128)S(1)} %get-tuple-element.18), channel_id=1, source_target_pairs={{0,1},{1,2},{2,3},{3,4},{4,5},{5,6},{6,7},{7,8},{8,9},{9,10},{10,1... | collective-permute-start | bytes 786440 | tf_op jit(solution)/shard_map/ppermute | solution.py:40
  136.9 20.6 %collective-permute-start.18 = (f32[4,128,128]{2,1,0:T(8,128)S(1)}, f32[4,128,128]{2,1,0:T(8,128)S(1)}, u32[]{:S(2)}, u32[]{:S(2)}) collective-permute-start(f32[4,128,128]{2,1,0:T(8,128)S(1)} %get-tuple-element.19), channel_id=1, source_target_pairs={{1,0},{2,1},{3,2},{4,3},{5,4},{6,5},{7,6},{8,7},{9,8},{10,9},{11,1... | collective-permute-start | bytes 786440 | tf_op jit(solution)/shard_map/ppermute | solution.py:42
  (8 other events, 37.1 us)

commit v4 on v3

--- a/solution.py
+++ b/solution.py
@@ -45,7 +45,7 @@
     )
 
 
-def ring_gather(x):
+def ring_gather(x, bounds):
     n = lax.axis_size("probe")
     rings = n // 2
     p = lax.axis_index("probe")
@@ -67,10 +67,16 @@
         [lax.ppermute(fwd[:cut], "probe", ahead), lax.ppermute(bwd[cut:], "probe", behind)], axis=0
     )
     by_offset[half] = far
-    ordered = jnp.concatenate([by_offset[d] for d in range(rings)] * 2, axis=1)
     width = pair.shape[1]
-    start = ((rings - p // 2) % rings) * width
-    return lax.dynamic_slice_in_dim(ordered, start, rings * width, 1)
+    zpos = p // 2
+    outs = []
+    for lo, hi in bounds:
+        buf = jnp.zeros((hi - lo, rings * width, x.shape[2]), x.dtype)
+        for d in range(rings):
+            at = ((zpos + d) % rings) * width
+            buf = lax.dynamic_update_slice_in_dim(buf, by_offset[d][lo:hi], at, 1)
+        outs.append(buf)
+    return outs
 
 
 def _ext(lo_ref, hi_ref, idx):
@@ -212,9 +218,11 @@
     msub = jnp.asarray(np.concatenate([ms, mg], axis=0))
 
     depth = u_cur.shape[0]
-    both = ring_gather(jnp.concatenate([halo_depth(u_cur), u_prev], axis=0))
-    u_cur_ext = both[: depth + 2 * HALO]
-    u_prev_all = both[depth + 2 * HALO:]
+    cur_rows = depth + 2 * HALO
+    u_cur_ext, u_prev_all = ring_gather(
+        jnp.concatenate([halo_depth(u_cur), u_prev], axis=0),
+        ((0, cur_rows), (cur_rows, cur_rows + depth)),
+    )
 
     buoyancy_ext = halo_depth(buoyancy)
     slopes = slopes_of(buoyancy_ext, mlane, msub)

time: 172 us -> 166 us (0.965)
  waiting for transfers between devices: 26.3 us -> 22.9 us
  local copies, waits for them, and re-layouts: 14.7 us -> 12.6 us
    ppermute x3, waiting for transfers between devices: 0.01 us -> 18.2 us  [ring_gather(): fwd = lax.ppermute(fwd, 'probe', ahead)]
    ppermute x3, waiting for transfers between devices: 10.1 us -> 0.01 us  [ring_gather(): bwd = lax.ppermute(bwd, 'probe', behind)]
    ppermute x1, waiting for transfers between devices: 6.26 us -> 0.01 us  [ring_gather(): partner = lax.ppermute(x, 'probe', [(i, i ^ 1) for i in range(n)])]
    ppermute x1, waiting for transfers between devices: 3.74 us -> 0.04 us  [ring_gather(): lax.ppermute(fwd[:cut], 'probe', ahead)]
    slice x2 -> x0, local copies, waits for them, and re-layouts: 3.34 us -> none  [the longest x1 1.8 us: local_body(): u_cur_ext = both[:depth + 2 * HALO]]
    unnamed x57 -> x31, local copies, waits for them, and re-layouts: 6.71 us -> 4.22 us
    dynamic_update_slice x0 -> x15, local copies, waits for them, and re-layouts: none -> 2.38 us  [ring_gather(): buf = lax.dynamic_update_slice_in_dim(buf, by_offset[d][lo:hi], at, 1)]
    ppermute x3, starting transfers between devices: 12.8 us -> 10.6 us  [ring_gather(): bwd = lax.ppermute(bwd, 'probe', behind)]
  transfers between devices with their start and end apart: 19 -> 19, of which waited for: 5 -> 4; matrix products, arithmetic and copies ran while one was open for 9% -> 11% of each run, Pallas kernels for 18% -> 18%
where the time goes in v4:
time: 166 us; the launch traced here: 164 us
  starting transfers between devices  63.7 us (38%)
  Pallas kernels  51.6 us (31%)
  waiting for transfers between devices  22.9 us (14%)
  local copies, waits for them, and re-layouts  12.6 us (8%)
  other arithmetic  12.1 us (7%)
    pallas_call x4, Pallas kernels, apply_op(): pl.pallas_call(functools.partial(_op_kernel, (with_prev, with_img, want_i...  41.3 us
    ppermute x5, starting transfers between devices, halo_depth(): lax.ppermute(head, 'slab', [(i + 1, i) for i in range(ends)])  36.7 us
    ppermute x3, waiting for transfers between devices, ring_gather(): fwd = lax.ppermute(fwd, 'probe', ahead)  18.2 us
    ppermute x3, starting transfers between devices, ring_gather(): bwd = lax.ppermute(bwd, 'probe', behind)  10.6 us
    pallas_call x1, Pallas kernels, slopes_of(): pl.pallas_call(_slope_kernel, grid=(depth // BZ,), in_specs=_ext_specs(n)...  10.3 us
    ppermute x5, starting transfers between devices, halo_depth(): lax.ppermute(tail, 'slab', [(i, i + 1) for i in range(ends)])  9.7 us
    concatenate x4, other arithmetic, halo_depth(): jnp.concatenate([lax.ppermute(tail, 'slab', [(i, i + 1) for i in range(en...  9.58 us
    unnamed x31, local copies, waits for them, and re-layouts  4.22 us
  transfers between devices with their start and end apart: 19, of which 4 were waited for; matrix products, arithmetic and copies ran while one was open for 11% of the time, Pallas kernels for 18%

profile of v4, /device:TPU:6, one launch (start us, length us, event | category | flops | bytes accessed | tf_op | source)
XLA Modules:
  0.0 164.3 jit_solution(996294001977085521)
XLA Ops:
  1.4 2.0 %collective-permute-start = (f32[4,8,128]{2,1,0:T(8,128)S(1)}, f32[4,8,128]{2,1,0:T(8,128)S(1)}, u32[]{:S(2)}, u32[]{:S(2)}) collective-permute-start(f32[4,8,128]{2,1,0:T(8,128)S(1)} %get-tuple-element.25), channel_id=1, source_target_pairs={{0,1},{1,2},{2,3},{3,4},{4,5},{5,6},{6,7},{7,8},{8,9},{9,10},{10,1... | collective-permute-start | bytes 49160 | tf_op jit(solution)/shard_map/ppermute | solution.py:40
  3.4 7.3 %collective-permute-start.1 = (f32[4,8,128]{2,1,0:T(8,128)S(1)}, f32[4,8,128]{2,1,0:T(8,128)S(1)}, u32[]{:S(2)}, u32[]{:S(2)}) collective-permute-start(f32[4,8,128]{2,1,0:T(8,128)S(1)} %get-tuple-element.24), channel_id=1, source_target_pairs={{1,0},{2,1},{3,2},{4,3},{5,4},{6,5},{7,6},{8,7},{9,8},{10,9},{11,1... | collective-permute-start | bytes 49160 | tf_op jit(solution)/shard_map/ppermute | solution.py:42
  13.9 1.9 %fusion.3 = (f32[4,128,128]{2,1,0:T(8,128)}, f32[4,128,128]{2,1,0:T(8,128)}) fusion(f32[32,128,128]{2,1,0:T(8,128)} %refs_2_.7), kind=kLoop, calls=%fused_computation.33 | loop fusion | bytes 1048576 | tf_op jit(solution)/shard_map/slice | solution.py:37
  15.8 1.9 %collective-permute-start.11 = (f32[4,128,128]{2,1,0:T(8,128)}, f32[4,128,128]{2,1,0:T(8,128)S(1)}, u32[]{:S(2)}, u32[]{:S(2)}) collective-permute-start(f32[4,128,128]{2,1,0:T(8,128)} %get-tuple-element.22), channel_id=1, source_target_pairs={{0,1},{1,2},{2,3},{3,4},{4,5},{5,6},{6,7},{7,8},{8,9},{9,10},{10,1... | collective-permute-start | bytes 786440 | tf_op jit(solution)/shard_map/ppermute | solution.py:40
  17.7 7.6 %collective-permute-start.12 = (f32[4,128,128]{2,1,0:T(8,128)}, f32[4,128,128]{2,1,0:T(8,128)}, u32[]{:S(2)}, u32[]{:S(2)}) collective-permute-start(f32[4,128,128]{2,1,0:T(8,128)} %get-tuple-element.23), channel_id=1, source_target_pairs={{1,0},{2,1},{3,2},{4,3},{5,4},{6,5},{7,6},{8,7},{9,8},{10,9},{11,1... | collective-permute-start | bytes 786440 | tf_op jit(solution)/shard_map/ppermute | solution.py:42
  25.4 2.0 %collective-permute-start.6 = (f32[72,16,128]{2,1,0:T(8,128)S(1)}, f32[72,16,128]{2,1,0:T(8,128)S(1)}, u32[]{:S(2)}, u32[]{:S(2)}) collective-permute-start(f32[72,16,128]{2,1,0:T(8,128)S(1)} %maximum_select_fusion), channel_id=1, source_target_pairs={{0,32},{16,48},{32,64},{48,80},{64,96},{80,112},{96,128},{112,144}... | collective-permute-start | bytes 1769480 | tf_op jit(solution)/shard_map/ppermute | solution.py:61
  27.4 4.0 %collective-permute-start.3 = (f32[72,16,128]{2,1,0:T(8,128)S(1)}, f32[72,16,128]{2,1,0:T(8,128)}, u32[]{:S(2)}, u32[]{:S(2)}) collective-permute-start(f32[72,16,128]{2,1,0:T(8,128)S(1)} %maximum_select_fusion), channel_id=1, source_target_pairs={{0,224},{16,240},{32,0},{48,16},{64,32},{80,48},{96,64},{112,80},{... | collective-permute-start | bytes 1769480 | tf_op jit(solution)/shard_map/ppermute | solution.py:62
  31.4 1.9 %slice_bitcast_fusion.1 = (f32[4,128,128]{2,1,0:T(8,128)}, f32[4,128,128]{2,1,0:T(8,128)}) fusion(f32[1,32,128,128]{3,2,1,0:T(8,128)} %param.15), kind=kLoop, calls=%fused_computation.24 | loop fusion | bytes 1048576 | tf_op jit(solution)/shard_map/slice | solution.py:37
  33.3 1.9 %collective-permute-start.15 = (f32[4,128,128]{2,1,0:T(8,128)}, f32[4,128,128]{2,1,0:T(8,128)}, u32[]{:S(2)}, u32[]{:S(2)}) collective-permute-start(f32[4,128,128]{2,1,0:T(8,128)} %get-tuple-element.18), channel_id=1, source_target_pairs={{0,1},{1,2},{2,3},{3,4},{4,5},{5,6},{6,7},{7,8},{8,9},{9,10},{10,1... | collective-permute-start | bytes 786440 | tf_op jit(solution)/shard_map/ppermute | solution.py:40
  35.2 7.3 %collective-permute-start.16 = (f32[4,128,128]{2,1,0:T(8,128)}, f32[4,128,128]{2,1,0:T(8,128)}, u32[]{:S(2)}, u32[]{:S(2)}) collective-permute-start(f32[4,128,128]{2,1,0:T(8,128)} %get-tuple-element.19), channel_id=1, source_target_pairs={{1,0},{2,1},{3,2},{4,3},{5,4},{6,5},{7,6},{8,7},{9,8},{10,9},{11,1... | collective-permute-start | bytes 786440 | tf_op jit(solution)/shard_map/ppermute | solution.py:42
  42.7 2.8 %pad_maximum_fusion.lo_ref.hi_ref = f32[40,128,128]{2,1,0:T(8,128)} fusion(f32[4,128,128]{2,1,0:T(8,128)} %collective-permute-done.12, f32[32,128,128]{2,1,0:T(8,128)S(1)} %copy-done, f32[4,128,128]{2,1,0:T(8,128)S(1)} %collective-permute-done.11), kind=kLoop, calls=%fused_computation | loop fusion | flops 1310720 | bytes 5242880 | tf_op jit(solution)/shard_map/concatenate | solution.py:38
  45.5 10.3 %shard_map.120 = (f32[32,128,128]{2,1,0:T(8,128)S(1)}, f32[32,128,128]{2,1,0:T(8,128)S(1)}, f32[32,128,128]{2,1,0:T(8,128)}) custom-call(f32[40,128,128]{2,1,0:T(8,128)} %pad_maximum_fusion.lo_ref.hi_ref, f32[40,128,128]{2,1,0:T(8,128)} %pad_maximum_fusion.lo_ref.hi_ref, f32[128,256]{1,0:T(8,128)S(1)} %copy-done.7, f32[256,128]{1,0:T(8,128)S(1)} %copy-done.6), custom_call_target="tpu_custom_call" | custom-call | tf_op jit(solution)/shard_map/pallas_call | solution.py:175
  55.9 3.2 %pad_maximum_fusion.2.refs_0_.refs_1_ = f32[40,128,128]{2,1,0:T(8,128)} fusion(f32[4,128,128]{2,1,0:T(8,128)} %collective-permute-done.16, f32[32,128,128]{2,1,0:T(8,128)S(1)} %bitcast.11, f32[4,128,128]{2,1,0:T(8,128)} %collective-permute-done.15), kind=kLoop, calls=%fused_computation.2 | loop fusion | flops 1310720 | bytes 5242880 | tf_op jit(solution)/shard_map/concatenate | solution.py:38
  59.1 9.9 %shard_map.123 = f32[32,128,128]{2,1,0:T(8,128)S(1)} custom-call(f32[40,128,128]{2,1,0:T(8,128)} %pad_maximum_fusion.2.refs_0_.refs_1_, f32[40,128,128]{2,1,0:T(8,128)} %pad_maximum_fusion.2.refs_0_.refs_1_, f32[32,128,128]{2,1,0:T(8,128)S(1)} %copy-done, f32[32,128,128]{2,1,0:T(8,128)} %copy-done.2, f32[32,128,128]{2,1,0:T(8,128)} %copy-done.4, ...), custom_call_target="tpu_custom_call" | custom-call | tf_op jit(solution)/shard_map/pallas_call | solution.py:200
  69.1 3.2 %collective-permute-start.4 = (f32[72,16,128]{2,1,0:T(8,128)}, f32[72,16,128]{2,1,0:T(8,128)S(1)}, u32[]{:S(2)}, u32[]{:S(2)}) collective-permute-start(f32[72,16,128]{2,1,0:T(8,128)} %collective-permute-done.3), channel_id=1, source_target_pairs={{0,224},{16,240},{32,0},{48,16},{64,32},{80,48},{96,64},{112,80},{... | collective-permute-start | bytes 1769480 | tf_op jit(solution)/shard_map/ppermute | solution.py:62
  74.0 8.6 %collective-permute-done.7 = f32[72,16,128]{2,1,0:T(8,128)S(1)} collective-permute-done((f32[72,16,128]{2,1,0:T(8,128)S(1)}, f32[72,16,128]{2,1,0:T(8,128)S(1)}, u32[]{:S(2)}, u32[]{:S(2)}) %collective-permute-start.7) | collective-permute-done | bytes 589856 | tf_op jit(solution)/shard_map/ppermute | solution.py:61
  82.6 3.4 %collective-permute-start.5 = (f32[72,16,128]{2,1,0:T(8,128)S(1)}, f32[72,16,128]{2,1,0:T(8,128)S(1)}, u32[]{:S(2)}, u32[]{:S(2)}) collective-permute-start(f32[72,16,128]{2,1,0:T(8,128)S(1)} %collective-permute-done.4), channel_id=1, source_target_pairs={{0,224},{16,240},{32,0},{48,16},{64,32},{80,48},{96,64},{112,80},{... | collective-permute-start | bytes 1769480 | tf_op jit(solution)/shard_map/ppermute | solution.py:62
  87.0 9.6 %collective-permute-done.8 = f32[72,16,128]{2,1,0:T(8,128)S(1)} collective-permute-done((f32[72,16,128]{2,1,0:T(8,128)S(1)}, f32[72,16,128]{2,1,0:T(8,128)S(1)}, u32[]{:S(2)}, u32[]{:S(2)}) %collective-permute-start.8) | collective-permute-done | bytes 589856 | tf_op jit(solution)/shard_map/ppermute | solution.py:61
  96.8 3.5 %collective-permute-start.10 = (f32[36,16,128]{2,1,0:T(8,128)S(1)}, f32[36,16,128]{2,1,0:T(8,128)S(1)}, u32[]{:S(2)}, u32[]{:S(2)}) collective-permute-start(f32[36,16,128]{2,1,0:T(8,128)S(1)} %slice.125), channel_id=1, source_target_pairs={{0,224},{16,240},{32,0},{48,16},{64,32},{80,48},{96,64},{112,80},{... | collective-permute-start | bytes 884744 | tf_op jit(solution)/shard_map/ppermute | solution.py:67
  100.4 4.2 %collective-permute-done.10 = f32[36,16,128]{2,1,0:T(8,128)S(1)} collective-permute-done((f32[36,16,128]{2,1,0:T(8,128)S(1)}, f32[36,16,128]{2,1,0:T(8,128)S(1)}, u32[]{:S(2)}, u32[]{:S(2)}) %collective-permute-start.10) | collective-permute-done | bytes 294944 | tf_op jit(solution)/shard_map/ppermute | solution.py:67
  104.9 1.3 copy-done.11
  106.2 1.5 copy-done.8
  107.6 10.4 %shard_map.121 = (f32[32,128,128]{2,1,0:T(8,128)S(1)}, f32[32,128,128]{2,1,0:T(8,128)S(1)}) custom-call(f32[40,128,128]{2,1,0:T(8,128)} %copy-done.8, f32[40,128,128]{2,1,0:T(8,128)} %copy-done.8, f32[32,128,128]{2,1,0:T(8,128)} %refs_2_.7, f32[32,128,128]{2,1,0:T(8,128)} %copy-done.2, f32[32,128,128]{2,1,0:T(8,128)} %copy-done.4, ...), custom_call_target="tpu_custom_call" | custom-call | tf_op jit(solution)/shard_map/pallas_call | solution.py:200
  118.1 1.9 %collective-permute-start.13 = (f32[4,128,128]{2,1,0:T(8,128)S(1)}, f32[4,128,128]{2,1,0:T(8,128)S(1)}, u32[]{:S(2)}, u32[]{:S(2)}) collective-permute-start(f32[4,128,128]{2,1,0:T(8,128)S(1)} %get-tuple-element.20), channel_id=1, source_target_pairs={{0,1},{1,2},{2,3},{3,4},{4,5},{5,6},{6,7},{7,8},{8,9},{9,10},{10,1... | collective-permute-start | bytes 786440 | tf_op jit(solution)/shard_map/ppermute | solution.py:40
  120.0 7.3 %collective-permute-start.14 = (f32[4,128,128]{2,1,0:T(8,128)S(1)}, f32[4,128,128]{2,1,0:T(8,128)S(1)}, u32[]{:S(2)}, u32[]{:S(2)}) collective-permute-start(f32[4,128,128]{2,1,0:T(8,128)S(1)} %get-tuple-element.21), channel_id=1, source_target_pairs={{1,0},{2,1},{3,2},{4,3},{5,4},{6,5},{7,6},{8,7},{9,8},{10,9},{11,1... | collective-permute-start | bytes 786440 | tf_op jit(solution)/shard_map/ppermute | solution.py:42
  128.0 1.9 %collective-permute-start.17 = (f32[4,128,128]{2,1,0:T(8,128)S(1)}, f32[4,128,128]{2,1,0:T(8,128)S(1)}, u32[]{:S(2)}, u32[]{:S(2)}) collective-permute-start(f32[4,128,128]{2,1,0:T(8,128)S(1)} %get-tuple-element.16), channel_id=1, source_target_pairs={{0,1},{1,2},{2,3},{3,4},{4,5},{5,6},{6,7},{7,8},{8,9},{9,10},{10,1... | collective-permute-start | bytes 786440 | tf_op jit(solution)/shard_map/ppermute | solution.py:40
  129.9 7.4 %collective-permute-start.18 = (f32[4,128,128]{2,1,0:T(8,128)S(1)}, f32[4,128,128]{2,1,0:T(8,128)S(1)}, u32[]{:S(2)}, u32[]{:S(2)}) collective-permute-start(f32[4,128,128]{2,1,0:T(8,128)S(1)} %get-tuple-element.17), channel_id=1, source_target_pairs={{1,0},{2,1},{3,2},{4,3},{5,4},{6,5},{7,6},{8,7},{9,8},{10,9},{11,1... | collective-permute-start | bytes 786440 | tf_op jit(solution)/shard_map/ppermute | solution.py:42
  137.3 1.8 %pad_maximum_fusion.1.refs_0_.refs_1_ = f32[40,128,128]{2,1,0:T(8,128)} fusion(f32[4,128,128]{2,1,0:T(8,128)S(1)} %collective-permute-done.14, f32[32,128,128]{2,1,0:T(8,128)S(1)} %get-tuple-element.12, f32[4,128,128]{2,1,0:T(8,128)S(1)} %collective-permute-done.13), kind=kLoop, calls=%fused_computation.1 | loop fusion | flops 1310720 | bytes 5242880 | tf_op jit(solution)/shard_map/concatenate | solution.py:38
  139.1 9.6 %shard_map.122.refs_11_ = f32[32,128,128]{2,1,0:T(8,128)S(1)} custom-call(f32[40,128,128]{2,1,0:T(8,128)} %pad_maximum_fusion.1.refs_0_.refs_1_, f32[40,128,128]{2,1,0:T(8,128)} %pad_maximum_fusion.1.refs_0_.refs_1_, f32[32,128,128]{2,1,0:T(8,128)S(1)} %copy-done.1, f32[32,128,128]{2,1,0:T(8,128)} %copy-done.2, f32[32,128,128]{2,1,0:T(8,128)} %copy-done.4, ...), custom_call_target="tpu_custom_call" | custom-call | tf_op jit(solution)/shard_map/pallas_call | solution.py:200
  148.8 1.8 %multiply_add_fusion.1 = (f32[32,8,128]{2,1,0:T(8,128)}, f32[32,8,128]{2,1,0:T(8,128)}) fusion(f32[32,128,128]{2,1,0:T(8,128)S(1)} %shard_map.122.refs_11_, s32[]{:T(128)S(6)} %select_n.124, f32[32,128,128]{2,1,0:T(8,128)} %refs_8_.5, f32[32,8,128]{2,1,0:T(8,128)S(1)} %copy-done.13, f32[32,128,128]{2,1,0:T(8,128)S(1)} %get-tuple-element.12), kind=kLoop, calls=%fused_computation.25 | loop fusion | flops 131072 | bytes 786436 | tf_op jit(solution)/shard_map/add | solution.py:249
  150.6 1.8 %pad_maximum_fusion.3.refs_0_.refs_1_ = f32[40,128,128]{2,1,0:T(8,128)} fusion(f32[4,128,128]{2,1,0:T(8,128)S(1)} %collective-permute-done.18, f32[32,128,128]{2,1,0:T(8,128)S(1)} %multiply_add_fusion, f32[4,128,128]{2,1,0:T(8,128)S(1)} %collective-permute-done.17), kind=kLoop, calls=%fused_computation.3 | loop fusion | flops 1310720 | bytes 5242880 | tf_op jit(solution)/shard_map/concatenate | solution.py:38
  152.9 11.4 %shard_map.124 = f32[32,128,128]{2,1,0:T(8,128)} custom-call(f32[40,128,128]{2,1,0:T(8,128)} %pad_maximum_fusion.3.refs_0_.refs_1_, f32[40,128,128]{2,1,0:T(8,128)} %pad_maximum_fusion.3.refs_0_.refs_1_, f32[32,128,128]{2,1,0:T(8,128)S(1)} %copy-done.1, f32[32,128,128]{2,1,0:T(8,128)S(1)} %copy-done.3, f32[32,128,128]{2,1,0:T(8,128)} %copy-done.4, ...), custom_call_target="tpu_custom_call" | custom-call | tf_op jit(solution)/shard_map/pallas_call | solution.py:200
  (75 shorter events, 8.5 us)
Async XLA Ops:
  1.4 41.3 %copy-start = (f32[32,128,128]{2,1,0:T(8,128)S(1)}, f32[32,128,128]{2,1,0:T(8,128)}, u32[]{:S(2)}) copy-start(f32[32,128,128]{2,1,0:T(8,128)} %refs_2_.7) | copy-start | bytes 6291460
  1.4 9.3 %collective-permute-start = (f32[4,8,128]{2,1,0:T(8,128)S(1)}, f32[4,8,128]{2,1,0:T(8,128)S(1)}, u32[]{:S(2)}, u32[]{:S(2)}) collective-permute-start(f32[4,8,128]{2,1,0:T(8,128)S(1)} %get-tuple-element.25), channel_id=1, source_target_pairs={{0,1},{1,2},{2,3},{3,4},{4,5},{5,6},{6,7},{7,8},{8,9},{9,10},{10,1... | collective-permute-start | bytes 49160 | tf_op jit(solution)/shard_map/ppermute | solution.py:40
  3.4 8.7 %collective-permute-start.1 = (f32[4,8,128]{2,1,0:T(8,128)S(1)}, f32[4,8,128]{2,1,0:T(8,128)S(1)}, u32[]{:S(2)}, u32[]{:S(2)}) collective-permute-start(f32[4,8,128]{2,1,0:T(8,128)S(1)} %get-tuple-element.24), channel_id=1, source_target_pairs={{1,0},{2,1},{3,2},{4,3},{5,4},{6,5},{7,6},{8,7},{9,8},{10,9},{11,1... | collective-permute-start | bytes 49160 | tf_op jit(solution)/shard_map/ppermute | solution.py:42
  13.0 12.3 %collective-permute-start.2 = (f32[72,8,128]{2,1,0:T(8,128)S(1)}, f32[72,8,128]{2,1,0:T(8,128)S(1)}, u32[]{:S(2)}, u32[]{:S(2)}) collective-permute-start(f32[72,8,128]{2,1,0:T(8,128)S(1)} %constant_dynamic-update-slice_fusion), channel_id=1, source_target_pairs={{0,16},{16,0},{32,48},{48,32},{64,80},{80,64},{96,112},{112,96},{1... | collective-permute-start | bytes 884744 | tf_op jit(solution)/shard_map/ppermute | solution.py:52
  15.8 19.4 %collective-permute-start.11 = (f32[4,128,128]{2,1,0:T(8,128)}, f32[4,128,128]{2,1,0:T(8,128)S(1)}, u32[]{:S(2)}, u32[]{:S(2)}) collective-permute-start(f32[4,128,128]{2,1,0:T(8,128)} %get-tuple-element.22), channel_id=1, source_target_pairs={{0,1},{1,2},{2,3},{3,4},{4,5},{5,6},{6,7},{7,8},{8,9},{9,10},{10,1... | collective-permute-start | bytes 786440 | tf_op jit(solution)/shard_map/ppermute | solution.py:40
  17.7 25.0 %collective-permute-start.12 = (f32[4,128,128]{2,1,0:T(8,128)}, f32[4,128,128]{2,1,0:T(8,128)}, u32[]{:S(2)}, u32[]{:S(2)}) collective-permute-start(f32[4,128,128]{2,1,0:T(8,128)} %get-tuple-element.23), channel_id=1, source_target_pairs={{1,0},{2,1},{3,2},{4,3},{5,4},{6,5},{7,6},{8,7},{9,8},{10,9},{11,1... | collective-permute-start | bytes 786440 | tf_op jit(solution)/shard_map/ppermute | solution.py:42
  25.4 43.6 %collective-permute-start.6 = (f32[72,16,128]{2,1,0:T(8,128)S(1)}, f32[72,16,128]{2,1,0:T(8,128)S(1)}, u32[]{:S(2)}, u32[]{:S(2)}) collective-permute-start(f32[72,16,128]{2,1,0:T(8,128)S(1)} %maximum_select_fusion), channel_id=1, source_target_pairs={{0,32},{16,48},{32,64},{48,80},{64,96},{80,112},{96,128},{112,144}... | collective-permute-start | bytes 1769480 | tf_op jit(solution)/shard_map/ppermute | solution.py:61
  27.4 41.7 %collective-permute-start.3 = (f32[72,16,128]{2,1,0:T(8,128)S(1)}, f32[72,16,128]{2,1,0:T(8,128)}, u32[]{:S(2)}, u32[]{:S(2)}) collective-permute-start(f32[72,16,128]{2,1,0:T(8,128)S(1)} %maximum_select_fusion), channel_id=1, source_target_pairs={{0,224},{16,240},{32,0},{48,16},{64,32},{80,48},{96,64},{112,80},{... | collective-permute-start | bytes 1769480 | tf_op jit(solution)/shard_map/ppermute | solution.py:62
  33.3 22.6 %collective-permute-start.15 = (f32[4,128,128]{2,1,0:T(8,128)}, f32[4,128,128]{2,1,0:T(8,128)}, u32[]{:S(2)}, u32[]{:S(2)}) collective-permute-start(f32[4,128,128]{2,1,0:T(8,128)} %get-tuple-element.18), channel_id=1, source_target_pairs={{0,1},{1,2},{2,3},{3,4},{4,5},{5,6},{6,7},{7,8},{8,9},{9,10},{10,1... | collective-permute-start | bytes 786440 | tf_op jit(solution)/shard_map/ppermute | solution.py:40
  35.2 20.6 %collective-permute-start.16 = (f32[4,128,128]{2,1,0:T(8,128)}, f32[4,128,128]{2,1,0:T(8,128)}, u32[]{:S(2)}, u32[]{:S(2)}) collective-permute-start(f32[4,128,128]{2,1,0:T(8,128)} %get-tuple-element.19), channel_id=1, source_target_pairs={{1,0},{2,1},{3,2},{4,3},{5,4},{6,5},{7,6},{8,7},{9,8},{10,9},{11,1... | collective-permute-start | bytes 786440 | tf_op jit(solution)/shard_map/ppermute | solution.py:42
  42.6 2.8 %copy-start.6 = (f32[256,128]{1,0:T(8,128)S(1)}, f32[256,128]{1,0:T(8,128)}, u32[]{:S(2)}) copy-start(f32[256,128]{1,0:T(8,128)} %constant.108.clone.msub_ref.refs_7_) | copy-start | bytes 393220
  42.7 2.8 %copy-start.7 = (f32[128,256]{1,0:T(8,128)S(1)}, f32[128,256]{1,0:T(8,128)}, u32[]{:S(2)}) copy-start(f32[128,256]{1,0:T(8,128)} %constant.107.clone.mlane_ref.refs_6_) | copy-start | bytes 393220
  45.5 10.4 %copy-start.9 = (f32[1,32,128,128]{3,2,1,0:T(8,128)S(1)}, f32[1,32,128,128]{3,2,1,0:T(8,128)}, u32[]{:S(2)}) copy-start(f32[1,32,128,128]{3,2,1,0:T(8,128)} %param.15) | copy-start | bytes 6291460
  55.8 3.2 %copy-start.2 = (f32[32,128,128]{2,1,0:T(8,128)}, f32[32,128,128]{2,1,0:T(8,128)S(1)}, u32[]{:S(2)}) copy-start(f32[32,128,128]{2,1,0:T(8,128)S(1)} %get-tuple-element.9.refs_3_) | copy-start | bytes 6291460
  55.8 3.2 %copy-start.4 = (f32[32,128,128]{2,1,0:T(8,128)}, f32[32,128,128]{2,1,0:T(8,128)S(1)}, u32[]{:S(2)}) copy-start(f32[32,128,128]{2,1,0:T(8,128)S(1)} %get-tuple-element.10.refs_4_) | copy-start | bytes 6291460
  69.0 13.6 %collective-permute-start.7 = (f32[72,16,128]{2,1,0:T(8,128)S(1)}, f32[72,16,128]{2,1,0:T(8,128)S(1)}, u32[]{:S(2)}, u32[]{:S(2)}) collective-permute-start(f32[72,16,128]{2,1,0:T(8,128)S(1)} %collective-permute-done.6), channel_id=1, source_target_pairs={{0,32},{16,48},{32,64},{48,80},{64,96},{80,112},{96,128},{112,144}... | collective-permute-start | bytes 1769480 | tf_op jit(solution)/shard_map/ppermute | solution.py:61
  69.1 13.5 %collective-permute-start.4 = (f32[72,16,128]{2,1,0:T(8,128)}, f32[72,16,128]{2,1,0:T(8,128)S(1)}, u32[]{:S(2)}, u32[]{:S(2)}) collective-permute-start(f32[72,16,128]{2,1,0:T(8,128)} %collective-permute-done.3), channel_id=1, source_target_pairs={{0,224},{16,240},{32,0},{48,16},{64,32},{80,48},{96,64},{112,80},{... | collective-permute-start | bytes 1769480 | tf_op jit(solution)/shard_map/ppermute | solution.py:62
  82.6 14.0 %collective-permute-start.8 = (f32[72,16,128]{2,1,0:T(8,128)S(1)}, f32[72,16,128]{2,1,0:T(8,128)S(1)}, u32[]{:S(2)}, u32[]{:S(2)}) collective-permute-start(f32[72,16,128]{2,1,0:T(8,128)S(1)} %collective-permute-done.7), channel_id=1, source_target_pairs={{0,32},{16,48},{32,64},{48,80},{64,96},{80,112},{96,128},{112,144}... | collective-permute-start | bytes 1769480 | tf_op jit(solution)/shard_map/ppermute | solution.py:61
  82.6 14.1 %collective-permute-start.5 = (f32[72,16,128]{2,1,0:T(8,128)S(1)}, f32[72,16,128]{2,1,0:T(8,128)S(1)}, u32[]{:S(2)}, u32[]{:S(2)}) collective-permute-start(f32[72,16,128]{2,1,0:T(8,128)S(1)} %collective-permute-done.4), channel_id=1, source_target_pairs={{0,224},{16,240},{32,0},{48,16},{64,32},{80,48},{96,64},{112,80},{... | collective-permute-start | bytes 1769480 | tf_op jit(solution)/shard_map/ppermute | solution.py:62
  96.6 8.0 %collective-permute-start.9 = (f32[36,16,128]{2,1,0:T(8,128)S(1)}, f32[36,16,128]{2,1,0:T(8,128)S(1)}, u32[]{:S(2)}, u32[]{:S(2)}) collective-permute-start(f32[36,16,128]{2,1,0:T(8,128)S(1)} %slice.124), channel_id=1, source_target_pairs={{0,32},{16,48},{32,64},{48,80},{64,96},{80,112},{96,128},{112,144}... | collective-permute-start | bytes 884744 | tf_op jit(solution)/shard_map/ppermute | solution.py:67
  96.8 7.8 %collective-permute-start.10 = (f32[36,16,128]{2,1,0:T(8,128)S(1)}, f32[36,16,128]{2,1,0:T(8,128)S(1)}, u32[]{:S(2)}, u32[]{:S(2)}) collective-permute-start(f32[36,16,128]{2,1,0:T(8,128)S(1)} %slice.125), channel_id=1, source_target_pairs={{0,224},{16,240},{32,0},{48,16},{64,32},{80,48},{96,64},{112,80},{... | collective-permute-start | bytes 884744 | tf_op jit(solution)/shard_map/ppermute | solution.py:67
  106.2 1.5 copy-start.8
  107.6 19.6 %copy-start.12 = (f32[1,32,128,128]{3,2,1,0:T(8,128)S(1)}, f32[1,32,128,128]{3,2,1,0:T(8,128)}, u32[]{:S(2)}) copy-start(f32[1,32,128,128]{3,2,1,0:T(8,128)} %param.13) | copy-start | bytes 6291460
  118.1 19.2 %collective-permute-start.13 = (f32[4,128,128]{2,1,0:T(8,128)S(1)}, f32[4,128,128]{2,1,0:T(8,128)S(1)}, u32[]{:S(2)}, u32[]{:S(2)}) collective-permute-start(f32[4,128,128]{2,1,0:T(8,128)S(1)} %get-tuple-element.20), channel_id=1, source_target_pairs={{0,1},{1,2},{2,3},{3,4},{4,5},{5,6},{6,7},{7,8},{8,9},{9,10},{10,1... | collective-permute-start | bytes 786440 | tf_op jit(solution)/shard_map/ppermute | solution.py:40
  120.0 17.3 %collective-permute-start.14 = (f32[4,128,128]{2,1,0:T(8,128)S(1)}, f32[4,128,128]{2,1,0:T(8,128)S(1)}, u32[]{:S(2)}, u32[]{:S(2)}) collective-permute-start(f32[4,128,128]{2,1,0:T(8,128)S(1)} %get-tuple-element.21), channel_id=1, source_target_pairs={{1,0},{2,1},{3,2},{4,3},{5,4},{6,5},{7,6},{8,7},{9,8},{10,9},{11,1... | collective-permute-start | bytes 786440 | tf_op jit(solution)/shard_map/ppermute | solution.py:42
  127.9 22.7 %copy-start.10 = (f32[32,128,128]{2,1,0:T(8,128)}, f32[32,128,128]{2,1,0:T(8,128)S(1)}, u32[]{:S(2)}) copy-start(f32[32,128,128]{2,1,0:T(8,128)S(1)} %multiply_add_fusion) | copy-start | bytes 6291460
  128.0 22.6 %collective-permute-start.17 = (f32[4,128,128]{2,1,0:T(8,128)S(1)}, f32[4,128,128]{2,1,0:T(8,128)S(1)}, u32[]{:S(2)}, u32[]{:S(2)}) collective-permute-start(f32[4,128,128]{2,1,0:T(8,128)S(1)} %get-tuple-element.16), channel_id=1, source_target_pairs={{0,1},{1,2},{2,3},{3,4},{4,5},{5,6},{6,7},{7,8},{8,9},{9,10},{10,1... | collective-permute-start | bytes 786440 | tf_op jit(solution)/shard_map/ppermute | solution.py:40
  129.9 9.2 %copy-start.1 = (f32[32,128,128]{2,1,0:T(8,128)S(1)}, f32[32,128,128]{2,1,0:T(8,128)}, u32[]{:S(2)}) copy-start(f32[32,128,128]{2,1,0:T(8,128)} %refs_2_.7) | copy-start | bytes 6291460
  129.9 20.7 %collective-permute-start.18 = (f32[4,128,128]{2,1,0:T(8,128)S(1)}, f32[4,128,128]{2,1,0:T(8,128)S(1)}, u32[]{:S(2)}, u32[]{:S(2)}) collective-permute-start(f32[4,128,128]{2,1,0:T(8,128)S(1)} %get-tuple-element.17), channel_id=1, source_target_pairs={{1,0},{2,1},{3,2},{4,3},{5,4},{6,5},{7,6},{8,7},{9,8},{10,9},{11,1... | collective-permute-start | bytes 786440 | tf_op jit(solution)/shard_map/ppermute | solution.py:42
  139.1 9.6 %copy-start.13 = (f32[32,8,128]{2,1,0:T(8,128)S(1)}, f32[32,8,128]{2,1,0:T(8,128)}, u32[]{:S(2)}) copy-start(f32[32,8,128]{2,1,0:T(8,128)} %param.10) | copy-start | bytes 393220
  148.7 3.7 %copy-start.5 = (f32[32,128,128]{2,1,0:T(8,128)}, f32[32,128,128]{2,1,0:T(8,128)S(1)}, u32[]{:S(2)}) copy-start(f32[32,128,128]{2,1,0:T(8,128)S(1)} %shard_map.122.refs_11_) | copy-start | bytes 6291460
  150.6 2.3 %copy-start.3 = (f32[32,128,128]{2,1,0:T(8,128)S(1)}, f32[32,128,128]{2,1,0:T(8,128)}, u32[]{:S(2)}) copy-start(f32[32,128,128]{2,1,0:T(8,128)} %copy-done.2) | copy-start | bytes 6291460
  (1 other events, 1.3 us)

commit v5 on v4

--- a/solution.py
+++ b/solution.py
@@ -85,33 +85,39 @@
     return hi_ref[idx - BZ]
 
 
-def _depth_terms(lo_ref, hi_ref, j):
+def _depth_terms(lo_ref, hi_ref, j, off, rows):
     c = j + HALO
-    centre = _ext(lo_ref, hi_ref, c)
+
+    def at(idx):
+        return _ext(lo_ref, hi_ref, idx)[off:off + rows]
+
+    whole = _ext(lo_ref, hi_ref, c)
+    centre = whole[off:off + rows]
     second = (3.0 * SECOND[0]) * centre
     grad = None
     for k in range(1, 5):
-        up = _ext(lo_ref, hi_ref, c + k)
-        down = _ext(lo_ref, hi_ref, c - k)
+        up = at(c + k)
+        down = at(c - k)
         second = second + SECOND[k] * (up + down)
         term = FIRST[k] * (up - down)
         grad = term if grad is None else grad + term
-    return centre, second, grad
-
-
-def _slope_kernel(lo_ref, hi_ref, mlane_ref, msub_ref, g0_ref, g1_ref, g2_ref):
+    return whole, centre, second, grad
+
+
+def _slope_kernel(off, lo_ref, hi_ref, mlane_ref, msub_ref, g0_ref, g1_ref, g2_ref):
     n = mlane_ref.shape[0]
+    rows = g0_ref.shape[1]
     for j in range(BZ):
-        centre, _, grad = _depth_terms(lo_ref, hi_ref, j)
+        whole, centre, _, grad = _depth_terms(lo_ref, hi_ref, j, off, rows)
         lane = jnp.dot(centre, mlane_ref[...], precision=HI, preferred_element_type=jnp.float32)
-        sub = jnp.dot(msub_ref[...], centre, precision=HI, preferred_element_type=jnp.float32)
+        sub = jnp.dot(msub_ref[...], whole, precision=HI, preferred_element_type=jnp.float32)
         g0_ref[j] = grad
-        g1_ref[j] = sub[n:]
+        g1_ref[j] = sub[rows:]
         g2_ref[j] = lane[:, n:]
 
 
 def _op_kernel(flags, *refs):
-    with_prev, with_img, want_image, want_step = flags
+    with_prev, with_img, want_image, want_step, off = flags
     refs = list(refs)
     lo_ref, hi_ref, b_ref, g0_ref, g1_ref, g2_ref, mlane_ref, msub_ref = refs[:8]
     rest = refs[8:]
@@ -125,15 +131,16 @@
             img_ref = rest.pop(0)
     outs = rest
     n = mlane_ref.shape[0]
+    rows = b_ref.shape[1]
     for j in range(BZ):
-        centre, second, grad = _depth_terms(lo_ref, hi_ref, j)
+        whole, centre, second, grad = _depth_terms(lo_ref, hi_ref, j, off, rows)
         lane = jnp.dot(centre, mlane_ref[...], precision=HI, preferred_element_type=jnp.float32)
-        sub = jnp.dot(msub_ref[...], centre, precision=HI, preferred_element_type=jnp.float32)
-        second = second + sub[:n] + lane[:, :n]
+        sub = jnp.dot(msub_ref[...], whole, precision=HI, preferred_element_type=jnp.float32)
+        second = second + sub[:rows] + lane[:, :n]
         image = (
             b_ref[j] * second
             + g0_ref[j] * grad
-            + g1_ref[j] * sub[n:]
+            + g1_ref[j] * sub[rows:]
             + g2_ref[j] * lane[:, n:]
         )
         at = 0
@@ -149,64 +156,87 @@
             outs[at][j] = step
 
 
-def _specs(n, count):
-    blk = pl.BlockSpec((BZ, n, n), lambda i: (i, 0, 0))
+def _specs(rows, n, count):
+    blk = pl.BlockSpec((BZ, rows, n), lambda i: (i, 0, 0))
     return [blk] * count
 
 
-def _ext_specs(n):
+def _ext_specs(rows, n):
     return [
-        pl.BlockSpec((BZ, n, n), lambda i: (i, 0, 0)),
-        pl.BlockSpec((BZ, n, n), lambda i: (i + 1, 0, 0)),
+        pl.BlockSpec((BZ, rows, n), lambda i: (i, 0, 0)),
+        pl.BlockSpec((BZ, rows, n), lambda i: (i + 1, 0, 0)),
     ]
 
 
-def _mat_specs(n):
+def _mat_specs(mlane, msub):
     return [
-        pl.BlockSpec((n, 2 * n), lambda i: (0, 0)),
-        pl.BlockSpec((2 * n, n), lambda i: (0, 0)),
+        pl.BlockSpec(mlane.shape, lambda i: (0, 0)),
+        pl.BlockSpec(msub.shape, lambda i: (0, 0)),
     ]
+
+
+PARAMS = pltpu.CompilerParams(vmem_limit_bytes=48 * 1024 * 1024)
 
 
 def slopes_of(b_ext, mlane, msub):
     depth = b_ext.shape[0] - 2 * HALO
-    n = b_ext.shape[1]
-    shape = jax.ShapeDtypeStruct((depth, n, n), jnp.float32)
+    rows_in = b_ext.shape[1]
+    rows = msub.shape[0] // 2
+    n = b_ext.shape[2]
+    shape = jax.ShapeDtypeStruct((depth, rows, n), jnp.float32)
     return pl.pallas_call(
-        _slope_kernel,
+        functools.partial(_slope_kernel, (rows_in - rows) // 2),
         grid=(depth // BZ,),
-        in_specs=_ext_specs(n) + _mat_specs(n),
-        out_specs=_specs(n, 3),
+        in_specs=_ext_specs(rows_in, n) + _mat_specs(mlane, msub),
+        out_specs=_specs(rows, n, 3),
         out_shape=[shape] * 3,
-        compiler_params=pltpu.CompilerParams(vmem_limit_bytes=48 * 1024 * 1024),
+        compiler_params=PARAMS,
         interpret=INTERPRET,
     )(b_ext, b_ext, mlane, msub)
 
 
 def apply_op(f_ext, b, slopes, mlane, msub, kappa=None, prev=None, dk=None, img=None, want_image=False):
     depth = f_ext.shape[0] - 2 * HALO
-    n = f_ext.shape[1]
+    rows_in = f_ext.shape[1]
+    rows = b.shape[1]
+    n = f_ext.shape[2]
+    off = (rows_in - rows) // 2
     want_step = kappa is not None
     with_prev = prev is not None
     with_img = img is not None
     args = [f_ext, f_ext, b, *slopes, mlane, msub]
-    in_specs = _ext_specs(n) + _specs(n, 4) + _mat_specs(n)
+    in_specs = _ext_specs(rows_in, n) + _specs(rows, n, 4) + _mat_specs(mlane, msub)
     if want_step:
         extra = [kappa] + ([prev] if with_prev else []) + ([dk, img] if with_img else [])
         args += extra
-        in_specs += _specs(n, len(extra))
+        in_specs += _specs(rows, n, len(extra))
     n_out = int(want_image) + int(want_step)
-    shape = jax.ShapeDtypeStruct((depth, n, n), jnp.float32)
+    shape = jax.ShapeDtypeStruct((depth, rows, n), jnp.float32)
     outs = pl.pallas_call(
-        functools.partial(_op_kernel, (with_prev, with_img, want_image, want_step)),
+        functools.partial(_op_kernel, (with_prev, with_img, want_image, want_step, off)),
         grid=(depth // BZ,),
         in_specs=in_specs,
-        out_specs=_specs(n, n_out),
+        out_specs=_specs(rows, n, n_out),
         out_shape=[shape] * n_out,
-        compiler_params=pltpu.CompilerParams(vmem_limit_bytes=48 * 1024 * 1024),
+        compiler_params=PARAMS,
         interpret=INTERPRET,
     )(*args)
     return outs
+
+
+def halo_rows(cells):
+    count = lax.axis_size("probe")
+    ends = count - 1
+    head = cells[:, :HALO]
+    tail = cells[:, cells.shape[1] - HALO:]
+    return jnp.concatenate(
+        [
+            lax.ppermute(tail, "probe", [(i, i + 1) for i in range(ends)]),
+            cells,
+            lax.ppermute(head, "probe", [(i + 1, i) for i in range(ends)]),
+        ],
+        axis=1,
+    )
 
 
 def local_body(u_prev, u_cur, buoyancy, kappa, dkappa, du_prev, du_cur):
@@ -216,44 +246,44 @@
     ms, mg = band_matrices(n)
     mlane = jnp.asarray(np.concatenate([ms, mg.T], axis=1))
     msub = jnp.asarray(np.concatenate([ms, mg], axis=0))
-
-    depth = u_cur.shape[0]
-    cur_rows = depth + 2 * HALO
-    u_cur_ext, u_prev_all = ring_gather(
-        jnp.concatenate([halo_depth(u_cur), u_prev], axis=0),
-        ((0, cur_rows), (cur_rows, cur_rows + depth)),
-    )
+    rows_in = strip + 2 * HALO
+    ms_s, mg_s = band_matrices(rows_in)
+    msub_strip = jnp.asarray(np.concatenate([ms_s[HALO:HALO + strip], mg_s[HALO:HALO + strip]], axis=0))
 
     buoyancy_ext = halo_depth(buoyancy)
     slopes = slopes_of(buoyancy_ext, mlane, msub)
+
+    def cut_strip(field):
+        return lax.dynamic_slice_in_dim(field, offset, strip, 1)
+
+    strip_b = cut_strip(buoyancy)
+    rimmed = jnp.pad(buoyancy_ext, [(0, 0), (HALO, HALO), (0, 0)])
+    strip_slopes = slopes_of(lax.dynamic_slice_in_dim(rimmed, offset, rows_in, 1), mlane, msub_strip)
+    strip_kappa = cut_strip(kappa)
+
+    image_first_strip, background_first = apply_op(
+        halo_rows(halo_depth(u_cur)), strip_b, strip_slopes, mlane, msub_strip,
+        kappa=strip_kappa, prev=u_prev, want_image=True,
+    )
+    (image_first,) = ring_gather(image_first_strip, ((0, image_first_strip.shape[0]),))
+    (image_second_strip,) = apply_op(
+        halo_rows(halo_depth(background_first)), strip_b, strip_slopes, mlane, msub_strip,
+        want_image=True,
+    )
+    background_second = 2.0 * background_first - u_cur + strip_kappa * image_second_strip
+    (image_second,) = ring_gather(image_second_strip, ((0, image_second_strip.shape[0]),))
 
     probe_kappa = dkappa[0]
     older = du_prev[0]
     newer = du_cur[0]
-
     newer_ext = halo_depth(newer)
     (partial_first,) = apply_op(newer_ext, buoyancy, slopes, mlane, msub, kappa=kappa, prev=older)
-
-    image_first, background_first = apply_op(
-        u_cur_ext, buoyancy, slopes, mlane, msub, kappa=kappa, prev=u_prev_all, want_image=True
-    )
     born_first = partial_first + probe_kappa * image_first
-
-    (image_second,) = apply_op(halo_depth(background_first), buoyancy, slopes, mlane, msub, want_image=True)
-
-    def cut_strip(field):
-        return lax.dynamic_slice_in_dim(field, offset, strip, 1)
-
-    background_first_strip = cut_strip(background_first)
-    background_second = (
-        2.0 * background_first_strip - u_cur + cut_strip(kappa) * cut_strip(image_second)
-    )
-
-    (born_second,) = apply_op(
-        halo_depth(born_first), buoyancy, slopes, mlane, msub,
-        kappa=kappa, prev=newer, dk=probe_kappa, img=image_second,
-    )
-    return background_first_strip, background_second, born_first[None], born_second[None]
+    (partial_second,) = apply_op(
+        halo_depth(born_first), buoyancy, slopes, mlane, msub, kappa=kappa, prev=newer
+    )
+    born_second = partial_second + probe_kappa * image_second
+    return background_first, background_second, born_first[None], born_second[None]
 
 
 def solution(mesh):

time: 166 us -> 181 us (1.090)
  the two profiles are of different devices: /device:TPU:6 before, /device:TPU:123 now
where the time goes in v5:
time: 181 us; the launch traced here: 180 us
  starting transfers between devices  71.5 us (40%)
  Pallas kernels  39.2 us (22%)
  waiting for transfers between devices  35.2 us (19%)
  local copies, waits for them, and re-layouts  20.3 us (11%)
  other arithmetic  13 us (7%)
    pallas_call x4, Pallas kernels, apply_op(): pl.pallas_call(functools.partial(_op_kernel, (with_prev, with_img, want_i...  26.3 us
    ppermute x5, starting transfers between devices, halo_depth(): lax.ppermute(tail, 'slab', [(i, i + 1) for i in range(ends)])  23.7 us
    ppermute x5, waiting for transfers between devices, halo_depth(): lax.ppermute(head, 'slab', [(i + 1, i) for i in range(ends)])  19 us
    ppermute x6, starting transfers between devices, ring_gather(): fwd = lax.ppermute(fwd, 'probe', ahead)  16 us
    pallas_call x2, Pallas kernels, slopes_of(): pl.pallas_call(functools.partial(_slope_kernel, (rows_in - rows) // 2), g...  13 us
    ppermute x5, starting transfers between devices, halo_depth(): lax.ppermute(head, 'slab', [(i + 1, i) for i in range(ends)])  9.59 us
    dynamic_update_slice x12, local copies, waits for them, and re-layouts, ring_gather(): buf = lax.dynamic_update_slice_in_dim(buf, by_offset[d][lo:hi], at, 1)  7.55 us
    ppermute x2, starting transfers between devices, halo_rows(): lax.ppermute(tail, 'probe', [(i, i + 1) for i in range(ends)])  7.02 us
  transfers between devices with their start and end apart: 32, of which 10 were waited for; matrix products, arithmetic and copies ran while one was open for 12% of the time, Pallas kernels for 13%

profile of v5, /device:TPU:123, one launch (start us, length us, event | category | flops | bytes accessed | tf_op | source)
XLA Modules:
  0.0 180.4 jit_solution(13177246441274344998)
XLA Ops:
  1.9 4.0 %collective-permute-start.4 = (f32[4,128,128]{2,1,0:T(8,128)S(1)}, f32[4,128,128]{2,1,0:T(8,128)S(1)}, u32[]{:S(2)}, u32[]{:S(2)}) collective-permute-start(f32[4,128,128]{2,1,0:T(8,128)S(1)} %get-tuple-element.29), channel_id=1, source_target_pairs={{0,1},{1,2},{2,3},{3,4},{4,5},{5,6},{6,7},{7,8},{8,9},{9,10},{10,1... | collective-permute-start | bytes 786440 | tf_op jit(solution)/shard_map/ppermute | solution.py:40
  8.5 7.2 %collective-permute-start = (f32[4,8,128]{2,1,0:T(8,128)S(1)}, f32[4,8,128]{2,1,0:T(8,128)S(1)}, u32[]{:S(2)}, u32[]{:S(2)}) collective-permute-start(f32[4,8,128]{2,1,0:T(8,128)S(1)} %get-tuple-element.37), channel_id=1, source_target_pairs={{0,1},{1,2},{2,3},{3,4},{4,5},{5,6},{6,7},{7,8},{8,9},{9,10},{10,1... | collective-permute-start | bytes 49160 | tf_op jit(solution)/shard_map/ppermute | solution.py:40
  15.8 1.9 %collective-permute-start.1 = (f32[4,8,128]{2,1,0:T(8,128)S(1)}, f32[4,8,128]{2,1,0:T(8,128)S(1)}, u32[]{:S(2)}, u32[]{:S(2)}) collective-permute-start(f32[4,8,128]{2,1,0:T(8,128)S(1)} %get-tuple-element.36), channel_id=1, source_target_pairs={{1,0},{2,1},{3,2},{4,3},{5,4},{6,5},{7,6},{8,7},{9,8},{10,9},{11,1... | collective-permute-start | bytes 49160 | tf_op jit(solution)/shard_map/ppermute | solution.py:42
  19.6 5.5 %collective-permute-done.1 = f32[4,8,128]{2,1,0:T(8,128)S(1)} collective-permute-done((f32[4,8,128]{2,1,0:T(8,128)S(1)}, f32[4,8,128]{2,1,0:T(8,128)S(1)}, u32[]{:S(2)}, u32[]{:S(2)}) %collective-permute-start.1) | collective-permute-done | bytes 16416 | tf_op jit(solution)/shard_map/ppermute | solution.py:42
  25.1 5.1 %collective-permute-start.2 = (f32[40,4,128]{2,1,0:T(4,128)S(1)}, f32[40,4,128]{2,1,0:T(4,128)S(1)}, u32[]{:S(2)}, u32[]{:S(2)}) collective-permute-start(f32[40,4,128]{2,1,0:T(4,128)S(1)} %get-tuple-element.32), channel_id=1, source_target_pairs={{0,16},{16,32},{32,48},{48,64},{64,80},{80,96},{96,112},{112,128},... | collective-permute-start | bytes 245768 | tf_op jit(solution)/shard_map/ppermute | solution.py:234
  30.2 1.9 %collective-permute-start.3 = (f32[40,4,128]{2,1,0:T(4,128)S(1)}, f32[40,4,128]{2,1,0:T(4,128)S(1)}, u32[]{:S(2)}, u32[]{:S(2)}) collective-permute-start(f32[40,4,128]{2,1,0:T(4,128)S(1)} %get-tuple-element.33), channel_id=1, source_target_pairs={{16,0},{32,16},{48,32},{64,48},{80,64},{96,80},{112,96},{128,112},... | collective-permute-start | bytes 245768 | tf_op jit(solution)/shard_map/ppermute | solution.py:236
  33.1 4.4 %collective-permute-done.3 = f32[40,4,128]{2,1,0:T(4,128)S(1)} collective-permute-done((f32[40,4,128]{2,1,0:T(4,128)S(1)}, f32[40,4,128]{2,1,0:T(4,128)S(1)}, u32[]{:S(2)}, u32[]{:S(2)}) %collective-permute-start.3) | collective-permute-done | bytes 81952 | tf_op jit(solution)/shard_map/ppermute | solution.py:236
  39.4 2.7 %shard_map.129 = (f32[32,8,128]{2,1,0:T(8,128)S(1)}, f32[32,8,128]{2,1,0:T(8,128)S(1)}, f32[32,8,128]{2,1,0:T(8,128)S(1)}) custom-call(f32[40,16,128]{2,1,0:T(8,128)S(1)} %pad_dynamic-slice_fusion.lo_ref.hi_ref, f32[40,16,128]{2,1,0:T(8,128)S(1)} %pad_dynamic-slice_fusion.lo_ref.hi_ref, f32[128,256]{1,0:T(8,128)S(1)} %copy-done.3, f32[16,16]{1,0:T(8,128)S(1)} %copy-done.6), custom_call_target="tpu_custom_call" | custom-call | tf_op jit(solution)/shard_map/pallas_call | solution.py:187
  42.1 3.5 %shard_map.130 = (f32[32,8,128]{2,1,0:T(8,128)S(1)}, f32[32,8,128]{2,1,0:T(8,128)}) custom-call(f32[40,16,128]{2,1,0:T(8,128)S(1)} %pad_maximum_fusion.2.refs_0_.refs_1_, f32[40,16,128]{2,1,0:T(8,128)S(1)} %pad_maximum_fusion.2.refs_0_.refs_1_, f32[32,8,128]{2,1,0:T(8,128)S(1)} %constant_dynamic-slice_fusion.1.refs_2_, ...), custom_call_target="tpu_custom_call" | custom-call | tf_op jit(solution)/shard_map/pallas_call | solution.py:215
  46.3 3.1 %collective-permute-start.6 = (f32[4,8,128]{2,1,0:T(8,128)S(1)}, f32[4,8,128]{2,1,0:T(8,128)S(1)}, u32[]{:S(2)}, u32[]{:S(2)}) collective-permute-start(f32[4,8,128]{2,1,0:T(8,128)S(1)} %get-tuple-element.35), channel_id=1, source_target_pairs={{0,1},{1,2},{2,3},{3,4},{4,5},{5,6},{6,7},{7,8},{8,9},{9,10},{10,1... | collective-permute-start | bytes 49160 | tf_op jit(solution)/shard_map/ppermute | solution.py:40
  52.4 6.4 %collective-permute-done.7 = f32[4,8,128]{2,1,0:T(8,128)S(1)} collective-permute-done((f32[4,8,128]{2,1,0:T(8,128)S(1)}, f32[4,8,128]{2,1,0:T(8,128)S(1)}, u32[]{:S(2)}, u32[]{:S(2)}) %collective-permute-start.7) | collective-permute-done | bytes 16416 | tf_op jit(solution)/shard_map/ppermute | solution.py:42
  58.8 1.9 %collective-permute-start.8 = (f32[40,4,128]{2,1,0:T(4,128)S(1)}, f32[40,4,128]{2,1,0:T(4,128)S(1)}, u32[]{:S(2)}, u32[]{:S(2)}) collective-permute-start(f32[40,4,128]{2,1,0:T(4,128)S(1)} %get-tuple-element.30), channel_id=1, source_target_pairs={{0,16},{16,32},{32,48},{48,64},{64,80},{80,96},{96,112},{112,128},... | collective-permute-start | bytes 245768 | tf_op jit(solution)/shard_map/ppermute | solution.py:234
  60.8 3.4 %collective-permute-start.9 = (f32[40,4,128]{2,1,0:T(4,128)S(1)}, f32[40,4,128]{2,1,0:T(4,128)S(1)}, u32[]{:S(2)}, u32[]{:S(2)}) collective-permute-start(f32[40,4,128]{2,1,0:T(4,128)S(1)} %get-tuple-element.31), channel_id=1, source_target_pairs={{16,0},{32,16},{48,32},{64,48},{80,64},{96,80},{112,96},{128,112},... | collective-permute-start | bytes 245768 | tf_op jit(solution)/shard_map/ppermute | solution.py:236
  68.1 2.8 %shard_map.131 = f32[32,8,128]{2,1,0:T(8,128)S(1)} custom-call(f32[40,16,128]{2,1,0:T(8,128)S(1)} %pad_maximum_fusion.3.refs_0_.refs_1_, f32[40,16,128]{2,1,0:T(8,128)S(1)} %pad_maximum_fusion.3.refs_0_.refs_1_, f32[32,8,128]{2,1,0:T(8,128)S(1)} %constant_dynamic-slice_fusion.1.refs_2_, f32[32,8,128]{2,1,0:T(8,128)S(1)} %get-tuple-element.12.refs_3_, ...), custom_call_target="tpu_custom_call" | custom-call | tf_op jit(solution)/shard_map/pallas_call | solution.py:215
  70.9 2.6 %collective-permute-start.23 = (f32[32,8,128]{2,1,0:T(8,128)S(1)}, f32[32,8,128]{2,1,0:T(8,128)}, u32[]{:S(2)}, u32[]{:S(2)}) collective-permute-start(f32[32,8,128]{2,1,0:T(8,128)S(1)} %shard_map.131), channel_id=1, source_target_pairs={{0,16},{16,0},{32,48},{48,32},{64,80},{80,64},{96,112},{112,96},{1... | collective-permute-start | bytes 393224 | tf_op jit(solution)/shard_map/ppermute | solution.py:52
  76.5 2.7 %collective-permute-start.16 = (f32[32,16,128]{2,1,0:T(8,128)}, f32[32,16,128]{2,1,0:T(8,128)}, u32[]{:S(2)}, u32[]{:S(2)}) collective-permute-start(f32[32,16,128]{2,1,0:T(8,128)} %get-tuple-element.23), channel_id=1, source_target_pairs={{0,32},{16,48},{32,64},{48,80},{64,96},{80,112},{96,128},{112,144}... | collective-permute-start | bytes 786440 | tf_op jit(solution)/shard_map/ppermute | solution.py:61
  82.7 2.7 %collective-permute-start.27 = (f32[32,16,128]{2,1,0:T(8,128)}, f32[32,16,128]{2,1,0:T(8,128)S(1)}, u32[]{:S(2)}, u32[]{:S(2)}) collective-permute-start(f32[32,16,128]{2,1,0:T(8,128)} %get-tuple-element.21), channel_id=1, source_target_pairs={{0,32},{16,48},{32,64},{48,80},{64,96},{80,112},{96,128},{112,144}... | collective-permute-start | bytes 786440 | tf_op jit(solution)/shard_map/ppermute | solution.py:61
  85.4 10.3 %shard_map.132 = (f32[32,128,128]{2,1,0:T(8,128)S(1)}, f32[32,128,128]{2,1,0:T(8,128)S(1)}, f32[32,128,128]{2,1,0:T(8,128)}) custom-call(f32[40,128,128]{2,1,0:T(8,128)} %copy-done.7, f32[40,128,128]{2,1,0:T(8,128)} %copy-done.7, f32[128,256]{1,0:T(8,128)S(1)} %copy-done.3, f32[256,128]{1,0:T(8,128)S(1)} %copy-done.4), custom_call_target="tpu_custom_call" | custom-call | tf_op jit(solution)/shard_map/pallas_call | solution.py:187
  95.7 2.0 %pad_maximum_fusion.refs_0_.refs_1_ = f32[40,128,128]{2,1,0:T(8,128)} fusion(f32[4,128,128]{2,1,0:T(8,128)S(1)} %collective-permute-done.11, f32[32,128,128]{2,1,0:T(8,128)S(1)} %bitcast.19, f32[4,128,128]{2,1,0:T(8,128)S(1)} %collective-permute-done.10), kind=kLoop, calls=%fused_computation.1 | loop fusion | flops 1310720 | bytes 5242880 | tf_op jit(solution)/shard_map/concatenate | solution.py:38
  98.5 10.1 %shard_map.133 = f32[32,128,128]{2,1,0:T(8,128)S(1)} custom-call(f32[40,128,128]{2,1,0:T(8,128)} %pad_maximum_fusion.refs_0_.refs_1_, f32[40,128,128]{2,1,0:T(8,128)} %pad_maximum_fusion.refs_0_.refs_1_, f32[32,128,128]{2,1,0:T(8,128)S(1)} %copy-done, f32[32,128,128]{2,1,0:T(8,128)} %copy-done.1, f32[32,128,128]{2,1,0:T(8,128)} %copy-done.2, ...), custom_call_target="tpu_custom_call" | custom-call | tf_op jit(solution)/shard_map/pallas_call | solution.py:215
  108.6 2.7 %collective-permute-start.17 = (f32[32,16,128]{2,1,0:T(8,128)}, f32[32,16,128]{2,1,0:T(8,128)S(1)}, u32[]{:S(2)}, u32[]{:S(2)}) collective-permute-start(f32[32,16,128]{2,1,0:T(8,128)} %collective-permute-done.16), channel_id=1, source_target_pairs={{0,32},{16,48},{32,64},{48,80},{64,96},{80,112},{96,128},{112,144}... | collective-permute-start | bytes 786440 | tf_op jit(solution)/shard_map/ppermute | solution.py:61
  111.3 2.7 %collective-permute-start.28 = (f32[32,16,128]{2,1,0:T(8,128)S(1)}, f32[32,16,128]{2,1,0:T(8,128)S(1)}, u32[]{:S(2)}, u32[]{:S(2)}) collective-permute-start(f32[32,16,128]{2,1,0:T(8,128)S(1)} %collective-permute-done.27), channel_id=1, source_target_pairs={{0,32},{16,48},{32,64},{48,80},{64,96},{80,112},{96,128},{112,144}... | collective-permute-start | bytes 786440 | tf_op jit(solution)/shard_map/ppermute | solution.py:61
  118.4 2.7 %collective-permute-start.18 = (f32[32,16,128]{2,1,0:T(8,128)S(1)}, f32[32,16,128]{2,1,0:T(8,128)S(1)}, u32[]{:S(2)}, u32[]{:S(2)}) collective-permute-start(f32[32,16,128]{2,1,0:T(8,128)S(1)} %collective-permute-done.17), channel_id=1, source_target_pairs={{0,32},{16,48},{32,64},{48,80},{64,96},{80,112},{96,128},{112,144}... | collective-permute-start | bytes 786440 | tf_op jit(solution)/shard_map/ppermute | solution.py:61
  121.0 2.9 %collective-permute-done.25 = f32[32,16,128]{2,1,0:T(8,128)S(1)} collective-permute-done((f32[32,16,128]{2,1,0:T(8,128)}, f32[32,16,128]{2,1,0:T(8,128)S(1)}, u32[]{:S(2)}, u32[]{:S(2)}) %collective-permute-start.25) | collective-permute-done | bytes 262176 | tf_op jit(solution)/shard_map/ppermute | solution.py:62
  124.0 2.7 %collective-permute-start.29 = (f32[32,16,128]{2,1,0:T(8,128)S(1)}, f32[32,16,128]{2,1,0:T(8,128)S(1)}, u32[]{:S(2)}, u32[]{:S(2)}) collective-permute-start(f32[32,16,128]{2,1,0:T(8,128)S(1)} %collective-permute-done.28), channel_id=1, source_target_pairs={{0,32},{16,48},{32,64},{48,80},{64,96},{80,112},{96,128},{112,144}... | collective-permute-start | bytes 786440 | tf_op jit(solution)/shard_map/ppermute | solution.py:61
  129.2 3.2 %collective-permute-start.19 = (f32[16,16,128]{2,1,0:T(8,128)S(1)}, f32[16,16,128]{2,1,0:T(8,128)S(1)}, u32[]{:S(2)}, u32[]{:S(2)}) collective-permute-start(f32[16,16,128]{2,1,0:T(8,128)S(1)} %slice.84), channel_id=1, source_target_pairs={{0,32},{16,48},{32,64},{48,80},{64,96},{80,112},{96,128},{112,144}... | collective-permute-start | bytes 393224 | tf_op jit(solution)/shard_map/ppermute | solution.py:67
  134.5 3.5 %collective-permute-start.30 = (f32[16,16,128]{2,1,0:T(8,128)S(1)}, f32[16,16,128]{2,1,0:T(8,128)S(1)}, u32[]{:S(2)}, u32[]{:S(2)}) collective-permute-start(f32[16,16,128]{2,1,0:T(8,128)S(1)} %slice.88), channel_id=1, source_target_pairs={{0,32},{16,48},{32,64},{48,80},{64,96},{80,112},{96,128},{112,144}... | collective-permute-start | bytes 393224 | tf_op jit(solution)/shard_map/ppermute | solution.py:67
  140.6 3.2 %collective-permute-done.31 = f32[16,16,128]{2,1,0:T(8,128)S(1)} collective-permute-done((f32[16,16,128]{2,1,0:T(8,128)S(1)}, f32[16,16,128]{2,1,0:T(8,128)S(1)}, u32[]{:S(2)}, u32[]{:S(2)}) %collective-permute-start.31) | collective-permute-done | bytes 131104 | tf_op jit(solution)/shard_map/ppermute | solution.py:67
  146.4 7.5 %collective-permute-start.21 = (f32[4,128,128]{2,1,0:T(8,128)S(1)}, f32[4,128,128]{2,1,0:T(8,128)S(1)}, u32[]{:S(2)}, u32[]{:S(2)}) collective-permute-start(f32[4,128,128]{2,1,0:T(8,128)S(1)} %get-tuple-element.24), channel_id=1, source_target_pairs={{0,1},{1,2},{2,3},{3,4},{4,5},{5,6},{6,7},{7,8},{8,9},{9,10},{10,1... | collective-permute-start | bytes 786440 | tf_op jit(solution)/shard_map/ppermute | solution.py:40
  158.1 7.1 %collective-permute-done.22 = f32[4,128,128]{2,1,0:T(8,128)S(1)} collective-permute-done((f32[4,128,128]{2,1,0:T(8,128)S(1)}, f32[4,128,128]{2,1,0:T(8,128)S(1)}, u32[]{:S(2)}, u32[]{:S(2)}) %collective-permute-start.22) | collective-permute-done | bytes 262176 | tf_op jit(solution)/shard_map/ppermute | solution.py:42
  167.0 9.9 %shard_map.134 = f32[32,128,128]{2,1,0:T(8,128)S(1)} custom-call(f32[40,128,128]{2,1,0:T(8,128)} %pad_maximum_fusion.1.refs_0_.refs_1_, f32[40,128,128]{2,1,0:T(8,128)} %pad_maximum_fusion.1.refs_0_.refs_1_, f32[32,128,128]{2,1,0:T(8,128)S(1)} %copy-done, f32[32,128,128]{2,1,0:T(8,128)} %copy-done.1, f32[32,128,128]{2,1,0:T(8,128)} %copy-done.2, ...), custom_call_target="tpu_custom_call" | custom-call | tf_op jit(solution)/shard_map/pallas_call | solution.py:215
  176.9 3.6 %fusion.2 = f32[1,32,128,128]{3,2,1,0:T(8,128)} fusion(f32[32,128,128]{2,1,0:T(8,128)S(1)} %shard_map.134, f32[32,128,128]{2,1,0:T(8,128)} %constant_dynamic-update-slice_fusion.9, f32[1,32,128,128]{3,2,1,0:T(8,128)S(1)} %copy-done.12), kind=kLoop, calls=%fused_computation.7 | loop fusion | flops 1048576 | bytes 8388608 | tf_op jit(solution)/shard_map/broadcast_in_dim | solution.py:286
  (115 shorter events, 43.5 us)
Async XLA Ops:
  1.9 35.7 %collective-permute-start.4 = (f32[4,128,128]{2,1,0:T(8,128)S(1)}, f32[4,128,128]{2,1,0:T(8,128)S(1)}, u32[]{:S(2)}, u32[]{:S(2)}) collective-permute-start(f32[4,128,128]{2,1,0:T(8,128)S(1)} %get-tuple-element.29), channel_id=1, source_target_pairs={{0,1},{1,2},{2,3},{3,4},{4,5},{5,6},{6,7},{7,8},{8,9},{9,10},{10,1... | collective-permute-start | bytes 786440 | tf_op jit(solution)/shard_map/ppermute | solution.py:40
  5.8 32.0 %collective-permute-start.5 = (f32[4,128,128]{2,1,0:T(8,128)S(1)}, f32[4,128,128]{2,1,0:T(8,128)S(1)}, u32[]{:S(2)}, u32[]{:S(2)}) collective-permute-start(f32[4,128,128]{2,1,0:T(8,128)S(1)} %get-tuple-element.28), channel_id=1, source_target_pairs={{1,0},{2,1},{3,2},{4,3},{5,4},{6,5},{7,6},{8,7},{9,8},{10,9},{11,1... | collective-permute-start | bytes 786440 | tf_op jit(solution)/shard_map/ppermute | solution.py:42
  8.5 10.1 %collective-permute-start = (f32[4,8,128]{2,1,0:T(8,128)S(1)}, f32[4,8,128]{2,1,0:T(8,128)S(1)}, u32[]{:S(2)}, u32[]{:S(2)}) collective-permute-start(f32[4,8,128]{2,1,0:T(8,128)S(1)} %get-tuple-element.37), channel_id=1, source_target_pairs={{0,1},{1,2},{2,3},{3,4},{4,5},{5,6},{6,7},{7,8},{8,9},{9,10},{10,1... | collective-permute-start | bytes 49160 | tf_op jit(solution)/shard_map/ppermute | solution.py:40
  15.8 9.3 %collective-permute-start.1 = (f32[4,8,128]{2,1,0:T(8,128)S(1)}, f32[4,8,128]{2,1,0:T(8,128)S(1)}, u32[]{:S(2)}, u32[]{:S(2)}) collective-permute-start(f32[4,8,128]{2,1,0:T(8,128)S(1)} %get-tuple-element.36), channel_id=1, source_target_pairs={{1,0},{2,1},{3,2},{4,3},{5,4},{6,5},{7,6},{8,7},{9,8},{10,9},{11,1... | collective-permute-start | bytes 49160 | tf_op jit(solution)/shard_map/ppermute | solution.py:42
  25.1 8.0 %collective-permute-start.2 = (f32[40,4,128]{2,1,0:T(4,128)S(1)}, f32[40,4,128]{2,1,0:T(4,128)S(1)}, u32[]{:S(2)}, u32[]{:S(2)}) collective-permute-start(f32[40,4,128]{2,1,0:T(4,128)S(1)} %get-tuple-element.32), channel_id=1, source_target_pairs={{0,16},{16,32},{32,48},{48,64},{64,80},{80,96},{96,112},{112,128},... | collective-permute-start | bytes 245768 | tf_op jit(solution)/shard_map/ppermute | solution.py:234
  30.2 7.3 %collective-permute-start.3 = (f32[40,4,128]{2,1,0:T(4,128)S(1)}, f32[40,4,128]{2,1,0:T(4,128)S(1)}, u32[]{:S(2)}, u32[]{:S(2)}) collective-permute-start(f32[40,4,128]{2,1,0:T(4,128)S(1)} %get-tuple-element.33), channel_id=1, source_target_pairs={{16,0},{32,16},{48,32},{64,48},{80,64},{96,80},{112,96},{128,112},... | collective-permute-start | bytes 245768 | tf_op jit(solution)/shard_map/ppermute | solution.py:236
  46.3 5.1 %collective-permute-start.6 = (f32[4,8,128]{2,1,0:T(8,128)S(1)}, f32[4,8,128]{2,1,0:T(8,128)S(1)}, u32[]{:S(2)}, u32[]{:S(2)}) collective-permute-start(f32[4,8,128]{2,1,0:T(8,128)S(1)} %get-tuple-element.35), channel_id=1, source_target_pairs={{0,1},{1,2},{2,3},{3,4},{4,5},{5,6},{6,7},{7,8},{8,9},{9,10},{10,1... | collective-permute-start | bytes 49160 | tf_op jit(solution)/shard_map/ppermute | solution.py:40
  49.4 9.4 %collective-permute-start.7 = (f32[4,8,128]{2,1,0:T(8,128)S(1)}, f32[4,8,128]{2,1,0:T(8,128)S(1)}, u32[]{:S(2)}, u32[]{:S(2)}) collective-permute-start(f32[4,8,128]{2,1,0:T(8,128)S(1)} %get-tuple-element.34), channel_id=1, source_target_pairs={{1,0},{2,1},{3,2},{4,3},{5,4},{6,5},{7,6},{8,7},{9,8},{10,9},{11,1... | collective-permute-start | bytes 49160 | tf_op jit(solution)/shard_map/ppermute | solution.py:42
  51.4 24.1 %collective-permute-start.12 = (f32[32,8,128]{2,1,0:T(8,128)S(1)}, f32[32,8,128]{2,1,0:T(8,128)S(1)}, u32[]{:S(2)}, u32[]{:S(2)}) collective-permute-start(f32[32,8,128]{2,1,0:T(8,128)S(1)} %get-tuple-element.19), channel_id=1, source_target_pairs={{0,16},{16,0},{32,48},{48,32},{64,80},{80,64},{96,112},{112,96},{1... | collective-permute-start | bytes 393224 | tf_op jit(solution)/shard_map/ppermute | solution.py:52
  58.8 9.0 %collective-permute-start.8 = (f32[40,4,128]{2,1,0:T(4,128)S(1)}, f32[40,4,128]{2,1,0:T(4,128)S(1)}, u32[]{:S(2)}, u32[]{:S(2)}) collective-permute-start(f32[40,4,128]{2,1,0:T(4,128)S(1)} %get-tuple-element.30), channel_id=1, source_target_pairs={{0,16},{16,32},{32,48},{48,64},{64,80},{80,96},{96,112},{112,128},... | collective-permute-start | bytes 245768 | tf_op jit(solution)/shard_map/ppermute | solution.py:234
  60.8 7.3 %collective-permute-start.9 = (f32[40,4,128]{2,1,0:T(4,128)S(1)}, f32[40,4,128]{2,1,0:T(4,128)S(1)}, u32[]{:S(2)}, u32[]{:S(2)}) collective-permute-start(f32[40,4,128]{2,1,0:T(4,128)S(1)} %get-tuple-element.31), channel_id=1, source_target_pairs={{16,0},{32,16},{48,32},{64,48},{80,64},{96,80},{112,96},{128,112},... | collective-permute-start | bytes 245768 | tf_op jit(solution)/shard_map/ppermute | solution.py:236
  65.9 16.8 %collective-permute-start.10 = (f32[4,128,128]{2,1,0:T(8,128)S(1)}, f32[4,128,128]{2,1,0:T(8,128)S(1)}, u32[]{:S(2)}, u32[]{:S(2)}) collective-permute-start(f32[4,128,128]{2,1,0:T(8,128)S(1)} %get-tuple-element.26), channel_id=1, source_target_pairs={{0,1},{1,2},{2,3},{3,4},{4,5},{5,6},{6,7},{7,8},{8,9},{9,10},{10,1... | collective-permute-start | bytes 786440 | tf_op jit(solution)/shard_map/ppermute | solution.py:40
  70.9 8.3 %collective-permute-start.23 = (f32[32,8,128]{2,1,0:T(8,128)S(1)}, f32[32,8,128]{2,1,0:T(8,128)}, u32[]{:S(2)}, u32[]{:S(2)}) collective-permute-start(f32[32,8,128]{2,1,0:T(8,128)S(1)} %shard_map.131), channel_id=1, source_target_pairs={{0,16},{16,0},{32,48},{48,32},{64,80},{80,64},{96,112},{112,96},{1... | collective-permute-start | bytes 393224 | tf_op jit(solution)/shard_map/ppermute | solution.py:52
  73.5 22.2 %collective-permute-start.11 = (f32[4,128,128]{2,1,0:T(8,128)}, f32[4,128,128]{2,1,0:T(8,128)S(1)}, u32[]{:S(2)}, u32[]{:S(2)}) collective-permute-start(f32[4,128,128]{2,1,0:T(8,128)} %get-tuple-element.27), channel_id=1, source_target_pairs={{1,0},{2,1},{3,2},{4,3},{5,4},{6,5},{7,6},{8,7},{9,8},{10,9},{11,1... | collective-permute-start | bytes 786440 | tf_op jit(solution)/shard_map/ppermute | solution.py:42
  76.5 32.0 %collective-permute-start.13 = (f32[32,16,128]{2,1,0:T(8,128)}, f32[32,16,128]{2,1,0:T(8,128)}, u32[]{:S(2)}, u32[]{:S(2)}) collective-permute-start(f32[32,16,128]{2,1,0:T(8,128)} %get-tuple-element.23), channel_id=1, source_target_pairs={{0,224},{16,240},{32,0},{48,16},{64,32},{80,48},{96,64},{112,80},{... | collective-permute-start | bytes 786440 | tf_op jit(solution)/shard_map/ppermute | solution.py:62
  76.5 32.1 %collective-permute-start.16 = (f32[32,16,128]{2,1,0:T(8,128)}, f32[32,16,128]{2,1,0:T(8,128)}, u32[]{:S(2)}, u32[]{:S(2)}) collective-permute-start(f32[32,16,128]{2,1,0:T(8,128)} %get-tuple-element.23), channel_id=1, source_target_pairs={{0,32},{16,48},{32,64},{48,80},{64,96},{80,112},{96,128},{112,144}... | collective-permute-start | bytes 786440 | tf_op jit(solution)/shard_map/ppermute | solution.py:61
  82.7 28.6 %collective-permute-start.24 = (f32[32,16,128]{2,1,0:T(8,128)}, f32[32,16,128]{2,1,0:T(8,128)}, u32[]{:S(2)}, u32[]{:S(2)}) collective-permute-start(f32[32,16,128]{2,1,0:T(8,128)} %get-tuple-element.21), channel_id=1, source_target_pairs={{0,224},{16,240},{32,0},{48,16},{64,32},{80,48},{96,64},{112,80},{... | collective-permute-start | bytes 786440 | tf_op jit(solution)/shard_map/ppermute | solution.py:62
  82.7 28.6 %collective-permute-start.27 = (f32[32,16,128]{2,1,0:T(8,128)}, f32[32,16,128]{2,1,0:T(8,128)S(1)}, u32[]{:S(2)}, u32[]{:S(2)}) collective-permute-start(f32[32,16,128]{2,1,0:T(8,128)} %get-tuple-element.21), channel_id=1, source_target_pairs={{0,32},{16,48},{32,64},{48,80},{64,96},{80,112},{96,128},{112,144}... | collective-permute-start | bytes 786440 | tf_op jit(solution)/shard_map/ppermute | solution.py:61
  108.5 9.8 %collective-permute-start.14 = (f32[32,16,128]{2,1,0:T(8,128)}, f32[32,16,128]{2,1,0:T(8,128)S(1)}, u32[]{:S(2)}, u32[]{:S(2)}) collective-permute-start(f32[32,16,128]{2,1,0:T(8,128)} %collective-permute-done.13), channel_id=1, source_target_pairs={{0,224},{16,240},{32,0},{48,16},{64,32},{80,48},{96,64},{112,80},{... | collective-permute-start | bytes 786440 | tf_op jit(solution)/shard_map/ppermute | solution.py:62
  108.6 9.7 %collective-permute-start.17 = (f32[32,16,128]{2,1,0:T(8,128)}, f32[32,16,128]{2,1,0:T(8,128)S(1)}, u32[]{:S(2)}, u32[]{:S(2)}) collective-permute-start(f32[32,16,128]{2,1,0:T(8,128)} %collective-permute-done.16), channel_id=1, source_target_pairs={{0,32},{16,48},{32,64},{48,80},{64,96},{80,112},{96,128},{112,144}... | collective-permute-start | bytes 786440 | tf_op jit(solution)/shard_map/ppermute | solution.py:61
  111.3 12.7 %collective-permute-start.25 = (f32[32,16,128]{2,1,0:T(8,128)}, f32[32,16,128]{2,1,0:T(8,128)S(1)}, u32[]{:S(2)}, u32[]{:S(2)}) collective-permute-start(f32[32,16,128]{2,1,0:T(8,128)} %collective-permute-done.24), channel_id=1, source_target_pairs={{0,224},{16,240},{32,0},{48,16},{64,32},{80,48},{96,64},{112,80},{... | collective-permute-start | bytes 786440 | tf_op jit(solution)/shard_map/ppermute | solution.py:62
  111.3 12.7 %collective-permute-start.28 = (f32[32,16,128]{2,1,0:T(8,128)S(1)}, f32[32,16,128]{2,1,0:T(8,128)S(1)}, u32[]{:S(2)}, u32[]{:S(2)}) collective-permute-start(f32[32,16,128]{2,1,0:T(8,128)S(1)} %collective-permute-done.27), channel_id=1, source_target_pairs={{0,32},{16,48},{32,64},{48,80},{64,96},{80,112},{96,128},{112,144}... | collective-permute-start | bytes 786440 | tf_op jit(solution)/shard_map/ppermute | solution.py:61
  118.4 14.0 %collective-permute-start.15 = (f32[32,16,128]{2,1,0:T(8,128)S(1)}, f32[32,16,128]{2,1,0:T(8,128)S(1)}, u32[]{:S(2)}, u32[]{:S(2)}) collective-permute-start(f32[32,16,128]{2,1,0:T(8,128)S(1)} %collective-permute-done.14), channel_id=1, source_target_pairs={{0,224},{16,240},{32,0},{48,16},{64,32},{80,48},{96,64},{112,80},{... | collective-permute-start | bytes 786440 | tf_op jit(solution)/shard_map/ppermute | solution.py:62
  118.4 10.8 %collective-permute-start.18 = (f32[32,16,128]{2,1,0:T(8,128)S(1)}, f32[32,16,128]{2,1,0:T(8,128)S(1)}, u32[]{:S(2)}, u32[]{:S(2)}) collective-permute-start(f32[32,16,128]{2,1,0:T(8,128)S(1)} %collective-permute-done.17), channel_id=1, source_target_pairs={{0,32},{16,48},{32,64},{48,80},{64,96},{80,112},{96,128},{112,144}... | collective-permute-start | bytes 786440 | tf_op jit(solution)/shard_map/ppermute | solution.py:61
  124.0 14.0 %collective-permute-start.26 = (f32[32,16,128]{2,1,0:T(8,128)S(1)}, f32[32,16,128]{2,1,0:T(8,128)S(1)}, u32[]{:S(2)}, u32[]{:S(2)}) collective-permute-start(f32[32,16,128]{2,1,0:T(8,128)S(1)} %collective-permute-done.25), channel_id=1, source_target_pairs={{0,224},{16,240},{32,0},{48,16},{64,32},{80,48},{96,64},{112,80},{... | collective-permute-start | bytes 786440 | tf_op jit(solution)/shard_map/ppermute | solution.py:62
  124.0 10.5 %collective-permute-start.29 = (f32[32,16,128]{2,1,0:T(8,128)S(1)}, f32[32,16,128]{2,1,0:T(8,128)S(1)}, u32[]{:S(2)}, u32[]{:S(2)}) collective-permute-start(f32[32,16,128]{2,1,0:T(8,128)S(1)} %collective-permute-done.28), channel_id=1, source_target_pairs={{0,32},{16,48},{32,64},{48,80},{64,96},{80,112},{96,128},{112,144}... | collective-permute-start | bytes 786440 | tf_op jit(solution)/shard_map/ppermute | solution.py:61
  129.2 9.7 %collective-permute-start.19 = (f32[16,16,128]{2,1,0:T(8,128)S(1)}, f32[16,16,128]{2,1,0:T(8,128)S(1)}, u32[]{:S(2)}, u32[]{:S(2)}) collective-permute-start(f32[16,16,128]{2,1,0:T(8,128)S(1)} %slice.84), channel_id=1, source_target_pairs={{0,32},{16,48},{32,64},{48,80},{64,96},{80,112},{96,128},{112,144}... | collective-permute-start | bytes 393224 | tf_op jit(solution)/shard_map/ppermute | solution.py:67
  132.4 6.5 %collective-permute-start.20 = (f32[16,16,128]{2,1,0:T(8,128)S(1)}, f32[16,16,128]{2,1,0:T(8,128)S(1)}, u32[]{:S(2)}, u32[]{:S(2)}) collective-permute-start(f32[16,16,128]{2,1,0:T(8,128)S(1)} %slice.85), channel_id=1, source_target_pairs={{0,224},{16,240},{32,0},{48,16},{64,32},{80,48},{96,64},{112,80},{... | collective-permute-start | bytes 393224 | tf_op jit(solution)/shard_map/ppermute | solution.py:67
  134.5 6.1 %collective-permute-start.30 = (f32[16,16,128]{2,1,0:T(8,128)S(1)}, f32[16,16,128]{2,1,0:T(8,128)S(1)}, u32[]{:S(2)}, u32[]{:S(2)}) collective-permute-start(f32[16,16,128]{2,1,0:T(8,128)S(1)} %slice.88), channel_id=1, source_target_pairs={{0,32},{16,48},{32,64},{48,80},{64,96},{80,112},{96,128},{112,144}... | collective-permute-start | bytes 393224 | tf_op jit(solution)/shard_map/ppermute | solution.py:67
  138.0 5.8 %collective-permute-start.31 = (f32[16,16,128]{2,1,0:T(8,128)S(1)}, f32[16,16,128]{2,1,0:T(8,128)S(1)}, u32[]{:S(2)}, u32[]{:S(2)}) collective-permute-start(f32[16,16,128]{2,1,0:T(8,128)S(1)} %slice.89), channel_id=1, source_target_pairs={{0,224},{16,240},{32,0},{48,16},{64,32},{80,48},{96,64},{112,80},{... | collective-permute-start | bytes 393224 | tf_op jit(solution)/shard_map/ppermute | solution.py:67
  146.4 11.7 %collective-permute-start.21 = (f32[4,128,128]{2,1,0:T(8,128)S(1)}, f32[4,128,128]{2,1,0:T(8,128)S(1)}, u32[]{:S(2)}, u32[]{:S(2)}) collective-permute-start(f32[4,128,128]{2,1,0:T(8,128)S(1)} %get-tuple-element.24), channel_id=1, source_target_pairs={{0,1},{1,2},{2,3},{3,4},{4,5},{5,6},{6,7},{7,8},{8,9},{9,10},{10,1... | collective-permute-start | bytes 786440 | tf_op jit(solution)/shard_map/ppermute | solution.py:40
  153.9 11.3 %collective-permute-start.22 = (f32[4,128,128]{2,1,0:T(8,128)S(1)}, f32[4,128,128]{2,1,0:T(8,128)S(1)}, u32[]{:S(2)}, u32[]{:S(2)}) collective-permute-start(f32[4,128,128]{2,1,0:T(8,128)S(1)} %get-tuple-element.25), channel_id=1, source_target_pairs={{1,0},{2,1},{3,2},{4,3},{5,4},{6,5},{7,6},{8,7},{9,8},{10,9},{11,1... | collective-permute-start | bytes 786440 | tf_op jit(solution)/shard_map/ppermute | solution.py:42
  (15 other events, 155.6 us)

commit v6 on v4

--- a/solution.py
+++ b/solution.py
@@ -30,19 +30,20 @@
     return ms, mg
 
 
-def halo_depth(cells):
+def halo_depth_many(fields):
     count = lax.axis_size("slab")
     ends = count - 1
-    head = cells[:HALO]
-    tail = cells[cells.shape[0] - HALO:]
-    return jnp.concatenate(
-        [
-            lax.ppermute(tail, "slab", [(i, i + 1) for i in range(ends)]),
-            cells,
-            lax.ppermute(head, "slab", [(i + 1, i) for i in range(ends)]),
-        ],
-        axis=0,
-    )
+    heads = jnp.concatenate([f[:HALO] for f in fields], axis=1)
+    tails = jnp.concatenate([f[f.shape[0] - HALO:] for f in fields], axis=1)
+    above = lax.ppermute(tails, "slab", [(i, i + 1) for i in range(ends)])
+    below = lax.ppermute(heads, "slab", [(i + 1, i) for i in range(ends)])
+    outs = []
+    at = 0
+    for f in fields:
+        w = f.shape[1]
+        outs.append(jnp.concatenate([above[:, at:at + w], f, below[:, at:at + w]], axis=0))
+        at += w
+    return outs
 
 
 def ring_gather(x, bounds):
@@ -219,19 +220,17 @@
 
     depth = u_cur.shape[0]
     cur_rows = depth + 2 * HALO
-    u_cur_ext, u_prev_all = ring_gather(
-        jnp.concatenate([halo_depth(u_cur), u_prev], axis=0),
-        ((0, cur_rows), (cur_rows, cur_rows + depth)),
-    )
-
-    buoyancy_ext = halo_depth(buoyancy)
-    slopes = slopes_of(buoyancy_ext, mlane, msub)
-
     probe_kappa = dkappa[0]
     older = du_prev[0]
     newer = du_cur[0]
-
-    newer_ext = halo_depth(newer)
+    u_cur_strip_ext, buoyancy_ext, newer_ext = halo_depth_many([u_cur, buoyancy, newer])
+    u_cur_ext, u_prev_all = ring_gather(
+        jnp.concatenate([u_cur_strip_ext, u_prev], axis=0),
+        ((0, cur_rows), (cur_rows, cur_rows + depth)),
+    )
+
+    slopes = slopes_of(buoyancy_ext, mlane, msub)
+
     (partial_first,) = apply_op(newer_ext, buoyancy, slopes, mlane, msub, kappa=kappa, prev=older)
 
     image_first, background_first = apply_op(
@@ -239,7 +238,8 @@
     )
     born_first = partial_first + probe_kappa * image_first
 
-    (image_second,) = apply_op(halo_depth(background_first), buoyancy, slopes, mlane, msub, want_image=True)
+    background_first_ext, born_first_ext = halo_depth_many([background_first, born_first])
+    (image_second,) = apply_op(background_first_ext, buoyancy, slopes, mlane, msub, want_image=True)
 
     def cut_strip(field):
         return lax.dynamic_slice_in_dim(field, offset, strip, 1)
@@ -250,7 +250,7 @@
     )
 
     (born_second,) = apply_op(
-        halo_depth(born_first), buoyancy, slopes, mlane, msub,
+        born_first_ext, buoyancy, slopes, mlane, msub,
         kappa=kappa, prev=newer, dk=probe_kappa, img=image_second,
     )
     return background_first_strip, background_second, born_first[None], born_second[None]

time: 166 us -> 163 us (0.982)
  starting transfers between devices: 63.7 us -> 29 us
  waiting for transfers between devices: 22.9 us -> 56.9 us
  local copies, waits for them, and re-layouts: 12.6 us -> 10.9 us
    ppermute x10 -> x4, starting transfers between devices: 46.4 us -> 12.8 us  [the longest x2 9 us: halo_depth_many(): below = lax.ppermute(heads, 'slab', [(i + 1, i) for i in range(ends)])]
    ppermute x10 -> x4, waiting for transfers between devices: 0.5 us -> 24.7 us  [the longest x2 15.6 us: halo_depth_many(): above = lax.ppermute(tails, 'slab', [(i, i + 1) for i in range(ends)])]
    ppermute x1, waiting for transfers between devices: 0.01 us -> 5.55 us  [ring_gather(): partner = lax.ppermute(x, 'probe', [(i, i ^ 1) for i in range(n)])]
    ppermute x3, waiting for transfers between devices: 18.2 us -> 22.4 us  [ring_gather(): fwd = lax.ppermute(fwd, 'probe', ahead)]
    dynamic_update_slice x15, local copies, waits for them, and re-layouts: 2.38 us -> 0.46 us  [ring_gather(): buf = lax.dynamic_update_slice_in_dim(buf, by_offset[d][lo:hi], at, 1)]
    unnamed x31 -> x32, local copies, waits for them, and re-layouts: 4.22 us -> 5.03 us
    concatenate x4 -> x9, other arithmetic: 9.58 us -> 9.03 us  [the longest x4 7.12 us: halo_depth_many(): jnp.concatenate([above[:, at:at + w], f, below[:, at:at + w]], axis=0)]
    slice x5 -> x10, local copies, waits for them, and re-layouts: 4.56 us -> 4.88 us  [the longest x4 2.99 us: halo_depth_many(): tails = jnp.concatenate([f[f.shape[0] - HALO:] for f in fields], axis=1)]
  transfers between devices with their start and end apart: 19 -> 13, of which waited for: 4 -> 9; matrix products, arithmetic and copies ran while one was open for 11% -> 4% of each run, Pallas kernels for 18% -> 12%
where the time goes in v6:
time: 163 us; the launch traced here: 162 us
  waiting for transfers between devices  56.9 us (35%)
  Pallas kernels  51.7 us (32%)
  starting transfers between devices  29 us (18%)
  other arithmetic  12.4 us (8%)
  local copies, waits for them, and re-layouts  10.9 us (7%)
    pallas_call x4, Pallas kernels, apply_op(): pl.pallas_call(functools.partial(_op_kernel, (with_prev, with_img, want_i...  41.4 us
    ppermute x3, waiting for transfers between devices, ring_gather(): fwd = lax.ppermute(fwd, 'probe', ahead)  22.4 us
    ppermute x2, waiting for transfers between devices, halo_depth_many(): above = lax.ppermute(tails, 'slab', [(i, i + 1) for i in range(ends)])  15.6 us
    ppermute x3, starting transfers between devices, ring_gather(): bwd = lax.ppermute(bwd, 'probe', behind)  10.5 us
    pallas_call x1, Pallas kernels, slopes_of(): pl.pallas_call(_slope_kernel, grid=(depth // BZ,), in_specs=_ext_specs(n)...  10.3 us
    ppermute x2, waiting for transfers between devices, halo_depth_many(): below = lax.ppermute(heads, 'slab', [(i + 1, i) for i in range(ends)])  9.1 us
    ppermute x2, starting transfers between devices, halo_depth_many(): below = lax.ppermute(heads, 'slab', [(i + 1, i) for i in range(ends)])  9 us
    concatenate x4, other arithmetic, halo_depth_many(): jnp.concatenate([above[:, at:at + w], f, below[:, at:at + w]], axis=0)  7.12 us
  transfers between devices with their start and end apart: 13, of which 9 were waited for; matrix products, arithmetic and copies ran while one was open for 4% of the time, Pallas kernels for 12%

profile of v6, /device:TPU:6, one launch (start us, length us, event | category | flops | bytes accessed | tf_op | source)
XLA Modules:
  0.0 162.3 jit_solution(17040992013317858911)
XLA Ops:
  1.4 1.1 slice_bitcast_fusion.1
  3.6 5.2 %collective-permute-start.1 = (f32[4,264,128]{2,1,0:T(8,128)S(1)}, f32[4,264,128]{2,1,0:T(8,128)}, u32[]{:S(2)}, u32[]{:S(2)}) collective-permute-start(f32[4,264,128]{2,1,0:T(8,128)S(1)} %pad_maximum_fusion.5), channel_id=1, source_target_pairs={{1,0},{2,1},{3,2},{4,3},{5,4},{6,5},{7,6},{8,7},{9,8},{10,9},{11,1... | collective-permute-start | bytes 1622024 | tf_op jit(solution)/shard_map/ppermute | solution.py:39
  8.9 1.9 %collective-permute-start = (f32[4,264,128]{2,1,0:T(8,128)S(1)}, f32[4,264,128]{2,1,0:T(8,128)S(1)}, u32[]{:S(2)}, u32[]{:S(2)}) collective-permute-start(f32[4,264,128]{2,1,0:T(8,128)S(1)} %pad_maximum_fusion.4), channel_id=1, source_target_pairs={{0,1},{1,2},{2,3},{3,4},{4,5},{5,6},{6,7},{7,8},{8,9},{9,10},{10,1... | collective-permute-start | bytes 1622024 | tf_op jit(solution)/shard_map/ppermute | solution.py:38
  10.8 4.9 %collective-permute-done.1 = f32[4,264,128]{2,1,0:T(8,128)} collective-permute-done((f32[4,264,128]{2,1,0:T(8,128)S(1)}, f32[4,264,128]{2,1,0:T(8,128)}, u32[]{:S(2)}, u32[]{:S(2)}) %collective-permute-start.1) | collective-permute-done | bytes 540704 | tf_op jit(solution)/shard_map/ppermute | solution.py:39
  16.4 7.4 %collective-permute-done = f32[4,264,128]{2,1,0:T(8,128)S(1)} collective-permute-done((f32[4,264,128]{2,1,0:T(8,128)S(1)}, f32[4,264,128]{2,1,0:T(8,128)S(1)}, u32[]{:S(2)}, u32[]{:S(2)}) %collective-permute-start) | collective-permute-done | bytes 540704 | tf_op jit(solution)/shard_map/ppermute | solution.py:38
  24.2 1.1 fusion.5
  25.2 5.5 %collective-permute-done.2 = f32[72,8,128]{2,1,0:T(8,128)} collective-permute-done((f32[72,8,128]{2,1,0:T(8,128)S(1)}, f32[72,8,128]{2,1,0:T(8,128)}, u32[]{:S(2)}, u32[]{:S(2)}) %collective-permute-start.2) | collective-permute-done | bytes 294944 | tf_op jit(solution)/shard_map/ppermute | solution.py:53
  30.8 1.1 maximum_select_fusion
  31.9 2.0 %collective-permute-start.6 = (f32[72,16,128]{2,1,0:T(8,128)S(1)}, f32[72,16,128]{2,1,0:T(8,128)S(1)}, u32[]{:S(2)}, u32[]{:S(2)}) collective-permute-start(f32[72,16,128]{2,1,0:T(8,128)S(1)} %maximum_select_fusion), channel_id=1, source_target_pairs={{0,32},{16,48},{32,64},{48,80},{64,96},{80,112},{96,128},{112,144}... | collective-permute-start | bytes 1769480 | tf_op jit(solution)/shard_map/ppermute | solution.py:62
  33.9 4.0 %collective-permute-start.3 = (f32[72,16,128]{2,1,0:T(8,128)S(1)}, f32[72,16,128]{2,1,0:T(8,128)S(1)}, u32[]{:S(2)}, u32[]{:S(2)}) collective-permute-start(f32[72,16,128]{2,1,0:T(8,128)S(1)} %maximum_select_fusion), channel_id=1, source_target_pairs={{0,224},{16,240},{32,0},{48,16},{64,32},{80,48},{96,64},{112,80},{... | collective-permute-start | bytes 1769480 | tf_op jit(solution)/shard_map/ppermute | solution.py:63
  38.0 1.7 %pad_maximum_fusion.lo_ref.hi_ref = f32[40,128,128]{2,1,0:T(8,128)} fusion(f32[4,128,128]{2,1,0:T(8,128)S(1)} %get-tuple-element.26, f32[32,128,128]{2,1,0:T(8,128)S(1)} %copy-done, f32[4,128,128]{2,1,0:T(8,128)S(1)} %get-tuple-element.24), kind=kLoop, calls=%fused_computation | loop fusion | flops 1310720 | bytes 5242880 | tf_op jit(solution)/shard_map/concatenate | solution.py:44
  39.7 10.3 %shard_map.120 = (f32[32,128,128]{2,1,0:T(8,128)S(1)}, f32[32,128,128]{2,1,0:T(8,128)S(1)}, f32[32,128,128]{2,1,0:T(8,128)}) custom-call(f32[40,128,128]{2,1,0:T(8,128)} %pad_maximum_fusion.lo_ref.hi_ref, f32[40,128,128]{2,1,0:T(8,128)} %pad_maximum_fusion.lo_ref.hi_ref, f32[128,256]{1,0:T(8,128)S(1)} %copy-done.7, f32[256,128]{1,0:T(8,128)S(1)} %copy-done.6), custom_call_target="tpu_custom_call" | custom-call | tf_op jit(solution)/shard_map/pallas_call | solution.py:176
  50.0 2.0 %pad_maximum_fusion.1.refs_0_.refs_1_ = f32[40,128,128]{2,1,0:T(8,128)} fusion(f32[4,128,128]{2,1,0:T(8,128)S(1)} %get-tuple-element.27, f32[32,128,128]{2,1,0:T(8,128)S(1)} %bitcast.11, f32[4,128,128]{2,1,0:T(8,128)S(1)} %get-tuple-element.25), kind=kLoop, calls=%fused_computation.1 | loop fusion | flops 1310720 | bytes 5242880 | tf_op jit(solution)/shard_map/concatenate | solution.py:44
  52.8 9.9 %shard_map.122 = f32[32,128,128]{2,1,0:T(8,128)S(1)} custom-call(f32[40,128,128]{2,1,0:T(8,128)} %pad_maximum_fusion.1.refs_0_.refs_1_, f32[40,128,128]{2,1,0:T(8,128)} %pad_maximum_fusion.1.refs_0_.refs_1_, f32[32,128,128]{2,1,0:T(8,128)S(1)} %copy-done, f32[32,128,128]{2,1,0:T(8,128)} %copy-done.2, f32[32,128,128]{2,1,0:T(8,128)} %copy-done.4, ...), custom_call_target="tpu_custom_call" | custom-call | tf_op jit(solution)/shard_map/pallas_call | solution.py:201
  62.8 3.2 %collective-permute-start.4 = (f32[72,16,128]{2,1,0:T(8,128)S(1)}, f32[72,16,128]{2,1,0:T(8,128)S(1)}, u32[]{:S(2)}, u32[]{:S(2)}) collective-permute-start(f32[72,16,128]{2,1,0:T(8,128)S(1)} %collective-permute-done.3), channel_id=1, source_target_pairs={{0,224},{16,240},{32,0},{48,16},{64,32},{80,48},{96,64},{112,80},{... | collective-permute-start | bytes 1769480 | tf_op jit(solution)/shard_map/ppermute | solution.py:63
  66.7 12.9 %collective-permute-done.7 = f32[72,16,128]{2,1,0:T(8,128)S(1)} collective-permute-done((f32[72,16,128]{2,1,0:T(8,128)S(1)}, f32[72,16,128]{2,1,0:T(8,128)S(1)}, u32[]{:S(2)}, u32[]{:S(2)}) %collective-permute-start.7) | collective-permute-done | bytes 589856 | tf_op jit(solution)/shard_map/ppermute | solution.py:62
  79.6 3.2 %collective-permute-start.5 = (f32[72,16,128]{2,1,0:T(8,128)S(1)}, f32[72,16,128]{2,1,0:T(8,128)S(1)}, u32[]{:S(2)}, u32[]{:S(2)}) collective-permute-start(f32[72,16,128]{2,1,0:T(8,128)S(1)} %collective-permute-done.4), channel_id=1, source_target_pairs={{0,224},{16,240},{32,0},{48,16},{64,32},{80,48},{96,64},{112,80},{... | collective-permute-start | bytes 1769480 | tf_op jit(solution)/shard_map/ppermute | solution.py:63
  82.9 9.5 %collective-permute-done.8 = f32[72,16,128]{2,1,0:T(8,128)S(1)} collective-permute-done((f32[72,16,128]{2,1,0:T(8,128)S(1)}, f32[72,16,128]{2,1,0:T(8,128)S(1)}, u32[]{:S(2)}, u32[]{:S(2)}) %collective-permute-start.8) | collective-permute-done | bytes 589856 | tf_op jit(solution)/shard_map/ppermute | solution.py:62
  92.6 3.5 %collective-permute-start.10 = (f32[36,16,128]{2,1,0:T(8,128)S(1)}, f32[36,16,128]{2,1,0:T(8,128)S(1)}, u32[]{:S(2)}, u32[]{:S(2)}) collective-permute-start(f32[36,16,128]{2,1,0:T(8,128)S(1)} %slice.167), channel_id=1, source_target_pairs={{0,224},{16,240},{32,0},{48,16},{64,32},{80,48},{96,64},{112,80},{... | collective-permute-start | bytes 884744 | tf_op jit(solution)/shard_map/ppermute | solution.py:68
  96.2 4.2 %collective-permute-done.10 = f32[36,16,128]{2,1,0:T(8,128)S(1)} collective-permute-done((f32[36,16,128]{2,1,0:T(8,128)S(1)}, f32[36,16,128]{2,1,0:T(8,128)S(1)}, u32[]{:S(2)}, u32[]{:S(2)}) %collective-permute-start.10) | collective-permute-done | bytes 294944 | tf_op jit(solution)/shard_map/ppermute | solution.py:68
  100.8 1.3 copy-done.12
  102.0 1.5 copy-done.8
  103.5 10.4 %shard_map.121 = (f32[32,128,128]{2,1,0:T(8,128)S(1)}, f32[32,128,128]{2,1,0:T(8,128)S(1)}) custom-call(f32[40,128,128]{2,1,0:T(8,128)} %copy-done.8, f32[40,128,128]{2,1,0:T(8,128)} %copy-done.8, f32[32,128,128]{2,1,0:T(8,128)} %refs_2_.7, f32[32,128,128]{2,1,0:T(8,128)} %copy-done.2, f32[32,128,128]{2,1,0:T(8,128)} %copy-done.4, ...), custom_call_target="tpu_custom_call" | custom-call | tf_op jit(solution)/shard_map/pallas_call | solution.py:201
  115.6 3.8 %collective-permute-start.12 = (f32[4,256,128]{2,1,0:T(8,128)}, f32[4,256,128]{2,1,0:T(8,128)S(1)}, u32[]{:S(2)}, u32[]{:S(2)}) collective-permute-start(f32[4,256,128]{2,1,0:T(8,128)} %pad_maximum_fusion.7), channel_id=1, source_target_pairs={{1,0},{2,1},{3,2},{4,3},{5,4},{6,5},{7,6},{8,7},{9,8},{10,9},{11,1... | collective-permute-start | bytes 1572872 | tf_op jit(solution)/shard_map/ppermute | solution.py:39
  120.3 1.9 %collective-permute-start.11 = (f32[4,256,128]{2,1,0:T(8,128)}, f32[4,256,128]{2,1,0:T(8,128)S(1)}, u32[]{:S(2)}, u32[]{:S(2)}) collective-permute-start(f32[4,256,128]{2,1,0:T(8,128)} %pad_maximum_fusion.6), channel_id=1, source_target_pairs={{0,1},{1,2},{2,3},{3,4},{4,5},{5,6},{6,7},{7,8},{8,9},{9,10},{10,1... | collective-permute-start | bytes 1572872 | tf_op jit(solution)/shard_map/ppermute | solution.py:38
  122.2 4.2 %collective-permute-done.12 = f32[4,256,128]{2,1,0:T(8,128)S(1)} collective-permute-done((f32[4,256,128]{2,1,0:T(8,128)}, f32[4,256,128]{2,1,0:T(8,128)S(1)}, u32[]{:S(2)}, u32[]{:S(2)}) %collective-permute-start.12) | collective-permute-done | bytes 524320 | tf_op jit(solution)/shard_map/ppermute | solution.py:39
  126.5 8.1 %collective-permute-done.11 = f32[4,256,128]{2,1,0:T(8,128)S(1)} collective-permute-done((f32[4,256,128]{2,1,0:T(8,128)}, f32[4,256,128]{2,1,0:T(8,128)S(1)}, u32[]{:S(2)}, u32[]{:S(2)}) %collective-permute-start.11) | collective-permute-done | bytes 524320 | tf_op jit(solution)/shard_map/ppermute | solution.py:38
  134.6 1.7 %pad_maximum_fusion.2.refs_0_.refs_1_ = f32[40,128,128]{2,1,0:T(8,128)} fusion(f32[4,128,128]{2,1,0:T(8,128)S(1)} %get-tuple-element.31, f32[32,128,128]{2,1,0:T(8,128)S(1)} %get-tuple-element.12, f32[4,128,128]{2,1,0:T(8,128)S(1)} %get-tuple-element.29), kind=kLoop, calls=%fused_computation.2 | loop fusion | flops 1310720 | bytes 5242880 | tf_op jit(solution)/shard_map/concatenate | solution.py:44
  137.2 9.7 %shard_map.123.refs_11_ = f32[32,128,128]{2,1,0:T(8,128)S(1)} custom-call(f32[40,128,128]{2,1,0:T(8,128)} %pad_maximum_fusion.2.refs_0_.refs_1_, f32[40,128,128]{2,1,0:T(8,128)} %pad_maximum_fusion.2.refs_0_.refs_1_, f32[32,128,128]{2,1,0:T(8,128)S(1)} %copy-done.1, f32[32,128,128]{2,1,0:T(8,128)} %copy-done.2, f32[32,128,128]{2,1,0:T(8,128)} %copy-done.4, ...), custom_call_target="tpu_custom_call" | custom-call | tf_op jit(solution)/shard_map/pallas_call | solution.py:201
  146.9 1.8 %pad_maximum_fusion.3.refs_0_.refs_1_ = f32[40,128,128]{2,1,0:T(8,128)} fusion(f32[4,128,128]{2,1,0:T(8,128)S(1)} %get-tuple-element.30, f32[32,128,128]{2,1,0:T(8,128)S(1)} %copy-done.11, f32[4,128,128]{2,1,0:T(8,128)S(1)} %get-tuple-element.28), kind=kLoop, calls=%fused_computation.3 | loop fusion | flops 1310720 | bytes 5242880 | tf_op jit(solution)/shard_map/concatenate | solution.py:44
  149.2 1.7 %multiply_add_fusion.1 = (f32[32,8,128]{2,1,0:T(8,128)}, f32[32,8,128]{2,1,0:T(8,128)}) fusion(f32[32,128,128]{2,1,0:T(8,128)S(1)} %shard_map.123.refs_11_, s32[]{:T(128)S(6)} %select_n.124, f32[32,128,128]{2,1,0:T(8,128)} %refs_8_.5, f32[32,8,128]{2,1,0:T(8,128)S(1)} %copy-done.14, f32[32,128,128]{2,1,0:T(8,128)S(1)} %get-tuple-element.12), kind=kLoop, calls=%fused_computation.30 | loop fusion | flops 131072 | bytes 786436 | tf_op jit(solution)/shard_map/add | solution.py:249
  150.9 11.4 %shard_map.124 = f32[32,128,128]{2,1,0:T(8,128)} custom-call(f32[40,128,128]{2,1,0:T(8,128)} %pad_maximum_fusion.3.refs_0_.refs_1_, f32[40,128,128]{2,1,0:T(8,128)} %pad_maximum_fusion.3.refs_0_.refs_1_, f32[32,128,128]{2,1,0:T(8,128)S(1)} %copy-done.1, f32[32,128,128]{2,1,0:T(8,128)S(1)} %copy-done.3, f32[32,128,128]{2,1,0:T(8,128)} %copy-done.4, ...), custom_call_target="tpu_custom_call" | custom-call | tf_op jit(solution)/shard_map/pallas_call | solution.py:201
  (73 shorter events, 9.0 us)
Async XLA Ops:
  1.4 22.5 %copy-start.14 = (f32[32,8,128]{2,1,0:T(8,128)S(1)}, f32[32,8,128]{2,1,0:T(8,128)}, u32[]{:S(2)}) copy-start(f32[32,8,128]{2,1,0:T(8,128)} %param.10) | copy-start | bytes 393220
  1.4 22.5 %copy-start.15 = (f32[32,8,128]{2,1,0:T(8,128)S(1)}, f32[32,8,128]{2,1,0:T(8,128)}, u32[]{:S(2)}) copy-start(f32[32,8,128]{2,1,0:T(8,128)} %param.9) | copy-start | bytes 393220
  3.6 12.1 %collective-permute-start.1 = (f32[4,264,128]{2,1,0:T(8,128)S(1)}, f32[4,264,128]{2,1,0:T(8,128)}, u32[]{:S(2)}, u32[]{:S(2)}) collective-permute-start(f32[4,264,128]{2,1,0:T(8,128)S(1)} %pad_maximum_fusion.5), channel_id=1, source_target_pairs={{1,0},{2,1},{3,2},{4,3},{5,4},{6,5},{7,6},{8,7},{9,8},{10,9},{11,1... | collective-permute-start | bytes 1622024 | tf_op jit(solution)/shard_map/ppermute | solution.py:39
  8.9 15.0 %collective-permute-start = (f32[4,264,128]{2,1,0:T(8,128)S(1)}, f32[4,264,128]{2,1,0:T(8,128)S(1)}, u32[]{:S(2)}, u32[]{:S(2)}) collective-permute-start(f32[4,264,128]{2,1,0:T(8,128)S(1)} %pad_maximum_fusion.4), channel_id=1, source_target_pairs={{0,1},{1,2},{2,3},{3,4},{4,5},{5,6},{6,7},{7,8},{8,9},{9,10},{10,1... | collective-permute-start | bytes 1622024 | tf_op jit(solution)/shard_map/ppermute | solution.py:38
  16.4 21.6 %copy-start = (f32[32,128,128]{2,1,0:T(8,128)S(1)}, f32[32,128,128]{2,1,0:T(8,128)}, u32[]{:S(2)}) copy-start(f32[32,128,128]{2,1,0:T(8,128)} %refs_2_.7) | copy-start | bytes 6291460
  23.9 6.9 %collective-permute-start.2 = (f32[72,8,128]{2,1,0:T(8,128)S(1)}, f32[72,8,128]{2,1,0:T(8,128)}, u32[]{:S(2)}, u32[]{:S(2)}) collective-permute-start(f32[72,8,128]{2,1,0:T(8,128)S(1)} %pad_maximum_fusion.9), channel_id=1, source_target_pairs={{0,16},{16,0},{32,48},{48,32},{64,80},{80,64},{96,112},{112,96},{1... | collective-permute-start | bytes 884744 | tf_op jit(solution)/shard_map/ppermute | solution.py:53
  31.9 30.8 %collective-permute-start.6 = (f32[72,16,128]{2,1,0:T(8,128)S(1)}, f32[72,16,128]{2,1,0:T(8,128)S(1)}, u32[]{:S(2)}, u32[]{:S(2)}) collective-permute-start(f32[72,16,128]{2,1,0:T(8,128)S(1)} %maximum_select_fusion), channel_id=1, source_target_pairs={{0,32},{16,48},{32,64},{48,80},{64,96},{80,112},{96,128},{112,144}... | collective-permute-start | bytes 1769480 | tf_op jit(solution)/shard_map/ppermute | solution.py:62
  33.9 28.9 %collective-permute-start.3 = (f32[72,16,128]{2,1,0:T(8,128)S(1)}, f32[72,16,128]{2,1,0:T(8,128)S(1)}, u32[]{:S(2)}, u32[]{:S(2)}) collective-permute-start(f32[72,16,128]{2,1,0:T(8,128)S(1)} %maximum_select_fusion), channel_id=1, source_target_pairs={{0,224},{16,240},{32,0},{48,16},{64,32},{80,48},{96,64},{112,80},{... | collective-permute-start | bytes 1769480 | tf_op jit(solution)/shard_map/ppermute | solution.py:63
  38.0 1.7 %copy-start.6 = (f32[256,128]{1,0:T(8,128)S(1)}, f32[256,128]{1,0:T(8,128)}, u32[]{:S(2)}) copy-start(f32[256,128]{1,0:T(8,128)} %constant.108.clone.msub_ref.refs_7_) | copy-start | bytes 393220
  38.0 1.7 %copy-start.7 = (f32[128,256]{1,0:T(8,128)S(1)}, f32[128,256]{1,0:T(8,128)}, u32[]{:S(2)}) copy-start(f32[128,256]{1,0:T(8,128)} %constant.107.clone.mlane_ref.refs_6_) | copy-start | bytes 393220
  39.7 10.3 %copy-start.9 = (f32[1,32,128,128]{3,2,1,0:T(8,128)S(1)}, f32[1,32,128,128]{3,2,1,0:T(8,128)}, u32[]{:S(2)}) copy-start(f32[1,32,128,128]{3,2,1,0:T(8,128)} %param.15) | copy-start | bytes 6291460
  50.0 2.1 %copy-start.2 = (f32[32,128,128]{2,1,0:T(8,128)}, f32[32,128,128]{2,1,0:T(8,128)S(1)}, u32[]{:S(2)}) copy-start(f32[32,128,128]{2,1,0:T(8,128)S(1)} %get-tuple-element.9.refs_3_) | copy-start | bytes 6291460
  50.0 2.8 %copy-start.4 = (f32[32,128,128]{2,1,0:T(8,128)}, f32[32,128,128]{2,1,0:T(8,128)S(1)}, u32[]{:S(2)}) copy-start(f32[32,128,128]{2,1,0:T(8,128)S(1)} %get-tuple-element.10.refs_4_) | copy-start | bytes 6291460
  62.7 16.9 %collective-permute-start.7 = (f32[72,16,128]{2,1,0:T(8,128)S(1)}, f32[72,16,128]{2,1,0:T(8,128)S(1)}, u32[]{:S(2)}, u32[]{:S(2)}) collective-permute-start(f32[72,16,128]{2,1,0:T(8,128)S(1)} %collective-permute-done.6), channel_id=1, source_target_pairs={{0,32},{16,48},{32,64},{48,80},{64,96},{80,112},{96,128},{112,144}... | collective-permute-start | bytes 1769480 | tf_op jit(solution)/shard_map/ppermute | solution.py:62
  62.8 16.8 %collective-permute-start.4 = (f32[72,16,128]{2,1,0:T(8,128)S(1)}, f32[72,16,128]{2,1,0:T(8,128)S(1)}, u32[]{:S(2)}, u32[]{:S(2)}) collective-permute-start(f32[72,16,128]{2,1,0:T(8,128)S(1)} %collective-permute-done.3), channel_id=1, source_target_pairs={{0,224},{16,240},{32,0},{48,16},{64,32},{80,48},{96,64},{112,80},{... | collective-permute-start | bytes 1769480 | tf_op jit(solution)/shard_map/ppermute | solution.py:63
  79.6 12.9 %collective-permute-start.8 = (f32[72,16,128]{2,1,0:T(8,128)S(1)}, f32[72,16,128]{2,1,0:T(8,128)S(1)}, u32[]{:S(2)}, u32[]{:S(2)}) collective-permute-start(f32[72,16,128]{2,1,0:T(8,128)S(1)} %collective-permute-done.7), channel_id=1, source_target_pairs={{0,32},{16,48},{32,64},{48,80},{64,96},{80,112},{96,128},{112,144}... | collective-permute-start | bytes 1769480 | tf_op jit(solution)/shard_map/ppermute | solution.py:62
  79.6 13.0 %collective-permute-start.5 = (f32[72,16,128]{2,1,0:T(8,128)S(1)}, f32[72,16,128]{2,1,0:T(8,128)S(1)}, u32[]{:S(2)}, u32[]{:S(2)}) collective-permute-start(f32[72,16,128]{2,1,0:T(8,128)S(1)} %collective-permute-done.4), channel_id=1, source_target_pairs={{0,224},{16,240},{32,0},{48,16},{64,32},{80,48},{96,64},{112,80},{... | collective-permute-start | bytes 1769480 | tf_op jit(solution)/shard_map/ppermute | solution.py:63
  92.5 8.0 %collective-permute-start.9 = (f32[36,16,128]{2,1,0:T(8,128)S(1)}, f32[36,16,128]{2,1,0:T(8,128)S(1)}, u32[]{:S(2)}, u32[]{:S(2)}) collective-permute-start(f32[36,16,128]{2,1,0:T(8,128)S(1)} %slice.166), channel_id=1, source_target_pairs={{0,32},{16,48},{32,64},{48,80},{64,96},{80,112},{96,128},{112,144}... | collective-permute-start | bytes 884744 | tf_op jit(solution)/shard_map/ppermute | solution.py:68
  92.6 7.7 %collective-permute-start.10 = (f32[36,16,128]{2,1,0:T(8,128)S(1)}, f32[36,16,128]{2,1,0:T(8,128)S(1)}, u32[]{:S(2)}, u32[]{:S(2)}) collective-permute-start(f32[36,16,128]{2,1,0:T(8,128)S(1)} %slice.167), channel_id=1, source_target_pairs={{0,224},{16,240},{32,0},{48,16},{64,32},{80,48},{96,64},{112,80},{... | collective-permute-start | bytes 884744 | tf_op jit(solution)/shard_map/ppermute | solution.py:68
  100.7 1.3 copy-start.12
  102.0 1.5 copy-start.8
  103.5 10.4 %copy-start.13 = (f32[1,32,128,128]{3,2,1,0:T(8,128)S(1)}, f32[1,32,128,128]{3,2,1,0:T(8,128)}, u32[]{:S(2)}) copy-start(f32[1,32,128,128]{3,2,1,0:T(8,128)} %param.13) | copy-start | bytes 6291460
  114.6 5.7 %copy-start.10 = (f32[32,128,128]{2,1,0:T(8,128)}, f32[32,128,128]{2,1,0:T(8,128)S(1)}, u32[]{:S(2)}) copy-start(f32[32,128,128]{2,1,0:T(8,128)S(1)} %multiply_add_fusion) | copy-start | bytes 6291460
  115.6 10.8 %collective-permute-start.12 = (f32[4,256,128]{2,1,0:T(8,128)}, f32[4,256,128]{2,1,0:T(8,128)S(1)}, u32[]{:S(2)}, u32[]{:S(2)}) collective-permute-start(f32[4,256,128]{2,1,0:T(8,128)} %pad_maximum_fusion.7), channel_id=1, source_target_pairs={{1,0},{2,1},{3,2},{4,3},{5,4},{6,5},{7,6},{8,7},{9,8},{10,9},{11,1... | collective-permute-start | bytes 1572872 | tf_op jit(solution)/shard_map/ppermute | solution.py:39
  120.3 14.3 %collective-permute-start.11 = (f32[4,256,128]{2,1,0:T(8,128)}, f32[4,256,128]{2,1,0:T(8,128)S(1)}, u32[]{:S(2)}, u32[]{:S(2)}) collective-permute-start(f32[4,256,128]{2,1,0:T(8,128)} %pad_maximum_fusion.6), channel_id=1, source_target_pairs={{0,1},{1,2},{2,3},{3,4},{4,5},{5,6},{6,7},{7,8},{8,9},{9,10},{10,1... | collective-permute-start | bytes 1572872 | tf_op jit(solution)/shard_map/ppermute | solution.py:38
  134.6 2.5 %copy-start.1 = (f32[32,128,128]{2,1,0:T(8,128)S(1)}, f32[32,128,128]{2,1,0:T(8,128)}, u32[]{:S(2)}) copy-start(f32[32,128,128]{2,1,0:T(8,128)} %refs_2_.7) | copy-start | bytes 6291460
  137.2 9.7 %copy-start.11 = (f32[32,128,128]{2,1,0:T(8,128)S(1)}, f32[32,128,128]{2,1,0:T(8,128)}, u32[]{:S(2)}) copy-start(f32[32,128,128]{2,1,0:T(8,128)} %copy-done.10) | copy-start | bytes 6291460
  146.9 2.3 %copy-start.5 = (f32[32,128,128]{2,1,0:T(8,128)}, f32[32,128,128]{2,1,0:T(8,128)S(1)}, u32[]{:S(2)}) copy-start(f32[32,128,128]{2,1,0:T(8,128)S(1)} %shard_map.123.refs_11_) | copy-start | bytes 6291460
  146.9 4.0 %copy-start.3 = (f32[32,128,128]{2,1,0:T(8,128)S(1)}, f32[32,128,128]{2,1,0:T(8,128)}, u32[]{:S(2)}) copy-start(f32[32,128,128]{2,1,0:T(8,128)} %copy-done.2) | copy-start | bytes 6291460

commit v7 on v6

--- a/solution.py
+++ b/solution.py
@@ -86,33 +86,55 @@
     return hi_ref[idx - BZ]
 
 
-def _depth_terms(lo_ref, hi_ref, j):
+def _depth_terms(lo_ref, hi_ref, j, off, rows):
     c = j + HALO
-    centre = _ext(lo_ref, hi_ref, c)
+
+    def at(idx):
+        return _ext(lo_ref, hi_ref, idx)[off:off + rows]
+
+    whole = _ext(lo_ref, hi_ref, c)
+    centre = whole[off:off + rows]
     second = (3.0 * SECOND[0]) * centre
     grad = None
     for k in range(1, 5):
-        up = _ext(lo_ref, hi_ref, c + k)
-        down = _ext(lo_ref, hi_ref, c - k)
+        up = at(c + k)
+        down = at(c - k)
         second = second + SECOND[k] * (up + down)
         term = FIRST[k] * (up - down)
         grad = term if grad is None else grad + term
-    return centre, second, grad
-
-
-def _slope_kernel(lo_ref, hi_ref, mlane_ref, msub_ref, g0_ref, g1_ref, g2_ref):
+    return whole, centre, second, grad
+
+
+def _slope_kernel(off, lo_ref, hi_ref, mlane_ref, msub_ref, g0_ref, g1_ref, g2_ref):
     n = mlane_ref.shape[0]
+    rows = g0_ref.shape[1]
     for j in range(BZ):
-        centre, _, grad = _depth_terms(lo_ref, hi_ref, j)
+        whole, centre, _, grad = _depth_terms(lo_ref, hi_ref, j, off, rows)
         lane = jnp.dot(centre, mlane_ref[...], precision=HI, preferred_element_type=jnp.float32)
-        sub = jnp.dot(msub_ref[...], centre, precision=HI, preferred_element_type=jnp.float32)
+        sub = jnp.dot(msub_ref[...], whole, precision=HI, preferred_element_type=jnp.float32)
         g0_ref[j] = grad
-        g1_ref[j] = sub[n:]
+        g1_ref[j] = sub[rows:]
         g2_ref[j] = lane[:, n:]
 
 
+def _image_of(lo_ref, hi_ref, j, coef, mlane_ref, msub_ref, off, rows):
+    b_ref, g0_ref, g1_ref, g2_ref = coef
+    n = mlane_ref.shape[0]
+    whole, centre, second, grad = _depth_terms(lo_ref, hi_ref, j, off, rows)
+    lane = jnp.dot(centre, mlane_ref[...], precision=HI, preferred_element_type=jnp.float32)
+    sub = jnp.dot(msub_ref[...], whole, precision=HI, preferred_element_type=jnp.float32)
+    second = second + sub[:rows] + lane[:, :n]
+    image = (
+        b_ref[j] * second
+        + g0_ref[j] * grad
+        + g1_ref[j] * sub[rows:]
+        + g2_ref[j] * lane[:, n:]
+    )
+    return centre, image
+
+
 def _op_kernel(flags, *refs):
-    with_prev, with_img, want_image, want_step = flags
+    with_prev, with_img, want_image, want_step, off = flags
     refs = list(refs)
     lo_ref, hi_ref, b_ref, g0_ref, g1_ref, g2_ref, mlane_ref, msub_ref = refs[:8]
     rest = refs[8:]
@@ -125,18 +147,10 @@
             dk_ref = rest.pop(0)
             img_ref = rest.pop(0)
     outs = rest
-    n = mlane_ref.shape[0]
+    rows = b_ref.shape[1]
+    coef = (b_ref, g0_ref, g1_ref, g2_ref)
     for j in range(BZ):
-        centre, second, grad = _depth_terms(lo_ref, hi_ref, j)
-        lane = jnp.dot(centre, mlane_ref[...], precision=HI, preferred_element_type=jnp.float32)
-        sub = jnp.dot(msub_ref[...], centre, precision=HI, preferred_element_type=jnp.float32)
-        second = second + sub[:n] + lane[:, :n]
-        image = (
-            b_ref[j] * second
-            + g0_ref[j] * grad
-            + g1_ref[j] * sub[n:]
-            + g2_ref[j] * lane[:, n:]
-        )
+        centre, image = _image_of(lo_ref, hi_ref, j, coef, mlane_ref, msub_ref, off, rows)
         at = 0
         if want_image:
             outs[at][j] = image
@@ -150,64 +164,123 @@
             outs[at][j] = step
 
 
-def _specs(n, count):
-    blk = pl.BlockSpec((BZ, n, n), lambda i: (i, 0, 0))
+def _first_kernel(lo_ref, hi_ref, b_ref, g0_ref, g1_ref, g2_ref, mlane_ref, msub_ref,
+                  kappa_ref, prev_ref, part_ref, dk_ref, bg_ref, born_ref):
+    rows = b_ref.shape[1]
+    coef = (b_ref, g0_ref, g1_ref, g2_ref)
+    for j in range(BZ):
+        centre, image = _image_of(lo_ref, hi_ref, j, coef, mlane_ref, msub_ref, 0, rows)
+        bg_ref[j] = 2.0 * centre - prev_ref[j] + kappa_ref[j] * image
+        born_ref[j] = part_ref[j] + dk_ref[j] * image
+
+
+def _second_kernel(lo1_ref, hi1_ref, lo2_ref, hi2_ref, b_ref, g0_ref, g1_ref, g2_ref,
+                   mlane_ref, msub_ref, kappa_ref, prev_ref, dk_ref, img_ref, born_ref):
+    rows = b_ref.shape[1]
+    coef = (b_ref, g0_ref, g1_ref, g2_ref)
+    for j in range(BZ):
+        _, image = _image_of(lo1_ref, hi1_ref, j, coef, mlane_ref, msub_ref, 0, rows)
+        img_ref[j] = image
+        centre, own = _image_of(lo2_ref, hi2_ref, j, coef, mlane_ref, msub_ref, 0, rows)
+        born_ref[j] = 2.0 * centre - prev_ref[j] + kappa_ref[j] * own + dk_ref[j] * image
+
+
+def _specs(rows, n, count):
+    blk = pl.BlockSpec((BZ, rows, n), lambda i: (i, 0, 0))
     return [blk] * count
 
 
-def _ext_specs(n):
+def _ext_specs(rows, n):
     return [
-        pl.BlockSpec((BZ, n, n), lambda i: (i, 0, 0)),
-        pl.BlockSpec((BZ, n, n), lambda i: (i + 1, 0, 0)),
+        pl.BlockSpec((BZ, rows, n), lambda i: (i, 0, 0)),
+        pl.BlockSpec((BZ, rows, n), lambda i: (i + 1, 0, 0)),
     ]
 
 
-def _mat_specs(n):
+def _mat_specs(mlane, msub):
     return [
-        pl.BlockSpec((n, 2 * n), lambda i: (0, 0)),
-        pl.BlockSpec((2 * n, n), lambda i: (0, 0)),
+        pl.BlockSpec(mlane.shape, lambda i: (0, 0)),
+        pl.BlockSpec(msub.shape, lambda i: (0, 0)),
     ]
+
+
+PARAMS = pltpu.CompilerParams(vmem_limit_bytes=48 * 1024 * 1024)
 
 
 def slopes_of(b_ext, mlane, msub):
     depth = b_ext.shape[0] - 2 * HALO
-    n = b_ext.shape[1]
-    shape = jax.ShapeDtypeStruct((depth, n, n), jnp.float32)
+    rows_in = b_ext.shape[1]
+    rows = msub.shape[0] // 2
+    n = b_ext.shape[2]
+    shape = jax.ShapeDtypeStruct((depth, rows, n), jnp.float32)
     return pl.pallas_call(
-        _slope_kernel,
+        functools.partial(_slope_kernel, (rows_in - rows) // 2),
         grid=(depth // BZ,),
-        in_specs=_ext_specs(n) + _mat_specs(n),
-        out_specs=_specs(n, 3),
+        in_specs=_ext_specs(rows_in, n) + _mat_specs(mlane, msub),
+        out_specs=_specs(rows, n, 3),
         out_shape=[shape] * 3,
-        compiler_params=pltpu.CompilerParams(vmem_limit_bytes=48 * 1024 * 1024),
+        compiler_params=PARAMS,
         interpret=INTERPRET,
     )(b_ext, b_ext, mlane, msub)
 
 
 def apply_op(f_ext, b, slopes, mlane, msub, kappa=None, prev=None, dk=None, img=None, want_image=False):
     depth = f_ext.shape[0] - 2 * HALO
-    n = f_ext.shape[1]
+    rows_in = f_ext.shape[1]
+    rows = b.shape[1]
+    n = f_ext.shape[2]
+    off = (rows_in - rows) // 2
     want_step = kappa is not None
     with_prev = prev is not None
     with_img = img is not None
     args = [f_ext, f_ext, b, *slopes, mlane, msub]
-    in_specs = _ext_specs(n) + _specs(n, 4) + _mat_specs(n)
+    in_specs = _ext_specs(rows_in, n) + _specs(rows, n, 4) + _mat_specs(mlane, msub)
     if want_step:
         extra = [kappa] + ([prev] if with_prev else []) + ([dk, img] if with_img else [])
         args += extra
-        in_specs += _specs(n, len(extra))
+        in_specs += _specs(rows, n, len(extra))
     n_out = int(want_image) + int(want_step)
-    shape = jax.ShapeDtypeStruct((depth, n, n), jnp.float32)
+    shape = jax.ShapeDtypeStruct((depth, rows, n), jnp.float32)
     outs = pl.pallas_call(
-        functools.partial(_op_kernel, (with_prev, with_img, want_image, want_step)),
+        functools.partial(_op_kernel, (with_prev, with_img, want_image, want_step, off)),
         grid=(depth // BZ,),
         in_specs=in_specs,
-        out_specs=_specs(n, n_out),
+        out_specs=_specs(rows, n, n_out),
         out_shape=[shape] * n_out,
-        compiler_params=pltpu.CompilerParams(vmem_limit_bytes=48 * 1024 * 1024),
+        compiler_params=PARAMS,
         interpret=INTERPRET,
     )(*args)
     return outs
+
+
+def first_step(u_cur_ext, b, slopes, mlane, msub, kappa, u_prev, partial, dk):
+    depth = u_cur_ext.shape[0] - 2 * HALO
+    n = u_cur_ext.shape[2]
+    shape = jax.ShapeDtypeStruct((depth, n, n), jnp.float32)
+    return pl.pallas_call(
+        _first_kernel,
+        grid=(depth // BZ,),
+        in_specs=_ext_specs(n, n) + _specs(n, n, 4) + _mat_specs(mlane, msub) + _specs(n, n, 4),
+        out_specs=_specs(n, n, 2),
+        out_shape=[shape] * 2,
+        compiler_params=PARAMS,
+        interpret=INTERPRET,
+    )(u_cur_ext, u_cur_ext, b, *slopes, mlane, msub, kappa, u_prev, partial, dk)
+
+
+def second_step(bg_ext, born_ext, b, slopes, mlane, msub, kappa, prev, dk):
+    depth = bg_ext.shape[0] - 2 * HALO
+    n = bg_ext.shape[2]
+    shape = jax.ShapeDtypeStruct((depth, n, n), jnp.float32)
+    return pl.pallas_call(
+        _second_kernel,
+        grid=(depth // BZ,),
+        in_specs=_ext_specs(n, n) * 2 + _specs(n, n, 4) + _mat_specs(mlane, msub) + _specs(n, n, 3),
+        out_specs=_specs(n, n, 2),
+        out_shape=[shape] * 2,
+        compiler_params=PARAMS,
+        interpret=INTERPRET,
+    )(bg_ext, bg_ext, born_ext, born_ext, b, *slopes, mlane, msub, kappa, prev, dk)
 
 
 def local_body(u_prev, u_cur, buoyancy, kappa, dkappa, du_prev, du_cur):
@@ -233,13 +306,14 @@
 
     (partial_first,) = apply_op(newer_ext, buoyancy, slopes, mlane, msub, kappa=kappa, prev=older)
 
-    image_first, background_first = apply_op(
-        u_cur_ext, buoyancy, slopes, mlane, msub, kappa=kappa, prev=u_prev_all, want_image=True
-    )
-    born_first = partial_first + probe_kappa * image_first
+    background_first, born_first = first_step(
+        u_cur_ext, buoyancy, slopes, mlane, msub, kappa, u_prev_all, partial_first, probe_kappa
+    )
 
     background_first_ext, born_first_ext = halo_depth_many([background_first, born_first])
-    (image_second,) = apply_op(background_first_ext, buoyancy, slopes, mlane, msub, want_image=True)
+    image_second, born_second = second_step(
+        background_first_ext, born_first_ext, buoyancy, slopes, mlane, msub, kappa, newer, probe_kappa
+    )
 
     def cut_strip(field):
         return lax.dynamic_slice_in_dim(field, offset, strip, 1)
@@ -247,11 +321,6 @@
     background_first_strip = cut_strip(background_first)
     background_second = (
         2.0 * background_first_strip - u_cur + cut_strip(kappa) * cut_strip(image_second)
-    )
-
-    (born_second,) = apply_op(
-        born_first_ext, buoyancy, slopes, mlane, msub,
-        kappa=kappa, prev=newer, dk=probe_kappa, img=image_second,
     )
     return background_first_strip, background_second, born_first[None], born_second[None]
 

time: 163 us -> 164 us (level)
  waiting for transfers between devices: 56.9 us -> 59.7 us
    pallas_call x4 -> x1, Pallas kernels: 41.4 us -> 9.92 us  [apply_op(): pl.pallas_call(functools.partial(_op_kernel, (with_prev, with_img, want_i...]
    pallas_call x1 -> x3, Pallas kernels: 10.3 us -> 40.4 us  [the longest x1 18.4 us: second_step(): pl.pallas_call(_second_kernel, grid=(depth // BZ,), in_specs=_ext_specs(n...]
    slice x3, local copies, waits for them, and re-layouts: 1.82 us -> 0.07 us  [halo_depth_many(): below[:, at:at + w]]
    concatenate x4 -> x3, other arithmetic: 7.12 us -> 8.23 us  [halo_depth_many(): jnp.concatenate([above[:, at:at + w], f, below[:, at:at + w]], axis=0)]
    slice x4 -> x5, local copies, waits for them, and re-layouts: 2.99 us -> 4.01 us  [halo_depth_many(): tails = jnp.concatenate([f[f.shape[0] - HALO:] for f in fields], axis=1)]
    unnamed x32 -> x26, local copies, waits for them, and re-layouts: 5.03 us -> 4.19 us
  transfers between devices with their start and end apart: 13 -> 13, of which waited for: 9 -> 9; matrix products, arithmetic and copies ran while one was open for 4% -> 3% of each run, Pallas kernels for 12% -> 12%
where the time goes in v7:
time: 164 us; the launch traced here: 163 us
  waiting for transfers between devices  59.7 us (36%)
  Pallas kernels  50.3 us (31%)
  starting transfers between devices  28.3 us (17%)
  other arithmetic  13.5 us (8%)
  local copies, waits for them, and re-layouts  10.4 us (6%)
    ppermute x3, waiting for transfers between devices, ring_gather(): fwd = lax.ppermute(fwd, 'probe', ahead)  23.6 us
    pallas_call x1, Pallas kernels, second_step(): pl.pallas_call(_second_kernel, grid=(depth // BZ,), in_specs=_ext_specs(n...  18.4 us
    ppermute x2, waiting for transfers between devices, halo_depth_many(): above = lax.ppermute(tails, 'slab', [(i, i + 1) for i in range(ends)])  15.9 us
    pallas_call x1, Pallas kernels, first_step(): pl.pallas_call(_first_kernel, grid=(depth // BZ,), in_specs=_ext_specs(n,...  11.7 us
    ppermute x3, starting transfers between devices, ring_gather(): bwd = lax.ppermute(bwd, 'probe', behind)  10.5 us
    pallas_call x1, Pallas kernels, slopes_of(): pl.pallas_call(functools.partial(_slope_kernel, (rows_in - rows) // 2), g...  10.3 us
    pallas_call x1, Pallas kernels, apply_op(): pl.pallas_call(functools.partial(_op_kernel, (with_prev, with_img, want_i...  9.92 us
    ppermute x2, waiting for transfers between devices, halo_depth_many(): below = lax.ppermute(heads, 'slab', [(i + 1, i) for i in range(ends)])  8.95 us
  transfers between devices with their start and end apart: 13, of which 9 were waited for; matrix products, arithmetic and copies ran while one was open for 3% of the time, Pallas kernels for 12%

profile of v7, /device:TPU:6, one launch (start us, length us, event | category | flops | bytes accessed | tf_op | source)
XLA Modules:
  0.0 163.3 jit_solution(6574138868643968505)
XLA Ops:
  1.4 1.1 slice_bitcast_fusion.1
  2.5 1.1 fusion.3
  3.6 5.2 %collective-permute-start.1 = (f32[4,264,128]{2,1,0:T(8,128)S(1)}, f32[4,264,128]{2,1,0:T(8,128)S(1)}, u32[]{:S(2)}, u32[]{:S(2)}) collective-permute-start(f32[4,264,128]{2,1,0:T(8,128)S(1)} %pad_maximum_fusion.5), channel_id=1, source_target_pairs={{1,0},{2,1},{3,2},{4,3},{5,4},{6,5},{7,6},{8,7},{9,8},{10,9},{11,1... | collective-permute-start | bytes 1622024 | tf_op jit(solution)/shard_map/ppermute | solution.py:39
  8.9 2.1 %collective-permute-start = (f32[4,264,128]{2,1,0:T(8,128)S(1)}, f32[4,264,128]{2,1,0:T(8,128)S(1)}, u32[]{:S(2)}, u32[]{:S(2)}) collective-permute-start(f32[4,264,128]{2,1,0:T(8,128)S(1)} %pad_maximum_fusion.4), channel_id=1, source_target_pairs={{0,1},{1,2},{2,3},{3,4},{4,5},{5,6},{6,7},{7,8},{8,9},{9,10},{10,1... | collective-permute-start | bytes 1622024 | tf_op jit(solution)/shard_map/ppermute | solution.py:38
  10.9 4.7 %collective-permute-done.1 = f32[4,264,128]{2,1,0:T(8,128)S(1)} collective-permute-done((f32[4,264,128]{2,1,0:T(8,128)S(1)}, f32[4,264,128]{2,1,0:T(8,128)S(1)}, u32[]{:S(2)}, u32[]{:S(2)}) %collective-permute-start.1) | collective-permute-done | bytes 540704 | tf_op jit(solution)/shard_map/ppermute | solution.py:39
  15.7 7.6 %collective-permute-done = f32[4,264,128]{2,1,0:T(8,128)S(1)} collective-permute-done((f32[4,264,128]{2,1,0:T(8,128)S(1)}, f32[4,264,128]{2,1,0:T(8,128)S(1)}, u32[]{:S(2)}, u32[]{:S(2)}) %collective-permute-start) | collective-permute-done | bytes 540704 | tf_op jit(solution)/shard_map/ppermute | solution.py:38
  24.1 7.0 %collective-permute-done.2 = f32[72,8,128]{2,1,0:T(8,128)} collective-permute-done((f32[72,8,128]{2,1,0:T(8,128)}, f32[72,8,128]{2,1,0:T(8,128)}, u32[]{:S(2)}, u32[]{:S(2)}) %collective-permute-start.2) | collective-permute-done | bytes 294944 | tf_op jit(solution)/shard_map/ppermute | solution.py:53
  31.1 1.1 maximum_select_fusion
  32.2 2.0 %collective-permute-start.6 = (f32[72,16,128]{2,1,0:T(8,128)S(1)}, f32[72,16,128]{2,1,0:T(8,128)S(1)}, u32[]{:S(2)}, u32[]{:S(2)}) collective-permute-start(f32[72,16,128]{2,1,0:T(8,128)S(1)} %maximum_select_fusion), channel_id=1, source_target_pairs={{0,32},{16,48},{32,64},{48,80},{64,96},{80,112},{96,128},{112,144}... | collective-permute-start | bytes 1769480 | tf_op jit(solution)/shard_map/ppermute | solution.py:62
  34.2 4.0 %collective-permute-start.3 = (f32[72,16,128]{2,1,0:T(8,128)S(1)}, f32[72,16,128]{2,1,0:T(8,128)S(1)}, u32[]{:S(2)}, u32[]{:S(2)}) collective-permute-start(f32[72,16,128]{2,1,0:T(8,128)S(1)} %maximum_select_fusion), channel_id=1, source_target_pairs={{0,224},{16,240},{32,0},{48,16},{64,32},{80,48},{96,64},{112,80},{... | collective-permute-start | bytes 1769480 | tf_op jit(solution)/shard_map/ppermute | solution.py:63
  38.3 1.7 %pad_maximum_fusion.lo_ref.hi_ref = f32[40,128,128]{2,1,0:T(8,128)} fusion(f32[4,128,128]{2,1,0:T(8,128)S(1)} %get-tuple-element.31, f32[32,128,128]{2,1,0:T(8,128)S(1)} %copy-done, f32[4,128,128]{2,1,0:T(8,128)S(1)} %get-tuple-element.29), kind=kLoop, calls=%fused_computation | loop fusion | flops 1310720 | bytes 5242880 | tf_op jit(solution)/shard_map/concatenate | solution.py:44
  40.0 10.3 %shard_map.120 = (f32[32,128,128]{2,1,0:T(8,128)S(1)}, f32[32,128,128]{2,1,0:T(8,128)S(1)}, f32[32,128,128]{2,1,0:T(8,128)}) custom-call(f32[40,128,128]{2,1,0:T(8,128)} %pad_maximum_fusion.lo_ref.hi_ref, f32[40,128,128]{2,1,0:T(8,128)} %pad_maximum_fusion.lo_ref.hi_ref, f32[128,256]{1,0:T(8,128)S(1)} %copy-done.7, f32[256,128]{1,0:T(8,128)S(1)} %copy-done.6), custom_call_target="tpu_custom_call" | custom-call | tf_op jit(solution)/shard_map/pallas_call | solution.py:216
  50.3 2.0 %pad_maximum_fusion.1.refs_0_.refs_1_ = f32[40,128,128]{2,1,0:T(8,128)} fusion(f32[4,128,128]{2,1,0:T(8,128)S(1)} %get-tuple-element.30, f32[32,128,128]{2,1,0:T(8,128)S(1)} %bitcast.10, f32[4,128,128]{2,1,0:T(8,128)S(1)} %get-tuple-element.28), kind=kLoop, calls=%fused_computation.1 | loop fusion | flops 1310720 | bytes 5242880 | tf_op jit(solution)/shard_map/concatenate | solution.py:44
  53.0 9.9 %shard_map.121.part_ref = f32[32,128,128]{2,1,0:T(8,128)S(1)} custom-call(f32[40,128,128]{2,1,0:T(8,128)} %pad_maximum_fusion.1.refs_0_.refs_1_, f32[40,128,128]{2,1,0:T(8,128)} %pad_maximum_fusion.1.refs_0_.refs_1_, f32[32,128,128]{2,1,0:T(8,128)S(1)} %copy-done, f32[32,128,128]{2,1,0:T(8,128)} %copy-done.1, f32[32,128,128]{2,1,0:T(8,128)} %copy-done.2, ...), custom_call_target="tpu_custom_call" | custom-call | tf_op jit(solution)/shard_map/pallas_call | solution.py:244
  63.1 3.2 %collective-permute-start.4 = (f32[72,16,128]{2,1,0:T(8,128)S(1)}, f32[72,16,128]{2,1,0:T(8,128)S(1)}, u32[]{:S(2)}, u32[]{:S(2)}) collective-permute-start(f32[72,16,128]{2,1,0:T(8,128)S(1)} %collective-permute-done.3), channel_id=1, source_target_pairs={{0,224},{16,240},{32,0},{48,16},{64,32},{80,48},{96,64},{112,80},{... | collective-permute-start | bytes 1769480 | tf_op jit(solution)/shard_map/ppermute | solution.py:63
  67.0 13.5 %collective-permute-done.7 = f32[72,16,128]{2,1,0:T(8,128)S(1)} collective-permute-done((f32[72,16,128]{2,1,0:T(8,128)S(1)}, f32[72,16,128]{2,1,0:T(8,128)S(1)}, u32[]{:S(2)}, u32[]{:S(2)}) %collective-permute-start.7) | collective-permute-done | bytes 589856 | tf_op jit(solution)/shard_map/ppermute | solution.py:62
  80.4 3.2 %collective-permute-start.5 = (f32[72,16,128]{2,1,0:T(8,128)S(1)}, f32[72,16,128]{2,1,0:T(8,128)S(1)}, u32[]{:S(2)}, u32[]{:S(2)}) collective-permute-start(f32[72,16,128]{2,1,0:T(8,128)S(1)} %collective-permute-done.4), channel_id=1, source_target_pairs={{0,224},{16,240},{32,0},{48,16},{64,32},{80,48},{96,64},{112,80},{... | collective-permute-start | bytes 1769480 | tf_op jit(solution)/shard_map/ppermute | solution.py:63
  83.8 10.2 %collective-permute-done.8 = f32[72,16,128]{2,1,0:T(8,128)S(1)} collective-permute-done((f32[72,16,128]{2,1,0:T(8,128)S(1)}, f32[72,16,128]{2,1,0:T(8,128)S(1)}, u32[]{:S(2)}, u32[]{:S(2)}) %collective-permute-start.8) | collective-permute-done | bytes 589856 | tf_op jit(solution)/shard_map/ppermute | solution.py:62
  94.1 3.5 %collective-permute-start.10 = (f32[36,16,128]{2,1,0:T(8,128)S(1)}, f32[36,16,128]{2,1,0:T(8,128)S(1)}, u32[]{:S(2)}, u32[]{:S(2)}) collective-permute-start(f32[36,16,128]{2,1,0:T(8,128)S(1)} %slice.167), channel_id=1, source_target_pairs={{0,224},{16,240},{32,0},{48,16},{64,32},{80,48},{96,64},{112,80},{... | collective-permute-start | bytes 884744 | tf_op jit(solution)/shard_map/ppermute | solution.py:68
  97.6 4.2 %collective-permute-done.10 = f32[36,16,128]{2,1,0:T(8,128)S(1)} collective-permute-done((f32[36,16,128]{2,1,0:T(8,128)S(1)}, f32[36,16,128]{2,1,0:T(8,128)S(1)}, u32[]{:S(2)}, u32[]{:S(2)}) %collective-permute-start.10) | collective-permute-done | bytes 294944 | tf_op jit(solution)/shard_map/ppermute | solution.py:68
  102.2 1.3 copy-done.10
  104.3 11.7 %shard_map.122 = (f32[32,128,128]{2,1,0:T(8,128)S(1)}, f32[32,128,128]{2,1,0:T(8,128)}) custom-call(f32[40,128,128]{2,1,0:T(8,128)} %copy-done.8, f32[40,128,128]{2,1,0:T(8,128)} %copy-done.8, f32[32,128,128]{2,1,0:T(8,128)S(1)} %copy-done, f32[32,128,128]{2,1,0:T(8,128)} %copy-done.1, f32[32,128,128]{2,1,0:T(8,128)} %copy-done.2, ...), custom_call_target="tpu_custom_call" | custom-call | tf_op jit(solution)/shard_map/pallas_call | solution.py:260
  116.1 1.3 copy-done.4
  117.4 1.1 fusion.2
  119.3 3.0 %collective-permute-start.12 = (f32[4,256,128]{2,1,0:T(8,128)}, f32[4,256,128]{2,1,0:T(8,128)S(1)}, u32[]{:S(2)}, u32[]{:S(2)}) collective-permute-start(f32[4,256,128]{2,1,0:T(8,128)} %pad_maximum_fusion.7), channel_id=1, source_target_pairs={{1,0},{2,1},{3,2},{4,3},{5,4},{6,5},{7,6},{8,7},{9,8},{10,9},{11,1... | collective-permute-start | bytes 1572872 | tf_op jit(solution)/shard_map/ppermute | solution.py:39
  123.2 1.9 %collective-permute-start.11 = (f32[4,256,128]{2,1,0:T(8,128)}, f32[4,256,128]{2,1,0:T(8,128)}, u32[]{:S(2)}, u32[]{:S(2)}) collective-permute-start(f32[4,256,128]{2,1,0:T(8,128)} %pad_maximum_fusion.6), channel_id=1, source_target_pairs={{0,1},{1,2},{2,3},{3,4},{4,5},{5,6},{6,7},{7,8},{8,9},{9,10},{10,1... | collective-permute-start | bytes 1572872 | tf_op jit(solution)/shard_map/ppermute | solution.py:38
  125.1 4.2 %collective-permute-done.12 = f32[4,256,128]{2,1,0:T(8,128)S(1)} collective-permute-done((f32[4,256,128]{2,1,0:T(8,128)}, f32[4,256,128]{2,1,0:T(8,128)S(1)}, u32[]{:S(2)}, u32[]{:S(2)}) %collective-permute-start.12) | collective-permute-done | bytes 524320 | tf_op jit(solution)/shard_map/ppermute | solution.py:39
  129.4 8.2 %collective-permute-done.11 = f32[4,256,128]{2,1,0:T(8,128)} collective-permute-done((f32[4,256,128]{2,1,0:T(8,128)}, f32[4,256,128]{2,1,0:T(8,128)}, u32[]{:S(2)}, u32[]{:S(2)}) %collective-permute-start.11) | collective-permute-done | bytes 524320 | tf_op jit(solution)/shard_map/ppermute | solution.py:38
  137.6 1.1 fusion.6
  138.7 4.5 %pad_maximum_fusion.2 = (f32[40,128,128]{2,1,0:T(8,128)}, f32[40,128,128]{2,1,0:T(8,128)}) fusion(f32[4,128,128]{2,1,0:T(8,128)S(1)} %get-tuple-element.35, f32[32,128,128]{2,1,0:T(8,128)S(1)} %copy-done.5, f32[4,128,128]{2,1,0:T(8,128)S(1)} %get-tuple-element.33, f32[4,128,128]{2,1,0:T(8,128)S(1)} %get-tuple-element.34, ...), kind=kLoop, calls=%fused_computation.2 | loop fusion | flops 2621440 | bytes 10485760 | tf_op jit(solution)/shard_map/concatenate | solution.py:44
  143.3 18.4 %shard_map.123 = (f32[32,128,128]{2,1,0:T(8,128)S(1)}, f32[32,128,128]{2,1,0:T(8,128)}) custom-call(f32[40,128,128]{2,1,0:T(8,128)} %get-tuple-element.38.lo1_ref.hi1_ref, f32[40,128,128]{2,1,0:T(8,128)} %get-tuple-element.38.lo1_ref.hi1_ref, f32[40,128,128]{2,1,0:T(8,128)} %get-tuple-element.39.lo2_ref.hi2_ref, ...), custom_call_target="tpu_custom_call" | custom-call | tf_op jit(solution)/shard_map/pallas_call | solution.py:275
  161.7 1.7 %multiply_add_fusion = (f32[32,8,128]{2,1,0:T(8,128)}, f32[32,8,128]{2,1,0:T(8,128)}) fusion(f32[32,128,128]{2,1,0:T(8,128)S(1)} %get-tuple-element.16, s32[]{:T(128)S(6)} %select_n.124, f32[32,128,128]{2,1,0:T(8,128)} %kappa_ref.3, f32[32,8,128]{2,1,0:T(8,128)S(1)} %copy-done.11, f32[32,128,128]{2,1,0:T(8,128)S(1)} %copy-done.5), kind=kLoop, calls=%fused_computation.29 | loop fusion | flops 131072 | bytes 786436 | tf_op jit(solution)/shard_map/add | solution.py:323
  (65 shorter events, 6.4 us)
Async XLA Ops:
  0.6 22.7 %copy-start.11 = (f32[32,8,128]{2,1,0:T(8,128)S(1)}, f32[32,8,128]{2,1,0:T(8,128)}, u32[]{:S(2)}) copy-start(f32[32,8,128]{2,1,0:T(8,128)} %param.10) | copy-start | bytes 393220
  0.6 22.7 %copy-start.12 = (f32[32,8,128]{2,1,0:T(8,128)S(1)}, f32[32,8,128]{2,1,0:T(8,128)}, u32[]{:S(2)}) copy-start(f32[32,8,128]{2,1,0:T(8,128)} %param.9) | copy-start | bytes 393220
  3.6 12.1 %collective-permute-start.1 = (f32[4,264,128]{2,1,0:T(8,128)S(1)}, f32[4,264,128]{2,1,0:T(8,128)S(1)}, u32[]{:S(2)}, u32[]{:S(2)}) collective-permute-start(f32[4,264,128]{2,1,0:T(8,128)S(1)} %pad_maximum_fusion.5), channel_id=1, source_target_pairs={{1,0},{2,1},{3,2},{4,3},{5,4},{6,5},{7,6},{8,7},{9,8},{10,9},{11,1... | collective-permute-start | bytes 1622024 | tf_op jit(solution)/shard_map/ppermute | solution.py:39
  8.8 29.4 %copy-start = (f32[32,128,128]{2,1,0:T(8,128)S(1)}, f32[32,128,128]{2,1,0:T(8,128)}, u32[]{:S(2)}) copy-start(f32[32,128,128]{2,1,0:T(8,128)} %b_ref.3) | copy-start | bytes 6291460
  8.9 14.4 %collective-permute-start = (f32[4,264,128]{2,1,0:T(8,128)S(1)}, f32[4,264,128]{2,1,0:T(8,128)S(1)}, u32[]{:S(2)}, u32[]{:S(2)}) collective-permute-start(f32[4,264,128]{2,1,0:T(8,128)S(1)} %pad_maximum_fusion.4), channel_id=1, source_target_pairs={{0,1},{1,2},{2,3},{3,4},{4,5},{5,6},{6,7},{7,8},{8,9},{9,10},{10,1... | collective-permute-start | bytes 1622024 | tf_op jit(solution)/shard_map/ppermute | solution.py:38
  24.1 7.0 %collective-permute-start.2 = (f32[72,8,128]{2,1,0:T(8,128)}, f32[72,8,128]{2,1,0:T(8,128)}, u32[]{:S(2)}, u32[]{:S(2)}) collective-permute-start(f32[72,8,128]{2,1,0:T(8,128)} %pad_maximum_fusion.9), channel_id=1, source_target_pairs={{0,16},{16,0},{32,48},{48,32},{64,80},{80,64},{96,112},{112,96},{1... | collective-permute-start | bytes 884744 | tf_op jit(solution)/shard_map/ppermute | solution.py:53
  32.2 30.8 %collective-permute-start.6 = (f32[72,16,128]{2,1,0:T(8,128)S(1)}, f32[72,16,128]{2,1,0:T(8,128)S(1)}, u32[]{:S(2)}, u32[]{:S(2)}) collective-permute-start(f32[72,16,128]{2,1,0:T(8,128)S(1)} %maximum_select_fusion), channel_id=1, source_target_pairs={{0,32},{16,48},{32,64},{48,80},{64,96},{80,112},{96,128},{112,144}... | collective-permute-start | bytes 1769480 | tf_op jit(solution)/shard_map/ppermute | solution.py:62
  34.2 28.9 %collective-permute-start.3 = (f32[72,16,128]{2,1,0:T(8,128)S(1)}, f32[72,16,128]{2,1,0:T(8,128)S(1)}, u32[]{:S(2)}, u32[]{:S(2)}) collective-permute-start(f32[72,16,128]{2,1,0:T(8,128)S(1)} %maximum_select_fusion), channel_id=1, source_target_pairs={{0,224},{16,240},{32,0},{48,16},{64,32},{80,48},{96,64},{112,80},{... | collective-permute-start | bytes 1769480 | tf_op jit(solution)/shard_map/ppermute | solution.py:63
  38.3 1.7 %copy-start.6 = (f32[256,128]{1,0:T(8,128)S(1)}, f32[256,128]{1,0:T(8,128)}, u32[]{:S(2)}) copy-start(f32[256,128]{1,0:T(8,128)} %constant.108.clone.msub_ref.refs_7_) | copy-start | bytes 393220
  38.3 1.7 %copy-start.7 = (f32[128,256]{1,0:T(8,128)S(1)}, f32[128,256]{1,0:T(8,128)}, u32[]{:S(2)}) copy-start(f32[128,256]{1,0:T(8,128)} %constant.107.clone.mlane_ref.refs_6_) | copy-start | bytes 393220
  40.0 10.3 %copy-start.9 = (f32[1,32,128,128]{3,2,1,0:T(8,128)S(1)}, f32[1,32,128,128]{3,2,1,0:T(8,128)}, u32[]{:S(2)}) copy-start(f32[1,32,128,128]{3,2,1,0:T(8,128)} %param.15) | copy-start | bytes 6291460
  50.3 2.2 %copy-start.1 = (f32[32,128,128]{2,1,0:T(8,128)}, f32[32,128,128]{2,1,0:T(8,128)S(1)}, u32[]{:S(2)}) copy-start(f32[32,128,128]{2,1,0:T(8,128)S(1)} %get-tuple-element.11.refs_3_.g0_ref) | copy-start | bytes 6291460
  50.3 2.7 %copy-start.2 = (f32[32,128,128]{2,1,0:T(8,128)}, f32[32,128,128]{2,1,0:T(8,128)S(1)}, u32[]{:S(2)}) copy-start(f32[32,128,128]{2,1,0:T(8,128)S(1)} %get-tuple-element.12.refs_4_.g1_ref) | copy-start | bytes 6291460
  62.9 3.9 %copy-start.3 = (f32[32,128,128]{2,1,0:T(8,128)}, f32[32,128,128]{2,1,0:T(8,128)S(1)}, u32[]{:S(2)}) copy-start(f32[32,128,128]{2,1,0:T(8,128)S(1)} %shard_map.121.part_ref) | copy-start | bytes 6291460
  63.0 17.4 %collective-permute-start.7 = (f32[72,16,128]{2,1,0:T(8,128)S(1)}, f32[72,16,128]{2,1,0:T(8,128)S(1)}, u32[]{:S(2)}, u32[]{:S(2)}) collective-permute-start(f32[72,16,128]{2,1,0:T(8,128)S(1)} %collective-permute-done.6), channel_id=1, source_target_pairs={{0,32},{16,48},{32,64},{48,80},{64,96},{80,112},{96,128},{112,144}... | collective-permute-start | bytes 1769480 | tf_op jit(solution)/shard_map/ppermute | solution.py:62
  63.1 17.4 %collective-permute-start.4 = (f32[72,16,128]{2,1,0:T(8,128)S(1)}, f32[72,16,128]{2,1,0:T(8,128)S(1)}, u32[]{:S(2)}, u32[]{:S(2)}) collective-permute-start(f32[72,16,128]{2,1,0:T(8,128)S(1)} %collective-permute-done.3), channel_id=1, source_target_pairs={{0,224},{16,240},{32,0},{48,16},{64,32},{80,48},{96,64},{112,80},{... | collective-permute-start | bytes 1769480 | tf_op jit(solution)/shard_map/ppermute | solution.py:63
  80.4 13.5 %collective-permute-start.8 = (f32[72,16,128]{2,1,0:T(8,128)S(1)}, f32[72,16,128]{2,1,0:T(8,128)S(1)}, u32[]{:S(2)}, u32[]{:S(2)}) collective-permute-start(f32[72,16,128]{2,1,0:T(8,128)S(1)} %collective-permute-done.7), channel_id=1, source_target_pairs={{0,32},{16,48},{32,64},{48,80},{64,96},{80,112},{96,128},{112,144}... | collective-permute-start | bytes 1769480 | tf_op jit(solution)/shard_map/ppermute | solution.py:62
  80.4 13.6 %collective-permute-start.5 = (f32[72,16,128]{2,1,0:T(8,128)S(1)}, f32[72,16,128]{2,1,0:T(8,128)S(1)}, u32[]{:S(2)}, u32[]{:S(2)}) collective-permute-start(f32[72,16,128]{2,1,0:T(8,128)S(1)} %collective-permute-done.4), channel_id=1, source_target_pairs={{0,224},{16,240},{32,0},{48,16},{64,32},{80,48},{96,64},{112,80},{... | collective-permute-start | bytes 1769480 | tf_op jit(solution)/shard_map/ppermute | solution.py:63
  93.9 8.0 %collective-permute-start.9 = (f32[36,16,128]{2,1,0:T(8,128)S(1)}, f32[36,16,128]{2,1,0:T(8,128)S(1)}, u32[]{:S(2)}, u32[]{:S(2)}) collective-permute-start(f32[36,16,128]{2,1,0:T(8,128)S(1)} %slice.166), channel_id=1, source_target_pairs={{0,32},{16,48},{32,64},{48,80},{64,96},{80,112},{96,128},{112,144}... | collective-permute-start | bytes 884744 | tf_op jit(solution)/shard_map/ppermute | solution.py:68
  94.1 7.7 %collective-permute-start.10 = (f32[36,16,128]{2,1,0:T(8,128)S(1)}, f32[36,16,128]{2,1,0:T(8,128)S(1)}, u32[]{:S(2)}, u32[]{:S(2)}) collective-permute-start(f32[36,16,128]{2,1,0:T(8,128)S(1)} %slice.167), channel_id=1, source_target_pairs={{0,224},{16,240},{32,0},{48,16},{64,32},{80,48},{96,64},{112,80},{... | collective-permute-start | bytes 884744 | tf_op jit(solution)/shard_map/ppermute | solution.py:68
  102.2 1.3 copy-start.10
  102.2 2.1 %copy-start.8 = (f32[40,128,128]{2,1,0:T(8,128)}, f32[40,128,128]{2,1,0:T(8,128)S(1)}, u32[]{:S(2)}) copy-start(f32[40,128,128]{2,1,0:T(8,128)S(1)} %slice_dynamic-update-slice_fusion.lo_ref.hi_ref) | copy-start | bytes 7864324
  116.1 1.3 copy-start.4
  119.3 10.0 %collective-permute-start.12 = (f32[4,256,128]{2,1,0:T(8,128)}, f32[4,256,128]{2,1,0:T(8,128)S(1)}, u32[]{:S(2)}, u32[]{:S(2)}) collective-permute-start(f32[4,256,128]{2,1,0:T(8,128)} %pad_maximum_fusion.7), channel_id=1, source_target_pairs={{1,0},{2,1},{3,2},{4,3},{5,4},{6,5},{7,6},{8,7},{9,8},{10,9},{11,1... | collective-permute-start | bytes 1572872 | tf_op jit(solution)/shard_map/ppermute | solution.py:39
  123.2 14.4 %collective-permute-start.11 = (f32[4,256,128]{2,1,0:T(8,128)}, f32[4,256,128]{2,1,0:T(8,128)}, u32[]{:S(2)}, u32[]{:S(2)}) collective-permute-start(f32[4,256,128]{2,1,0:T(8,128)} %pad_maximum_fusion.6), channel_id=1, source_target_pairs={{0,1},{1,2},{2,3},{3,4},{4,5},{5,6},{6,7},{7,8},{8,9},{9,10},{10,1... | collective-permute-start | bytes 1572872 | tf_op jit(solution)/shard_map/ppermute | solution.py:38
  125.1 13.6 %copy-start.5 = (f32[32,128,128]{2,1,0:T(8,128)S(1)}, f32[32,128,128]{2,1,0:T(8,128)}, u32[]{:S(2)}) copy-start(f32[32,128,128]{2,1,0:T(8,128)} %copy-done.4) | copy-start | bytes 6291460

commit v8 on v7

--- a/solution.py
+++ b/solution.py
@@ -80,19 +80,18 @@
     return outs
 
 
-def _ext(lo_ref, hi_ref, idx):
-    if idx < BZ:
-        return lo_ref[idx]
-    return hi_ref[idx - BZ]
-
-
-def _depth_terms(lo_ref, hi_ref, j, off, rows):
+def _ext(win, idx):
+    size = win[0].shape[0]
+    return win[idx // size][idx % size]
+
+
+def _depth_terms(win, j, off, rows):
     c = j + HALO
 
     def at(idx):
-        return _ext(lo_ref, hi_ref, idx)[off:off + rows]
-
-    whole = _ext(lo_ref, hi_ref, c)
+        return _ext(win, idx)[off:off + rows]
+
+    whole = _ext(win, c)
     centre = whole[off:off + rows]
     second = (3.0 * SECOND[0]) * centre
     grad = None
@@ -109,7 +108,7 @@
     n = mlane_ref.shape[0]
     rows = g0_ref.shape[1]
     for j in range(BZ):
-        whole, centre, _, grad = _depth_terms(lo_ref, hi_ref, j, off, rows)
+        whole, centre, _, grad = _depth_terms((lo_ref, hi_ref), j, off, rows)
         lane = jnp.dot(centre, mlane_ref[...], precision=HI, preferred_element_type=jnp.float32)
         sub = jnp.dot(msub_ref[...], whole, precision=HI, preferred_element_type=jnp.float32)
         g0_ref[j] = grad
@@ -117,10 +116,10 @@
         g2_ref[j] = lane[:, n:]
 
 
-def _image_of(lo_ref, hi_ref, j, coef, mlane_ref, msub_ref, off, rows):
+def _image_of(win, j, coef, mlane_ref, msub_ref, off, rows):
     b_ref, g0_ref, g1_ref, g2_ref = coef
     n = mlane_ref.shape[0]
-    whole, centre, second, grad = _depth_terms(lo_ref, hi_ref, j, off, rows)
+    whole, centre, second, grad = _depth_terms(win, j, off, rows)
     lane = jnp.dot(centre, mlane_ref[...], precision=HI, preferred_element_type=jnp.float32)
     sub = jnp.dot(msub_ref[...], whole, precision=HI, preferred_element_type=jnp.float32)
     second = second + sub[:rows] + lane[:, :n]
@@ -150,7 +149,7 @@
     rows = b_ref.shape[1]
     coef = (b_ref, g0_ref, g1_ref, g2_ref)
     for j in range(BZ):
-        centre, image = _image_of(lo_ref, hi_ref, j, coef, mlane_ref, msub_ref, off, rows)
+        centre, image = _image_of((lo_ref, hi_ref), j, coef, mlane_ref, msub_ref, off, rows)
         at = 0
         if want_image:
             outs[at][j] = image
@@ -169,19 +168,22 @@
     rows = b_ref.shape[1]
     coef = (b_ref, g0_ref, g1_ref, g2_ref)
     for j in range(BZ):
-        centre, image = _image_of(lo_ref, hi_ref, j, coef, mlane_ref, msub_ref, 0, rows)
+        centre, image = _image_of((lo_ref, hi_ref), j, coef, mlane_ref, msub_ref, 0, rows)
         bg_ref[j] = 2.0 * centre - prev_ref[j] + kappa_ref[j] * image
         born_ref[j] = part_ref[j] + dk_ref[j] * image
 
 
-def _second_kernel(lo1_ref, hi1_ref, lo2_ref, hi2_ref, b_ref, g0_ref, g1_ref, g2_ref,
-                   mlane_ref, msub_ref, kappa_ref, prev_ref, dk_ref, img_ref, born_ref):
+def _second_kernel(nwin, *refs):
+    win1 = refs[:nwin]
+    win2 = refs[nwin:2 * nwin]
+    b_ref, g0_ref, g1_ref, g2_ref, mlane_ref, msub_ref, kappa_ref, prev_ref, dk_ref = refs[2 * nwin:2 * nwin + 9]
+    img_ref, born_ref = refs[-2:]
     rows = b_ref.shape[1]
     coef = (b_ref, g0_ref, g1_ref, g2_ref)
     for j in range(BZ):
-        _, image = _image_of(lo1_ref, hi1_ref, j, coef, mlane_ref, msub_ref, 0, rows)
+        _, image = _image_of(win1, j, coef, mlane_ref, msub_ref, 0, rows)
         img_ref[j] = image
-        centre, own = _image_of(lo2_ref, hi2_ref, j, coef, mlane_ref, msub_ref, 0, rows)
+        centre, own = _image_of(win2, j, coef, mlane_ref, msub_ref, 0, rows)
         born_ref[j] = 2.0 * centre - prev_ref[j] + kappa_ref[j] * own + dk_ref[j] * image
 
 
@@ -268,19 +270,66 @@
     )(u_cur_ext, u_cur_ext, b, *slopes, mlane, msub, kappa, u_prev, partial, dk)
 
 
-def second_step(bg_ext, born_ext, b, slopes, mlane, msub, kappa, prev, dk):
-    depth = bg_ext.shape[0] - 2 * HALO
-    n = bg_ext.shape[2]
+def second_inner(bg, born, b, slopes, mlane, msub, kappa, prev, dk):
+    depth = bg.shape[0]
+    n = bg.shape[2]
+    q = HALO
+    blocks = depth // BZ
+    win = [pl.BlockSpec((q, n, n), lambda i, t=t: ((i + 1) * (BZ // q) - 1 + t, 0, 0)) for t in range(4)]
+    inner = [pl.BlockSpec((BZ, n, n), lambda i: (i + 1, 0, 0))]
     shape = jax.ShapeDtypeStruct((depth, n, n), jnp.float32)
     return pl.pallas_call(
-        _second_kernel,
-        grid=(depth // BZ,),
-        in_specs=_ext_specs(n, n) * 2 + _specs(n, n, 4) + _mat_specs(mlane, msub) + _specs(n, n, 3),
-        out_specs=_specs(n, n, 2),
+        functools.partial(_second_kernel, 4),
+        grid=(blocks - 2,),
+        in_specs=win * 2 + inner * 4 + _mat_specs(mlane, msub) + inner * 3,
+        out_specs=inner * 2,
         out_shape=[shape] * 2,
         compiler_params=PARAMS,
         interpret=INTERPRET,
-    )(bg_ext, bg_ext, born_ext, born_ext, b, *slopes, mlane, msub, kappa, prev, dk)
+    )(*([bg] * 4), *([born] * 4), b, *slopes, mlane, msub, kappa, prev, dk)
+
+
+def _edge_kernel(*refs):
+    _second_kernel(2, *refs[:-4], *refs[-2:])
+
+
+def second_edges(bg_rim, born_rim, b, slopes, mlane, msub, kappa, prev, dk, img, born_out):
+    depth = b.shape[0]
+    n = b.shape[2]
+    last = depth // BZ - 1
+    win = [pl.BlockSpec((BZ, n, n), lambda i, t=t: (2 * i + t, 0, 0)) for t in range(2)]
+    edge = [pl.BlockSpec((BZ, n, n), lambda i: (i * last, 0, 0))]
+    anyspec = [pl.BlockSpec(memory_space=pl.ANY)]
+    shape = jax.ShapeDtypeStruct((depth, n, n), jnp.float32)
+    return pl.pallas_call(
+        _edge_kernel,
+        grid=(2,),
+        in_specs=win * 2 + edge * 4 + _mat_specs(mlane, msub) + edge * 3 + anyspec * 2,
+        out_specs=edge * 2,
+        out_shape=[shape] * 2,
+        input_output_aliases={13: 0, 14: 1},
+        compiler_params=PARAMS,
+        interpret=INTERPRET,
+    )(bg_rim, bg_rim, born_rim, born_rim, b, *slopes, mlane, msub, kappa, prev, dk, img, born_out)
+
+
+def depth_rims(fields):
+    count = lax.axis_size("slab")
+    ends = count - 1
+    heads = jnp.concatenate([f[:HALO] for f in fields], axis=1)
+    tails = jnp.concatenate([f[f.shape[0] - HALO:] for f in fields], axis=1)
+    above = lax.ppermute(tails, "slab", [(i, i + 1) for i in range(ends)])
+    below = lax.ppermute(heads, "slab", [(i + 1, i) for i in range(ends)])
+    outs = []
+    at = 0
+    span = BZ + HALO
+    for f in fields:
+        w = f.shape[1]
+        d = f.shape[0]
+        outs.append(jnp.concatenate(
+            [above[:, at:at + w], f[:span], f[d - span:], below[:, at:at + w]], axis=0))
+        at += w
+    return outs
 
 
 def local_body(u_prev, u_cur, buoyancy, kappa, dkappa, du_prev, du_cur):
@@ -310,9 +359,13 @@
         u_cur_ext, buoyancy, slopes, mlane, msub, kappa, u_prev_all, partial_first, probe_kappa
     )
 
-    background_first_ext, born_first_ext = halo_depth_many([background_first, born_first])
-    image_second, born_second = second_step(
-        background_first_ext, born_first_ext, buoyancy, slopes, mlane, msub, kappa, newer, probe_kappa
+    bg_rim, born_rim = depth_rims([background_first, born_first])
+    image_second, born_second = second_inner(
+        background_first, born_first, buoyancy, slopes, mlane, msub, kappa, newer, probe_kappa
+    )
+    image_second, born_second = second_edges(
+        bg_rim, born_rim, buoyancy, slopes, mlane, msub, kappa, newer, probe_kappa,
+        image_second, born_second,
     )
 
     def cut_strip(field):

time: 164 us -> 163 us (level)
  other arithmetic: 13.5 us -> 9.87 us
  Pallas kernels: 50.3 us -> 53.4 us
    ppermute x0 -> x2, waiting for transfers between devices: none -> 11.8 us  [the longest x1 11.8 us: depth_rims(): above = lax.ppermute(tails, 'slab', [(i, i + 1) for i in range(ends)])]
    ppermute x2 -> x1, waiting for transfers between devices: 15.9 us -> 7.48 us  [halo_depth_many(): above = lax.ppermute(tails, 'slab', [(i, i + 1) for i in range(ends)])]
    ppermute x0 -> x2, starting transfers between devices: none -> 4.98 us  [the longest x1 3.06 us: depth_rims(): below = lax.ppermute(heads, 'slab', [(i + 1, i) for i in range(ends)])]
    concatenate x3 -> x2, other arithmetic: 8.23 us -> 3.64 us  [halo_depth_many(): jnp.concatenate([above[:, at:at + w], f, below[:, at:at + w]], axis=0)]
    ppermute x2 -> x1, waiting for transfers between devices: 8.95 us -> 4.88 us  [halo_depth_many(): below = lax.ppermute(heads, 'slab', [(i + 1, i) for i in range(ends)])]
    pallas_call x1 -> x2, Pallas kernels: 18.4 us -> 21.5 us  [the longest x1 10.8 us: second_inner(): pl.pallas_call(functools.partial(_second_kernel, 4), grid=(blocks - 2,),...]
    ppermute x2 -> x1, starting transfers between devices: 8.25 us -> 5.2 us  [halo_depth_many(): below = lax.ppermute(heads, 'slab', [(i + 1, i) for i in range(ends)])]
    concatenate x0 -> x4, other arithmetic: none -> 2.59 us  [the longest x2 1.72 us: depth_rims(): jnp.concatenate([above[:, at:at + w], f[:span], f[d - span:], below[:, at...]
  transfers between devices with their start and end apart: 13 -> 13, of which waited for: 9 -> 8; matrix products, arithmetic and copies ran while one was open for 3% -> 3% of each run, Pallas kernels for 12% -> 19%
where the time goes in v8:
time: 163 us
  waiting for transfers between devices  59 us (36%)
  Pallas kernels  53.4 us (33%)
  starting transfers between devices  28.2 us (17%)
  local copies, waits for them, and re-layouts  11.4 us (7%)
  other arithmetic  9.87 us (6%)
    ppermute x3, waiting for transfers between devices, ring_gather(): fwd = lax.ppermute(fwd, 'probe', ahead)  23.6 us
    ppermute x1, waiting for transfers between devices, depth_rims(): above = lax.ppermute(tails, 'slab', [(i, i + 1) for i in range(ends)])  11.8 us
    pallas_call x1, Pallas kernels, first_step(): pl.pallas_call(_first_kernel, grid=(depth // BZ,), in_specs=_ext_specs(n,...  11.7 us
    pallas_call x1, Pallas kernels, second_inner(): pl.pallas_call(functools.partial(_second_kernel, 4), grid=(blocks - 2,),...  10.8 us
    pallas_call x1, Pallas kernels, second_edges(): pl.pallas_call(_edge_kernel, grid=(2,), in_specs=win * 2 + edge * 4 + _ma...  10.7 us
    ppermute x3, starting transfers between devices, ring_gather(): bwd = lax.ppermute(bwd, 'probe', behind)  10.5 us
    pallas_call x1, Pallas kernels, slopes_of(): pl.pallas_call(functools.partial(_slope_kernel, (rows_in - rows) // 2), g...  10.3 us
    pallas_call x1, Pallas kernels, apply_op(): pl.pallas_call(functools.partial(_op_kernel, (with_prev, with_img, want_i...  9.89 us
  transfers between devices with their start and end apart: 13, of which 8 were waited for; matrix products, arithmetic and copies ran while one was open for 3% of the time, Pallas kernels for 19%

profile of v8, /device:TPU:6, one launch (start us, length us, event | category | flops | bytes accessed | tf_op | source)
XLA Modules:
  0.0 163.0 jit_solution(18175506876696660017)
XLA Ops:
  1.4 1.1 slice_bitcast_fusion.1
  2.5 1.1 fusion.5
  3.6 5.2 %collective-permute-start.1 = (f32[4,264,128]{2,1,0:T(8,128)S(1)}, f32[4,264,128]{2,1,0:T(8,128)S(1)}, u32[]{:S(2)}, u32[]{:S(2)}) collective-permute-start(f32[4,264,128]{2,1,0:T(8,128)S(1)} %pad_maximum_fusion.5), channel_id=1, source_target_pairs={{1,0},{2,1},{3,2},{4,3},{5,4},{6,5},{7,6},{8,7},{9,8},{10,9},{11,1... | collective-permute-start | bytes 1622024 | tf_op jit(solution)/shard_map/ppermute | solution.py:39
  8.9 1.9 %collective-permute-start = (f32[4,264,128]{2,1,0:T(8,128)S(1)}, f32[4,264,128]{2,1,0:T(8,128)S(1)}, u32[]{:S(2)}, u32[]{:S(2)}) collective-permute-start(f32[4,264,128]{2,1,0:T(8,128)S(1)} %pad_maximum_fusion.4), channel_id=1, source_target_pairs={{0,1},{1,2},{2,3},{3,4},{4,5},{5,6},{6,7},{7,8},{8,9},{9,10},{10,1... | collective-permute-start | bytes 1622024 | tf_op jit(solution)/shard_map/ppermute | solution.py:38
  10.8 4.9 %collective-permute-done.1 = f32[4,264,128]{2,1,0:T(8,128)S(1)} collective-permute-done((f32[4,264,128]{2,1,0:T(8,128)S(1)}, f32[4,264,128]{2,1,0:T(8,128)S(1)}, u32[]{:S(2)}, u32[]{:S(2)}) %collective-permute-start.1) | collective-permute-done | bytes 540704 | tf_op jit(solution)/shard_map/ppermute | solution.py:39
  15.7 7.5 %collective-permute-done = f32[4,264,128]{2,1,0:T(8,128)S(1)} collective-permute-done((f32[4,264,128]{2,1,0:T(8,128)S(1)}, f32[4,264,128]{2,1,0:T(8,128)S(1)}, u32[]{:S(2)}, u32[]{:S(2)}) %collective-permute-start) | collective-permute-done | bytes 540704 | tf_op jit(solution)/shard_map/ppermute | solution.py:38
  23.9 7.0 %collective-permute-done.2 = f32[72,8,128]{2,1,0:T(8,128)} collective-permute-done((f32[72,8,128]{2,1,0:T(8,128)}, f32[72,8,128]{2,1,0:T(8,128)}, u32[]{:S(2)}, u32[]{:S(2)}) %collective-permute-start.2) | collective-permute-done | bytes 294944 | tf_op jit(solution)/shard_map/ppermute | solution.py:53
  30.9 1.1 maximum_select_fusion
  32.0 2.0 %collective-permute-start.6 = (f32[72,16,128]{2,1,0:T(8,128)S(1)}, f32[72,16,128]{2,1,0:T(8,128)S(1)}, u32[]{:S(2)}, u32[]{:S(2)}) collective-permute-start(f32[72,16,128]{2,1,0:T(8,128)S(1)} %maximum_select_fusion), channel_id=1, source_target_pairs={{0,32},{16,48},{32,64},{48,80},{64,96},{80,112},{96,128},{112,144}... | collective-permute-start | bytes 1769480 | tf_op jit(solution)/shard_map/ppermute | solution.py:62
  34.0 4.0 %collective-permute-start.3 = (f32[72,16,128]{2,1,0:T(8,128)S(1)}, f32[72,16,128]{2,1,0:T(8,128)S(1)}, u32[]{:S(2)}, u32[]{:S(2)}) collective-permute-start(f32[72,16,128]{2,1,0:T(8,128)S(1)} %maximum_select_fusion), channel_id=1, source_target_pairs={{0,224},{16,240},{32,0},{48,16},{64,32},{80,48},{96,64},{112,80},{... | collective-permute-start | bytes 1769480 | tf_op jit(solution)/shard_map/ppermute | solution.py:63
  38.1 1.7 %pad_maximum_fusion.lo_ref.hi_ref = f32[40,128,128]{2,1,0:T(8,128)} fusion(f32[4,128,128]{2,1,0:T(8,128)S(1)} %get-tuple-element.39, f32[32,128,128]{2,1,0:T(8,128)S(1)} %copy-done, f32[4,128,128]{2,1,0:T(8,128)S(1)} %get-tuple-element.37), kind=kLoop, calls=%fused_computation | loop fusion | flops 1310720 | bytes 5242880 | tf_op jit(solution)/shard_map/concatenate | solution.py:44
  39.8 10.3 %shard_map.120 = (f32[32,128,128]{2,1,0:T(8,128)S(1)}, f32[32,128,128]{2,1,0:T(8,128)S(1)}, f32[32,128,128]{2,1,0:T(8,128)}) custom-call(f32[40,128,128]{2,1,0:T(8,128)} %pad_maximum_fusion.lo_ref.hi_ref, f32[40,128,128]{2,1,0:T(8,128)} %pad_maximum_fusion.lo_ref.hi_ref, f32[128,256]{1,0:T(8,128)S(1)} %copy-done.7, f32[256,128]{1,0:T(8,128)S(1)} %copy-done.6), custom_call_target="tpu_custom_call" | custom-call | tf_op jit(solution)/shard_map/pallas_call | solution.py:218
  50.1 2.0 %pad_maximum_fusion.1.refs_0_.refs_1_ = f32[40,128,128]{2,1,0:T(8,128)} fusion(f32[4,128,128]{2,1,0:T(8,128)S(1)} %get-tuple-element.38, f32[32,128,128]{2,1,0:T(8,128)S(1)} %bitcast.12, f32[4,128,128]{2,1,0:T(8,128)S(1)} %get-tuple-element.36), kind=kLoop, calls=%fused_computation.1 | loop fusion | flops 1310720 | bytes 5242880 | tf_op jit(solution)/shard_map/concatenate | solution.py:44
  52.9 9.9 %shard_map.121.part_ref = f32[32,128,128]{2,1,0:T(8,128)S(1)} custom-call(f32[40,128,128]{2,1,0:T(8,128)} %pad_maximum_fusion.1.refs_0_.refs_1_, f32[40,128,128]{2,1,0:T(8,128)} %pad_maximum_fusion.1.refs_0_.refs_1_, f32[32,128,128]{2,1,0:T(8,128)S(1)} %copy-done, f32[32,128,128]{2,1,0:T(8,128)} %copy-done.3, f32[32,128,128]{2,1,0:T(8,128)} %copy-done.4, ...), custom_call_target="tpu_custom_call" | custom-call | tf_op jit(solution)/shard_map/pallas_call | solution.py:246
  63.0 3.2 %collective-permute-start.4 = (f32[72,16,128]{2,1,0:T(8,128)S(1)}, f32[72,16,128]{2,1,0:T(8,128)S(1)}, u32[]{:S(2)}, u32[]{:S(2)}) collective-permute-start(f32[72,16,128]{2,1,0:T(8,128)S(1)} %collective-permute-done.3), channel_id=1, source_target_pairs={{0,224},{16,240},{32,0},{48,16},{64,32},{80,48},{96,64},{112,80},{... | collective-permute-start | bytes 1769480 | tf_op jit(solution)/shard_map/ppermute | solution.py:63
  66.9 13.5 %collective-permute-done.7 = f32[72,16,128]{2,1,0:T(8,128)S(1)} collective-permute-done((f32[72,16,128]{2,1,0:T(8,128)S(1)}, f32[72,16,128]{2,1,0:T(8,128)S(1)}, u32[]{:S(2)}, u32[]{:S(2)}) %collective-permute-start.7) | collective-permute-done | bytes 589856 | tf_op jit(solution)/shard_map/ppermute | solution.py:62
  80.3 3.2 %collective-permute-start.5 = (f32[72,16,128]{2,1,0:T(8,128)S(1)}, f32[72,16,128]{2,1,0:T(8,128)S(1)}, u32[]{:S(2)}, u32[]{:S(2)}) collective-permute-start(f32[72,16,128]{2,1,0:T(8,128)S(1)} %collective-permute-done.4), channel_id=1, source_target_pairs={{0,224},{16,240},{32,0},{48,16},{64,32},{80,48},{96,64},{112,80},{... | collective-permute-start | bytes 1769480 | tf_op jit(solution)/shard_map/ppermute | solution.py:63
  83.7 10.2 %collective-permute-done.8 = f32[72,16,128]{2,1,0:T(8,128)S(1)} collective-permute-done((f32[72,16,128]{2,1,0:T(8,128)S(1)}, f32[72,16,128]{2,1,0:T(8,128)S(1)}, u32[]{:S(2)}, u32[]{:S(2)}) %collective-permute-start.8) | collective-permute-done | bytes 589856 | tf_op jit(solution)/shard_map/ppermute | solution.py:62
  94.0 3.5 %collective-permute-start.10 = (f32[36,16,128]{2,1,0:T(8,128)S(1)}, f32[36,16,128]{2,1,0:T(8,128)S(1)}, u32[]{:S(2)}, u32[]{:S(2)}) collective-permute-start(f32[36,16,128]{2,1,0:T(8,128)S(1)} %slice.183), channel_id=1, source_target_pairs={{0,224},{16,240},{32,0},{48,16},{64,32},{80,48},{96,64},{112,80},{... | collective-permute-start | bytes 884744 | tf_op jit(solution)/shard_map/ppermute | solution.py:68
  97.5 4.2 %collective-permute-done.10 = f32[36,16,128]{2,1,0:T(8,128)S(1)} collective-permute-done((f32[36,16,128]{2,1,0:T(8,128)S(1)}, f32[36,16,128]{2,1,0:T(8,128)S(1)}, u32[]{:S(2)}, u32[]{:S(2)}) %collective-permute-start.10) | collective-permute-done | bytes 294944 | tf_op jit(solution)/shard_map/ppermute | solution.py:68
  102.1 1.3 copy-done.11
  104.2 11.7 %shard_map.122 = (f32[32,128,128]{2,1,0:T(8,128)S(1)}, f32[32,128,128]{2,1,0:T(8,128)}) custom-call(f32[40,128,128]{2,1,0:T(8,128)} %copy-done.9, f32[40,128,128]{2,1,0:T(8,128)} %copy-done.9, f32[32,128,128]{2,1,0:T(8,128)S(1)} %copy-done, f32[32,128,128]{2,1,0:T(8,128)} %copy-done.3, f32[32,128,128]{2,1,0:T(8,128)} %copy-done.4, ...), custom_call_target="tpu_custom_call" | custom-call | tf_op jit(solution)/shard_map/pallas_call | solution.py:262
  116.0 1.1 fusion.2
  117.1 1.3 copy-done.1
  119.3 3.1 %collective-permute-start.12 = (f32[4,256,128]{2,1,0:T(8,128)}, f32[4,256,128]{2,1,0:T(8,128)S(1)}, u32[]{:S(2)}, u32[]{:S(2)}) collective-permute-start(f32[4,256,128]{2,1,0:T(8,128)} %pad_maximum_fusion.7), channel_id=1, source_target_pairs={{1,0},{2,1},{3,2},{4,3},{5,4},{6,5},{7,6},{8,7},{9,8},{10,9},{11,1... | collective-permute-start | bytes 1572872 | tf_op jit(solution)/shard_map/ppermute | solution.py:322
  122.3 1.6 copy-done.2
  123.9 10.8 %shard_map.123 = (f32[32,128,128]{2,1,0:T(8,128)S(1)}, f32[32,128,128]{2,1,0:T(8,128)}) custom-call(f32[32,128,128]{2,1,0:T(8,128)S(1)} %copy-done.2, f32[32,128,128]{2,1,0:T(8,128)S(1)} %copy-done.2, f32[32,128,128]{2,1,0:T(8,128)S(1)} %copy-done.2, f32[32,128,128]{2,1,0:T(8,128)S(1)} %copy-done.2, ...), custom_call_target="tpu_custom_call" | custom-call | tf_op jit(solution)/shard_map/pallas_call | solution.py:281
  134.8 1.9 %collective-permute-start.11 = (f32[4,256,128]{2,1,0:T(8,128)S(1)}, f32[4,256,128]{2,1,0:T(8,128)S(1)}, u32[]{:S(2)}, u32[]{:S(2)}) collective-permute-start(f32[4,256,128]{2,1,0:T(8,128)S(1)} %pad_maximum_fusion.6), channel_id=1, source_target_pairs={{0,1},{1,2},{2,3},{3,4},{4,5},{5,6},{6,7},{7,8},{8,9},{9,10},{10,1... | collective-permute-start | bytes 1572872 | tf_op jit(solution)/shard_map/ppermute | solution.py:321
  137.1 11.8 %collective-permute-done.11 = f32[4,256,128]{2,1,0:T(8,128)S(1)} collective-permute-done((f32[4,256,128]{2,1,0:T(8,128)S(1)}, f32[4,256,128]{2,1,0:T(8,128)S(1)}, u32[]{:S(2)}, u32[]{:S(2)}) %collective-permute-start.11) | collective-permute-done | bytes 524320 | tf_op jit(solution)/shard_map/ppermute | solution.py:321
  148.9 1.5 pad_maximum_fusion.3.refs_2_.refs_3_
  150.7 10.7 %shard_map.124 = (f32[32,128,128]{2,1,0:T(8,128)S(1)}, f32[32,128,128]{2,1,0:T(8,128)}) custom-call(f32[32,128,128]{2,1,0:T(8,128)S(1)} %pad_maximum_fusion.2.refs_0_.refs_1_, f32[32,128,128]{2,1,0:T(8,128)S(1)} %pad_maximum_fusion.2.refs_0_.refs_1_, ...), custom_call_target="tpu_custom_call", output_to_operand_aliasing={{0}: (13, {}), {1}: (14, {})} | custom-call | tf_op jit(solution)/shard_map/pallas_call | solution.py:304
  161.3 1.7 %multiply_add_fusion = (f32[32,8,128]{2,1,0:T(8,128)}, f32[32,8,128]{2,1,0:T(8,128)}) fusion(f32[32,128,128]{2,1,0:T(8,128)S(1)} %get-tuple-element.20, s32[]{:T(128)S(6)} %select_n.124, f32[32,128,128]{2,1,0:T(8,128)} %refs_10_.1, f32[32,8,128]{2,1,0:T(8,128)S(1)} %copy-done.12, f32[32,128,128]{2,1,0:T(8,128)} %copy-done.1), kind=kLoop, calls=%fused_computation.29 | loop fusion | flops 131072 | bytes 786436 | tf_op jit(solution)/shard_map/add | solution.py:376
  (69 shorter events, 6.2 us)
Async XLA Ops:
  1.4 21.8 %copy-start.12 = (f32[32,8,128]{2,1,0:T(8,128)S(1)}, f32[32,8,128]{2,1,0:T(8,128)}, u32[]{:S(2)}) copy-start(f32[32,8,128]{2,1,0:T(8,128)} %param.10) | copy-start | bytes 393220
  1.4 21.8 %copy-start.13 = (f32[32,8,128]{2,1,0:T(8,128)S(1)}, f32[32,8,128]{2,1,0:T(8,128)}, u32[]{:S(2)}) copy-start(f32[32,8,128]{2,1,0:T(8,128)} %param.9) | copy-start | bytes 393220
  3.6 12.1 %collective-permute-start.1 = (f32[4,264,128]{2,1,0:T(8,128)S(1)}, f32[4,264,128]{2,1,0:T(8,128)S(1)}, u32[]{:S(2)}, u32[]{:S(2)}) collective-permute-start(f32[4,264,128]{2,1,0:T(8,128)S(1)} %pad_maximum_fusion.5), channel_id=1, source_target_pairs={{1,0},{2,1},{3,2},{4,3},{5,4},{6,5},{7,6},{8,7},{9,8},{10,9},{11,1... | collective-permute-start | bytes 1622024 | tf_op jit(solution)/shard_map/ppermute | solution.py:39
  8.9 14.3 %collective-permute-start = (f32[4,264,128]{2,1,0:T(8,128)S(1)}, f32[4,264,128]{2,1,0:T(8,128)S(1)}, u32[]{:S(2)}, u32[]{:S(2)}) collective-permute-start(f32[4,264,128]{2,1,0:T(8,128)S(1)} %pad_maximum_fusion.4), channel_id=1, source_target_pairs={{0,1},{1,2},{2,3},{3,4},{4,5},{5,6},{6,7},{7,8},{8,9},{9,10},{10,1... | collective-permute-start | bytes 1622024 | tf_op jit(solution)/shard_map/ppermute | solution.py:38
  15.7 22.4 %copy-start = (f32[32,128,128]{2,1,0:T(8,128)S(1)}, f32[32,128,128]{2,1,0:T(8,128)}, u32[]{:S(2)}) copy-start(f32[32,128,128]{2,1,0:T(8,128)} %refs_4_.1) | copy-start | bytes 6291460
  23.9 7.0 %collective-permute-start.2 = (f32[72,8,128]{2,1,0:T(8,128)}, f32[72,8,128]{2,1,0:T(8,128)}, u32[]{:S(2)}, u32[]{:S(2)}) collective-permute-start(f32[72,8,128]{2,1,0:T(8,128)} %pad_maximum_fusion.9), channel_id=1, source_target_pairs={{0,16},{16,0},{32,48},{48,32},{64,80},{80,64},{96,112},{112,96},{1... | collective-permute-start | bytes 884744 | tf_op jit(solution)/shard_map/ppermute | solution.py:53
  32.0 30.8 %collective-permute-start.6 = (f32[72,16,128]{2,1,0:T(8,128)S(1)}, f32[72,16,128]{2,1,0:T(8,128)S(1)}, u32[]{:S(2)}, u32[]{:S(2)}) collective-permute-start(f32[72,16,128]{2,1,0:T(8,128)S(1)} %maximum_select_fusion), channel_id=1, source_target_pairs={{0,32},{16,48},{32,64},{48,80},{64,96},{80,112},{96,128},{112,144}... | collective-permute-start | bytes 1769480 | tf_op jit(solution)/shard_map/ppermute | solution.py:62
  34.0 28.9 %collective-permute-start.3 = (f32[72,16,128]{2,1,0:T(8,128)S(1)}, f32[72,16,128]{2,1,0:T(8,128)S(1)}, u32[]{:S(2)}, u32[]{:S(2)}) collective-permute-start(f32[72,16,128]{2,1,0:T(8,128)S(1)} %maximum_select_fusion), channel_id=1, source_target_pairs={{0,224},{16,240},{32,0},{48,16},{64,32},{80,48},{96,64},{112,80},{... | collective-permute-start | bytes 1769480 | tf_op jit(solution)/shard_map/ppermute | solution.py:63
  38.1 1.7 %copy-start.6 = (f32[256,128]{1,0:T(8,128)S(1)}, f32[256,128]{1,0:T(8,128)}, u32[]{:S(2)}) copy-start(f32[256,128]{1,0:T(8,128)} %constant.108.clone.msub_ref.refs_7_.refs_13_.refs_9_) | copy-start | bytes 393220
  38.1 1.7 %copy-start.7 = (f32[128,256]{1,0:T(8,128)S(1)}, f32[128,256]{1,0:T(8,128)}, u32[]{:S(2)}) copy-start(f32[128,256]{1,0:T(8,128)} %constant.107.clone.mlane_ref.refs_6_.refs_12_.refs_8_) | copy-start | bytes 393220
  39.8 10.3 %copy-start.10 = (f32[1,32,128,128]{3,2,1,0:T(8,128)S(1)}, f32[1,32,128,128]{3,2,1,0:T(8,128)}, u32[]{:S(2)}) copy-start(f32[1,32,128,128]{3,2,1,0:T(8,128)} %param.15) | copy-start | bytes 6291460
  50.1 2.1 %copy-start.3 = (f32[32,128,128]{2,1,0:T(8,128)}, f32[32,128,128]{2,1,0:T(8,128)S(1)}, u32[]{:S(2)}) copy-start(f32[32,128,128]{2,1,0:T(8,128)S(1)} %get-tuple-element.13.refs_3_.g0_ref.refs_9_.refs_5_) | copy-start | bytes 6291460
  50.1 2.8 %copy-start.4 = (f32[32,128,128]{2,1,0:T(8,128)}, f32[32,128,128]{2,1,0:T(8,128)S(1)}, u32[]{:S(2)}) copy-start(f32[32,128,128]{2,1,0:T(8,128)S(1)} %get-tuple-element.14.refs_4_.g1_ref.refs_10_.refs_6_) | copy-start | bytes 6291460
  62.8 3.9 %copy-start.5 = (f32[32,128,128]{2,1,0:T(8,128)}, f32[32,128,128]{2,1,0:T(8,128)S(1)}, u32[]{:S(2)}) copy-start(f32[32,128,128]{2,1,0:T(8,128)S(1)} %shard_map.121.part_ref) | copy-start | bytes 6291460
  62.9 17.4 %collective-permute-start.7 = (f32[72,16,128]{2,1,0:T(8,128)S(1)}, f32[72,16,128]{2,1,0:T(8,128)S(1)}, u32[]{:S(2)}, u32[]{:S(2)}) collective-permute-start(f32[72,16,128]{2,1,0:T(8,128)S(1)} %collective-permute-done.6), channel_id=1, source_target_pairs={{0,32},{16,48},{32,64},{48,80},{64,96},{80,112},{96,128},{112,144}... | collective-permute-start | bytes 1769480 | tf_op jit(solution)/shard_map/ppermute | solution.py:62
  63.0 17.4 %collective-permute-start.4 = (f32[72,16,128]{2,1,0:T(8,128)S(1)}, f32[72,16,128]{2,1,0:T(8,128)S(1)}, u32[]{:S(2)}, u32[]{:S(2)}) collective-permute-start(f32[72,16,128]{2,1,0:T(8,128)S(1)} %collective-permute-done.3), channel_id=1, source_target_pairs={{0,224},{16,240},{32,0},{48,16},{64,32},{80,48},{96,64},{112,80},{... | collective-permute-start | bytes 1769480 | tf_op jit(solution)/shard_map/ppermute | solution.py:63
  80.3 13.5 %collective-permute-start.8 = (f32[72,16,128]{2,1,0:T(8,128)S(1)}, f32[72,16,128]{2,1,0:T(8,128)S(1)}, u32[]{:S(2)}, u32[]{:S(2)}) collective-permute-start(f32[72,16,128]{2,1,0:T(8,128)S(1)} %collective-permute-done.7), channel_id=1, source_target_pairs={{0,32},{16,48},{32,64},{48,80},{64,96},{80,112},{96,128},{112,144}... | collective-permute-start | bytes 1769480 | tf_op jit(solution)/shard_map/ppermute | solution.py:62
  80.3 13.6 %collective-permute-start.5 = (f32[72,16,128]{2,1,0:T(8,128)S(1)}, f32[72,16,128]{2,1,0:T(8,128)S(1)}, u32[]{:S(2)}, u32[]{:S(2)}) collective-permute-start(f32[72,16,128]{2,1,0:T(8,128)S(1)} %collective-permute-done.4), channel_id=1, source_target_pairs={{0,224},{16,240},{32,0},{48,16},{64,32},{80,48},{96,64},{112,80},{... | collective-permute-start | bytes 1769480 | tf_op jit(solution)/shard_map/ppermute | solution.py:63
  93.8 8.0 %collective-permute-start.9 = (f32[36,16,128]{2,1,0:T(8,128)S(1)}, f32[36,16,128]{2,1,0:T(8,128)S(1)}, u32[]{:S(2)}, u32[]{:S(2)}) collective-permute-start(f32[36,16,128]{2,1,0:T(8,128)S(1)} %slice.182), channel_id=1, source_target_pairs={{0,32},{16,48},{32,64},{48,80},{64,96},{80,112},{96,128},{112,144}... | collective-permute-start | bytes 884744 | tf_op jit(solution)/shard_map/ppermute | solution.py:68
  94.0 7.7 %collective-permute-start.10 = (f32[36,16,128]{2,1,0:T(8,128)S(1)}, f32[36,16,128]{2,1,0:T(8,128)S(1)}, u32[]{:S(2)}, u32[]{:S(2)}) collective-permute-start(f32[36,16,128]{2,1,0:T(8,128)S(1)} %slice.183), channel_id=1, source_target_pairs={{0,224},{16,240},{32,0},{48,16},{64,32},{80,48},{96,64},{112,80},{... | collective-permute-start | bytes 884744 | tf_op jit(solution)/shard_map/ppermute | solution.py:68
  102.0 1.3 copy-start.11
  102.1 2.1 %copy-start.9 = (f32[40,128,128]{2,1,0:T(8,128)}, f32[40,128,128]{2,1,0:T(8,128)S(1)}, u32[]{:S(2)}) copy-start(f32[40,128,128]{2,1,0:T(8,128)S(1)} %slice_dynamic-update-slice_fusion.lo_ref.hi_ref) | copy-start | bytes 7864324
  117.1 1.4 copy-start.1
  119.3 17.8 %collective-permute-start.12 = (f32[4,256,128]{2,1,0:T(8,128)}, f32[4,256,128]{2,1,0:T(8,128)S(1)}, u32[]{:S(2)}, u32[]{:S(2)}) collective-permute-start(f32[4,256,128]{2,1,0:T(8,128)} %pad_maximum_fusion.7), channel_id=1, source_target_pairs={{1,0},{2,1},{3,2},{4,3},{5,4},{6,5},{7,6},{8,7},{9,8},{10,9},{11,1... | collective-permute-start | bytes 1572872 | tf_op jit(solution)/shard_map/ppermute | solution.py:322
  122.3 1.6 copy-start.2
  123.9 12.8 %copy-start.8 = (f32[32,128,128]{2,1,0:T(8,128)S(1)}, f32[32,128,128]{2,1,0:T(8,128)}, u32[]{:S(2)}) copy-start(f32[32,128,128]{2,1,0:T(8,128)} %get-tuple-element.17.refs_4_.refs_5_.refs_6_.refs_7_) | copy-start | bytes 6291460
  134.8 14.1 %collective-permute-start.11 = (f32[4,256,128]{2,1,0:T(8,128)S(1)}, f32[4,256,128]{2,1,0:T(8,128)S(1)}, u32[]{:S(2)}, u32[]{:S(2)}) collective-permute-start(f32[4,256,128]{2,1,0:T(8,128)S(1)} %pad_maximum_fusion.6), channel_id=1, source_target_pairs={{0,1},{1,2},{2,3},{3,4},{4,5},{5,6},{6,7},{7,8},{8,9},{9,10},{10,1... | collective-permute-start | bytes 1572872 | tf_op jit(solution)/shard_map/ppermute | solution.py:321

commit v9 on v8

--- a/solution.py
+++ b/solution.py
@@ -180,7 +180,7 @@
     img_ref, born_ref = refs[-2:]
     rows = b_ref.shape[1]
     coef = (b_ref, g0_ref, g1_ref, g2_ref)
-    for j in range(BZ):
+    for j in range(b_ref.shape[0]):
         _, image = _image_of(win1, j, coef, mlane_ref, msub_ref, 0, rows)
         img_ref[j] = image
         centre, own = _image_of(win2, j, coef, mlane_ref, msub_ref, 0, rows)
@@ -270,35 +270,37 @@
     )(u_cur_ext, u_cur_ext, b, *slopes, mlane, msub, kappa, u_prev, partial, dk)
 
 
+QB = HALO
+
+
 def second_inner(bg, born, b, slopes, mlane, msub, kappa, prev, dk):
     depth = bg.shape[0]
     n = bg.shape[2]
-    q = HALO
-    blocks = depth // BZ
-    win = [pl.BlockSpec((q, n, n), lambda i, t=t: ((i + 1) * (BZ // q) - 1 + t, 0, 0)) for t in range(4)]
-    inner = [pl.BlockSpec((BZ, n, n), lambda i: (i + 1, 0, 0))]
+    blocks = depth // QB
+    win = [pl.BlockSpec((QB, n, n), lambda i, t=t: (i + t, 0, 0)) for t in range(3)]
+    inner = [pl.BlockSpec((QB, n, n), lambda i: (i + 1, 0, 0))]
     shape = jax.ShapeDtypeStruct((depth, n, n), jnp.float32)
     return pl.pallas_call(
-        functools.partial(_second_kernel, 4),
+        functools.partial(_second_kernel, 3),
         grid=(blocks - 2,),
         in_specs=win * 2 + inner * 4 + _mat_specs(mlane, msub) + inner * 3,
         out_specs=inner * 2,
         out_shape=[shape] * 2,
         compiler_params=PARAMS,
         interpret=INTERPRET,
-    )(*([bg] * 4), *([born] * 4), b, *slopes, mlane, msub, kappa, prev, dk)
+    )(*([bg] * 3), *([born] * 3), b, *slopes, mlane, msub, kappa, prev, dk)
 
 
 def _edge_kernel(*refs):
-    _second_kernel(2, *refs[:-4], *refs[-2:])
+    _second_kernel(3, *refs[:-4], *refs[-2:])
 
 
 def second_edges(bg_rim, born_rim, b, slopes, mlane, msub, kappa, prev, dk, img, born_out):
     depth = b.shape[0]
     n = b.shape[2]
-    last = depth // BZ - 1
-    win = [pl.BlockSpec((BZ, n, n), lambda i, t=t: (2 * i + t, 0, 0)) for t in range(2)]
-    edge = [pl.BlockSpec((BZ, n, n), lambda i: (i * last, 0, 0))]
+    last = depth // QB - 1
+    win = [pl.BlockSpec((QB, n, n), lambda i, t=t: (3 * i + t, 0, 0)) for t in range(3)]
+    edge = [pl.BlockSpec((QB, n, n), lambda i: (i * last, 0, 0))]
     anyspec = [pl.BlockSpec(memory_space=pl.ANY)]
     shape = jax.ShapeDtypeStruct((depth, n, n), jnp.float32)
     return pl.pallas_call(
@@ -307,10 +309,10 @@
         in_specs=win * 2 + edge * 4 + _mat_specs(mlane, msub) + edge * 3 + anyspec * 2,
         out_specs=edge * 2,
         out_shape=[shape] * 2,
-        input_output_aliases={13: 0, 14: 1},
+        input_output_aliases={15: 0, 16: 1},
         compiler_params=PARAMS,
         interpret=INTERPRET,
-    )(bg_rim, bg_rim, born_rim, born_rim, b, *slopes, mlane, msub, kappa, prev, dk, img, born_out)
+    )(*([bg_rim] * 3), *([born_rim] * 3), b, *slopes, mlane, msub, kappa, prev, dk, img, born_out)
 
 
 def depth_rims(fields):
@@ -322,7 +324,7 @@
     below = lax.ppermute(heads, "slab", [(i + 1, i) for i in range(ends)])
     outs = []
     at = 0
-    span = BZ + HALO
+    span = QB + HALO
     for f in fields:
         w = f.shape[1]
         d = f.shape[0]
@@ -341,15 +343,16 @@
     msub = jnp.asarray(np.concatenate([ms, mg], axis=0))
 
     depth = u_cur.shape[0]
-    cur_rows = depth + 2 * HALO
     probe_kappa = dkappa[0]
     older = du_prev[0]
     newer = du_cur[0]
     u_cur_strip_ext, buoyancy_ext, newer_ext = halo_depth_many([u_cur, buoyancy, newer])
-    u_cur_ext, u_prev_all = ring_gather(
-        jnp.concatenate([u_cur_strip_ext, u_prev], axis=0),
-        ((0, cur_rows), (cur_rows, cur_rows + depth)),
-    )
+    rims = jnp.concatenate([u_cur_strip_ext[:HALO], u_cur_strip_ext[depth + HALO:]], axis=0)
+    rims_all = lax.all_gather(rims, "probe", axis=1, tiled=True)
+    u_cur_all, u_prev_all = ring_gather(
+        jnp.concatenate([u_cur, u_prev], axis=0), ((0, depth), (depth, 2 * depth))
+    )
+    u_cur_ext = jnp.concatenate([rims_all[:HALO], u_cur_all, rims_all[HALO:]], axis=0)
 
     slopes = slopes_of(buoyancy_ext, mlane, msub)
 

time: 163 us -> 178 us (1.092)
  blocking collectives: 0 us -> 37.5 us
  waiting for transfers between devices: 59 us -> 32.5 us
  local copies, waits for them, and re-layouts: 11.4 us -> 16.2 us
    all_gather x0 -> x1, blocking collectives: none -> 37.5 us  [local_body(): rims_all = lax.all_gather(rims, 'probe', axis=1, tiled=True)]
    ppermute x3, waiting for transfers between devices: 23.6 us -> 13.2 us  [ring_gather(): fwd = lax.ppermute(fwd, 'probe', ahead)]
    ppermute x1, waiting for transfers between devices: 7.48 us -> 0.01 us  [halo_depth_many(): above = lax.ppermute(tails, 'slab', [(i, i + 1) for i in range(ends)])]
    ppermute x1, waiting for transfers between devices: 4.88 us -> 0.01 us  [halo_depth_many(): below = lax.ppermute(heads, 'slab', [(i + 1, i) for i in range(ends)])]
    pallas_call x1, Pallas kernels: 10.7 us -> 6.08 us  [second_edges(): pl.pallas_call(_edge_kernel, grid=(2,), in_specs=win * 2 + edge * 4 + _ma...]
    ppermute x1, waiting for transfers between devices: 4.17 us -> 0.01 us  [ring_gather(): lax.ppermute(bwd[cut:], 'probe', behind)]
    pallas_call x1, Pallas kernels: 10.8 us -> 14.5 us  [second_inner(): pl.pallas_call(functools.partial(_second_kernel, 3), grid=(blocks - 2,),...]
    ppermute x3, starting transfers between devices: 10.5 us -> 13.3 us  [ring_gather(): bwd = lax.ppermute(bwd, 'probe', behind)]
  transfers between devices with their start and end apart: 13 -> 13, of which waited for: 8 -> 7; matrix products, arithmetic and copies ran while one was open for 3% -> 6% of each run, Pallas kernels for 19% -> 19%
where the time goes in v9:
time: 178 us
  Pallas kernels  52.4 us (29%)
  blocking collectives  37.5 us (21%)
  waiting for transfers between devices  32.5 us (18%)
  starting transfers between devices  28.6 us (16%)
  local copies, waits for them, and re-layouts  16.2 us (9%)
  other arithmetic  9.35 us (5%)
    all_gather x1, blocking collectives, local_body(): rims_all = lax.all_gather(rims, 'probe', axis=1, tiled=True)  37.5 us
    pallas_call x1, Pallas kernels, second_inner(): pl.pallas_call(functools.partial(_second_kernel, 3), grid=(blocks - 2,),...  14.5 us
    ppermute x3, starting transfers between devices, ring_gather(): bwd = lax.ppermute(bwd, 'probe', behind)  13.3 us
    ppermute x3, waiting for transfers between devices, ring_gather(): fwd = lax.ppermute(fwd, 'probe', ahead)  13.2 us
    pallas_call x1, Pallas kernels, first_step(): pl.pallas_call(_first_kernel, grid=(depth // BZ,), in_specs=_ext_specs(n,...  11.7 us
    ppermute x1, waiting for transfers between devices, depth_rims(): above = lax.ppermute(tails, 'slab', [(i, i + 1) for i in range(ends)])  11.4 us
    pallas_call x1, Pallas kernels, slopes_of(): pl.pallas_call(functools.partial(_slope_kernel, (rows_in - rows) // 2), g...  10.2 us
    pallas_call x1, Pallas kernels, apply_op(): pl.pallas_call(functools.partial(_op_kernel, (with_prev, with_img, want_i...  9.89 us
  transfers between devices with their start and end apart: 13, of which 7 were waited for; matrix products, arithmetic and copies ran while one was open for 6% of the time, Pallas kernels for 19%

profile of v9, /device:TPU:6, one launch (start us, length us, event | category | flops | bytes accessed | tf_op | source)
XLA Modules:
  0.0 177.7 jit_solution(6396974838383296675)
XLA Ops:
  3.5 1.1 slice_bitcast_fusion.1
  4.5 1.1 fusion.4
  5.6 5.1 %collective-permute-done.2 = f32[64,8,128]{2,1,0:T(8,128)S(1)} collective-permute-done((f32[64,8,128]{2,1,0:T(8,128)S(1)}, f32[64,8,128]{2,1,0:T(8,128)S(1)}, u32[]{:S(2)}, u32[]{:S(2)}) %collective-permute-start.2) | collective-permute-done | bytes 262176 | tf_op jit(solution)/shard_map/ppermute | solution.py:53
  10.7 5.9 %collective-permute-start.3 = (f32[64,16,128]{2,1,0:T(8,128)S(1)}, f32[64,16,128]{2,1,0:T(8,128)}, u32[]{:S(2)}, u32[]{:S(2)}) collective-permute-start(f32[64,16,128]{2,1,0:T(8,128)S(1)} %maximum_select_fusion), channel_id=1, source_target_pairs={{0,224},{16,240},{32,0},{48,16},{64,32},{80,48},{96,64},{112,80},{... | collective-permute-start | bytes 1572872 | tf_op jit(solution)/shard_map/ppermute | solution.py:63
  17.5 4.1 %collective-permute-start.1 = (f32[4,264,128]{2,1,0:T(8,128)}, f32[4,264,128]{2,1,0:T(8,128)S(1)}, u32[]{:S(2)}, u32[]{:S(2)}) collective-permute-start(f32[4,264,128]{2,1,0:T(8,128)} %pad_maximum_fusion.6), channel_id=1, source_target_pairs={{1,0},{2,1},{3,2},{4,3},{5,4},{6,5},{7,6},{8,7},{9,8},{10,9},{11,1... | collective-permute-start | bytes 1622024 | tf_op jit(solution)/shard_map/ppermute | solution.py:39
  22.4 1.9 %collective-permute-start = (f32[4,264,128]{2,1,0:T(8,128)}, f32[4,264,128]{2,1,0:T(8,128)}, u32[]{:S(2)}, u32[]{:S(2)}) collective-permute-start(f32[4,264,128]{2,1,0:T(8,128)} %pad_maximum_fusion.5), channel_id=1, source_target_pairs={{0,1},{1,2},{2,3},{3,4},{4,5},{5,6},{6,7},{7,8},{8,9},{9,10},{10,1... | collective-permute-start | bytes 1622024 | tf_op jit(solution)/shard_map/ppermute | solution.py:38
  24.9 2.1 %collective-permute-done.3 = f32[64,16,128]{2,1,0:T(8,128)} collective-permute-done((f32[64,16,128]{2,1,0:T(8,128)S(1)}, f32[64,16,128]{2,1,0:T(8,128)}, u32[]{:S(2)}, u32[]{:S(2)}) %collective-permute-start.3) | collective-permute-done | bytes 524320 | tf_op jit(solution)/shard_map/ppermute | solution.py:63
  27.0 3.8 %collective-permute-start.4 = (f32[64,16,128]{2,1,0:T(8,128)}, f32[64,16,128]{2,1,0:T(8,128)S(1)}, u32[]{:S(2)}, u32[]{:S(2)}) collective-permute-start(f32[64,16,128]{2,1,0:T(8,128)} %collective-permute-done.3), channel_id=1, source_target_pairs={{0,224},{16,240},{32,0},{48,16},{64,32},{80,48},{96,64},{112,80},{... | collective-permute-start | bytes 1572872 | tf_op jit(solution)/shard_map/ppermute | solution.py:63
  31.1 8.0 %collective-permute-done.6 = f32[64,16,128]{2,1,0:T(8,128)S(1)} collective-permute-done((f32[64,16,128]{2,1,0:T(8,128)S(1)}, f32[64,16,128]{2,1,0:T(8,128)S(1)}, u32[]{:S(2)}, u32[]{:S(2)}) %collective-permute-start.6) | collective-permute-done | bytes 524320 | tf_op jit(solution)/shard_map/ppermute | solution.py:62
  39.1 1.1 fusion.5
  40.6 3.6 %collective-permute-start.5 = (f32[64,16,128]{2,1,0:T(8,128)S(1)}, f32[64,16,128]{2,1,0:T(8,128)S(1)}, u32[]{:S(2)}, u32[]{:S(2)}) collective-permute-start(f32[64,16,128]{2,1,0:T(8,128)S(1)} %collective-permute-done.4), channel_id=1, source_target_pairs={{0,224},{16,240},{32,0},{48,16},{64,32},{80,48},{96,64},{112,80},{... | collective-permute-start | bytes 1572872 | tf_op jit(solution)/shard_map/ppermute | solution.py:63
  44.1 1.7 pad_maximum_fusion.1.lo_ref.hi_ref
  46.6 1.1 slice_dynamic-update-slice_fusion.4
  47.7 5.2 %collective-permute-done.7 = f32[64,16,128]{2,1,0:T(8,128)S(1)} collective-permute-done((f32[64,16,128]{2,1,0:T(8,128)S(1)}, f32[64,16,128]{2,1,0:T(8,128)S(1)}, u32[]{:S(2)}, u32[]{:S(2)}) %collective-permute-start.7) | collective-permute-done | bytes 524320 | tf_op jit(solution)/shard_map/ppermute | solution.py:62
  53.4 3.8 %collective-permute-start.10 = (f32[32,16,128]{2,1,0:T(8,128)S(1)}, f32[32,16,128]{2,1,0:T(8,128)S(1)}, u32[]{:S(2)}, u32[]{:S(2)}) collective-permute-start(f32[32,16,128]{2,1,0:T(8,128)S(1)} %get-tuple-element.50), channel_id=1, source_target_pairs={{0,224},{16,240},{32,0},{48,16},{64,32},{80,48},{96,64},{112,80},{... | collective-permute-start | bytes 786440 | tf_op jit(solution)/shard_map/ppermute | solution.py:68
  57.1 37.5 %all_gather.3 = f32[8,128,128]{2,1,0:T(8,128)S(1)} all-gather(f32[8,8,128]{2,1,0:T(8,128)S(1)} %pad_maximum_fusion.9), channel_id=1, replica_groups=mesh['probe'=16,'slab'=16] {'probe'}, dimensions={1}, use_global_device_ids=true | all-gather | bytes 557056 | tf_op jit(solution)/shard_map/all_gather | solution.py:351
  95.0 1.8 %pad_maximum_fusion.2.refs_0_.refs_1_ = f32[40,128,128]{2,1,0:T(8,128)} fusion(f32[4,128,128]{2,1,0:T(8,128)S(1)} %get-tuple-element.38, f32[32,128,128]{2,1,0:T(8,128)S(1)} %bitcast.12, f32[4,128,128]{2,1,0:T(8,128)S(1)} %get-tuple-element.36), kind=kLoop, calls=%fused_computation.2 | loop fusion | flops 1310720 | bytes 5242880 | tf_op jit(solution)/shard_map/concatenate | solution.py:44
  96.9 10.2 %shard_map.120 = (f32[32,128,128]{2,1,0:T(8,128)S(1)}, f32[32,128,128]{2,1,0:T(8,128)S(1)}, f32[32,128,128]{2,1,0:T(8,128)}) custom-call(f32[40,128,128]{2,1,0:T(8,128)} %pad_maximum_fusion.1.lo_ref.hi_ref, f32[40,128,128]{2,1,0:T(8,128)} %pad_maximum_fusion.1.lo_ref.hi_ref, f32[128,256]{1,0:T(8,128)S(1)} %copy-done.7, f32[256,128]{1,0:T(8,128)S(1)} %copy-done.6), custom_call_target="tpu_custom_call" | custom-call | tf_op jit(solution)/shard_map/pallas_call | solution.py:218
  107.1 1.3 copy-done.1
  108.4 1.4 copy-done.2
  109.8 9.9 %shard_map.121.part_ref = f32[32,128,128]{2,1,0:T(8,128)S(1)} custom-call(f32[40,128,128]{2,1,0:T(8,128)} %pad_maximum_fusion.2.refs_0_.refs_1_, f32[40,128,128]{2,1,0:T(8,128)} %pad_maximum_fusion.2.refs_0_.refs_1_, f32[32,128,128]{2,1,0:T(8,128)S(1)} %copy-done, f32[32,128,128]{2,1,0:T(8,128)} %copy-done.1, f32[32,128,128]{2,1,0:T(8,128)} %copy-done.2, ...), custom_call_target="tpu_custom_call" | custom-call | tf_op jit(solution)/shard_map/pallas_call | solution.py:246
  121.0 2.0 %pad_maximum_fusion.lo_ref.hi_ref = f32[40,128,128]{2,1,0:T(8,128)} fusion(f32[4,128,128]{2,1,0:T(8,128)S(1)} %get-tuple-element.58, f32[32,128,128]{2,1,0:T(8,128)S(1)} %get-tuple-element.45, f32[4,128,128]{2,1,0:T(8,128)S(1)} %get-tuple-element.57), kind=kLoop, calls=%fused_computation | loop fusion | flops 1310720 | bytes 5242880 | tf_op jit(solution)/shard_map/concatenate | solution.py:355
  123.2 11.7 %shard_map.122 = (f32[32,128,128]{2,1,0:T(8,128)S(1)}, f32[32,128,128]{2,1,0:T(8,128)}) custom-call(f32[40,128,128]{2,1,0:T(8,128)} %pad_maximum_fusion.lo_ref.hi_ref, f32[40,128,128]{2,1,0:T(8,128)} %pad_maximum_fusion.lo_ref.hi_ref, f32[32,128,128]{2,1,0:T(8,128)S(1)} %copy-done, f32[32,128,128]{2,1,0:T(8,128)} %copy-done.1, f32[32,128,128]{2,1,0:T(8,128)} %copy-done.2, ...), custom_call_target="tpu_custom_call" | custom-call | tf_op jit(solution)/shard_map/pallas_call | solution.py:262
  134.9 1.1 fusion.1
  136.0 1.4 copy-done.3
  137.5 1.9 %collective-permute-start.12 = (f32[4,256,128]{2,1,0:T(8,128)S(1)}, f32[4,256,128]{2,1,0:T(8,128)S(1)}, u32[]{:S(2)}, u32[]{:S(2)}) collective-permute-start(f32[4,256,128]{2,1,0:T(8,128)S(1)} %pad_maximum_fusion.8), channel_id=1, source_target_pairs={{1,0},{2,1},{3,2},{4,3},{5,4},{6,5},{7,6},{8,7},{9,8},{10,9},{11,1... | collective-permute-start | bytes 1572872 | tf_op jit(solution)/shard_map/ppermute | solution.py:324
  139.4 1.6 copy-done.4
  141.0 14.5 %shard_map.123 = (f32[32,128,128]{2,1,0:T(8,128)S(1)}, f32[32,128,128]{2,1,0:T(8,128)}) custom-call(f32[32,128,128]{2,1,0:T(8,128)S(1)} %copy-done.4, f32[32,128,128]{2,1,0:T(8,128)S(1)} %copy-done.4, f32[32,128,128]{2,1,0:T(8,128)S(1)} %copy-done.4, f32[32,128,128]{2,1,0:T(8,128)} %get-tuple-element.17.refs_3_.refs_4_.refs_5_, ...), custom_call_target="tpu_custom_call" | custom-call | tf_op jit(solution)/shard_map/pallas_call | solution.py:283
  155.5 2.4 %collective-permute-start.11 = (f32[4,256,128]{2,1,0:T(8,128)S(1)}, f32[4,256,128]{2,1,0:T(8,128)S(1)}, u32[]{:S(2)}, u32[]{:S(2)}) collective-permute-start(f32[4,256,128]{2,1,0:T(8,128)S(1)} %pad_maximum_fusion.7), channel_id=1, source_target_pairs={{0,1},{1,2},{2,3},{3,4},{4,5},{5,6},{6,7},{7,8},{8,9},{9,10},{10,1... | collective-permute-start | bytes 1572872 | tf_op jit(solution)/shard_map/ppermute | solution.py:323
  158.2 11.4 %collective-permute-done.11 = f32[4,256,128]{2,1,0:T(8,128)S(1)} collective-permute-done((f32[4,256,128]{2,1,0:T(8,128)S(1)}, f32[4,256,128]{2,1,0:T(8,128)S(1)}, u32[]{:S(2)}, u32[]{:S(2)}) %collective-permute-start.11) | collective-permute-done | bytes 524320 | tf_op jit(solution)/shard_map/ppermute | solution.py:323
  170.0 6.1 %shard_map.124 = (f32[32,128,128]{2,1,0:T(8,128)S(1)}, f32[32,128,128]{2,1,0:T(8,128)}) custom-call(f32[24,128,128]{2,1,0:T(8,128)S(1)} %pad_maximum_fusion.3.refs_0_.refs_1_.refs_2_, f32[24,128,128]{2,1,0:T(8,128)S(1)} %pad_maximum_fusion.3.refs_0_.refs_1_.refs_2_, ...), custom_call_target="tpu_custom_call", output_to_operand_aliasing={{0}: (15, {}), {1}: (16, {})} | custom-call | tf_op jit(solution)/shard_map/pallas_call | solution.py:306
  176.0 1.7 multiply_add_fusion
  (66 shorter events, 9.2 us)
Async XLA Ops:
  0.6 16.0 %copy-start.11 = (f32[32,8,128]{2,1,0:T(8,128)S(1)}, f32[32,8,128]{2,1,0:T(8,128)}, u32[]{:S(2)}) copy-start(f32[32,8,128]{2,1,0:T(8,128)} %param.10) | copy-start | bytes 393220
  2.5 8.1 %collective-permute-start.2 = (f32[64,8,128]{2,1,0:T(8,128)S(1)}, f32[64,8,128]{2,1,0:T(8,128)S(1)}, u32[]{:S(2)}, u32[]{:S(2)}) collective-permute-start(f32[64,8,128]{2,1,0:T(8,128)S(1)} %constant_dynamic-update-slice_fusion), channel_id=1, source_target_pairs={{0,16},{16,0},{32,48},{48,32},{64,80},{80,64},{96,112},{112,96},{1... | collective-permute-start | bytes 786440 | tf_op jit(solution)/shard_map/ppermute | solution.py:53
  10.7 16.3 %collective-permute-start.3 = (f32[64,16,128]{2,1,0:T(8,128)S(1)}, f32[64,16,128]{2,1,0:T(8,128)}, u32[]{:S(2)}, u32[]{:S(2)}) collective-permute-start(f32[64,16,128]{2,1,0:T(8,128)S(1)} %maximum_select_fusion), channel_id=1, source_target_pairs={{0,224},{16,240},{32,0},{48,16},{64,32},{80,48},{96,64},{112,80},{... | collective-permute-start | bytes 1572872 | tf_op jit(solution)/shard_map/ppermute | solution.py:63
  17.5 13.6 %collective-permute-start.1 = (f32[4,264,128]{2,1,0:T(8,128)}, f32[4,264,128]{2,1,0:T(8,128)S(1)}, u32[]{:S(2)}, u32[]{:S(2)}) collective-permute-start(f32[4,264,128]{2,1,0:T(8,128)} %pad_maximum_fusion.6), channel_id=1, source_target_pairs={{1,0},{2,1},{3,2},{4,3},{5,4},{6,5},{7,6},{8,7},{9,8},{10,9},{11,1... | collective-permute-start | bytes 1622024 | tf_op jit(solution)/shard_map/ppermute | solution.py:39
  22.4 16.8 %collective-permute-start = (f32[4,264,128]{2,1,0:T(8,128)}, f32[4,264,128]{2,1,0:T(8,128)}, u32[]{:S(2)}, u32[]{:S(2)}) collective-permute-start(f32[4,264,128]{2,1,0:T(8,128)} %pad_maximum_fusion.5), channel_id=1, source_target_pairs={{0,1},{1,2},{2,3},{3,4},{4,5},{5,6},{6,7},{7,8},{8,9},{9,10},{10,1... | collective-permute-start | bytes 1622024 | tf_op jit(solution)/shard_map/ppermute | solution.py:38
  24.5 14.6 %collective-permute-start.6 = (f32[64,16,128]{2,1,0:T(8,128)S(1)}, f32[64,16,128]{2,1,0:T(8,128)S(1)}, u32[]{:S(2)}, u32[]{:S(2)}) collective-permute-start(f32[64,16,128]{2,1,0:T(8,128)S(1)} %maximum_select_fusion), channel_id=1, source_target_pairs={{0,32},{16,48},{32,64},{48,80},{64,96},{80,112},{96,128},{112,144}... | collective-permute-start | bytes 1572872 | tf_op jit(solution)/shard_map/ppermute | solution.py:62
  24.9 19.3 %copy-start = (f32[32,128,128]{2,1,0:T(8,128)S(1)}, f32[32,128,128]{2,1,0:T(8,128)}, u32[]{:S(2)}) copy-start(f32[32,128,128]{2,1,0:T(8,128)} %refs_6_.4) | copy-start | bytes 6291460
  27.0 13.6 %collective-permute-start.4 = (f32[64,16,128]{2,1,0:T(8,128)}, f32[64,16,128]{2,1,0:T(8,128)S(1)}, u32[]{:S(2)}, u32[]{:S(2)}) collective-permute-start(f32[64,16,128]{2,1,0:T(8,128)} %collective-permute-done.3), channel_id=1, source_target_pairs={{0,224},{16,240},{32,0},{48,16},{64,32},{80,48},{96,64},{112,80},{... | collective-permute-start | bytes 1572872 | tf_op jit(solution)/shard_map/ppermute | solution.py:63
  31.1 14.8 %copy-start.12 = (f32[4,264,128]{2,1,0:T(8,128)}, f32[4,264,128]{2,1,0:T(8,128)S(1)}, u32[]{:S(2)}) copy-start(f32[4,264,128]{2,1,0:T(8,128)S(1)} %collective-permute-done.1) | copy-start | bytes 1622020
  39.1 13.7 %collective-permute-start.7 = (f32[64,16,128]{2,1,0:T(8,128)S(1)}, f32[64,16,128]{2,1,0:T(8,128)S(1)}, u32[]{:S(2)}, u32[]{:S(2)}) collective-permute-start(f32[64,16,128]{2,1,0:T(8,128)S(1)} %collective-permute-done.6), channel_id=1, source_target_pairs={{0,32},{16,48},{32,64},{48,80},{64,96},{80,112},{96,128},{112,144}... | collective-permute-start | bytes 1572872 | tf_op jit(solution)/shard_map/ppermute | solution.py:62
  40.6 12.7 %collective-permute-start.5 = (f32[64,16,128]{2,1,0:T(8,128)S(1)}, f32[64,16,128]{2,1,0:T(8,128)S(1)}, u32[]{:S(2)}, u32[]{:S(2)}) collective-permute-start(f32[64,16,128]{2,1,0:T(8,128)S(1)} %collective-permute-done.4), channel_id=1, source_target_pairs={{0,224},{16,240},{32,0},{48,16},{64,32},{80,48},{96,64},{112,80},{... | collective-permute-start | bytes 1572872 | tf_op jit(solution)/shard_map/ppermute | solution.py:63
  45.8 11.3 %slice-start = ((f32[4,264,128]{2,1,0:T(8,128)}), f32[4,8,128]{2,1,0:T(8,128)S(1)}, s32[]{:S(2)}) async-start(f32[4,264,128]{2,1,0:T(8,128)} %copy-done.12), calls=%async_computation | async-start | bytes 32768 | tf_op jit(solution)/shard_map/slice | solution.py:44
  52.8 41.8 %collective-permute-start.8 = (f32[64,16,128]{2,1,0:T(8,128)S(1)}, f32[64,16,128]{2,1,0:T(8,128)S(1)}, u32[]{:S(2)}, u32[]{:S(2)}) collective-permute-start(f32[64,16,128]{2,1,0:T(8,128)S(1)} %collective-permute-done.7), channel_id=1, source_target_pairs={{0,32},{16,48},{32,64},{48,80},{64,96},{80,112},{96,128},{112,144}... | collective-permute-start | bytes 1572872 | tf_op jit(solution)/shard_map/ppermute | solution.py:62
  52.9 42.2 %copy-start.9 = (f32[1,32,128,128]{3,2,1,0:T(8,128)S(1)}, f32[1,32,128,128]{3,2,1,0:T(8,128)}, u32[]{:S(2)}) copy-start(f32[1,32,128,128]{3,2,1,0:T(8,128)} %param.15) | copy-start | bytes 6291460
  53.4 41.3 %collective-permute-start.10 = (f32[32,16,128]{2,1,0:T(8,128)S(1)}, f32[32,16,128]{2,1,0:T(8,128)S(1)}, u32[]{:S(2)}, u32[]{:S(2)}) collective-permute-start(f32[32,16,128]{2,1,0:T(8,128)S(1)} %get-tuple-element.50), channel_id=1, source_target_pairs={{0,224},{16,240},{32,0},{48,16},{64,32},{80,48},{96,64},{112,80},{... | collective-permute-start | bytes 786440 | tf_op jit(solution)/shard_map/ppermute | solution.py:68
  94.7 25.0 %collective-permute-start.9 = (f32[32,16,128]{2,1,0:T(8,128)S(1)}, f32[32,16,128]{2,1,0:T(8,128)S(1)}, u32[]{:S(2)}, u32[]{:S(2)}) collective-permute-start(f32[32,16,128]{2,1,0:T(8,128)S(1)} %get-tuple-element.49), channel_id=1, source_target_pairs={{0,32},{16,48},{32,64},{48,80},{64,96},{80,112},{96,128},{112,144}... | collective-permute-start | bytes 786440 | tf_op jit(solution)/shard_map/ppermute | solution.py:68
  95.0 1.9 %copy-start.6 = (f32[256,128]{1,0:T(8,128)S(1)}, f32[256,128]{1,0:T(8,128)}, u32[]{:S(2)}) copy-start(f32[256,128]{1,0:T(8,128)} %constant.107.clone.msub_ref.refs_7_.refs_11_) | copy-start | bytes 393220
  95.0 1.9 %copy-start.7 = (f32[128,256]{1,0:T(8,128)S(1)}, f32[128,256]{1,0:T(8,128)}, u32[]{:S(2)}) copy-start(f32[128,256]{1,0:T(8,128)} %constant.106.clone.mlane_ref.refs_6_.refs_10_) | copy-start | bytes 393220
  107.1 1.3 copy-start.1
  108.4 1.4 copy-start.2
  119.7 1.3 copy-start.5
  121.0 2.2 %copy-start.10 = (f32[32,128,128]{2,1,0:T(8,128)}, f32[32,128,128]{2,1,0:T(8,128)S(1)}, u32[]{:S(2)}) copy-start(f32[32,128,128]{2,1,0:T(8,128)S(1)} %get-tuple-element.44.prev_ref) | copy-start | bytes 6291460
  136.0 1.4 copy-start.3
  137.5 20.7 %collective-permute-start.12 = (f32[4,256,128]{2,1,0:T(8,128)S(1)}, f32[4,256,128]{2,1,0:T(8,128)S(1)}, u32[]{:S(2)}, u32[]{:S(2)}) collective-permute-start(f32[4,256,128]{2,1,0:T(8,128)S(1)} %pad_maximum_fusion.8), channel_id=1, source_target_pairs={{1,0},{2,1},{3,2},{4,3},{5,4},{6,5},{7,6},{8,7},{9,8},{10,9},{11,1... | collective-permute-start | bytes 1572872 | tf_op jit(solution)/shard_map/ppermute | solution.py:324
  139.4 1.6 copy-start.4
  141.0 16.9 %copy-start.8 = (f32[32,128,128]{2,1,0:T(8,128)S(1)}, f32[32,128,128]{2,1,0:T(8,128)}, u32[]{:S(2)}) copy-start(f32[32,128,128]{2,1,0:T(8,128)} %get-tuple-element.17.refs_3_.refs_4_.refs_5_) | copy-start | bytes 6291460
  155.5 14.1 %collective-permute-start.11 = (f32[4,256,128]{2,1,0:T(8,128)S(1)}, f32[4,256,128]{2,1,0:T(8,128)S(1)}, u32[]{:S(2)}, u32[]{:S(2)}) collective-permute-start(f32[4,256,128]{2,1,0:T(8,128)S(1)} %pad_maximum_fusion.7), channel_id=1, source_target_pairs={{0,1},{1,2},{2,3},{3,4},{4,5},{5,6},{6,7},{7,8},{8,9},{9,10},{10,1... | collective-permute-start | bytes 1572872 | tf_op jit(solution)/shard_map/ppermute | solution.py:323

commit v10 on v9

--- a/solution.py
+++ b/solution.py
@@ -343,16 +343,16 @@
     msub = jnp.asarray(np.concatenate([ms, mg], axis=0))
 
     depth = u_cur.shape[0]
+    cur_rows = depth + 2 * HALO
     probe_kappa = dkappa[0]
     older = du_prev[0]
     newer = du_cur[0]
-    u_cur_strip_ext, buoyancy_ext, newer_ext = halo_depth_many([u_cur, buoyancy, newer])
-    rims = jnp.concatenate([u_cur_strip_ext[:HALO], u_cur_strip_ext[depth + HALO:]], axis=0)
-    rims_all = lax.all_gather(rims, "probe", axis=1, tiled=True)
-    u_cur_all, u_prev_all = ring_gather(
-        jnp.concatenate([u_cur, u_prev], axis=0), ((0, depth), (depth, 2 * depth))
-    )
-    u_cur_ext = jnp.concatenate([rims_all[:HALO], u_cur_all, rims_all[HALO:]], axis=0)
+    (u_cur_strip_ext,) = halo_depth_many([u_cur])
+    buoyancy_ext, newer_ext = halo_depth_many([buoyancy, newer])
+    u_cur_ext, u_prev_all = ring_gather(
+        jnp.concatenate([u_cur_strip_ext, u_prev], axis=0),
+        ((0, cur_rows), (cur_rows, cur_rows + depth)),
+    )
 
     slopes = slopes_of(buoyancy_ext, mlane, msub)
 

time: 178 us -> 156 us (0.88); the launches traced: 178 us -> 154 us
  blocking collectives: 37.5 us -> 0 us
  waiting for transfers between devices: 32.5 us -> 42.3 us
  starting transfers between devices: 28.6 us -> 31.9 us
  local copies, waits for them, and re-layouts: 16.2 us -> 18.2 us
  other arithmetic: 9.35 us -> 7.42 us
    all_gather x1 -> x0, blocking collectives: 37.5 us -> none  [local_body(): rims_all = lax.all_gather(rims, 'probe', axis=1, tiled=True)]
    ppermute x1 -> x2, waiting for transfers between devices: 0.01 us -> 10.7 us  [halo_depth_many(): above = lax.ppermute(tails, 'slab', [(i, i + 1) for i in range(ends)])]
    ppermute x1, waiting for transfers between devices: 5.06 us -> 0.01 us  [ring_gather(): partner = lax.ppermute(x, 'probe', [(i, i ^ 1) for i in range(n)])]
    ppermute x1, waiting for transfers between devices: 0.01 us -> 4.16 us  [ring_gather(): lax.ppermute(bwd[cut:], 'probe', behind)]
    dynamic_update_slice x10 -> x15, local copies, waits for them, and re-layouts: 1.47 us -> 4.54 us  [ring_gather(): buf = lax.dynamic_update_slice_in_dim(buf, by_offset[d][lo:hi], at, 1)]
    ppermute x1 -> x2, starting transfers between devices: 4.06 us -> 7.1 us  [halo_depth_many(): below = lax.ppermute(heads, 'slab', [(i + 1, i) for i in range(ends)])]
    ppermute x3, starting transfers between devices: 13.3 us -> 10.5 us  [ring_gather(): bwd = lax.ppermute(bwd, 'probe', behind)]
    ppermute x3, waiting for transfers between devices: 2.8 us -> 0.01 us  [ring_gather(): bwd = lax.ppermute(bwd, 'probe', behind)]
  transfers between devices with their start and end apart: 13 -> 15, of which waited for: 7 -> 7; matrix products, arithmetic and copies ran while one was open for 6% -> 10% of each run, Pallas kernels for 19% -> 23%
where the time goes in v10:
time: 156 us; the launch traced here: 154 us
  Pallas kernels  52.5 us (34%)
  waiting for transfers between devices  42.3 us (27%)
  starting transfers between devices  31.9 us (20%)
  local copies, waits for them, and re-layouts  18.2 us (12%)
  other arithmetic  7.42 us (5%)
    ppermute x3, waiting for transfers between devices, ring_gather(): fwd = lax.ppermute(fwd, 'probe', ahead)  15.7 us
    pallas_call x1, Pallas kernels, second_inner(): pl.pallas_call(functools.partial(_second_kernel, 3), grid=(blocks - 2,),...  14.5 us
    pallas_call x1, Pallas kernels, first_step(): pl.pallas_call(_first_kernel, grid=(depth // BZ,), in_specs=_ext_specs(n,...  11.7 us
    ppermute x1, waiting for transfers between devices, depth_rims(): above = lax.ppermute(tails, 'slab', [(i, i + 1) for i in range(ends)])  11.4 us
    ppermute x2, waiting for transfers between devices, halo_depth_many(): above = lax.ppermute(tails, 'slab', [(i, i + 1) for i in range(ends)])  10.7 us
    ppermute x3, starting transfers between devices, ring_gather(): bwd = lax.ppermute(bwd, 'probe', behind)  10.5 us
    pallas_call x1, Pallas kernels, slopes_of(): pl.pallas_call(functools.partial(_slope_kernel, (rows_in - rows) // 2), g...  10.3 us
    pallas_call x1, Pallas kernels, apply_op(): pl.pallas_call(functools.partial(_op_kernel, (with_prev, with_img, want_i...  9.89 us
  transfers between devices with their start and end apart: 15, of which 7 were waited for; matrix products, arithmetic and copies ran while one was open for 10% of the time, Pallas kernels for 23%

profile of v10, /device:TPU:6, one launch (start us, length us, event | category | flops | bytes accessed | tf_op | source)
XLA Modules:
  0.0 153.7 jit_solution(13897573759794507994)
XLA Ops:
  1.4 5.2 %collective-permute-start.1 = (f32[4,8,128]{2,1,0:T(8,128)S(1)}, f32[4,8,128]{2,1,0:T(8,128)S(1)}, u32[]{:S(2)}, u32[]{:S(2)}) collective-permute-start(f32[4,8,128]{2,1,0:T(8,128)S(1)} %get-tuple-element.44), channel_id=1, source_target_pairs={{1,0},{2,1},{3,2},{4,3},{5,4},{6,5},{7,6},{8,7},{9,8},{10,9},{11,1... | collective-permute-start | bytes 49160 | tf_op jit(solution)/shard_map/ppermute | solution.py:39
  6.6 1.9 %collective-permute-start = (f32[4,8,128]{2,1,0:T(8,128)S(1)}, f32[4,8,128]{2,1,0:T(8,128)S(1)}, u32[]{:S(2)}, u32[]{:S(2)}) collective-permute-start(f32[4,8,128]{2,1,0:T(8,128)S(1)} %get-tuple-element.45), channel_id=1, source_target_pairs={{0,1},{1,2},{2,3},{3,4},{4,5},{5,6},{6,7},{7,8},{8,9},{9,10},{10,1... | collective-permute-start | bytes 49160 | tf_op jit(solution)/shard_map/ppermute | solution.py:38
  8.5 1.1 slice_bitcast_fusion.1
  9.6 5.7 %collective-permute-done = f32[4,8,128]{2,1,0:T(8,128)S(1)} collective-permute-done((f32[4,8,128]{2,1,0:T(8,128)S(1)}, f32[4,8,128]{2,1,0:T(8,128)S(1)}, u32[]{:S(2)}, u32[]{:S(2)}) %collective-permute-start) | collective-permute-done | bytes 16416 | tf_op jit(solution)/shard_map/ppermute | solution.py:38
  17.2 1.1 fusion.5
  19.1 1.9 %collective-permute-start.12 = (f32[4,256,128]{2,1,0:T(8,128)}, f32[4,256,128]{2,1,0:T(8,128)S(1)}, u32[]{:S(2)}, u32[]{:S(2)}) collective-permute-start(f32[4,256,128]{2,1,0:T(8,128)} %pad_maximum_fusion.5), channel_id=1, source_target_pairs={{1,0},{2,1},{3,2},{4,3},{5,4},{6,5},{7,6},{8,7},{9,8},{10,9},{11,1... | collective-permute-start | bytes 1572872 | tf_op jit(solution)/shard_map/ppermute | solution.py:39
  21.9 2.4 %collective-permute-start.11 = (f32[4,256,128]{2,1,0:T(8,128)}, f32[4,256,128]{2,1,0:T(8,128)}, u32[]{:S(2)}, u32[]{:S(2)}) collective-permute-start(f32[4,256,128]{2,1,0:T(8,128)} %pad_maximum_fusion.4), channel_id=1, source_target_pairs={{0,1},{1,2},{2,3},{3,4},{4,5},{5,6},{6,7},{7,8},{8,9},{9,10},{10,1... | collective-permute-start | bytes 1572872 | tf_op jit(solution)/shard_map/ppermute | solution.py:38
  24.5 2.0 %collective-permute-start.6 = (f32[72,16,128]{2,1,0:T(8,128)S(1)}, f32[72,16,128]{2,1,0:T(8,128)S(1)}, u32[]{:S(2)}, u32[]{:S(2)}) collective-permute-start(f32[72,16,128]{2,1,0:T(8,128)S(1)} %maximum_select_fusion), channel_id=1, source_target_pairs={{0,32},{16,48},{32,64},{48,80},{64,96},{80,112},{96,128},{112,144}... | collective-permute-start | bytes 1769480 | tf_op jit(solution)/shard_map/ppermute | solution.py:62
  26.5 4.0 %collective-permute-start.3 = (f32[72,16,128]{2,1,0:T(8,128)S(1)}, f32[72,16,128]{2,1,0:T(8,128)}, u32[]{:S(2)}, u32[]{:S(2)}) collective-permute-start(f32[72,16,128]{2,1,0:T(8,128)S(1)} %maximum_select_fusion), channel_id=1, source_target_pairs={{0,224},{16,240},{32,0},{48,16},{64,32},{80,48},{96,64},{112,80},{... | collective-permute-start | bytes 1769480 | tf_op jit(solution)/shard_map/ppermute | solution.py:63
  31.2 5.1 %collective-permute-done.11 = f32[4,256,128]{2,1,0:T(8,128)} collective-permute-done((f32[4,256,128]{2,1,0:T(8,128)}, f32[4,256,128]{2,1,0:T(8,128)}, u32[]{:S(2)}, u32[]{:S(2)}) %collective-permute-start.11) | collective-permute-done | bytes 524320 | tf_op jit(solution)/shard_map/ppermute | solution.py:38
  37.3 6.6 %collective-permute-done.6 = f32[72,16,128]{2,1,0:T(8,128)S(1)} collective-permute-done((f32[72,16,128]{2,1,0:T(8,128)S(1)}, f32[72,16,128]{2,1,0:T(8,128)S(1)}, u32[]{:S(2)}, u32[]{:S(2)}) %collective-permute-start.6) | collective-permute-done | bytes 589856 | tf_op jit(solution)/shard_map/ppermute | solution.py:62
  43.9 3.2 %collective-permute-start.4 = (f32[72,16,128]{2,1,0:T(8,128)}, f32[72,16,128]{2,1,0:T(8,128)}, u32[]{:S(2)}, u32[]{:S(2)}) collective-permute-start(f32[72,16,128]{2,1,0:T(8,128)} %collective-permute-done.3), channel_id=1, source_target_pairs={{0,224},{16,240},{32,0},{48,16},{64,32},{80,48},{96,64},{112,80},{... | collective-permute-start | bytes 1769480 | tf_op jit(solution)/shard_map/ppermute | solution.py:63
  47.2 1.7 %pad_maximum_fusion.lo_ref.hi_ref = f32[40,128,128]{2,1,0:T(8,128)} fusion(f32[4,128,128]{2,1,0:T(8,128)S(1)} %get-tuple-element.43, f32[32,128,128]{2,1,0:T(8,128)S(1)} %copy-done, f32[4,128,128]{2,1,0:T(8,128)S(1)} %get-tuple-element.41), kind=kLoop, calls=%fused_computation | loop fusion | flops 1310720 | bytes 5242880 | tf_op jit(solution)/shard_map/concatenate | solution.py:44
  48.9 10.3 %shard_map.120 = (f32[32,128,128]{2,1,0:T(8,128)S(1)}, f32[32,128,128]{2,1,0:T(8,128)S(1)}, f32[32,128,128]{2,1,0:T(8,128)}) custom-call(f32[40,128,128]{2,1,0:T(8,128)} %pad_maximum_fusion.lo_ref.hi_ref, f32[40,128,128]{2,1,0:T(8,128)} %pad_maximum_fusion.lo_ref.hi_ref, f32[128,256]{1,0:T(8,128)S(1)} %copy-done.7, f32[256,128]{1,0:T(8,128)S(1)} %copy-done.6), custom_call_target="tpu_custom_call" | custom-call | tf_op jit(solution)/shard_map/pallas_call | solution.py:218
  59.2 2.0 %pad_maximum_fusion.1.refs_0_.refs_1_ = f32[40,128,128]{2,1,0:T(8,128)} fusion(f32[4,128,128]{2,1,0:T(8,128)S(1)} %get-tuple-element.42, f32[32,128,128]{2,1,0:T(8,128)S(1)} %bitcast.12, f32[4,128,128]{2,1,0:T(8,128)S(1)} %get-tuple-element.40), kind=kLoop, calls=%fused_computation.1 | loop fusion | flops 1310720 | bytes 5242880 | tf_op jit(solution)/shard_map/concatenate | solution.py:44
  62.0 9.9 %shard_map.121.part_ref = f32[32,128,128]{2,1,0:T(8,128)S(1)} custom-call(f32[40,128,128]{2,1,0:T(8,128)} %pad_maximum_fusion.1.refs_0_.refs_1_, f32[40,128,128]{2,1,0:T(8,128)} %pad_maximum_fusion.1.refs_0_.refs_1_, f32[32,128,128]{2,1,0:T(8,128)S(1)} %copy-done, f32[32,128,128]{2,1,0:T(8,128)} %copy-done.1, f32[32,128,128]{2,1,0:T(8,128)} %copy-done.2, ...), custom_call_target="tpu_custom_call" | custom-call | tf_op jit(solution)/shard_map/pallas_call | solution.py:246
  71.9 1.2 slice_dynamic-update-slice_fusion.5
  73.3 3.2 %collective-permute-start.5 = (f32[72,16,128]{2,1,0:T(8,128)}, f32[72,16,128]{2,1,0:T(8,128)S(1)}, u32[]{:S(2)}, u32[]{:S(2)}) collective-permute-start(f32[72,16,128]{2,1,0:T(8,128)} %collective-permute-done.4), channel_id=1, source_target_pairs={{0,224},{16,240},{32,0},{48,16},{64,32},{80,48},{96,64},{112,80},{... | collective-permute-start | bytes 1769480 | tf_op jit(solution)/shard_map/ppermute | solution.py:63
  79.5 9.1 %collective-permute-done.8 = f32[72,16,128]{2,1,0:T(8,128)S(1)} collective-permute-done((f32[72,16,128]{2,1,0:T(8,128)S(1)}, f32[72,16,128]{2,1,0:T(8,128)S(1)}, u32[]{:S(2)}, u32[]{:S(2)}) %collective-permute-start.8) | collective-permute-done | bytes 589856 | tf_op jit(solution)/shard_map/ppermute | solution.py:62
  88.7 3.5 %collective-permute-start.10 = (f32[36,16,128]{2,1,0:T(8,128)S(1)}, f32[36,16,128]{2,1,0:T(8,128)S(1)}, u32[]{:S(2)}, u32[]{:S(2)}) collective-permute-start(f32[36,16,128]{2,1,0:T(8,128)S(1)} %slice.173), channel_id=1, source_target_pairs={{0,224},{16,240},{32,0},{48,16},{64,32},{80,48},{96,64},{112,80},{... | collective-permute-start | bytes 884744 | tf_op jit(solution)/shard_map/ppermute | solution.py:68
  92.3 4.2 %collective-permute-done.10 = f32[36,16,128]{2,1,0:T(8,128)S(1)} collective-permute-done((f32[36,16,128]{2,1,0:T(8,128)S(1)}, f32[36,16,128]{2,1,0:T(8,128)S(1)}, u32[]{:S(2)}, u32[]{:S(2)}) %collective-permute-start.10) | collective-permute-done | bytes 294944 | tf_op jit(solution)/shard_map/ppermute | solution.py:68
  97.1 1.3 copy-done.11
  99.2 11.7 %shard_map.122 = (f32[32,128,128]{2,1,0:T(8,128)S(1)}, f32[32,128,128]{2,1,0:T(8,128)}) custom-call(f32[40,128,128]{2,1,0:T(8,128)} %copy-done.9, f32[40,128,128]{2,1,0:T(8,128)} %copy-done.9, f32[32,128,128]{2,1,0:T(8,128)S(1)} %copy-done, f32[32,128,128]{2,1,0:T(8,128)} %copy-done.1, f32[32,128,128]{2,1,0:T(8,128)} %copy-done.2, ...), custom_call_target="tpu_custom_call" | custom-call | tf_op jit(solution)/shard_map/pallas_call | solution.py:262
  110.9 1.1 fusion.2
  112.0 1.3 copy-done.3
  113.4 1.9 %collective-permute-start.14 = (f32[4,256,128]{2,1,0:T(8,128)S(1)}, f32[4,256,128]{2,1,0:T(8,128)S(1)}, u32[]{:S(2)}, u32[]{:S(2)}) collective-permute-start(f32[4,256,128]{2,1,0:T(8,128)S(1)} %pad_maximum_fusion.7), channel_id=1, source_target_pairs={{1,0},{2,1},{3,2},{4,3},{5,4},{6,5},{7,6},{8,7},{9,8},{10,9},{11,1... | collective-permute-start | bytes 1572872 | tf_op jit(solution)/shard_map/ppermute | solution.py:324
  115.3 1.6 %copy-done.4 = f32[32,128,128]{2,1,0:T(8,128)S(1)} copy-done((f32[32,128,128]{2,1,0:T(8,128)S(1)}, f32[32,128,128]{2,1,0:T(8,128)}, u32[]{:S(2)}) %copy-start.4) | copy-done | bytes 2097176
  116.9 14.5 %shard_map.123 = (f32[32,128,128]{2,1,0:T(8,128)S(1)}, f32[32,128,128]{2,1,0:T(8,128)}) custom-call(f32[32,128,128]{2,1,0:T(8,128)S(1)} %copy-done.4, f32[32,128,128]{2,1,0:T(8,128)S(1)} %copy-done.4, f32[32,128,128]{2,1,0:T(8,128)S(1)} %copy-done.4, f32[32,128,128]{2,1,0:T(8,128)} %get-tuple-element.17.refs_3_.refs_4_.refs_5_, ...), custom_call_target="tpu_custom_call" | custom-call | tf_op jit(solution)/shard_map/pallas_call | solution.py:283
  131.4 2.4 %collective-permute-start.13 = (f32[4,256,128]{2,1,0:T(8,128)S(1)}, f32[4,256,128]{2,1,0:T(8,128)S(1)}, u32[]{:S(2)}, u32[]{:S(2)}) collective-permute-start(f32[4,256,128]{2,1,0:T(8,128)S(1)} %pad_maximum_fusion.6), channel_id=1, source_target_pairs={{0,1},{1,2},{2,3},{3,4},{4,5},{5,6},{6,7},{7,8},{8,9},{9,10},{10,1... | collective-permute-start | bytes 1572872 | tf_op jit(solution)/shard_map/ppermute | solution.py:323
  134.1 11.4 %collective-permute-done.13 = f32[4,256,128]{2,1,0:T(8,128)S(1)} collective-permute-done((f32[4,256,128]{2,1,0:T(8,128)S(1)}, f32[4,256,128]{2,1,0:T(8,128)S(1)}, u32[]{:S(2)}, u32[]{:S(2)}) %collective-permute-start.13) | collective-permute-done | bytes 524320 | tf_op jit(solution)/shard_map/ppermute | solution.py:323
  145.9 6.1 %shard_map.124 = (f32[32,128,128]{2,1,0:T(8,128)S(1)}, f32[32,128,128]{2,1,0:T(8,128)}) custom-call(f32[24,128,128]{2,1,0:T(8,128)S(1)} %pad_maximum_fusion.2.refs_0_.refs_1_.refs_2_, f32[24,128,128]{2,1,0:T(8,128)S(1)} %pad_maximum_fusion.2.refs_0_.refs_1_.refs_2_, ...), custom_call_target="tpu_custom_call", output_to_operand_aliasing={{0}: (15, {}), {1}: (16, {})} | custom-call | tf_op jit(solution)/shard_map/pallas_call | solution.py:306
  152.0 1.7 %multiply_add_fusion = (f32[32,8,128]{2,1,0:T(8,128)}, f32[32,8,128]{2,1,0:T(8,128)}) fusion(f32[32,128,128]{2,1,0:T(8,128)S(1)} %get-tuple-element.20, s32[]{:T(128)S(6)} %select_n.124, f32[32,128,128]{2,1,0:T(8,128)} %refs_12_.3, f32[32,8,128]{2,1,0:T(8,128)S(1)} %copy-done.12, f32[32,128,128]{2,1,0:T(8,128)} %copy-done.3), kind=kLoop, calls=%fused_computation.28 | loop fusion | flops 131072 | bytes 786436 | tf_op jit(solution)/shard_map/add | solution.py:379
  (72 shorter events, 12.2 us)
Async XLA Ops:
  1.4 14.8 %collective-permute-start.1 = (f32[4,8,128]{2,1,0:T(8,128)S(1)}, f32[4,8,128]{2,1,0:T(8,128)S(1)}, u32[]{:S(2)}, u32[]{:S(2)}) collective-permute-start(f32[4,8,128]{2,1,0:T(8,128)S(1)} %get-tuple-element.44), channel_id=1, source_target_pairs={{1,0},{2,1},{3,2},{4,3},{5,4},{6,5},{7,6},{8,7},{9,8},{10,9},{11,1... | collective-permute-start | bytes 49160 | tf_op jit(solution)/shard_map/ppermute | solution.py:39
  6.6 8.7 %collective-permute-start = (f32[4,8,128]{2,1,0:T(8,128)S(1)}, f32[4,8,128]{2,1,0:T(8,128)S(1)}, u32[]{:S(2)}, u32[]{:S(2)}) collective-permute-start(f32[4,8,128]{2,1,0:T(8,128)S(1)} %get-tuple-element.45), channel_id=1, source_target_pairs={{0,1},{1,2},{2,3},{3,4},{4,5},{5,6},{6,7},{7,8},{8,9},{9,10},{10,1... | collective-permute-start | bytes 49160 | tf_op jit(solution)/shard_map/ppermute | solution.py:38
  17.1 7.3 %collective-permute-start.2 = (f32[72,8,128]{2,1,0:T(8,128)S(1)}, f32[72,8,128]{2,1,0:T(8,128)S(1)}, u32[]{:S(2)}, u32[]{:S(2)}) collective-permute-start(f32[72,8,128]{2,1,0:T(8,128)S(1)} %constant_dynamic-update-slice_fusion), channel_id=1, source_target_pairs={{0,16},{16,0},{32,48},{48,32},{64,80},{80,64},{96,112},{112,96},{1... | collective-permute-start | bytes 884744 | tf_op jit(solution)/shard_map/ppermute | solution.py:53
  19.1 12.0 %collective-permute-start.12 = (f32[4,256,128]{2,1,0:T(8,128)}, f32[4,256,128]{2,1,0:T(8,128)S(1)}, u32[]{:S(2)}, u32[]{:S(2)}) collective-permute-start(f32[4,256,128]{2,1,0:T(8,128)} %pad_maximum_fusion.5), channel_id=1, source_target_pairs={{1,0},{2,1},{3,2},{4,3},{5,4},{6,5},{7,6},{8,7},{9,8},{10,9},{11,1... | collective-permute-start | bytes 1572872 | tf_op jit(solution)/shard_map/ppermute | solution.py:39
  21.9 14.4 %collective-permute-start.11 = (f32[4,256,128]{2,1,0:T(8,128)}, f32[4,256,128]{2,1,0:T(8,128)}, u32[]{:S(2)}, u32[]{:S(2)}) collective-permute-start(f32[4,256,128]{2,1,0:T(8,128)} %pad_maximum_fusion.4), channel_id=1, source_target_pairs={{0,1},{1,2},{2,3},{3,4},{4,5},{5,6},{6,7},{7,8},{8,9},{9,10},{10,1... | collective-permute-start | bytes 1572872 | tf_op jit(solution)/shard_map/ppermute | solution.py:38
  24.5 19.4 %collective-permute-start.6 = (f32[72,16,128]{2,1,0:T(8,128)S(1)}, f32[72,16,128]{2,1,0:T(8,128)S(1)}, u32[]{:S(2)}, u32[]{:S(2)}) collective-permute-start(f32[72,16,128]{2,1,0:T(8,128)S(1)} %maximum_select_fusion), channel_id=1, source_target_pairs={{0,32},{16,48},{32,64},{48,80},{64,96},{80,112},{96,128},{112,144}... | collective-permute-start | bytes 1769480 | tf_op jit(solution)/shard_map/ppermute | solution.py:62
  26.5 17.4 %collective-permute-start.3 = (f32[72,16,128]{2,1,0:T(8,128)S(1)}, f32[72,16,128]{2,1,0:T(8,128)}, u32[]{:S(2)}, u32[]{:S(2)}) collective-permute-start(f32[72,16,128]{2,1,0:T(8,128)S(1)} %maximum_select_fusion), channel_id=1, source_target_pairs={{0,224},{16,240},{32,0},{48,16},{64,32},{80,48},{96,64},{112,80},{... | collective-permute-start | bytes 1769480 | tf_op jit(solution)/shard_map/ppermute | solution.py:63
  30.9 16.3 %copy-start = (f32[32,128,128]{2,1,0:T(8,128)S(1)}, f32[32,128,128]{2,1,0:T(8,128)}, u32[]{:S(2)}) copy-start(f32[32,128,128]{2,1,0:T(8,128)} %refs_6_.4) | copy-start | bytes 6291460
  43.9 29.2 %collective-permute-start.7 = (f32[72,16,128]{2,1,0:T(8,128)S(1)}, f32[72,16,128]{2,1,0:T(8,128)S(1)}, u32[]{:S(2)}, u32[]{:S(2)}) collective-permute-start(f32[72,16,128]{2,1,0:T(8,128)S(1)} %collective-permute-done.6), channel_id=1, source_target_pairs={{0,32},{16,48},{32,64},{48,80},{64,96},{80,112},{96,128},{112,144}... | collective-permute-start | bytes 1769480 | tf_op jit(solution)/shard_map/ppermute | solution.py:62
  43.9 29.3 %collective-permute-start.4 = (f32[72,16,128]{2,1,0:T(8,128)}, f32[72,16,128]{2,1,0:T(8,128)}, u32[]{:S(2)}, u32[]{:S(2)}) collective-permute-start(f32[72,16,128]{2,1,0:T(8,128)} %collective-permute-done.3), channel_id=1, source_target_pairs={{0,224},{16,240},{32,0},{48,16},{64,32},{80,48},{96,64},{112,80},{... | collective-permute-start | bytes 1769480 | tf_op jit(solution)/shard_map/ppermute | solution.py:63
  47.2 1.7 %copy-start.6 = (f32[256,128]{1,0:T(8,128)S(1)}, f32[256,128]{1,0:T(8,128)}, u32[]{:S(2)}) copy-start(f32[256,128]{1,0:T(8,128)} %constant.108.clone.msub_ref.refs_7_.refs_11_) | copy-start | bytes 393220
  47.2 1.7 %copy-start.7 = (f32[128,256]{1,0:T(8,128)S(1)}, f32[128,256]{1,0:T(8,128)}, u32[]{:S(2)}) copy-start(f32[128,256]{1,0:T(8,128)} %constant.107.clone.mlane_ref.refs_6_.refs_10_) | copy-start | bytes 393220
  48.9 10.3 %copy-start.10 = (f32[1,32,128,128]{3,2,1,0:T(8,128)S(1)}, f32[1,32,128,128]{3,2,1,0:T(8,128)}, u32[]{:S(2)}) copy-start(f32[1,32,128,128]{3,2,1,0:T(8,128)} %param.15) | copy-start | bytes 6291460
  59.2 2.1 %copy-start.1 = (f32[32,128,128]{2,1,0:T(8,128)}, f32[32,128,128]{2,1,0:T(8,128)S(1)}, u32[]{:S(2)}) copy-start(f32[32,128,128]{2,1,0:T(8,128)S(1)} %get-tuple-element.13.refs_3_.g0_ref.refs_7_) | copy-start | bytes 6291460
  59.2 2.8 %copy-start.2 = (f32[32,128,128]{2,1,0:T(8,128)}, f32[32,128,128]{2,1,0:T(8,128)S(1)}, u32[]{:S(2)}) copy-start(f32[32,128,128]{2,1,0:T(8,128)S(1)} %get-tuple-element.14.refs_4_.g1_ref.refs_8_) | copy-start | bytes 6291460
  71.9 20.4 %copy-start.5 = (f32[32,128,128]{2,1,0:T(8,128)}, f32[32,128,128]{2,1,0:T(8,128)S(1)}, u32[]{:S(2)}) copy-start(f32[32,128,128]{2,1,0:T(8,128)S(1)} %shard_map.121.part_ref) | copy-start | bytes 6291460
  73.2 15.4 %collective-permute-start.8 = (f32[72,16,128]{2,1,0:T(8,128)S(1)}, f32[72,16,128]{2,1,0:T(8,128)S(1)}, u32[]{:S(2)}, u32[]{:S(2)}) collective-permute-start(f32[72,16,128]{2,1,0:T(8,128)S(1)} %collective-permute-done.7), channel_id=1, source_target_pairs={{0,32},{16,48},{32,64},{48,80},{64,96},{80,112},{96,128},{112,144}... | collective-permute-start | bytes 1769480 | tf_op jit(solution)/shard_map/ppermute | solution.py:62
  73.3 15.4 %collective-permute-start.5 = (f32[72,16,128]{2,1,0:T(8,128)}, f32[72,16,128]{2,1,0:T(8,128)S(1)}, u32[]{:S(2)}, u32[]{:S(2)}) collective-permute-start(f32[72,16,128]{2,1,0:T(8,128)} %collective-permute-done.4), channel_id=1, source_target_pairs={{0,224},{16,240},{32,0},{48,16},{64,32},{80,48},{96,64},{112,80},{... | collective-permute-start | bytes 1769480 | tf_op jit(solution)/shard_map/ppermute | solution.py:63
  88.6 8.2 %collective-permute-start.9 = (f32[36,16,128]{2,1,0:T(8,128)S(1)}, f32[36,16,128]{2,1,0:T(8,128)S(1)}, u32[]{:S(2)}, u32[]{:S(2)}) collective-permute-start(f32[36,16,128]{2,1,0:T(8,128)S(1)} %slice.172), channel_id=1, source_target_pairs={{0,32},{16,48},{32,64},{48,80},{64,96},{80,112},{96,128},{112,144}... | collective-permute-start | bytes 884744 | tf_op jit(solution)/shard_map/ppermute | solution.py:68
  88.7 7.7 %collective-permute-start.10 = (f32[36,16,128]{2,1,0:T(8,128)S(1)}, f32[36,16,128]{2,1,0:T(8,128)S(1)}, u32[]{:S(2)}, u32[]{:S(2)}) collective-permute-start(f32[36,16,128]{2,1,0:T(8,128)S(1)} %slice.173), channel_id=1, source_target_pairs={{0,224},{16,240},{32,0},{48,16},{64,32},{80,48},{96,64},{112,80},{... | collective-permute-start | bytes 884744 | tf_op jit(solution)/shard_map/ppermute | solution.py:68
  97.0 1.3 copy-start.11
  97.0 2.1 %copy-start.9 = (f32[40,128,128]{2,1,0:T(8,128)}, f32[40,128,128]{2,1,0:T(8,128)S(1)}, u32[]{:S(2)}) copy-start(f32[40,128,128]{2,1,0:T(8,128)S(1)} %slice_dynamic-update-slice_fusion.lo_ref.hi_ref) | copy-start | bytes 7864324
  112.0 1.4 copy-start.3
  113.4 20.7 %collective-permute-start.14 = (f32[4,256,128]{2,1,0:T(8,128)S(1)}, f32[4,256,128]{2,1,0:T(8,128)S(1)}, u32[]{:S(2)}, u32[]{:S(2)}) collective-permute-start(f32[4,256,128]{2,1,0:T(8,128)S(1)} %pad_maximum_fusion.7), channel_id=1, source_target_pairs={{1,0},{2,1},{3,2},{4,3},{5,4},{6,5},{7,6},{8,7},{9,8},{10,9},{11,1... | collective-permute-start | bytes 1572872 | tf_op jit(solution)/shard_map/ppermute | solution.py:324
  115.3 1.6 %copy-start.4 = (f32[32,128,128]{2,1,0:T(8,128)S(1)}, f32[32,128,128]{2,1,0:T(8,128)}, u32[]{:S(2)}) copy-start(f32[32,128,128]{2,1,0:T(8,128)} %copy-done.3) | copy-start | bytes 6291460
  116.9 16.9 %copy-start.8 = (f32[32,128,128]{2,1,0:T(8,128)S(1)}, f32[32,128,128]{2,1,0:T(8,128)}, u32[]{:S(2)}) copy-start(f32[32,128,128]{2,1,0:T(8,128)} %get-tuple-element.17.refs_3_.refs_4_.refs_5_) | copy-start | bytes 6291460
  131.4 14.1 %collective-permute-start.13 = (f32[4,256,128]{2,1,0:T(8,128)S(1)}, f32[4,256,128]{2,1,0:T(8,128)S(1)}, u32[]{:S(2)}, u32[]{:S(2)}) collective-permute-start(f32[4,256,128]{2,1,0:T(8,128)S(1)} %pad_maximum_fusion.6), channel_id=1, source_target_pairs={{0,1},{1,2},{2,3},{3,4},{4,5},{5,6},{6,7},{7,8},{8,9},{9,10},{10,1... | collective-permute-start | bytes 1572872 | tf_op jit(solution)/shard_map/ppermute | solution.py:323
  145.9 6.1 %copy-start.12 = (f32[32,8,128]{2,1,0:T(8,128)S(1)}, f32[32,8,128]{2,1,0:T(8,128)}, u32[]{:S(2)}) copy-start(f32[32,8,128]{2,1,0:T(8,128)} %param.10) | copy-start | bytes 393220

commit v11 on v10

--- a/solution.py
+++ b/solution.py
@@ -51,7 +51,7 @@
     rings = n // 2
     p = lax.axis_index("probe")
     partner = lax.ppermute(x, "probe", [(i, i ^ 1) for i in range(n)])
-    pair = jnp.where(p % 2 == 0, jnp.concatenate([x, partner], 1), jnp.concatenate([partner, x], 1))
+    pair = jnp.concatenate([x, partner], 1)
     ahead = [(i, (i + 2) % n) for i in range(n)]
     behind = [(i, (i - 2) % n) for i in range(n)]
     by_offset = {0: pair}
@@ -69,13 +69,17 @@
     )
     by_offset[half] = far
     width = pair.shape[1]
+    strip = x.shape[1]
     zpos = p // 2
+    parity = p % 2
     outs = []
     for lo, hi in bounds:
         buf = jnp.zeros((hi - lo, rings * width, x.shape[2]), x.dtype)
         for d in range(rings):
             at = ((zpos + d) % rings) * width
-            buf = lax.dynamic_update_slice_in_dim(buf, by_offset[d][lo:hi], at, 1)
+            chunk = by_offset[d][lo:hi]
+            buf = lax.dynamic_update_slice_in_dim(buf, chunk[:, :strip], at + parity * strip, 1)
+            buf = lax.dynamic_update_slice_in_dim(buf, chunk[:, strip:], at + (1 - parity) * strip, 1)
         outs.append(buf)
     return outs
 

time: 156 us -> 169 us (1.083); the launches traced: 154 us -> 169 us
  starting transfers between devices: 31.9 us -> 40.7 us
  local copies, waits for them, and re-layouts: 18.2 us -> 25.5 us
  waiting for transfers between devices: 42.3 us -> 40 us
    ppermute x2, waiting for transfers between devices: 10.7 us -> 4.03 us  [halo_depth_many(): above = lax.ppermute(tails, 'slab', [(i, i + 1) for i in range(ends)])]
    dynamic_update_slice x15 -> x31, local copies, waits for them, and re-layouts: 4.54 us -> 11 us  [the longest x15 5.5 us: ring_gather(): lax.dynamic_update_slice_in_dim(buf, chunk[:, :strip], at + parity * stri...]
    ppermute x3, waiting for transfers between devices: 15.7 us -> 21.5 us  [ring_gather(): fwd = lax.ppermute(fwd, 'probe', ahead)]
    ppermute x2, starting transfers between devices: 7.1 us -> 12.9 us  [halo_depth_many(): below = lax.ppermute(heads, 'slab', [(i + 1, i) for i in range(ends)])]
    ppermute x1, waiting for transfers between devices: 4.16 us -> 0.01 us  [ring_gather(): lax.ppermute(bwd[cut:], 'probe', behind)]
    ppermute x1, waiting for transfers between devices: 0.31 us -> 3.02 us  [ring_gather(): lax.ppermute(fwd[:cut], 'probe', ahead)]
    ppermute x3, starting transfers between devices: 2.08 us -> 3.99 us  [ring_gather(): fwd = lax.ppermute(fwd, 'probe', ahead)]
    unnamed x29 -> x30, local copies, waits for them, and re-layouts: 6.82 us -> 7.19 us
  transfers between devices with their start and end apart: 15 -> 15, of which waited for: 7 -> 5; matrix products, arithmetic and copies ran while one was open for 10% -> 10% of each run, Pallas kernels for 23% -> 21%
where the time goes in v11:
time: 169 us
  Pallas kernels  52.5 us (31%)
  starting transfers between devices  40.7 us (24%)
  waiting for transfers between devices  40 us (24%)
  local copies, waits for them, and re-layouts  25.5 us (15%)
  other arithmetic  8.49 us (5%)
    ppermute x3, waiting for transfers between devices, ring_gather(): fwd = lax.ppermute(fwd, 'probe', ahead)  21.5 us
    pallas_call x1, Pallas kernels, second_inner(): pl.pallas_call(functools.partial(_second_kernel, 3), grid=(blocks - 2,),...  14.5 us
    ppermute x2, starting transfers between devices, halo_depth_many(): below = lax.ppermute(heads, 'slab', [(i + 1, i) for i in range(ends)])  12.9 us
    pallas_call x1, Pallas kernels, first_step(): pl.pallas_call(_first_kernel, grid=(depth // BZ,), in_specs=_ext_specs(n,...  11.7 us
    ppermute x1, waiting for transfers between devices, depth_rims(): above = lax.ppermute(tails, 'slab', [(i, i + 1) for i in range(ends)])  11.4 us
    ppermute x3, starting transfers between devices, ring_gather(): bwd = lax.ppermute(bwd, 'probe', behind)  11.3 us
    pallas_call x1, Pallas kernels, slopes_of(): pl.pallas_call(functools.partial(_slope_kernel, (rows_in - rows) // 2), g...  10.3 us
    pallas_call x1, Pallas kernels, apply_op(): pl.pallas_call(functools.partial(_op_kernel, (with_prev, with_img, want_i...  9.89 us
  transfers between devices with their start and end apart: 15, of which 5 were waited for; matrix products, arithmetic and copies ran while one was open for 10% of the time, Pallas kernels for 21%

profile of v11, /device:TPU:6, one launch (start us, length us, event | category | flops | bytes accessed | tf_op | source)
XLA Modules:
  0.0 168.5 jit_solution(7107501210637453357)
XLA Ops:
  1.4 1.9 %collective-permute-start = (f32[4,8,128]{2,1,0:T(8,128)S(1)}, f32[4,8,128]{2,1,0:T(8,128)S(1)}, u32[]{:S(2)}, u32[]{:S(2)}) collective-permute-start(f32[4,8,128]{2,1,0:T(8,128)S(1)} %get-tuple-element.46), channel_id=1, source_target_pairs={{0,1},{1,2},{2,3},{3,4},{4,5},{5,6},{6,7},{7,8},{8,9},{9,10},{10,1... | collective-permute-start | bytes 49160 | tf_op jit(solution)/shard_map/ppermute | solution.py:38
  3.4 7.4 %collective-permute-start.1 = (f32[4,8,128]{2,1,0:T(8,128)S(1)}, f32[4,8,128]{2,1,0:T(8,128)S(1)}, u32[]{:S(2)}, u32[]{:S(2)}) collective-permute-start(f32[4,8,128]{2,1,0:T(8,128)S(1)} %get-tuple-element.47), channel_id=1, source_target_pairs={{1,0},{2,1},{3,2},{4,3},{5,4},{6,5},{7,6},{8,7},{9,8},{10,9},{11,1... | collective-permute-start | bytes 49160 | tf_op jit(solution)/shard_map/ppermute | solution.py:39
  10.8 1.1 slice_bitcast_fusion.1
  14.8 1.6 broadcast_in_dim.13
  18.8 5.5 %collective-permute-start.12 = (f32[4,256,128]{2,1,0:T(8,128)}, f32[4,256,128]{2,1,0:T(8,128)S(1)}, u32[]{:S(2)}, u32[]{:S(2)}) collective-permute-start(f32[4,256,128]{2,1,0:T(8,128)} %pad_maximum_fusion.6), channel_id=1, source_target_pairs={{1,0},{2,1},{3,2},{4,3},{5,4},{6,5},{7,6},{8,7},{9,8},{10,9},{11,1... | collective-permute-start | bytes 1572872 | tf_op jit(solution)/shard_map/ppermute | solution.py:39
  25.1 1.9 %collective-permute-start.11 = (f32[4,256,128]{2,1,0:T(8,128)}, f32[4,256,128]{2,1,0:T(8,128)}, u32[]{:S(2)}, u32[]{:S(2)}) collective-permute-start(f32[4,256,128]{2,1,0:T(8,128)} %pad_maximum_fusion.5), channel_id=1, source_target_pairs={{0,1},{1,2},{2,3},{3,4},{4,5},{5,6},{6,7},{7,8},{8,9},{9,10},{10,1... | collective-permute-start | bytes 1572872 | tf_op jit(solution)/shard_map/ppermute | solution.py:38
  27.6 1.1 pad_maximum_fusion.4
  28.7 2.0 %collective-permute-start.6 = (f32[72,16,128]{2,1,0:T(8,128)S(1)}, f32[72,16,128]{2,1,0:T(8,128)S(1)}, u32[]{:S(2)}, u32[]{:S(2)}) collective-permute-start(f32[72,16,128]{2,1,0:T(8,128)S(1)} %pad_maximum_fusion.4), channel_id=1, source_target_pairs={{0,32},{16,48},{32,64},{48,80},{64,96},{80,112},{96,128},{112,144}... | collective-permute-start | bytes 1769480 | tf_op jit(solution)/shard_map/ppermute | solution.py:62
  30.7 4.0 %collective-permute-start.3 = (f32[72,16,128]{2,1,0:T(8,128)S(1)}, f32[72,16,128]{2,1,0:T(8,128)S(1)}, u32[]{:S(2)}, u32[]{:S(2)}) collective-permute-start(f32[72,16,128]{2,1,0:T(8,128)S(1)} %pad_maximum_fusion.4), channel_id=1, source_target_pairs={{0,224},{16,240},{32,0},{48,16},{64,32},{80,48},{96,64},{112,80},{... | collective-permute-start | bytes 1769480 | tf_op jit(solution)/shard_map/ppermute | solution.py:63
  35.5 4.0 %collective-permute-done.11 = f32[4,256,128]{2,1,0:T(8,128)} collective-permute-done((f32[4,256,128]{2,1,0:T(8,128)}, f32[4,256,128]{2,1,0:T(8,128)}, u32[]{:S(2)}, u32[]{:S(2)}) %collective-permute-start.11) | collective-permute-done | bytes 524320 | tf_op jit(solution)/shard_map/ppermute | solution.py:38
  40.6 1.7 pad_maximum_fusion.lo_ref.hi_ref
  42.3 10.3 %shard_map.120 = (f32[32,128,128]{2,1,0:T(8,128)S(1)}, f32[32,128,128]{2,1,0:T(8,128)S(1)}, f32[32,128,128]{2,1,0:T(8,128)}) custom-call(f32[40,128,128]{2,1,0:T(8,128)} %pad_maximum_fusion.lo_ref.hi_ref, f32[40,128,128]{2,1,0:T(8,128)} %pad_maximum_fusion.lo_ref.hi_ref, f32[128,256]{1,0:T(8,128)S(1)} %copy-done.7, f32[256,128]{1,0:T(8,128)S(1)} %copy-done.6), custom_call_target="tpu_custom_call" | custom-call | tf_op jit(solution)/shard_map/pallas_call | solution.py:222
  52.6 2.0 %pad_maximum_fusion.1.refs_0_.refs_1_ = f32[40,128,128]{2,1,0:T(8,128)} fusion(f32[4,128,128]{2,1,0:T(8,128)S(1)} %get-tuple-element.42, f32[32,128,128]{2,1,0:T(8,128)S(1)} %bitcast.12, f32[4,128,128]{2,1,0:T(8,128)S(1)} %get-tuple-element.40), kind=kLoop, calls=%fused_computation.1 | loop fusion | flops 1310720 | bytes 5242880 | tf_op jit(solution)/shard_map/concatenate | solution.py:44
  55.4 9.9 %shard_map.121.part_ref = f32[32,128,128]{2,1,0:T(8,128)S(1)} custom-call(f32[40,128,128]{2,1,0:T(8,128)} %pad_maximum_fusion.1.refs_0_.refs_1_, f32[40,128,128]{2,1,0:T(8,128)} %pad_maximum_fusion.1.refs_0_.refs_1_, f32[32,128,128]{2,1,0:T(8,128)S(1)} %copy-done, f32[32,128,128]{2,1,0:T(8,128)} %copy-done.1, f32[32,128,128]{2,1,0:T(8,128)} %copy-done.2, ...), custom_call_target="tpu_custom_call" | custom-call | tf_op jit(solution)/shard_map/pallas_call | solution.py:250
  65.3 2.0 %collective-permute-start.7 = (f32[72,16,128]{2,1,0:T(8,128)S(1)}, f32[72,16,128]{2,1,0:T(8,128)S(1)}, u32[]{:S(2)}, u32[]{:S(2)}) collective-permute-start(f32[72,16,128]{2,1,0:T(8,128)S(1)} %collective-permute-done.6), channel_id=1, source_target_pairs={{0,32},{16,48},{32,64},{48,80},{64,96},{80,112},{96,128},{112,144}... | collective-permute-start | bytes 1769480 | tf_op jit(solution)/shard_map/ppermute | solution.py:62
  67.3 4.0 %collective-permute-start.4 = (f32[72,16,128]{2,1,0:T(8,128)S(1)}, f32[72,16,128]{2,1,0:T(8,128)S(1)}, u32[]{:S(2)}, u32[]{:S(2)}) collective-permute-start(f32[72,16,128]{2,1,0:T(8,128)S(1)} %collective-permute-done.3), channel_id=1, source_target_pairs={{0,224},{16,240},{32,0},{48,16},{64,32},{80,48},{96,64},{112,80},{... | collective-permute-start | bytes 1769480 | tf_op jit(solution)/shard_map/ppermute | solution.py:63
  72.7 12.6 %collective-permute-done.7 = f32[72,16,128]{2,1,0:T(8,128)S(1)} collective-permute-done((f32[72,16,128]{2,1,0:T(8,128)S(1)}, f32[72,16,128]{2,1,0:T(8,128)S(1)}, u32[]{:S(2)}, u32[]{:S(2)}) %collective-permute-start.7) | collective-permute-done | bytes 589856 | tf_op jit(solution)/shard_map/ppermute | solution.py:62
  85.4 3.2 %collective-permute-start.5 = (f32[72,16,128]{2,1,0:T(8,128)S(1)}, f32[72,16,128]{2,1,0:T(8,128)S(1)}, u32[]{:S(2)}, u32[]{:S(2)}) collective-permute-start(f32[72,16,128]{2,1,0:T(8,128)S(1)} %collective-permute-done.4), channel_id=1, source_target_pairs={{0,224},{16,240},{32,0},{48,16},{64,32},{80,48},{96,64},{112,80},{... | collective-permute-start | bytes 1769480 | tf_op jit(solution)/shard_map/ppermute | solution.py:63
  90.0 8.9 %collective-permute-done.8 = f32[72,16,128]{2,1,0:T(8,128)S(1)} collective-permute-done((f32[72,16,128]{2,1,0:T(8,128)S(1)}, f32[72,16,128]{2,1,0:T(8,128)S(1)}, u32[]{:S(2)}, u32[]{:S(2)}) %collective-permute-start.8) | collective-permute-done | bytes 589856 | tf_op jit(solution)/shard_map/ppermute | solution.py:62
  99.0 3.5 %collective-permute-start.10 = (f32[36,16,128]{2,1,0:T(8,128)S(1)}, f32[36,16,128]{2,1,0:T(8,128)S(1)}, u32[]{:S(2)}, u32[]{:S(2)}) collective-permute-start(f32[36,16,128]{2,1,0:T(8,128)S(1)} %slice.287), channel_id=1, source_target_pairs={{0,224},{16,240},{32,0},{48,16},{64,32},{80,48},{96,64},{112,80},{... | collective-permute-start | bytes 884744 | tf_op jit(solution)/shard_map/ppermute | solution.py:68
  103.9 3.0 %collective-permute-done.9 = f32[36,16,128]{2,1,0:T(8,128)S(1)} collective-permute-done((f32[36,16,128]{2,1,0:T(8,128)S(1)}, f32[36,16,128]{2,1,0:T(8,128)S(1)}, u32[]{:S(2)}, u32[]{:S(2)}) %collective-permute-start.9) | collective-permute-done | bytes 294944 | tf_op jit(solution)/shard_map/ppermute | solution.py:68
  112.5 1.5 copy-done.9
  114.0 11.7 %shard_map.122 = (f32[32,128,128]{2,1,0:T(8,128)S(1)}, f32[32,128,128]{2,1,0:T(8,128)}) custom-call(f32[40,128,128]{2,1,0:T(8,128)} %copy-done.9, f32[40,128,128]{2,1,0:T(8,128)} %copy-done.9, f32[32,128,128]{2,1,0:T(8,128)S(1)} %copy-done, f32[32,128,128]{2,1,0:T(8,128)} %copy-done.1, f32[32,128,128]{2,1,0:T(8,128)} %copy-done.2, ...), custom_call_target="tpu_custom_call" | custom-call | tf_op jit(solution)/shard_map/pallas_call | solution.py:266
  125.7 1.1 fusion.1
  126.8 1.4 copy-done.3
  128.2 1.9 %collective-permute-start.14 = (f32[4,256,128]{2,1,0:T(8,128)S(1)}, f32[4,256,128]{2,1,0:T(8,128)S(1)}, u32[]{:S(2)}, u32[]{:S(2)}) collective-permute-start(f32[4,256,128]{2,1,0:T(8,128)S(1)} %pad_maximum_fusion.8), channel_id=1, source_target_pairs={{1,0},{2,1},{3,2},{4,3},{5,4},{6,5},{7,6},{8,7},{9,8},{10,9},{11,1... | collective-permute-start | bytes 1572872 | tf_op jit(solution)/shard_map/ppermute | solution.py:328
  130.1 1.6 copy-done.4
  131.7 14.5 %shard_map.123 = (f32[32,128,128]{2,1,0:T(8,128)S(1)}, f32[32,128,128]{2,1,0:T(8,128)}) custom-call(f32[32,128,128]{2,1,0:T(8,128)S(1)} %copy-done.4, f32[32,128,128]{2,1,0:T(8,128)S(1)} %copy-done.4, f32[32,128,128]{2,1,0:T(8,128)S(1)} %copy-done.4, f32[32,128,128]{2,1,0:T(8,128)} %get-tuple-element.17.refs_3_.refs_4_.refs_5_, ...), custom_call_target="tpu_custom_call" | custom-call | tf_op jit(solution)/shard_map/pallas_call | solution.py:287
  146.3 2.4 %collective-permute-start.13 = (f32[4,256,128]{2,1,0:T(8,128)S(1)}, f32[4,256,128]{2,1,0:T(8,128)S(1)}, u32[]{:S(2)}, u32[]{:S(2)}) collective-permute-start(f32[4,256,128]{2,1,0:T(8,128)S(1)} %pad_maximum_fusion.7), channel_id=1, source_target_pairs={{0,1},{1,2},{2,3},{3,4},{4,5},{5,6},{6,7},{7,8},{8,9},{9,10},{10,1... | collective-permute-start | bytes 1572872 | tf_op jit(solution)/shard_map/ppermute | solution.py:327
  149.0 11.4 %collective-permute-done.13 = f32[4,256,128]{2,1,0:T(8,128)S(1)} collective-permute-done((f32[4,256,128]{2,1,0:T(8,128)S(1)}, f32[4,256,128]{2,1,0:T(8,128)S(1)}, u32[]{:S(2)}, u32[]{:S(2)}) %collective-permute-start.13) | collective-permute-done | bytes 524320 | tf_op jit(solution)/shard_map/ppermute | solution.py:327
  160.7 6.1 %shard_map.124 = (f32[32,128,128]{2,1,0:T(8,128)S(1)}, f32[32,128,128]{2,1,0:T(8,128)}) custom-call(f32[24,128,128]{2,1,0:T(8,128)S(1)} %pad_maximum_fusion.2.refs_0_.refs_1_.refs_2_, f32[24,128,128]{2,1,0:T(8,128)S(1)} %pad_maximum_fusion.2.refs_0_.refs_1_.refs_2_, ...), custom_call_target="tpu_custom_call", output_to_operand_aliasing={{0}: (15, {}), {1}: (16, {})} | custom-call | tf_op jit(solution)/shard_map/pallas_call | solution.py:310
  166.8 1.7 %multiply_add_fusion = (f32[32,8,128]{2,1,0:T(8,128)}, f32[32,8,128]{2,1,0:T(8,128)}) fusion(f32[32,128,128]{2,1,0:T(8,128)S(1)} %get-tuple-element.20, s32[]{:T(128)S(6)} %select_n.154, f32[32,128,128]{2,1,0:T(8,128)} %refs_12_.3, f32[32,8,128]{2,1,0:T(8,128)S(1)} %copy-done.11, f32[32,128,128]{2,1,0:T(8,128)} %copy-done.3), kind=kLoop, calls=%fused_computation.42 | loop fusion | flops 131072 | bytes 786436 | tf_op jit(solution)/shard_map/add | solution.py:383
  (89 shorter events, 20.3 us)
Async XLA Ops:
  0.6 12.9 %copy-start.11 = (f32[32,8,128]{2,1,0:T(8,128)S(1)}, f32[32,8,128]{2,1,0:T(8,128)}, u32[]{:S(2)}) copy-start(f32[32,8,128]{2,1,0:T(8,128)} %param.10) | copy-start | bytes 393220
  1.4 11.5 %collective-permute-start = (f32[4,8,128]{2,1,0:T(8,128)S(1)}, f32[4,8,128]{2,1,0:T(8,128)S(1)}, u32[]{:S(2)}, u32[]{:S(2)}) collective-permute-start(f32[4,8,128]{2,1,0:T(8,128)S(1)} %get-tuple-element.46), channel_id=1, source_target_pairs={{0,1},{1,2},{2,3},{3,4},{4,5},{5,6},{6,7},{7,8},{8,9},{9,10},{10,1... | collective-permute-start | bytes 49160 | tf_op jit(solution)/shard_map/ppermute | solution.py:38
  3.3 13.0 %copy-start.12 = (f32[32,8,128]{2,1,0:T(8,128)S(1)}, f32[32,8,128]{2,1,0:T(8,128)}, u32[]{:S(2)}) copy-start(f32[32,8,128]{2,1,0:T(8,128)} %param.9) | copy-start | bytes 393220
  3.4 10.9 %collective-permute-start.1 = (f32[4,8,128]{2,1,0:T(8,128)S(1)}, f32[4,8,128]{2,1,0:T(8,128)S(1)}, u32[]{:S(2)}, u32[]{:S(2)}) collective-permute-start(f32[4,8,128]{2,1,0:T(8,128)S(1)} %get-tuple-element.47), channel_id=1, source_target_pairs={{1,0},{2,1},{3,2},{4,3},{5,4},{6,5},{7,6},{8,7},{9,8},{10,9},{11,1... | collective-permute-start | bytes 49160 | tf_op jit(solution)/shard_map/ppermute | solution.py:39
  17.1 10.5 %collective-permute-start.2 = (f32[72,8,128]{2,1,0:T(8,128)}, f32[72,8,128]{2,1,0:T(8,128)S(1)}, u32[]{:S(2)}, u32[]{:S(2)}) collective-permute-start(f32[72,8,128]{2,1,0:T(8,128)} %get-tuple-element.45), channel_id=1, source_target_pairs={{0,16},{16,0},{32,48},{48,32},{64,80},{80,64},{96,112},{112,96},{1... | collective-permute-start | bytes 884744 | tf_op jit(solution)/shard_map/ppermute | solution.py:53
  18.8 16.7 %collective-permute-start.12 = (f32[4,256,128]{2,1,0:T(8,128)}, f32[4,256,128]{2,1,0:T(8,128)S(1)}, u32[]{:S(2)}, u32[]{:S(2)}) collective-permute-start(f32[4,256,128]{2,1,0:T(8,128)} %pad_maximum_fusion.6), channel_id=1, source_target_pairs={{1,0},{2,1},{3,2},{4,3},{5,4},{6,5},{7,6},{8,7},{9,8},{10,9},{11,1... | collective-permute-start | bytes 1572872 | tf_op jit(solution)/shard_map/ppermute | solution.py:39
  25.1 14.4 %collective-permute-start.11 = (f32[4,256,128]{2,1,0:T(8,128)}, f32[4,256,128]{2,1,0:T(8,128)}, u32[]{:S(2)}, u32[]{:S(2)}) collective-permute-start(f32[4,256,128]{2,1,0:T(8,128)} %pad_maximum_fusion.5), channel_id=1, source_target_pairs={{0,1},{1,2},{2,3},{3,4},{4,5},{5,6},{6,7},{7,8},{8,9},{9,10},{10,1... | collective-permute-start | bytes 1572872 | tf_op jit(solution)/shard_map/ppermute | solution.py:38
  27.5 13.1 %copy-start = (f32[32,128,128]{2,1,0:T(8,128)S(1)}, f32[32,128,128]{2,1,0:T(8,128)}, u32[]{:S(2)}) copy-start(f32[32,128,128]{2,1,0:T(8,128)} %refs_6_.4) | copy-start | bytes 6291460
  28.7 36.6 %collective-permute-start.6 = (f32[72,16,128]{2,1,0:T(8,128)S(1)}, f32[72,16,128]{2,1,0:T(8,128)S(1)}, u32[]{:S(2)}, u32[]{:S(2)}) collective-permute-start(f32[72,16,128]{2,1,0:T(8,128)S(1)} %pad_maximum_fusion.4), channel_id=1, source_target_pairs={{0,32},{16,48},{32,64},{48,80},{64,96},{80,112},{96,128},{112,144}... | collective-permute-start | bytes 1769480 | tf_op jit(solution)/shard_map/ppermute | solution.py:62
  30.7 36.6 %collective-permute-start.3 = (f32[72,16,128]{2,1,0:T(8,128)S(1)}, f32[72,16,128]{2,1,0:T(8,128)S(1)}, u32[]{:S(2)}, u32[]{:S(2)}) collective-permute-start(f32[72,16,128]{2,1,0:T(8,128)S(1)} %pad_maximum_fusion.4), channel_id=1, source_target_pairs={{0,224},{16,240},{32,0},{48,16},{64,32},{80,48},{96,64},{112,80},{... | collective-permute-start | bytes 1769480 | tf_op jit(solution)/shard_map/ppermute | solution.py:63
  40.6 1.7 copy-start.6
  40.6 1.7 copy-start.7
  42.3 10.3 %copy-start.10 = (f32[1,32,128,128]{3,2,1,0:T(8,128)S(1)}, f32[1,32,128,128]{3,2,1,0:T(8,128)}, u32[]{:S(2)}) copy-start(f32[1,32,128,128]{3,2,1,0:T(8,128)} %param.15) | copy-start | bytes 6291460
  52.6 2.1 %copy-start.1 = (f32[32,128,128]{2,1,0:T(8,128)}, f32[32,128,128]{2,1,0:T(8,128)S(1)}, u32[]{:S(2)}) copy-start(f32[32,128,128]{2,1,0:T(8,128)S(1)} %get-tuple-element.13.refs_3_.g0_ref.refs_7_) | copy-start | bytes 6291460
  52.6 2.8 %copy-start.2 = (f32[32,128,128]{2,1,0:T(8,128)}, f32[32,128,128]{2,1,0:T(8,128)S(1)}, u32[]{:S(2)}) copy-start(f32[32,128,128]{2,1,0:T(8,128)S(1)} %get-tuple-element.14.refs_4_.g1_ref.refs_8_) | copy-start | bytes 6291460
  65.3 37.2 %copy-start.5 = (f32[32,128,128]{2,1,0:T(8,128)}, f32[32,128,128]{2,1,0:T(8,128)S(1)}, u32[]{:S(2)}) copy-start(f32[32,128,128]{2,1,0:T(8,128)S(1)} %shard_map.121.part_ref) | copy-start | bytes 6291460
  65.3 20.0 %collective-permute-start.7 = (f32[72,16,128]{2,1,0:T(8,128)S(1)}, f32[72,16,128]{2,1,0:T(8,128)S(1)}, u32[]{:S(2)}, u32[]{:S(2)}) collective-permute-start(f32[72,16,128]{2,1,0:T(8,128)S(1)} %collective-permute-done.6), channel_id=1, source_target_pairs={{0,32},{16,48},{32,64},{48,80},{64,96},{80,112},{96,128},{112,144}... | collective-permute-start | bytes 1769480 | tf_op jit(solution)/shard_map/ppermute | solution.py:62
  67.3 18.0 %collective-permute-start.4 = (f32[72,16,128]{2,1,0:T(8,128)S(1)}, f32[72,16,128]{2,1,0:T(8,128)S(1)}, u32[]{:S(2)}, u32[]{:S(2)}) collective-permute-start(f32[72,16,128]{2,1,0:T(8,128)S(1)} %collective-permute-done.3), channel_id=1, source_target_pairs={{0,224},{16,240},{32,0},{48,16},{64,32},{80,48},{96,64},{112,80},{... | collective-permute-start | bytes 1769480 | tf_op jit(solution)/shard_map/ppermute | solution.py:63
  85.4 13.5 %collective-permute-start.8 = (f32[72,16,128]{2,1,0:T(8,128)S(1)}, f32[72,16,128]{2,1,0:T(8,128)S(1)}, u32[]{:S(2)}, u32[]{:S(2)}) collective-permute-start(f32[72,16,128]{2,1,0:T(8,128)S(1)} %collective-permute-done.7), channel_id=1, source_target_pairs={{0,32},{16,48},{32,64},{48,80},{64,96},{80,112},{96,128},{112,144}... | collective-permute-start | bytes 1769480 | tf_op jit(solution)/shard_map/ppermute | solution.py:62
  85.4 13.6 %collective-permute-start.5 = (f32[72,16,128]{2,1,0:T(8,128)S(1)}, f32[72,16,128]{2,1,0:T(8,128)S(1)}, u32[]{:S(2)}, u32[]{:S(2)}) collective-permute-start(f32[72,16,128]{2,1,0:T(8,128)S(1)} %collective-permute-done.4), channel_id=1, source_target_pairs={{0,224},{16,240},{32,0},{48,16},{64,32},{80,48},{96,64},{112,80},{... | collective-permute-start | bytes 1769480 | tf_op jit(solution)/shard_map/ppermute | solution.py:63
  98.9 8.0 %collective-permute-start.9 = (f32[36,16,128]{2,1,0:T(8,128)S(1)}, f32[36,16,128]{2,1,0:T(8,128)S(1)}, u32[]{:S(2)}, u32[]{:S(2)}) collective-permute-start(f32[36,16,128]{2,1,0:T(8,128)S(1)} %slice.286), channel_id=1, source_target_pairs={{0,32},{16,48},{32,64},{48,80},{64,96},{80,112},{96,128},{112,144}... | collective-permute-start | bytes 884744 | tf_op jit(solution)/shard_map/ppermute | solution.py:68
  99.0 7.9 %collective-permute-start.10 = (f32[36,16,128]{2,1,0:T(8,128)S(1)}, f32[36,16,128]{2,1,0:T(8,128)S(1)}, u32[]{:S(2)}, u32[]{:S(2)}) collective-permute-start(f32[36,16,128]{2,1,0:T(8,128)S(1)} %slice.287), channel_id=1, source_target_pairs={{0,224},{16,240},{32,0},{48,16},{64,32},{80,48},{96,64},{112,80},{... | collective-permute-start | bytes 884744 | tf_op jit(solution)/shard_map/ppermute | solution.py:68
  112.5 1.5 copy-start.9
  126.8 1.4 copy-start.3
  128.2 20.7 %collective-permute-start.14 = (f32[4,256,128]{2,1,0:T(8,128)S(1)}, f32[4,256,128]{2,1,0:T(8,128)S(1)}, u32[]{:S(2)}, u32[]{:S(2)}) collective-permute-start(f32[4,256,128]{2,1,0:T(8,128)S(1)} %pad_maximum_fusion.8), channel_id=1, source_target_pairs={{1,0},{2,1},{3,2},{4,3},{5,4},{6,5},{7,6},{8,7},{9,8},{10,9},{11,1... | collective-permute-start | bytes 1572872 | tf_op jit(solution)/shard_map/ppermute | solution.py:328
  130.1 1.6 copy-start.4
  131.7 16.9 %copy-start.8 = (f32[32,128,128]{2,1,0:T(8,128)S(1)}, f32[32,128,128]{2,1,0:T(8,128)}, u32[]{:S(2)}) copy-start(f32[32,128,128]{2,1,0:T(8,128)} %get-tuple-element.17.refs_3_.refs_4_.refs_5_) | copy-start | bytes 6291460
  146.3 14.1 %collective-permute-start.13 = (f32[4,256,128]{2,1,0:T(8,128)S(1)}, f32[4,256,128]{2,1,0:T(8,128)S(1)}, u32[]{:S(2)}, u32[]{:S(2)}) collective-permute-start(f32[4,256,128]{2,1,0:T(8,128)S(1)} %pad_maximum_fusion.7), channel_id=1, source_target_pairs={{0,1},{1,2},{2,3},{3,4},{4,5},{5,6},{6,7},{7,8},{8,9},{9,10},{10,1... | collective-permute-start | bytes 1572872 | tf_op jit(solution)/shard_map/ppermute | solution.py:327
